TPU v7x, 32 devices: a whole 2x2x4 slice. The times are simulated.
32 devices in a mesh: groups: 2 (over x), seq: 16 (over z, y, core).
Axes of the slice: x: 2, y: 2, z: 4, core: 2. Of those that a mesh axis runs over, the one named last changes fastest.
Arguments:
- clean: bfloat16 [8192, 2048], P(('groups', 'seq')), parts along dimension 0, may hold values from -6 to 6
- delta: bfloat16 [8192, 2048], P(('groups', 'seq')), parts along dimension 0, may hold values from -0.25 to 0.25
- cotangent: bfloat16 [8192, 1024], P(('groups', 'seq')), parts along dimension 0, may hold values from -6 to 6
- w_query: bfloat16 [2048, 1024], P('seq'), may hold values from -0.125 to 0.125
- w_key: bfloat16 [2048, 1024], P('seq'), may hold values from -0.125 to 0.125
- w_value: bfloat16 [2048, 1024], P('seq'), may hold values from -0.125 to 0.125
- masks: int32 [32, 2, 2], P(('groups', 'seq')), parts along dimension 0, may hold values 0 or 1
Outputs:
- output: bfloat16 [8192, 1024], P(('groups', 'seq')), parts along dimension 0
- grad_input: bfloat16 [8192, 2048], P(('groups', 'seq')), parts along dimension 0
There are 2 independent parts, one for each index of `groups`. A program takes and returns all parts, laid end to end along the dimension named above; an argument that names none is the same for every part. Nothing has to cross between parts.
All inputs are finite; a program needn't handle non-finite values. No bound on the sum of `masks` on one device may be relied on, other than what follows from the above.
Results may differ from a plain program's by a relative error of at most 0.012.
Values may be sent and summed in bfloat16 or wider, within the bound.
No kernel may reach another device: no remote copies, remote signals or barrier semaphores. Data moves between devices by JAX's collectives and lax.ppermute only.
A program may use at most 128 MiB of HBM per device.

v0:
```python
import jax
import jax.numpy as jnp
from jax import lax
from jax.sharding import PartitionSpec as P

NH = 8
DH = 128
BLK = 128


EPSILON = 1e-06


def carried_in(shard, axis, combine, identity, reverse):
    peers, index = (lax.axis_size(axis), lax.axis_index(axis))
    everything = lax.all_gather(shard, axis)
    start = jnp.broadcast_to(jnp.asarray(identity, shard.dtype), shard.shape)

    def turn(k, before):
        at = peers - 1 - k if reverse else k
        reached = at > index if reverse else at < index
        new = combine(before, everything[at])
        return jnp.where(reached, new, before)

    return lax.fori_loop(0, peers, turn, start)


def allowed_pairs(blocks, width):
    count = blocks.shape[0]
    row = jnp.arange(count)[:, None]
    col = jnp.arange(count)[None, :]
    inner_row = jnp.arange(width)[:, None]
    inner_col = jnp.arange(width)[None, :]
    lower = (row > col).astype(jnp.float32)[:, :, None, None]
    same = (row == col).astype(jnp.float32)[:, :, None, None] * (inner_row >= inner_col).astype(
        jnp.float32
    )[None, None]
    return blocks.astype(jnp.float32)[:, :, None, None] * (lower + same)


def add_states(earlier, later_one):
    return earlier + later_one


def on_device(clean, delta, cotangent, w_query, w_key, w_value, masks):
    tok_rows = clean.shape[0]
    features = w_query.shape[1]
    blocks_here = tok_rows // BLK
    f32 = jnp.float32
    x_in = (clean.astype(f32) + delta.astype(f32)).astype(jnp.bfloat16)
    w_cat = jnp.concatenate([w_query, w_key, w_value], axis=1)
    full_weights = lax.all_gather(w_cat, "seq", axis=0, tiled=True)
    projected = jnp.dot(x_in, full_weights, preferred_element_type=f32)
    projected = projected.astype(jnp.bfloat16)
    query = projected[:, :features].reshape(blocks_here, BLK, NH, DH)
    key = projected[:, features : 2 * features].reshape(blocks_here, BLK, NH, DH)
    value = projected[:, 2 * features :].reshape(blocks_here, BLK, NH, DH)
    zero_state = jnp.zeros((NH, DH, DH), f32)
    state_local = jnp.einsum("ibhd,ibhe->hde", key, value, preferred_element_type=f32)
    state = carried_in(state_local, "seq", add_states, zero_state, False)
    state_b = state.astype(jnp.bfloat16)
    allow = allowed_pairs(masks[0], BLK)
    scores = jnp.einsum("ibhd,jchd->hijbc", query, key, preferred_element_type=f32)
    attn = (scores * allow).astype(jnp.bfloat16)
    mixed = jnp.einsum("hijbc,jchd->ibhd", attn, value, preferred_element_type=f32)
    mixed = mixed + jnp.einsum("ibhd,hde->ibhe", query, state_b, preferred_element_type=f32)
    root = jnp.sqrt(jnp.mean(mixed * mixed, axis=-1, keepdims=True) + EPSILON)
    normed = mixed / root
    output = normed.astype(jnp.bfloat16).reshape(tok_rows, features)
    grad_out = cotangent.astype(f32).reshape(blocks_here, BLK, NH, DH)
    d_mixed = (grad_out - normed * jnp.mean(grad_out * normed, axis=-1, keepdims=True)) / root
    d_mixed_b = d_mixed.astype(jnp.bfloat16)
    grad_local = jnp.einsum("ibhd,ibhe->hde", query, d_mixed_b, preferred_element_type=f32)
    later = carried_in(grad_local, "seq", add_states, zero_state, True)
    later_b = later.astype(jnp.bfloat16)
    d_attn = (
        jnp.einsum("ibhe,jche->hijbc", d_mixed_b, value, preferred_element_type=f32) * allow
    ).astype(jnp.bfloat16)
    d_query = jnp.einsum("hijbc,jchd->ibhd", d_attn, key, preferred_element_type=f32)
    d_query = d_query + jnp.einsum("ibhe,hde->ibhd", d_mixed_b, state_b, preferred_element_type=f32)
    d_key = jnp.einsum("hijbc,ibhd->jchd", d_attn, query, preferred_element_type=f32)
    d_key = d_key + jnp.einsum("jche,hde->jchd", value, later_b, preferred_element_type=f32)
    d_value = jnp.einsum("hijbc,ibhe->jche", attn, d_mixed_b, preferred_element_type=f32)
    d_value = d_value + jnp.einsum("jchd,hde->jche", key, later_b, preferred_element_type=f32)
    d_proj = jnp.concatenate(
        [
            d_query.reshape(tok_rows, features),
            d_key.reshape(tok_rows, features),
            d_value.reshape(tok_rows, features),
        ],
        axis=1,
    ).astype(jnp.bfloat16)
    grad_input = lax.dot_general(
        d_proj, full_weights, (((1,), (1,)), ((), ())), preferred_element_type=f32
    )
    return (output, grad_input.astype(jnp.bfloat16))


def solution(mesh):
    return jax.shard_map(
        on_device,
        mesh=mesh,
        in_specs=(
            P(("groups", "seq"), None),
            P(("groups", "seq"), None),
            P(("groups", "seq"), None),
            P("seq", None),
            P("seq", None),
            P("seq", None),
            P(("groups", "seq"), None, None),
        ),
        out_specs=(P(("groups", "seq"), None), P(("groups", "seq"), None)),
        check_vma=False,
    )
```

profile of v0, /device:TPU:15, one launch (start us, length us, event | category | flops | bytes accessed | tf_op | source)
XLA Modules:
  0.0 331.7 jit_solution(9458282480844987957)
XLA Ops:
  7.2 2.2 pad_maximum_fusion
  9.5 101.5 %all-gather.6.cloned.1.call-done = bf16[2048,3072]{1,0:T(8,128)(2,1)} async-done(((bf16[128,3072]{1,0:T(8,128)(2,1)}), bf16[2048,3072]{1,0:T(8,128)(2,1)}) %all-gather.6.cloned.1.call-update) | async-done | bytes 12582928 | tf_op jit(solution)/shard_map/all_gather | solution.py:52
  111.0 8.0 %convolution_convert_fusion = bf16[256,3072]{1,0:T(8,128)(2,1)S(1)} fusion(bf16[2048,3072]{1,0:T(8,128)(2,1)} %all-gather.6.cloned.1.call-done, bf16[256,2048]{1,0:T(8,128)(2,1)S(1)} %copy-done.12, bf16[256,2048]{1,0:T(8,128)(2,1)S(1)} %copy-done.13), kind=kOutput, calls=%fused_computation.2 | convolution fusion | flops 3224109056 | bytes 16252928 | tf_op jit(solution)/shard_map/dot_general | solution.py:53
  123.1 1.6 copy.70
  126.6 1.4 copy.101
  128.8 2.2 copy.96
  131.0 2.1 copy.79
  133.2 1.7 fusion.1
  135.9 1.3 convolution_bitcast_fusion
  137.2 57.2 %all-gather.8.cloned.1.call-done = f32[128,128,128]{2,1,0:T(8,128)} async-done(((f32[8,128,128]{2,1,0:T(8,128)}), f32[128,128,128]{2,1,0:T(8,128)}) %all-gather.8.cloned.1.call-update) | async-done | bytes 8388624 | tf_op jit(solution)/shard_map/all_gather | solution.py:16
  194.4 20.1 %while.30 = (s32[]{:T(128)}, f32[8,128,128]{2,1,0:T(8,128)S(1)}, s32[]{:T(128)}, f32[16,8,128,128]{3,2,1,0:T(8,128)}, s32[]{:T(128)}, /*index=5*/s32[]{:T(128)}) while((s32[]{:T(128)}, f32[8,128,128]{2,1,0:T(8,128)S(1)}, s32[]{:T(128)}, f32[16,8,128,128]{3,2,1,0:T(8,128)}, s32[]{:T(128)}, /*index=5*/s32[]{:T(128)}) %tuple.88), condition=%wide.region_1.2_spmd.clone, body=%wide.region_0.1_spmd.clone.sunk | while | flops 393220 | bytes 1572957 | solution.py:25
  194.4 1.3 add_select_fusion.4
  195.7 1.2 add_select_fusion.4
  197.0 1.2 add_select_fusion.4
  198.2 1.2 add_select_fusion.4
  199.5 1.2 add_select_fusion.4
  200.7 1.2 add_select_fusion.4
  214.5 1.6 multiply_reduce_fusion.1
  218.6 1.5 fusion
  220.0 1.4 convolution_bitcast_fusion.3
  222.5 2.2 copy.76
  224.6 1.9 copy.159
  226.6 2.1 copy.68
  228.7 2.0 copy.160
  230.7 1.4 convolution_bitcast_fusion.2
  232.7 59.2 %all-gather.10.cloned.1.call-done = f32[128,128,128]{2,1,0:T(8,128)} async-done(((f32[8,128,128]{2,1,0:T(8,128)}), f32[128,128,128]{2,1,0:T(8,128)}) %all-gather.10.cloned.1.call-update) | async-done | bytes 8388624 | tf_op jit(solution)/shard_map/all_gather | solution.py:16
  291.8 20.2 %while.31 = (s32[]{:T(128)}, f32[8,128,128]{2,1,0:T(8,128)S(1)}, s32[]{:T(128)}, f32[16,8,128,128]{3,2,1,0:T(8,128)}, s32[]{:T(128)}, /*index=5*/s32[]{:T(128)}, s32[]{:T(128)}, s32[]{:T(128)}) while((s32[]{:T(128)}, f32[8,128,128]{2,1,0:T(8,128)S(1)}, s32[]{:T(128)}, f32[16,8,128,128]{3,2,1,0:T(8,128)}, s32[]{:T(128)}, ...), condition=%wide.region_5.6_spmd.clone, body=%wide.region_4.5_spmd.clone.sunk | while | flops 393224 | bytes 1573019 | solution.py:25
  291.8 1.3 add_select_fusion.5
  293.2 1.2 add_select_fusion.5
  294.4 1.2 add_select_fusion.5
  312.0 1.5 fusion.12
  316.2 9.0 %convolution_convert_fusion.1 = bf16[256,2048]{1,0:T(8,128)(2,1)} fusion(bf16[2048,3072]{1,0:T(8,128)(2,1)} %all-gather.6.cloned.1.call-done, bf16[256,1024]{1,0:T(8,128)(2,1)S(1)} %bitcast.167, bf16[256,1024]{1,0:T(8,128)(2,1)S(1)} %bitcast.166, bf16[256,1024]{1,0:T(8,128)(2,1)S(1)} %bitcast.165), kind=kOutput, calls=%fused_computation.3 | convolution fusion | flops 3226468352 | bytes 15204352 | tf_op jit(solution)/shard_map/dot_general | solution.py:93
  (86 shorter events, 42.8 us)
Async XLA Ops:
  7.2 103.8 %copy-start.13 = (bf16[256,2048]{1,0:T(8,128)(2,1)S(1)}, bf16[256,2048]{1,0:T(8,128)(2,1)}, u32[]{:S(2)}) copy-start(bf16[256,2048]{1,0:T(8,128)(2,1)} %param.11) | copy-start | bytes 3145732
  7.2 103.8 %copy-start.12 = (bf16[256,2048]{1,0:T(8,128)(2,1)S(1)}, bf16[256,2048]{1,0:T(8,128)(2,1)}, u32[]{:S(2)}) copy-start(bf16[256,2048]{1,0:T(8,128)(2,1)} %param.12) | copy-start | bytes 3145732
  7.2 103.8 %all-gather.6.cloned.1.call-start = ((), (), s32[]{:S(2)}) async-start(), calls=%async_computation | async-start | bytes 13369344 | tf_op jit(solution)/shard_map/all_gather | solution.py:52
  9.4 185.0 %all-gather.8.cloned.1.call-start = ((), (), s32[]{:S(2)}) async-start(), calls=%async_computation.1 | async-start | bytes 8912896 | tf_op jit(solution)/shard_map/all_gather | solution.py:16
  119.1 1.6 copy-start.11
  119.3 13.8 %copy-start.2 = (bf16[32,8,8,128]{3,2,1,0:T(8,128)(2,1)}, bf16[32,8,8,128]{3,2,1,0:T(8,128)(2,1)S(1)}, u32[]{:S(2)}) copy-start(bf16[32,8,8,128]{3,2,1,0:T(8,128)(2,1)S(1)} %copy.131) | copy-start | bytes 1572868
  120.5 171.4 %all-gather.10.cloned.1.call-start = ((), (), s32[]{:S(2)}) async-start(), calls=%async_computation.2 | async-start | bytes 8912896 | tf_op jit(solution)/shard_map/all_gather | solution.py:16
  124.9 0.8 copy-start.8
  127.9 5.2 %copy-start.4 = (bf16[2,128,8,128,1]{1,3,0,4,2:T(8,128)(2,1)}, bf16[2,128,8,128,1]{1,3,0,4,2:T(8,128)(2,1)S(1)}, u32[]{:S(2)}) copy-start(bf16[2,128,8,128,1]{1,3,0,4,2:T(8,128)(2,1)S(1)} %copy.101) | copy-start | bytes 1572868
  133.2 1.7 copy-start.6
  134.9 1.0 copy-start
  194.4 20.1 %copy-start.7 = (bf16[2,128,8,128]{1,3,0,2:T(8,128)(2,1)S(1)}, bf16[2,128,8,128]{1,3,0,2:T(8,128)(2,1)}, u32[]{:S(2)}) copy-start(bf16[2,128,8,128]{1,3,0,2:T(8,128)(2,1)} %copy.79) | copy-start | bytes 1572868
  222.5 8.3 %copy-start.5 = (bf16[2,128,8,128,1]{1,3,0,4,2:T(8,128)(2,1)S(1)}, bf16[2,128,8,128,1]{1,3,0,4,2:T(8,128)(2,1)}, u32[]{:S(2)}) copy-start(bf16[2,128,8,128,1]{1,3,0,4,2:T(8,128)(2,1)} %copy-done.4) | copy-start | bytes 1572868
  228.7 3.5 %copy-start.1 = (bf16[8,2,2,128,128]{3,4,1,2,0:T(8,128)(2,1)S(1)}, bf16[8,2,2,128,128]{3,4,1,2,0:T(8,128)(2,1)}, u32[]{:S(2)}) copy-start(bf16[8,2,2,128,128]{3,4,1,2,0:T(8,128)(2,1)} %copy-done) | copy-start | bytes 3145732
  291.8 20.2 %copy-start.3 = (bf16[32,8,8,128]{3,2,1,0:T(8,128)(2,1)S(1)}, bf16[32,8,8,128]{3,2,1,0:T(8,128)(2,1)}, u32[]{:S(2)}) copy-start(bf16[32,8,8,128]{3,2,1,0:T(8,128)(2,1)} %copy-done.2) | copy-start | bytes 1572868
  314.8 1.0 copy-start.9
  315.1 1.1 copy-start.10
Sparse Core Ops, SparseCore 0:
  10.9 100.0 all-gather.5
  120.6 73.7 all-gather.7
  218.7 73.1 all-gather.9
where the time goes:
time: 337 us; the launch traced here: 332 us
  waiting for transfers between devices  218 us (65%)
  other arithmetic  44.2 us (13%)
  matrix products  31.5 us (9%)
  local copies, waits for them, and re-layouts  22.9 us (7%)
  between operations  14.1 us (4%)
    all_gather x2, waiting for transfers between devices, carried_in(): everything = lax.all_gather(shard, axis)  116 us
    all_gather x1, waiting for transfers between devices, on_device(): full_weights = lax.all_gather(w_cat, 'seq', axis=0, tiled=True)  101 us
    select_n x32, other arithmetic, turn(): return jnp.where(reached, new, before)  39.4 us
    unnamed x37, local copies, waits for them, and re-layouts  9 us
    dot_general x1, matrix products, on_device(): lax.dot_general(d_proj, full_weights, (((1,), (1,)), ((), ())), preferred...  8.99 us
    dot_general x1, matrix products, on_device(): projected = jnp.dot(x_in, full_weights, preferred_element_type=f32)  7.98 us
  transfers between devices with their start and end apart: 3, of which 3 were waited for; matrix products, arithmetic and copies ran while one was open for 9% of the time, Pallas kernels for 0%

commit v1 on v0

v1 whole, which is shorter than its diff:
```python
import jax
import jax.numpy as jnp
import numpy as np
from jax import lax
from jax.sharding import Mesh
from jax.sharding import PartitionSpec as P

DH = 128
BLK = 128

EPSILON = 1e-06

TOKENS = ("groups", "chip", "core")


def dense_allow(block_masks, tokens):
    blk = jnp.arange(tokens) // BLK
    gate = block_masks.astype(jnp.float32)[blk[:, None], blk[None, :]]
    causal = (jnp.arange(tokens)[None, :] <= jnp.arange(tokens)[:, None]).astype(jnp.float32)
    return gate * causal


def on_device(clean, delta, cotangent, w_query, w_key, w_value, masks):
    f32, bf16 = jnp.float32, jnp.bfloat16
    tok = clean.shape[0]
    feat = w_query.shape[1]
    half = feat // 2
    heads = half // DH
    k = lax.axis_index("core")
    c = lax.axis_index("chip")
    chips = lax.axis_size("chip")

    x_in = (clean.astype(f32) + delta.astype(f32)).astype(bf16)
    x_pair = lax.all_gather(x_in, "core", axis=0, tiled=True)

    def by_half(w):
        return w.reshape(w.shape[0], 2, half)

    w_loc = jnp.concatenate([by_half(w_query), by_half(w_key), by_half(w_value)], axis=2)
    w_loc = jnp.swapaxes(w_loc, 0, 1)
    w_chip = lax.all_to_all(w_loc, "core", 0, 0)
    w_chip = w_chip.reshape(-1, 3 * half)
    w_half = lax.all_gather(w_chip, "chip", axis=0, tiled=True)

    projected = jnp.dot(x_pair, w_half, preferred_element_type=f32).astype(bf16)
    projected = projected.reshape(2, tok, 3, heads, DH)
    query = projected[:, :, 0]
    key = projected[:, :, 1]
    value = projected[:, :, 2]

    local = jnp.einsum("jthd,jthe->jhde", key, value, preferred_element_type=f32)
    chip_total = local[0] + local[1]
    every = lax.all_gather(chip_total, "chip")
    before = (jnp.arange(chips) < c)[:, None, None, None]
    state0 = jnp.sum(jnp.where(before, every, 0.0), axis=0)
    state = jnp.stack([state0, state0 + local[0]])
    state_b = state.astype(bf16)

    pair_masks = lax.all_gather(masks[0], "core")
    allow = jax.vmap(dense_allow, in_axes=(0, None))(pair_masks, tok)

    scores = jnp.einsum("jthd,jshd->jhts", query, key, preferred_element_type=f32)
    attn = (scores * allow[:, None]).astype(bf16)
    mixed = jnp.einsum("jhts,jshd->jthd", attn, value, preferred_element_type=f32)
    mixed = mixed + jnp.einsum("jthd,jhde->jthe", query, state_b, preferred_element_type=f32)
    root = jnp.sqrt(jnp.mean(mixed * mixed, axis=-1, keepdims=True) + EPSILON)
    normed = mixed / root

    out_b = normed.astype(bf16).reshape(2, tok, half)
    out_b = lax.all_to_all(out_b, "core", 0, 0)
    output = jnp.swapaxes(out_b, 0, 1).reshape(tok, feat)

    cot = jnp.swapaxes(cotangent.reshape(tok, 2, half), 0, 1)
    cot = lax.all_to_all(cot, "core", 0, 0)
    grad_out = cot.astype(f32).reshape(2, tok, heads, DH)
    d_mixed = (grad_out - normed * jnp.mean(grad_out * normed, axis=-1, keepdims=True)) / root
    d_mixed_b = d_mixed.astype(bf16)
    grad_local = jnp.einsum("jthd,jthe->jhde", query, d_mixed_b, preferred_element_type=f32)

    grad_total = grad_local[0] + grad_local[1]
    every_g = lax.all_gather(grad_total, "chip")
    after = (jnp.arange(chips) > c)[:, None, None, None]
    later1 = jnp.sum(jnp.where(after, every_g, 0.0), axis=0)
    later = jnp.stack([later1 + grad_local[1], later1])
    later_b = later.astype(bf16)

    d_attn = (
        jnp.einsum("jthe,jshe->jhts", d_mixed_b, value, preferred_element_type=f32) * allow[:, None]
    ).astype(bf16)
    d_query = jnp.einsum("jhts,jshd->jthd", d_attn, key, preferred_element_type=f32)
    d_query = d_query + jnp.einsum("jthe,jhde->jthd", d_mixed_b, state_b, preferred_element_type=f32)
    d_key = jnp.einsum("jhts,jthd->jshd", d_attn, query, preferred_element_type=f32)
    d_key = d_key + jnp.einsum("jshe,jhde->jshd", value, later_b, preferred_element_type=f32)
    d_value = jnp.einsum("jhts,jthe->jshe", attn, d_mixed_b, preferred_element_type=f32)
    d_value = d_value + jnp.einsum("jshd,jhde->jshe", key, later_b, preferred_element_type=f32)
    d_proj = jnp.stack([d_query, d_key, d_value], axis=2).astype(bf16).reshape(2 * tok, 3 * half)

    partial = lax.dot_general(d_proj, w_half, (((1,), (1,)), ((), ())), preferred_element_type=f32)
    partial = partial.reshape(2, tok, -1)
    mine = jnp.where(k == 0, partial[0], partial[1])
    theirs = jnp.where(k == 0, partial[1], partial[0])
    received = lax.ppermute(theirs, "core", [(0, 1), (1, 0)])
    grad_input = (mine + received).astype(bf16)
    return (output, grad_input)


def solution(mesh):
    groups = mesh.shape["groups"]
    seq = mesh.shape["seq"]
    devices = np.asarray(mesh.devices).reshape(groups, seq // 2, 2)
    inner = Mesh(devices, TOKENS)
    rows = P(TOKENS, None)
    weights = P(("chip", "core"), None)
    return jax.shard_map(
        on_device,
        mesh=inner,
        in_specs=(rows, rows, rows, weights, weights, weights, P(TOKENS, None, None)),
        out_specs=(rows, rows),
        check_vma=False,
    )
```

time: 337 us -> 815 us (2.42)
  local copies, waits for them, and re-layouts: 22.9 us -> 593 us
  waiting for transfers between devices: 218 us -> 147 us
  other arithmetic: 44.2 us -> 18.4 us
  blocking collectives: 0 us -> 10.8 us
  matrix products: 31.5 us -> 22.7 us
    gather x0 -> x2, local copies, waits for them, and re-layouts: none -> 580 us  [dense_allow(): gate = block_masks.astype(jnp.float32)[blk[:, None], blk[None, :]]]
    all_gather x3 -> x4, waiting for transfers between devices: 218 us -> 146 us  [the longest x1 98.5 us: on_device(): w_half = lax.all_gather(w_chip, 'chip', axis=0, tiled=True)]
    select_n x32 -> x1, other arithmetic: 39.4 us -> 1.65 us  [on_device(): theirs = jnp.where(k == 0, partial[1], partial[0])]
    dot_general x14, matrix products: 31.5 us -> 22.7 us  [the longest x1 6.83 us: on_device(): projected = jnp.dot(x_pair, w_half, preferred_element_type=f32).astype(bf16)]
    all_to_all x0 -> x2, blocking collectives: none -> 8.83 us  [the longest x1 4.67 us: on_device(): w_chip = lax.all_to_all(w_loc, 'core', 0, 0)]
    convert_element_type x4 -> x5, other arithmetic: 1.12 us -> 9.41 us  [the longest x1 4.27 us: on_device(): grad_input = (mine + received).astype(bf16)]
  transfers between devices with their start and end apart: 3 -> 6, of which waited for: 3 -> 3; matrix products, arithmetic and copies ran while one was open for 9% -> 73% of each run, Pallas kernels for 0% -> 0%
where the time goes in v1:
time: 815 us; the launch traced here: 812 us
  local copies, waits for them, and re-layouts  593 us (73%)
  waiting for transfers between devices  147 us (18%)
  matrix products  22.7 us (3%)
  other arithmetic  18.4 us (2%)
  between operations  14.2 us (2%)
  blocking collectives  10.8 us (1%)
    gather x2, local copies, waits for them, and re-layouts, dense_allow(): gate = block_masks.astype(jnp.float32)[blk[:, None], blk[None, :]]  580 us
    all_gather x1, waiting for transfers between devices, on_device(): w_half = lax.all_gather(w_chip, 'chip', axis=0, tiled=True)  98.5 us
    all_gather x1, waiting for transfers between devices, on_device(): every_g = lax.all_gather(grad_total, 'chip')  42 us
  transfers between devices with their start and end apart: 6, of which 3 were waited for; matrix products, arithmetic and copies ran while one was open for 73% of the time, Pallas kernels for 0%

profile of v1, /device:TPU:15, one launch (start us, length us, event | category | flops | bytes accessed | tf_op | source)
XLA Modules:
  0.0 812.0 jit_solution(685270762797420210)
XLA Ops:
  7.2 3.0 add_convert_fusion.1
  10.9 4.7 all_to_all.15
  15.6 1.2 copy.75
  16.8 6.0 all-gather.5.cloned.1.call-done
  22.8 98.5 %all-gather.7.cloned.1.call-done = bf16[2048,1536]{1,0:T(8,128)(2,1)} async-done(((bf16[256,1536]{1,0:T(8,128)(2,1)}), bf16[2048,1536]{1,0:T(8,128)(2,1)}) %all-gather.7.cloned.1.call-update) | async-done | bytes 6291472 | tf_op jit(solution)/shard_map/all_gather | solution.py:43
  121.3 6.8 convolution_convert_fusion
  128.5 1.3 fusion.28
  129.8 1.3 copy.110
  133.1 1.0 copy.109
  134.1 5.0 all-to-all-start.2
  139.1 2.0 all_gather.19
  141.4 560.9 %gather_fusion = f32[65536,2]{1,0:T(8,128)} fusion(f32[2,2,2]{0,2,1:T(2,128)S(1)} %convert_element_type.49, s32[65536]{0:T(1024)S(1)} %bitcast.83), kind=kCustom, calls=%fused_computation | custom fusion | bytes 1572864 | tf_op jit(solution)/shard_map/vmap()/gather | solution.py:18
  702.4 18.8 %copy.80 = f32[256,256,2]{1,0,2:T(8,128)S(1)} copy(f32[256,256,2]{2,1,0:T(8,128)} %bitcast.84) | data formatting | bytes 1048576 | tf_op jit(solution)/shard_map/vmap()/gather | solution.py:18
  722.5 1.5 fusion.14
  723.9 2.0 select_reduce_fusion.1
  726.0 1.3 multiply_reduce_fusion
  727.4 1.6 fusion.7
  729.1 2.2 fusion.9
  733.2 1.5 multiply_convert_fusion
  735.2 1.1 fusion.6
  736.3 1.3 fusion.29
  737.6 1.4 fusion.17
  738.9 42.0 %all-gather.11.cloned.1.call-done = f32[8,4,128,128]{3,2,1,0:T(8,128)} async-done(((f32[1,4,128,128]{3,2,1,0:T(8,128)}), f32[8,4,128,128]{3,2,1,0:T(8,128)}) %all-gather.11.cloned.1.call-update) | async-done | bytes 2097168 | tf_op jit(solution)/shard_map/all_gather | solution.py:81
  780.9 1.9 select_reduce_fusion
  784.4 1.3 copy.95
  786.4 5.6 fusion.30
  792.0 1.6 slice_select_fusion
  793.6 0.9 copy-done
  794.5 1.5 collective-permute-start
  796.1 4.2 all_to_all.16
  800.2 1.0 copy.108
  801.2 4.3 add_convert_fusion
  (76 shorter events, 9.5 us)
Async XLA Ops:
  7.2 3.1 copy-start.14
  7.2 3.3 copy-start.15
  7.2 3.5 copy-start.16
  7.2 15.6 %all-gather.5.cloned.1.call-start = ((), (), s32[]{:S(2)}) async-start(), calls=%async_computation.3 | async-start | bytes 3145728 | tf_op jit(solution)/shard_map/all_gather | solution.py:34
  10.2 111.0 %all-gather.7.cloned.1.call-start = ((), (), s32[]{:S(2)}) async-start(), calls=%async_computation.4 | async-start | bytes 7077888 | tf_op jit(solution)/shard_map/all_gather | solution.py:43
  16.8 707.2 %all-gather.9.cloned.1.call-start = ((), (), s32[]{:S(2)}) async-start(), calls=%async_computation.5 | async-start | bytes 2359296 | tf_op jit(solution)/shard_map/all_gather | solution.py:53
  129.8 3.2 copy-start.13
  131.2 7.9 copy-start.17
  131.5 0.8 copy-start.7
  134.1 593.3 %all-to-all-start.2 = ((bf16[2,256,512]{1,2,0:T(8,128)(2,1)}), bf16[2,256,512]{1,2,0:T(8,128)(2,1)S(1)}, u32[]{:S(2)}, u32[]{:S(2)}) async-start(bf16[2,256,512]{1,2,0:T(8,128)(2,1)} %bitcast.16), calls=%async_computation.2 | async-start | bytes 1048576 | tf_op jit(solution)/shard_map/all_to_all | solution.py:74
  139.1 641.8 %all-gather.11.cloned.1.call-start = ((), (), s32[]{:S(2)}) async-start(), calls=%async_computation.6 | async-start | bytes 2359296 | tf_op jit(solution)/shard_map/all_gather | solution.py:81
  721.2 0.8 copy-start.3
  723.9 2.0 copy-start.8
  723.9 2.1 copy-start.6
  727.4 1.6 copy-start.2
  727.4 1.7 copy-start.1
  731.6 0.8 copy-start.9
  737.6 45.2 %copy-start.10 = (f32[2,4,128,128]{3,2,1,0:T(8,128)S(1)}, f32[2,4,128,128]{3,2,1,0:T(8,128)}, u32[]{:S(2)}) copy-start(f32[2,4,128,128]{3,2,1,0:T(8,128)} %copy-done.9) | copy-start | bytes 1572868
  738.9 43.9 %copy-start.4 = (f32[2,4,128,256]{3,2,1,0:T(8,128)S(1)}, f32[2,4,128,256]{3,2,1,0:T(8,128)}, u32[]{:S(2)}) copy-start(f32[2,4,128,256]{3,2,1,0:T(8,128)} %fusion.29) | copy-start | bytes 3145732
  782.7 1.2 copy-start.5
  782.8 1.4 copy-start.12
  792.0 2.6 copy-start
  792.0 4.1 copy-start.11
  794.5 6.7 collective-permute-start
Sparse Core Ops, SparseCore 0:
  10.4 12.3 all-gather.4
  25.0 96.2 all-gather.6
  133.2 48.9 all-gather.8
  733.3 47.5 all-gather.10

commit v2 on v1

v2 whole, which is shorter than its diff:
```python
import jax
import jax.numpy as jnp
import numpy as np
from jax import lax
from jax.sharding import Mesh
from jax.sharding import PartitionSpec as P

DH = 128
BLK = 128

EPSILON = 1e-06

TOKENS = ("groups", "chip", "core")


def swap(x):
    return lax.ppermute(x, "core", [(0, 1), (1, 0)])


def ring_order(chips):
    if chips % 2:
        return list(range(chips))
    return list(range(0, chips, 2)) + list(range(chips - 1, 0, -2))


def ring_gather(block, chips, c):
    order = ring_order(chips)
    place = np.zeros(chips, np.int32)
    place[np.asarray(order)] = np.arange(chips)
    order_t = jnp.asarray(order, jnp.int32)
    here = jnp.asarray(place)[c]
    ahead = [(order[p], order[(p + 1) % chips]) for p in range(chips)]
    behind = [(order[p], order[(p - 1) % chips]) for p in range(chips)]
    got = [(c, block)]
    fwd = block
    bwd = block
    for step in range(1, chips // 2 + 1):
        fwd = lax.ppermute(fwd, "chip", ahead)
        got.append((order_t[(here - step) % chips], fwd))
        if step <= (chips - 1) // 2:
            bwd = lax.ppermute(bwd, "chip", behind)
            got.append((order_t[(here + step) % chips], bwd))
    return got


def exclusive_scan(total, chips, reverse):
    incl = total
    excl = jnp.zeros_like(total)
    d = 1
    while d < chips:
        if reverse:
            perm = [(i, i - d) for i in range(d, chips)]
        else:
            perm = [(i, i + d) for i in range(chips - d)]
        got = lax.ppermute(incl, "chip", perm)
        incl = incl + got
        excl = excl + got
        d *= 2
    return excl


def dense_allow(block_masks, tokens):
    nb = tokens // BLK
    gate = jnp.broadcast_to(
        block_masks.astype(jnp.float32)[:, None, :, None], (nb, BLK, nb, BLK)
    ).reshape(tokens, tokens)
    rows = lax.broadcasted_iota(jnp.int32, (tokens, tokens), 0)
    cols = lax.broadcasted_iota(jnp.int32, (tokens, tokens), 1)
    return jnp.where(cols <= rows, gate, 0.0)


def on_device(clean, delta, cotangent, w_query, w_key, w_value, masks):
    f32, bf16 = jnp.float32, jnp.bfloat16
    tok = clean.shape[0]
    feat = w_query.shape[1]
    half = feat // 2
    heads = half // DH
    rows_dev = w_query.shape[0]
    k = lax.axis_index("core")
    c = lax.axis_index("chip")
    chips = lax.axis_size("chip")
    first = k == 0

    x_in = (clean.astype(f32) + delta.astype(f32)).astype(bf16)
    x_pair = jnp.concatenate([x_in, swap(x_in)], axis=0)

    w_cat = jnp.concatenate(
        [w.reshape(rows_dev, 2, half) for w in (w_query, w_key, w_value)], axis=2
    )
    w_mine = jnp.where(first, w_cat[:, 0], w_cat[:, 1])
    w_other = jnp.where(first, w_cat[:, 1], w_cat[:, 0])
    w_recv = swap(w_other)
    chip_rows = jnp.where(
        first,
        jnp.concatenate([w_mine, w_recv], axis=0),
        jnp.concatenate([w_recv, w_mine], axis=0),
    )
    pieces = ring_gather(chip_rows, chips, c)

    span = 2 * rows_dev
    projected = None
    w_half = jnp.zeros((chips * span, 3 * half), bf16)
    for src, piece in pieces:
        x_cols = lax.dynamic_slice_in_dim(x_pair, src * span, span, axis=1)
        term = jnp.dot(x_cols, piece, preferred_element_type=f32)
        projected = term if projected is None else projected + term
        w_half = lax.dynamic_update_slice_in_dim(w_half, piece, src * span, axis=0)
    projected = projected.astype(bf16).reshape(2, tok, 3, heads, DH)
    query = projected[:, :, 0]
    key = projected[:, :, 1]
    value = projected[:, :, 2]

    local = jnp.einsum("jthd,jthe->jhde", key, value, preferred_element_type=f32)
    state0 = exclusive_scan(local[0] + local[1], chips, False)
    state_mine = jnp.where(first, state0, state0 + local[1])
    state_other = jnp.where(first, state0 + local[0], state0)
    state_b = jnp.stack([state_mine, state_other]).astype(bf16)

    pair_masks = jnp.stack([masks[0], swap(masks[0])])
    allow = jax.vmap(dense_allow, in_axes=(0, None))(pair_masks, tok)

    scores = jnp.einsum("jthd,jshd->jhts", query, key, preferred_element_type=f32)
    attn = (scores * allow[:, None]).astype(bf16)
    mixed = jnp.einsum("jhts,jshd->jthd", attn, value, preferred_element_type=f32)
    mixed = mixed + jnp.einsum("jthd,jhde->jthe", query, state_b, preferred_element_type=f32)
    root = jnp.sqrt(jnp.mean(mixed * mixed, axis=-1, keepdims=True) + EPSILON)
    normed = mixed / root

    out_b = normed.astype(bf16).reshape(2, tok, half)
    out_recv = swap(out_b[1])
    output = jnp.where(
        first,
        jnp.concatenate([out_b[0], out_recv], axis=1),
        jnp.concatenate([out_recv, out_b[0]], axis=1),
    )

    cot = cotangent.reshape(tok, 2, half)
    cot_mine = jnp.where(first, cot[:, 0], cot[:, 1])
    cot_other = jnp.where(first, cot[:, 1], cot[:, 0])
    grad_out = jnp.stack([cot_mine, swap(cot_other)]).astype(f32).reshape(2, tok, heads, DH)
    d_mixed = (grad_out - normed * jnp.mean(grad_out * normed, axis=-1, keepdims=True)) / root
    d_mixed_b = d_mixed.astype(bf16)
    grad_local = jnp.einsum("jthd,jthe->jhde", query, d_mixed_b, preferred_element_type=f32)

    later1 = exclusive_scan(grad_local[0] + grad_local[1], chips, True)
    later_mine = jnp.where(first, later1 + grad_local[1], later1)
    later_other = jnp.where(first, later1, later1 + grad_local[0])
    later_b = jnp.stack([later_mine, later_other]).astype(bf16)

    d_attn = (
        jnp.einsum("jthe,jshe->jhts", d_mixed_b, value, preferred_element_type=f32) * allow[:, None]
    ).astype(bf16)
    d_query = jnp.einsum("jhts,jshd->jthd", d_attn, key, preferred_element_type=f32)
    d_query = d_query + jnp.einsum("jthe,jhde->jthd", d_mixed_b, state_b, preferred_element_type=f32)
    d_key = jnp.einsum("jhts,jthd->jshd", d_attn, query, preferred_element_type=f32)
    d_key = d_key + jnp.einsum("jshe,jhde->jshd", value, later_b, preferred_element_type=f32)
    d_value = jnp.einsum("jhts,jthe->jshe", attn, d_mixed_b, preferred_element_type=f32)
    d_value = d_value + jnp.einsum("jshd,jhde->jshe", key, later_b, preferred_element_type=f32)
    d_proj = jnp.stack([d_query, d_key, d_value], axis=2).astype(bf16).reshape(2 * tok, 3 * half)

    partial = lax.dot_general(d_proj, w_half, (((1,), (1,)), ((), ())), preferred_element_type=f32)
    partial = partial.reshape(2, tok, -1)
    grad_input = (partial[0] + swap(partial[1])).astype(bf16)
    return (output, grad_input)


def solution(mesh):
    groups = mesh.shape["groups"]
    seq = mesh.shape["seq"]
    devices = np.asarray(mesh.devices).reshape(groups, seq // 2, 2)
    inner = Mesh(devices, TOKENS)
    rows = P(TOKENS, None)
    weights = P(("chip", "core"), None)
    return jax.shard_map(
        on_device,
        mesh=inner,
        in_specs=(rows, rows, rows, weights, weights, weights, P(TOKENS, None, None)),
        out_specs=(rows, rows),
        check_vma=False,
    )
```

time: 815 us -> 186 us (0.23)
  local copies, waits for them, and re-layouts: 593 us -> 32.7 us
  waiting for transfers between devices: 147 us -> 69.1 us
  starting transfers between devices: 6.65 us -> 37.4 us
  blocking collectives: 10.8 us -> 0 us
    gather x2 -> x0, local copies, waits for them, and re-layouts: 580 us -> none  [dense_allow(): gate = block_masks.astype(jnp.float32)[blk[:, None], blk[None, :]]]
    all_gather x4 -> x0, waiting for transfers between devices: 146 us -> none  [the longest x1 98.5 us: on_device(): w_half = lax.all_gather(w_chip, 'chip', axis=0, tiled=True)]
    ppermute x1 -> x19, waiting for transfers between devices: 0.01 us -> 69.1 us  [the longest x4 38.4 us: ring_gather(): fwd = lax.ppermute(fwd, 'chip', ahead)]
    ppermute x1 -> x19, starting transfers between devices: 1.52 us -> 37.4 us  [the longest x6 17 us: exclusive_scan(): got = lax.ppermute(incl, 'chip', perm)]
    all_to_all x2 -> x0, blocking collectives: 8.83 us -> none  [the longest x1 4.67 us: on_device(): w_chip = lax.all_to_all(w_loc, 'core', 0, 0)]
  transfers between devices with their start and end apart: 6 -> 19, of which waited for: 3 -> 11; matrix products, arithmetic and copies ran while one was open for 73% -> 23% of each run, Pallas kernels for 0% -> 0%
where the time goes in v2:
time: 186 us; the launch traced here: 185 us
  waiting for transfers between devices  69.1 us (37%)
  starting transfers between devices  37.4 us (20%)
  local copies, waits for them, and re-layouts  32.7 us (18%)
  matrix products  20.6 us (11%)
  other arithmetic  15 us (8%)
  between operations  10.2 us (5%)
    ppermute x4, waiting for transfers between devices, ring_gather(): fwd = lax.ppermute(fwd, 'chip', ahead)  38.4 us
    ppermute x6, waiting for transfers between devices, exclusive_scan(): got = lax.ppermute(incl, 'chip', perm)  25.7 us
    ppermute x6, starting transfers between devices, exclusive_scan(): got = lax.ppermute(incl, 'chip', perm)  17 us
    ppermute x6, starting transfers between devices, swap(): return lax.ppermute(x, 'core', [(0, 1), (1, 0)])  15.8 us
    dot_general x8, matrix products, on_device(): term = jnp.dot(x_cols, piece, preferred_element_type=f32)  8.34 us
    dynamic_update_slice x7, local copies, waits for them, and re-layouts, on_device(): w_half = lax.dynamic_update_slice_in_dim(w_half, piece, src * span, axis=0)  8.13 us
    dot_general x1, matrix products, on_device(): lax.dot_general(d_proj, w_half, (((1,), (1,)), ((), ())), preferred_eleme...  7.77 us
    unnamed x32, local copies, waits for them, and re-layouts  5.87 us
  transfers between devices with their start and end apart: 19, of which 11 were waited for; matrix products, arithmetic and copies ran while one was open for 23% of the time, Pallas kernels for 0%

profile of v2, /device:TPU:15, one launch (start us, length us, event | category | flops | bytes accessed | tf_op | source)
XLA Modules:
  0.0 185.1 jit_solution(15479491393660989906)
XLA Ops:
  7.4 3.4 %broadcast_in_dim.24 = bf16[2048,1536]{0,1:T(8,128)(2,1)} broadcast(bf16[]{:T(256)} %constant.93.clone.1), dimensions={} | broadcast | bytes 6291458 | tf_op jit(solution)/shard_map/broadcast_in_dim | solution.py:102
  10.9 2.6 %constant_dynamic-update-slice_fusion.7 = (bf16[2048,1536]{0,1:T(8,128)(2,1)}, bf16[256,1536]{0,1:T(8,128)(2,1)}) fusion(bf16[2048,1536]{0,1:T(8,128)(2,1)} %broadcast_in_dim.24, s32[]{:T(128)S(6)} %select_n.176, bf16[128,1536]{0,1:T(8,128)(2,1)S(1)} %get-tuple-element.14, bf16[128,1536]{0,1:T(8,128)(2,1)} %collective-permute-done.1, pred[]{:T(512)S(6)} %eq.11), kind=kLoop, calls=%fused_computation.111 | loop fusion | flops 3538944 | bytes 2359301 | tf_op jit(solution)/shard_map/dynamic_update_slice | solution.py:107
  16.9 1.8 broadcast_select_fusion.1
  30.1 2.3 %reshape.131 = f32[2,256,256]{2,1,0:T(8,128)} reshape(f32[2,2,128,2,128]{4,3,2,1,0:T(2,128)} %broadcast_in_dim.22) | data formatting | bytes 1048576 | tf_op jit(solution)/shard_map/vmap()/reshape | solution.py:66
  32.4 1.9 %broadcast_select_fusion = f32[2,256,256]{2,1,0:T(8,128)} fusion(f32[2,256,256]{2,1,0:T(8,128)} %reshape.131, pred[256,256]{1,0:T(8,128)(4,1)S(1)} %iota_compare_fusion), kind=kLoop, calls=%fused_computation.94 | loop fusion | flops 131072 | bytes 1114112 | tf_op jit(solution)/shard_map/vmap(jit(_where))/select_n | solution.py:69
  35.7 2.1 %constant_dynamic-update-slice_fusion.6 = bf16[2048,1536]{0,1:T(8,128)(2,1)} fusion(bf16[2048,1536]{0,1:T(8,128)(2,1)} %get-tuple-element.2, bf16[256,1536]{0,1:T(8,128)(2,1)} %collective-permute-done.2, s32[]{:T(128)S(6)} %select_n.187), kind=kLoop, calls=%fused_computation.110 | loop fusion | bytes 1572868 | tf_op jit(solution)/shard_map/dynamic_update_slice | solution.py:107
  37.9 1.7 fusion.34
  41.2 1.8 fusion.2
  43.0 10.1 %collective-permute-done.4 = bf16[256,1536]{0,1:T(8,128)(2,1)S(1)} collective-permute-done((bf16[256,1536]{0,1:T(8,128)(2,1)}, bf16[256,1536]{0,1:T(8,128)(2,1)S(1)}, u32[]{:S(2)}, u32[]{:S(2)}) %collective-permute-start.4) | collective-permute-done | bytes 786464 | tf_op jit(solution)/shard_map/ppermute | solution.py:38
  57.8 13.0 %collective-permute-done.6 = bf16[256,1536]{0,1:T(8,128)(2,1)S(1)} collective-permute-done((bf16[256,1536]{0,1:T(8,128)(2,1)S(1)}, bf16[256,1536]{0,1:T(8,128)(2,1)S(1)}, u32[]{:S(2)}, u32[]{:S(2)}) %collective-permute-start.6) | collective-permute-done | bytes 786464 | tf_op jit(solution)/shard_map/ppermute | solution.py:38
  72.2 15.4 %collective-permute-done.8 = bf16[256,1536]{0,1:T(8,128)(2,1)S(1)} collective-permute-done((bf16[256,1536]{0,1:T(8,128)(2,1)S(1)}, bf16[256,1536]{0,1:T(8,128)(2,1)S(1)}, u32[]{:S(2)}, u32[]{:S(2)}) %collective-permute-start.8) | collective-permute-done | bytes 786464 | tf_op jit(solution)/shard_map/ppermute | solution.py:38
  88.5 1.8 fusion.3
  90.2 3.0 %reshape.130 = bf16[2,256,3,4,128]{4,3,2,1,0:T(4,128)(2,1)S(1)} reshape(bf16[512,1536]{1,0:T(8,128)(2,1)} %fusion.3) | data formatting | bytes 3145728 | tf_op jit(solution)/shard_map/reshape | solution.py:108
  93.2 1.3 fusion.75
  94.6 1.4 copy.96
  96.3 3.1 %collective-permute-start.10 = (f32[4,128,128]{2,1,0:T(8,128)S(1)}, f32[4,128,128]{2,1,0:T(8,128)S(1)}, u32[]{:S(2)}, u32[]{:S(2)}) collective-permute-start(f32[4,128,128]{2,1,0:T(8,128)S(1)} %fusion.48), channel_id=1, source_target_pairs={{0,2},{2,4},{4,6},{6,8},{8,10},{10,12},{12,14},{1,3},{3,5},{5,7},{... | collective-permute-start | bytes 786440 | tf_op jit(solution)/shard_map/ppermute | solution.py:55
  101.5 1.9 %collective-permute-done.10 = f32[4,128,128]{2,1,0:T(8,128)S(1)} collective-permute-done((f32[4,128,128]{2,1,0:T(8,128)S(1)}, f32[4,128,128]{2,1,0:T(8,128)S(1)}, u32[]{:S(2)}, u32[]{:S(2)}) %collective-permute-start.10) | collective-permute-done | bytes 262176 | tf_op jit(solution)/shard_map/ppermute | solution.py:55
  103.5 3.3 %collective-permute-start.11 = (f32[4,128,128]{2,1,0:T(8,128)S(1)}, f32[4,128,128]{2,1,0:T(8,128)S(1)}, u32[]{:S(2)}, u32[]{:S(2)}) collective-permute-start(f32[4,128,128]{2,1,0:T(8,128)S(1)} %fusion.99), channel_id=1, source_target_pairs={{0,4},{2,6},{4,8},{6,10},{8,12},{10,14},{1,5},{3,7},{5,9},{7,11},{... | collective-permute-start | bytes 786440 | tf_op jit(solution)/shard_map/ppermute | solution.py:55
  107.3 3.5 %collective-permute-done.11 = f32[4,128,128]{2,1,0:T(8,128)S(1)} collective-permute-done((f32[4,128,128]{2,1,0:T(8,128)S(1)}, f32[4,128,128]{2,1,0:T(8,128)S(1)}, u32[]{:S(2)}, u32[]{:S(2)}) %collective-permute-start.11) | collective-permute-done | bytes 262176 | tf_op jit(solution)/shard_map/ppermute | solution.py:55
  110.8 4.4 %collective-permute-start.12 = (f32[4,128,128]{2,1,0:T(8,128)S(1)}, f32[4,128,128]{2,1,0:T(8,128)S(1)}, u32[]{:S(2)}, u32[]{:S(2)}) collective-permute-start(f32[4,128,128]{2,1,0:T(8,128)S(1)} %add.248), channel_id=1, source_target_pairs={{0,8},{2,10},{4,12},{6,14},{1,9},{3,11},{5,13},{7,15},{16,24},{18,... | collective-permute-start | bytes 786440 | tf_op jit(solution)/shard_map/ppermute | solution.py:55
  116.7 4.3 %collective-permute-done.12 = f32[4,128,128]{2,1,0:T(8,128)S(1)} collective-permute-done((f32[4,128,128]{2,1,0:T(8,128)S(1)}, f32[4,128,128]{2,1,0:T(8,128)S(1)}, u32[]{:S(2)}, u32[]{:S(2)}) %collective-permute-start.12) | collective-permute-done | bytes 262176 | tf_op jit(solution)/shard_map/ppermute | solution.py:55
  122.6 2.0 %fusion.14 = (bf16[2,256,4,128]{1,3,2,0:T(8,128)(2,1)S(1)}, bf16[2,256,4,128]{1,3,2,0:T(8,128)(2,1)}) fusion(f32[2,256,4]{1,2,0:T(4,128)S(1)} %broadcast_multiply_fusion, f32[2,256,4]{1,2,0:T(4,128)S(1)} %add_sqrt_fusion, bf16[1,256,4,128]{1,3,2,0:T(8,128)(2,1)} %bitcast.33, bf16[1,256,4,128]{1,3,2,0:T(8,128)(2,1)S(1)} %bitcast.134, ...), kind=kLoop, calls=%fused_computation.45 | loop fusion | flops 2097152 | bytes 2637824 | tf_op jit(solution)/shard_map/convert_element_type | solution.py:142
  125.5 3.1 %collective-permute-start.15 = (f32[4,128,128]{2,1,0:T(8,128)S(1)}, f32[4,128,128]{2,1,0:T(8,128)S(1)}, u32[]{:S(2)}, u32[]{:S(2)}) collective-permute-start(f32[4,128,128]{2,1,0:T(8,128)S(1)} %fusion.49), channel_id=1, source_target_pairs={{2,0},{4,2},{6,4},{8,6},{10,8},{12,10},{14,12},{3,1},{5,3},{7,5},{... | collective-permute-start | bytes 786440 | tf_op jit(solution)/shard_map/ppermute | solution.py:55
  129.3 4.2 %collective-permute-done.15 = f32[4,128,128]{2,1,0:T(8,128)S(1)} collective-permute-done((f32[4,128,128]{2,1,0:T(8,128)S(1)}, f32[4,128,128]{2,1,0:T(8,128)S(1)}, u32[]{:S(2)}, u32[]{:S(2)}) %collective-permute-start.15) | collective-permute-done | bytes 262176 | tf_op jit(solution)/shard_map/ppermute | solution.py:55
  133.5 1.9 %collective-permute-start.16 = (f32[4,128,128]{2,1,0:T(8,128)S(1)}, f32[4,128,128]{2,1,0:T(8,128)S(1)}, u32[]{:S(2)}, u32[]{:S(2)}) collective-permute-start(f32[4,128,128]{2,1,0:T(8,128)S(1)} %fusion.98), channel_id=1, source_target_pairs={{4,0},{6,2},{8,4},{10,6},{12,8},{14,10},{5,1},{7,3},{9,5},{11,7},{... | collective-permute-start | bytes 786440 | tf_op jit(solution)/shard_map/ppermute | solution.py:55
  135.8 5.3 %collective-permute-done.16 = f32[4,128,128]{2,1,0:T(8,128)S(1)} collective-permute-done((f32[4,128,128]{2,1,0:T(8,128)S(1)}, f32[4,128,128]{2,1,0:T(8,128)S(1)}, u32[]{:S(2)}, u32[]{:S(2)}) %collective-permute-start.16) | collective-permute-done | bytes 262176 | tf_op jit(solution)/shard_map/ppermute | solution.py:55
  142.8 6.5 %collective-permute-done.17 = f32[4,128,128]{2,1,0:T(8,128)S(1)} collective-permute-done((f32[4,128,128]{2,1,0:T(8,128)S(1)}, f32[4,128,128]{2,1,0:T(8,128)S(1)}, u32[]{:S(2)}, u32[]{:S(2)}) %collective-permute-start.17) | collective-permute-done | bytes 262176 | tf_op jit(solution)/shard_map/ppermute | solution.py:55
  152.2 7.8 %fusion.79 = f32[512,2048]{1,0:T(8,128)} fusion(bf16[512,1536]{1,0:T(8,128)(2,1)S(1)} %convert_element_type.55, bf16[2048,1536]{0,1:T(8,128)(2,1)} %constant_dynamic-update-slice_fusion), kind=kOutput, calls=%fused_computation.139 | convolution fusion | flops 3221225472 | bytes 12058624 | tf_op jit(solution)/shard_map/dot_general | solution.py:161
  159.9 3.2 %slice.87 = f32[256,2048]{1,0:T(8,128)} slice(f32[512,2048]{1,0:T(8,128)} %fusion.79), slice={[256:512], [0:2048]} | slice | bytes 4194304 | tf_op jit(solution)/shard_map/slice | solution.py:163
  163.2 14.1 %collective-permute-start.18 = (f32[256,2048]{1,0:T(8,128)}, f32[256,2048]{1,0:T(8,128)S(1)}, u32[]{:S(2)}, u32[]{:S(2)}) collective-permute-start(f32[256,2048]{1,0:T(8,128)} %slice.87), channel_id=1, source_target_pairs={{0,1},{1,0},{2,3},{3,2},{4,5},{5,4},{6,7},{7,6},{8,9},{9,8},{10,11... | collective-permute-start | bytes 6291464 | tf_op jit(solution)/shard_map/ppermute | solution.py:17
  177.7 3.7 %collective-permute-done.13 = bf16[256,512]{1,0:T(8,128)(2,1)S(1)} collective-permute-done((bf16[256,512]{1,0:T(8,128)(2,1)S(1)}, bf16[256,512]{1,0:T(8,128)(2,1)S(1)}, u32[]{:S(2)}, u32[]{:S(2)}) %collective-permute-start.13) | collective-permute-done | bytes 262176 | tf_op jit(solution)/shard_map/ppermute | solution.py:17
  182.3 2.8 %fusion.4 = bf16[256,2048]{1,0:T(8,128)(2,1)} fusion(f32[256,2048]{1,0:T(8,128)S(1)} %collective-permute-done.18, f32[512,2048]{1,0:T(8,128)} %fusion.79), kind=kLoop, calls=%fused_computation.25 | loop fusion | flops 1048576 | bytes 5242880 | tf_op jit(solution)/shard_map/convert_element_type | solution.py:163
  (103 shorter events, 36.4 us)
Async XLA Ops:
  0.6 5.1 %copy-start.8 = (bf16[256,2048]{1,0:T(8,128)(2,1)S(1)}, bf16[256,2048]{1,0:T(8,128)(2,1)}, u32[]{:S(2)}) copy-start(bf16[256,2048]{1,0:T(8,128)(2,1)} %param.10) | copy-start | bytes 3145732
  0.6 5.1 %copy-start.9 = (bf16[256,2048]{1,0:T(8,128)(2,1)S(1)}, bf16[256,2048]{1,0:T(8,128)(2,1)}, u32[]{:S(2)}) copy-start(bf16[256,2048]{1,0:T(8,128)(2,1)} %param.9) | copy-start | bytes 3145732
  5.0 2.4 %collective-permute-start.1 = (bf16[128,1536]{0,1:T(8,128)(2,1)}, bf16[128,1536]{0,1:T(8,128)(2,1)}, u32[]{:S(2)}, u32[]{:S(2)}) collective-permute-start(bf16[128,1536]{0,1:T(8,128)(2,1)} %get-tuple-element.13), channel_id=1, source_target_pairs={{0,1},{1,0},{2,3},{3,2},{4,5},{5,4},{6,7},{7,6},{8,9},{9,8},{10,11... | collective-permute-start | bytes 1179656 | tf_op jit(solution)/shard_map/ppermute | solution.py:17
  6.1 31.7 %collective-permute-start = (bf16[256,2048]{1,0:T(8,128)(2,1)S(1)}, bf16[256,2048]{1,0:T(8,128)(2,1)S(1)}, u32[]{:S(2)}, u32[]{:S(2)}) collective-permute-start(bf16[256,2048]{1,0:T(8,128)(2,1)S(1)} %add_convert_fusion), channel_id=1, source_target_pairs={{0,1},{1,0},{2,3},{3,2},{4,5},{5,4},{6,7},{7,6},{8,9},{9,8},{10,11... | collective-permute-start | bytes 3145736 | tf_op jit(solution)/shard_map/ppermute | solution.py:17
  7.4 7.5 %copy-start.12 = (s32[1,2,2]{2,1,0:T(2,128)S(1)}, s32[1,2,2]{2,1,0:T(2,128)}, u32[]{:S(2)}) copy-start(s32[1,2,2]{2,1,0:T(2,128)} %param.15) | copy-start | bytes 52
  7.4 8.5 %copy-start.10 = (bf16[256,1024]{1,0:T(8,128)(2,1)S(1)}, bf16[256,1024]{1,0:T(8,128)(2,1)}, u32[]{:S(2)}) copy-start(bf16[256,1024]{1,0:T(8,128)(2,1)} %param.11) | copy-start | bytes 1572868
  10.8 7.8 %copy-start.13 = (s32[8]{0:T(128)S(1)}, s32[8]{0:T(128)}, u32[]{:S(2)}) copy-start(s32[8]{0:T(128)} %constant.95.clone) | copy-start | bytes 100
  10.8 13.0 %copy-start.11 = (s32[8]{0:T(128)S(1)}, s32[8]{0:T(128)}, u32[]{:S(2)}) copy-start(s32[8]{0:T(128)} %constant.94.clone) | copy-start | bytes 100
  13.5 20.8 %collective-permute-start.2 = (bf16[256,1536]{0,1:T(8,128)(2,1)}, bf16[256,1536]{0,1:T(8,128)(2,1)}, u32[]{:S(2)}, u32[]{:S(2)}) collective-permute-start(bf16[256,1536]{0,1:T(8,128)(2,1)} %get-tuple-element.3), channel_id=1, source_target_pairs={{0,4},{4,8},{8,12},{12,14},{14,10},{10,6},{6,2},{2,0},{1,5},{5,9},... | collective-permute-start | bytes 2359304 | tf_op jit(solution)/shard_map/ppermute | solution.py:38
  13.6 20.8 %collective-permute-start.3 = (bf16[256,1536]{0,1:T(8,128)(2,1)}, bf16[256,1536]{0,1:T(8,128)(2,1)S(1)}, u32[]{:S(2)}, u32[]{:S(2)}) collective-permute-start(bf16[256,1536]{0,1:T(8,128)(2,1)} %get-tuple-element.3), channel_id=1, source_target_pairs={{0,2},{4,0},{8,4},{12,8},{14,12},{10,14},{6,10},{2,6},{1,3},{5,1},... | collective-permute-start | bytes 2359304 | tf_op jit(solution)/shard_map/ppermute | solution.py:41
  14.9 14.2 %collective-permute-start.9 = (s32[2,2]{1,0:T(2,128)S(1)}, s32[2,2]{1,0:T(2,128)S(1)}, u32[]{:S(2)}, u32[]{:S(2)}) collective-permute-start(s32[2,2]{1,0:T(2,128)S(1)} %bitcast.141), channel_id=1, source_target_pairs={{0,1},{1,0},{2,3},{3,2},{4,5},{5,4},{6,7},{7,6},{8,9},{9,8},{10,11... | collective-permute-start | bytes 56 | tf_op jit(solution)/shard_map/ppermute | solution.py:17
  18.6 102.8 %collective-permute-start.14 = (bf16[256,512]{0,1:T(8,128)(2,1)}, bf16[256,512]{0,1:T(8,128)(2,1)}, u32[]{:S(2)}, u32[]{:S(2)}) collective-permute-start(bf16[256,512]{0,1:T(8,128)(2,1)} %get-tuple-element.16), channel_id=1, source_target_pairs={{0,1},{1,0},{2,3},{3,2},{4,5},{5,4},{6,7},{7,6},{8,9},{9,8},{10,11... | collective-permute-start | bytes 786440 | tf_op jit(solution)/shard_map/ppermute | solution.py:17
  34.3 18.8 %collective-permute-start.4 = (bf16[256,1536]{0,1:T(8,128)(2,1)}, bf16[256,1536]{0,1:T(8,128)(2,1)S(1)}, u32[]{:S(2)}, u32[]{:S(2)}) collective-permute-start(bf16[256,1536]{0,1:T(8,128)(2,1)} %collective-permute-done.2), channel_id=1, source_target_pairs={{0,4},{4,8},{8,12},{12,14},{14,10},{10,6},{6,2},{2,0},{1,5},{5,9},... | collective-permute-start | bytes 2359304 | tf_op jit(solution)/shard_map/ppermute | solution.py:38
  34.4 18.8 %collective-permute-start.5 = (bf16[256,1536]{0,1:T(8,128)(2,1)S(1)}, bf16[256,1536]{0,1:T(8,128)(2,1)S(1)}, u32[]{:S(2)}, u32[]{:S(2)}) collective-permute-start(bf16[256,1536]{0,1:T(8,128)(2,1)S(1)} %collective-permute-done.3), channel_id=1, source_target_pairs={{0,2},{4,0},{8,4},{12,8},{14,12},{10,14},{6,10},{2,6},{1,3},{5,1},... | collective-permute-start | bytes 2359304 | tf_op jit(solution)/shard_map/ppermute | solution.py:41
  53.1 17.7 %collective-permute-start.6 = (bf16[256,1536]{0,1:T(8,128)(2,1)S(1)}, bf16[256,1536]{0,1:T(8,128)(2,1)S(1)}, u32[]{:S(2)}, u32[]{:S(2)}) collective-permute-start(bf16[256,1536]{0,1:T(8,128)(2,1)S(1)} %collective-permute-done.4), channel_id=1, source_target_pairs={{0,4},{4,8},{8,12},{12,14},{14,10},{10,6},{6,2},{2,0},{1,5},{5,9},... | collective-permute-start | bytes 2359304 | tf_op jit(solution)/shard_map/ppermute | solution.py:38
  53.2 17.7 %collective-permute-start.7 = (bf16[256,1536]{0,1:T(8,128)(2,1)S(1)}, bf16[256,1536]{0,1:T(8,128)(2,1)S(1)}, u32[]{:S(2)}, u32[]{:S(2)}) collective-permute-start(bf16[256,1536]{0,1:T(8,128)(2,1)S(1)} %collective-permute-done.5), channel_id=1, source_target_pairs={{0,2},{4,0},{8,4},{12,8},{14,12},{10,14},{6,10},{2,6},{1,3},{5,1},... | collective-permute-start | bytes 2359304 | tf_op jit(solution)/shard_map/ppermute | solution.py:41
  70.8 1.4 copy-start.3
  70.8 16.8 %collective-permute-start.8 = (bf16[256,1536]{0,1:T(8,128)(2,1)S(1)}, bf16[256,1536]{0,1:T(8,128)(2,1)S(1)}, u32[]{:S(2)}, u32[]{:S(2)}) collective-permute-start(bf16[256,1536]{0,1:T(8,128)(2,1)S(1)} %collective-permute-done.6), channel_id=1, source_target_pairs={{0,4},{4,8},{8,12},{12,14},{14,10},{10,6},{6,2},{2,0},{1,5},{5,9},... | collective-permute-start | bytes 2359304 | tf_op jit(solution)/shard_map/ppermute | solution.py:38
  70.9 1.2 copy-start.5
  94.6 4.9 %copy-start.4 = (bf16[256,1536]{0,1:T(8,128)(2,1)S(1)}, bf16[256,1536]{0,1:T(8,128)(2,1)}, u32[]{:S(2)}) copy-start(bf16[256,1536]{0,1:T(8,128)(2,1)} %copy-done.3) | copy-start | bytes 2359300
  94.6 6.0 %copy-start.6 = (bf16[256,1536]{0,1:T(8,128)(2,1)S(1)}, bf16[256,1536]{0,1:T(8,128)(2,1)}, u32[]{:S(2)}) copy-start(bf16[256,1536]{0,1:T(8,128)(2,1)} %copy-done.5) | copy-start | bytes 2359300
  95.9 10.9 %copy-start = (f32[2,256,256]{2,1,0:T(8,128)S(1)}, f32[2,256,256]{2,1,0:T(8,128)}, u32[]{:S(2)}) copy-start(f32[2,256,256]{2,1,0:T(8,128)} %broadcast_select_fusion) | copy-start | bytes 1572868
  96.3 7.1 %collective-permute-start.10 = (f32[4,128,128]{2,1,0:T(8,128)S(1)}, f32[4,128,128]{2,1,0:T(8,128)S(1)}, u32[]{:S(2)}, u32[]{:S(2)}) collective-permute-start(f32[4,128,128]{2,1,0:T(8,128)S(1)} %fusion.48), channel_id=1, source_target_pairs={{0,2},{2,4},{4,6},{6,8},{8,10},{10,12},{12,14},{1,3},{3,5},{5,7},{... | collective-permute-start | bytes 786440 | tf_op jit(solution)/shard_map/ppermute | solution.py:55
  103.5 12.1 %copy-start.2 = (bf16[256,1536]{0,1:T(8,128)(2,1)S(1)}, bf16[256,1536]{0,1:T(8,128)(2,1)}, u32[]{:S(2)}) copy-start(bf16[256,1536]{0,1:T(8,128)(2,1)} %copy-done.1) | copy-start | bytes 2359300
  103.5 7.2 %collective-permute-start.11 = (f32[4,128,128]{2,1,0:T(8,128)S(1)}, f32[4,128,128]{2,1,0:T(8,128)S(1)}, u32[]{:S(2)}, u32[]{:S(2)}) collective-permute-start(f32[4,128,128]{2,1,0:T(8,128)S(1)} %fusion.99), channel_id=1, source_target_pairs={{0,4},{2,6},{4,8},{6,10},{8,12},{10,14},{1,5},{3,7},{5,9},{7,11},{... | collective-permute-start | bytes 786440 | tf_op jit(solution)/shard_map/ppermute | solution.py:55
  110.8 10.2 %collective-permute-start.12 = (f32[4,128,128]{2,1,0:T(8,128)S(1)}, f32[4,128,128]{2,1,0:T(8,128)S(1)}, u32[]{:S(2)}, u32[]{:S(2)}) collective-permute-start(f32[4,128,128]{2,1,0:T(8,128)S(1)} %add.248), channel_id=1, source_target_pairs={{0,8},{2,10},{4,12},{6,14},{1,9},{3,11},{5,13},{7,15},{16,24},{18,... | collective-permute-start | bytes 786440 | tf_op jit(solution)/shard_map/ppermute | solution.py:55
  125.5 8.0 %collective-permute-start.15 = (f32[4,128,128]{2,1,0:T(8,128)S(1)}, f32[4,128,128]{2,1,0:T(8,128)S(1)}, u32[]{:S(2)}, u32[]{:S(2)}) collective-permute-start(f32[4,128,128]{2,1,0:T(8,128)S(1)} %fusion.49), channel_id=1, source_target_pairs={{2,0},{4,2},{6,4},{8,6},{10,8},{12,10},{14,12},{3,1},{5,3},{7,5},{... | collective-permute-start | bytes 786440 | tf_op jit(solution)/shard_map/ppermute | solution.py:55
  133.5 7.6 %collective-permute-start.16 = (f32[4,128,128]{2,1,0:T(8,128)S(1)}, f32[4,128,128]{2,1,0:T(8,128)S(1)}, u32[]{:S(2)}, u32[]{:S(2)}) collective-permute-start(f32[4,128,128]{2,1,0:T(8,128)S(1)} %fusion.98), channel_id=1, source_target_pairs={{4,0},{6,2},{8,4},{10,6},{12,8},{14,10},{5,1},{7,3},{9,5},{11,7},{... | collective-permute-start | bytes 786440 | tf_op jit(solution)/shard_map/ppermute | solution.py:55
  141.1 8.1 %collective-permute-start.17 = (f32[4,128,128]{2,1,0:T(8,128)S(1)}, f32[4,128,128]{2,1,0:T(8,128)S(1)}, u32[]{:S(2)}, u32[]{:S(2)}) collective-permute-start(f32[4,128,128]{2,1,0:T(8,128)S(1)} %add.261), channel_id=1, source_target_pairs={{8,0},{10,2},{12,4},{14,6},{9,1},{11,3},{13,5},{15,7},{24,16},{26,... | collective-permute-start | bytes 786440 | tf_op jit(solution)/shard_map/ppermute | solution.py:55
  159.9 17.3 %copy-start.7 = (bf16[2,256,4,128]{1,3,2,0:T(8,128)(2,1)S(1)}, bf16[2,256,4,128]{1,3,2,0:T(8,128)(2,1)}, u32[]{:S(2)}) copy-start(bf16[2,256,4,128]{1,3,2,0:T(8,128)(2,1)} %get-tuple-element.12) | copy-start | bytes 1572868
  163.2 19.2 %collective-permute-start.18 = (f32[256,2048]{1,0:T(8,128)}, f32[256,2048]{1,0:T(8,128)S(1)}, u32[]{:S(2)}, u32[]{:S(2)}) collective-permute-start(f32[256,2048]{1,0:T(8,128)} %slice.87), channel_id=1, source_target_pairs={{0,1},{1,0},{2,3},{3,2},{4,5},{5,4},{6,7},{7,6},{8,9},{9,8},{10,11... | collective-permute-start | bytes 6291464 | tf_op jit(solution)/shard_map/ppermute | solution.py:17
  177.4 4.0 %collective-permute-start.13 = (bf16[256,512]{1,0:T(8,128)(2,1)S(1)}, bf16[256,512]{1,0:T(8,128)(2,1)S(1)}, u32[]{:S(2)}, u32[]{:S(2)}) collective-permute-start(bf16[256,512]{1,0:T(8,128)(2,1)S(1)} %copy.67), channel_id=1, source_target_pairs={{0,1},{1,0},{2,3},{3,2},{4,5},{5,4},{6,7},{7,6},{8,9},{9,8},{10,11... | collective-permute-start | bytes 786440 | tf_op jit(solution)/shard_map/ppermute | solution.py:17
  (1 other events, 0.9 us)

commit v3 on v2

--- a/solution.py
+++ b/solution.py
@@ -84,31 +84,37 @@
     x_in = (clean.astype(f32) + delta.astype(f32)).astype(bf16)
     x_pair = jnp.concatenate([x_in, swap(x_in)], axis=0)
 
-    w_cat = jnp.concatenate(
-        [w.reshape(rows_dev, 2, half) for w in (w_query, w_key, w_value)], axis=2
-    )
-    w_mine = jnp.where(first, w_cat[:, 0], w_cat[:, 1])
-    w_other = jnp.where(first, w_cat[:, 1], w_cat[:, 0])
-    w_recv = swap(w_other)
-    chip_rows = jnp.where(
-        first,
-        jnp.concatenate([w_mine, w_recv], axis=0),
-        jnp.concatenate([w_recv, w_mine], axis=0),
-    )
-    pieces = ring_gather(chip_rows, chips, c)
+    def cols(w, which):
+        return lax.dynamic_slice_in_dim(w, which * half, half, axis=1)
+
+    def chip_block(mats):
+        mine = jnp.concatenate([cols(w, k) for w in mats], axis=1)
+        recv = swap(jnp.concatenate([cols(w, 1 - k) for w in mats], axis=1))
+        block = jnp.zeros((2 * rows_dev, mine.shape[1]), mine.dtype)
+        block = lax.dynamic_update_slice_in_dim(block, mine, k * rows_dev, axis=0)
+        return lax.dynamic_update_slice_in_dim(block, recv, (1 - k) * rows_dev, axis=0)
 
     span = 2 * rows_dev
-    projected = None
-    w_half = jnp.zeros((chips * span, 3 * half), bf16)
-    for src, piece in pieces:
-        x_cols = lax.dynamic_slice_in_dim(x_pair, src * span, span, axis=1)
-        term = jnp.dot(x_cols, piece, preferred_element_type=f32)
-        projected = term if projected is None else projected + term
-        w_half = lax.dynamic_update_slice_in_dim(w_half, piece, src * span, axis=0)
-    projected = projected.astype(bf16).reshape(2, tok, 3, heads, DH)
-    query = projected[:, :, 0]
-    key = projected[:, :, 1]
-    value = projected[:, :, 2]
+
+    def project(pieces):
+        out = None
+        full = jnp.zeros((chips * span, pieces[0][1].shape[1]), bf16)
+        for src, piece in pieces:
+            x_cols = lax.dynamic_slice_in_dim(x_pair, src * span, span, axis=1)
+            term = jnp.dot(x_cols, piece, preferred_element_type=f32)
+            out = term if out is None else out + term
+            full = lax.dynamic_update_slice_in_dim(full, piece, src * span, axis=0)
+        return out.astype(bf16), full
+
+    kv_pieces = ring_gather(chip_block((w_key, w_value)), chips, c)
+    q_block, _ = lax.optimization_barrier((chip_block((w_query,)), kv_pieces[-1][1]))
+    q_pieces = ring_gather(q_block, chips, c)
+    kv_proj, w_kv = project(kv_pieces)
+    q_proj, w_q = project(q_pieces)
+    kv_proj = kv_proj.reshape(2, tok, 2, heads, DH)
+    query = q_proj.reshape(2, tok, heads, DH)
+    key = kv_proj[:, :, 0]
+    value = kv_proj[:, :, 1]
 
     local = jnp.einsum("jthd,jthe->jhde", key, value, preferred_element_type=f32)
     state0 = exclusive_scan(local[0] + local[1], chips, False)
@@ -156,11 +162,15 @@
     d_key = d_key + jnp.einsum("jshe,jhde->jshd", value, later_b, preferred_element_type=f32)
     d_value = jnp.einsum("jhts,jthe->jshe", attn, d_mixed_b, preferred_element_type=f32)
     d_value = d_value + jnp.einsum("jshd,jhde->jshe", key, later_b, preferred_element_type=f32)
-    d_proj = jnp.stack([d_query, d_key, d_value], axis=2).astype(bf16).reshape(2 * tok, 3 * half)
+    dq_b = d_query.astype(bf16).reshape(2, tok, half)
+    dkv_b = jnp.stack([d_key, d_value], axis=2).astype(bf16).reshape(2, tok, 2 * half)
 
-    partial = lax.dot_general(d_proj, w_half, (((1,), (1,)), ((), ())), preferred_element_type=f32)
-    partial = partial.reshape(2, tok, -1)
-    grad_input = (partial[0] + swap(partial[1])).astype(bf16)
+    def grad_rows(j):
+        g = lax.dot_general(dq_b[j], w_q, (((1,), (1,)), ((), ())), preferred_element_type=f32)
+        return g + lax.dot_general(dkv_b[j], w_kv, (((1,), (1,)), ((), ())), preferred_element_type=f32)
+
+    received = swap(grad_rows(1))
+    grad_input = (grad_rows(0) + received).astype(bf16)
     return (output, grad_input)
 
 

time: 186 us -> 191 us (1.027)
  matrix products: 20.6 us -> 28.4 us
  local copies, waits for them, and re-layouts: 32.7 us -> 37.7 us
  other arithmetic: 15 us -> 10.2 us
  waiting for transfers between devices: 69.1 us -> 65.4 us
    ppermute x3 -> x6, waiting for transfers between devices: 0.01 us -> 14.6 us  [ring_gather(): bwd = lax.ppermute(bwd, 'chip', behind)]
    ppermute x4 -> x8, waiting for transfers between devices: 38.4 us -> 26.3 us  [ring_gather(): fwd = lax.ppermute(fwd, 'chip', ahead)]
    dynamic_update_slice x7 -> x18, local copies, waits for them, and re-layouts: 8.13 us -> 16.5 us  [the longest x16 14.7 us: project(): full = lax.dynamic_update_slice_in_dim(full, piece, src * span, axis=0)]
    dot_general x9 -> x20, matrix products: 16.1 us -> 22.8 us  [the longest x16 9.22 us: project(): term = jnp.dot(x_cols, piece, preferred_element_type=f32)]
    ppermute x6, waiting for transfers between devices: 25.7 us -> 20.7 us  [exclusive_scan(): got = lax.ppermute(incl, 'chip', perm)]
    ppermute x3 -> x6, starting transfers between devices: 3.98 us -> 7.27 us  [ring_gather(): bwd = lax.ppermute(bwd, 'chip', behind)]
    convert_element_type x1 -> x0, other arithmetic: 2.8 us -> none  [on_device(): grad_input = (partial[0] + swap(partial[1])).astype(bf16)]
    dynamic_update_slice x1, other arithmetic: 2.62 us -> 0.03 us  [chip_block(): block = lax.dynamic_update_slice_in_dim(block, mine, k * rows_dev, axis=0)]
  transfers between devices with their start and end apart: 19 -> 27, of which waited for: 11 -> 12; matrix products, arithmetic and copies ran while one was open for 23% -> 30% of each run, Pallas kernels for 0% -> 0%
where the time goes in v3:
time: 191 us; the launch traced here: 190 us
  waiting for transfers between devices  65.4 us (34%)
  starting transfers between devices  38 us (20%)
  local copies, waits for them, and re-layouts  37.7 us (20%)
  matrix products  28.4 us (15%)
  between operations  10.3 us (5%)
  other arithmetic  10.2 us (5%)
    ppermute x8, waiting for transfers between devices, ring_gather(): fwd = lax.ppermute(fwd, 'chip', ahead)  26.3 us
    ppermute x6, waiting for transfers between devices, exclusive_scan(): got = lax.ppermute(incl, 'chip', perm)  20.7 us
    dynamic_update_slice x16, local copies, waits for them, and re-layouts, project(): full = lax.dynamic_update_slice_in_dim(full, piece, src * span, axis=0)  14.7 us
    ppermute x6, waiting for transfers between devices, ring_gather(): bwd = lax.ppermute(bwd, 'chip', behind)  14.6 us
    ppermute x6, starting transfers between devices, exclusive_scan(): got = lax.ppermute(incl, 'chip', perm)  14.5 us
    ppermute x7, starting transfers between devices, swap(): return lax.ppermute(x, 'core', [(0, 1), (1, 0)])  14 us
    dot_general x16, matrix products, project(): term = jnp.dot(x_cols, piece, preferred_element_type=f32)  9.22 us
    ppermute x6, starting transfers between devices, ring_gather(): bwd = lax.ppermute(bwd, 'chip', behind)  7.27 us
  transfers between devices with their start and end apart: 27, of which 12 were waited for; matrix products, arithmetic and copies ran while one was open for 30% of the time, Pallas kernels for 0%

profile of v3, /device:TPU:15, one launch (start us, length us, event | category | flops | bytes accessed | tf_op | source)
XLA Modules:
  0.0 190.1 jit_solution(5662949302776627492)
XLA Ops:
  3.3 1.6 add_convert_fusion.1
  22.2 2.3 %reshape.149 = f32[2,256,256]{2,1,0:T(8,128)} reshape(f32[2,2,128,2,128]{4,3,2,1,0:T(2,128)} %broadcast_in_dim.33) | data formatting | bytes 1048576 | tf_op jit(solution)/shard_map/vmap()/reshape | solution.py:66
  24.5 1.9 %broadcast_select_fusion = f32[2,256,256]{2,1,0:T(8,128)} fusion(f32[2,256,256]{2,1,0:T(8,128)} %reshape.149, pred[256,256]{1,0:T(8,128)(4,1)S(1)} %iota_compare_fusion), kind=kLoop, calls=%fused_computation.91 | loop fusion | flops 131072 | bytes 1114112 | tf_op jit(solution)/shard_map/vmap(jit(_where))/select_n | solution.py:69
  27.3 2.5 %broadcast_in_dim.36 = bf16[2048,1024]{1,0:T(8,128)(2,1)} broadcast(bf16[]{:T(256)} %constant.132.clone.1), dimensions={} | broadcast | bytes 4194306 | tf_op jit(solution)/shard_map/broadcast_in_dim | solution.py:101
  30.6 2.7 %collective-permute-done.2 = bf16[256,1024]{1,0:T(8,128)(2,1)} collective-permute-done((bf16[256,1024]{1,0:T(8,128)(2,1)S(1)}, bf16[256,1024]{1,0:T(8,128)(2,1)}, u32[]{:S(2)}, u32[]{:S(2)}) %collective-permute-start.2) | collective-permute-done | bytes 524320 | tf_op jit(solution)/shard_map/ppermute | solution.py:38
  34.8 1.9 constant_dynamic-update-slice_fusion.9
  36.7 1.9 constant_dynamic-update-slice_fusion.10
  42.0 4.1 %collective-permute-done.4 = bf16[256,1024]{1,0:T(8,128)(2,1)S(1)} collective-permute-done((bf16[256,1024]{1,0:T(8,128)(2,1)}, bf16[256,1024]{1,0:T(8,128)(2,1)S(1)}, u32[]{:S(2)}, u32[]{:S(2)}) %collective-permute-start.4) | collective-permute-done | bytes 524320 | tf_op jit(solution)/shard_map/ppermute | solution.py:38
  50.1 7.6 %collective-permute-done.6 = bf16[256,1024]{1,0:T(8,128)(2,1)S(1)} collective-permute-done((bf16[256,1024]{1,0:T(8,128)(2,1)S(1)}, bf16[256,1024]{1,0:T(8,128)(2,1)S(1)}, u32[]{:S(2)}, u32[]{:S(2)}) %collective-permute-start.6) | collective-permute-done | bytes 524320 | tf_op jit(solution)/shard_map/ppermute | solution.py:38
  60.0 8.4 %collective-permute-done.8 = bf16[256,1024]{1,0:T(8,128)(2,1)S(1)} collective-permute-done((bf16[256,1024]{1,0:T(8,128)(2,1)S(1)}, bf16[256,1024]{1,0:T(8,128)(2,1)S(1)}, u32[]{:S(2)}, u32[]{:S(2)}) %collective-permute-start.8) | collective-permute-done | bytes 524320 | tf_op jit(solution)/shard_map/ppermute | solution.py:38
  70.2 1.5 reshape.147
  71.8 2.4 %fusion.74 = (bf16[2,256,1,4,128]{4,3,2,1,0:T(4,128)(2,1)}, bf16[2,256,1,4,128]{4,3,2,1,0:T(4,128)(2,1)S(1)}) fusion(bf16[2,256,2,4,128]{4,3,2,1,0:T(4,128)(2,1)} %reshape.147), kind=kLoop, calls=%fused_computation.143 | loop fusion | bytes 2097152 | tf_op jit(solution)/shard_map/slice | solution.py:117
  75.8 3.1 %collective-permute-start.18 = (f32[4,128,128]{2,1,0:T(8,128)S(1)}, f32[4,128,128]{2,1,0:T(8,128)S(1)}, u32[]{:S(2)}, u32[]{:S(2)}) collective-permute-start(f32[4,128,128]{2,1,0:T(8,128)S(1)} %fusion.36), channel_id=1, source_target_pairs={{0,2},{2,4},{4,6},{6,8},{8,10},{10,12},{12,14},{1,3},{3,5},{5,7},{... | collective-permute-start | bytes 786440 | tf_op jit(solution)/shard_map/ppermute | solution.py:55
  82.1 1.5 broadcast_in_dim.35
  84.4 3.2 %collective-permute-start.19 = (f32[4,128,128]{2,1,0:T(8,128)S(1)}, f32[4,128,128]{2,1,0:T(8,128)S(1)}, u32[]{:S(2)}, u32[]{:S(2)}) collective-permute-start(f32[4,128,128]{2,1,0:T(8,128)S(1)} %fusion.120), channel_id=1, source_target_pairs={{0,4},{2,6},{4,8},{6,10},{8,12},{10,14},{1,5},{3,7},{5,9},{7,11},{... | collective-permute-start | bytes 786440 | tf_op jit(solution)/shard_map/ppermute | solution.py:55
  91.6 3.1 %collective-permute-done.19 = f32[4,128,128]{2,1,0:T(8,128)S(1)} collective-permute-done((f32[4,128,128]{2,1,0:T(8,128)S(1)}, f32[4,128,128]{2,1,0:T(8,128)S(1)}, u32[]{:S(2)}, u32[]{:S(2)}) %collective-permute-start.19) | collective-permute-done | bytes 262176 | tf_op jit(solution)/shard_map/ppermute | solution.py:55
  94.7 3.0 %collective-permute-start.20 = (f32[4,128,128]{2,1,0:T(8,128)S(1)}, f32[4,128,128]{2,1,0:T(8,128)S(1)}, u32[]{:S(2)}, u32[]{:S(2)}) collective-permute-start(f32[4,128,128]{2,1,0:T(8,128)S(1)} %add.428), channel_id=1, source_target_pairs={{0,8},{2,10},{4,12},{6,14},{1,9},{3,11},{5,13},{7,15},{16,24},{18,... | collective-permute-start | bytes 786440 | tf_op jit(solution)/shard_map/ppermute | solution.py:55
  97.8 2.6 %collective-permute-done.13 = bf16[256,512]{1,0:T(8,128)(2,1)S(1)} collective-permute-done((bf16[256,512]{1,0:T(8,128)(2,1)S(1)}, bf16[256,512]{1,0:T(8,128)(2,1)S(1)}, u32[]{:S(2)}, u32[]{:S(2)}) %collective-permute-start.13) | collective-permute-done | bytes 262176 | tf_op jit(solution)/shard_map/ppermute | solution.py:41
  103.9 12.1 %collective-permute-done.15 = bf16[256,512]{1,0:T(8,128)(2,1)S(1)} collective-permute-done((bf16[256,512]{1,0:T(8,128)(2,1)S(1)}, bf16[256,512]{1,0:T(8,128)(2,1)S(1)}, u32[]{:S(2)}, u32[]{:S(2)}) %collective-permute-start.15) | collective-permute-done | bytes 262176 | tf_op jit(solution)/shard_map/ppermute | solution.py:41
  119.1 3.4 %collective-permute-done.16 = bf16[256,512]{1,0:T(8,128)(2,1)S(1)} collective-permute-done((bf16[256,512]{1,0:T(8,128)(2,1)S(1)}, bf16[256,512]{1,0:T(8,128)(2,1)S(1)}, u32[]{:S(2)}, u32[]{:S(2)}) %collective-permute-start.16) | collective-permute-done | bytes 262176 | tf_op jit(solution)/shard_map/ppermute | solution.py:38
  125.7 1.6 multiply_convert_fusion.1
  132.1 1.9 %collective-permute-start.23 = (f32[4,128,128]{2,1,0:T(8,128)S(1)}, f32[4,128,128]{2,1,0:T(8,128)S(1)}, u32[]{:S(2)}, u32[]{:S(2)}) collective-permute-start(f32[4,128,128]{2,1,0:T(8,128)S(1)} %fusion.37), channel_id=1, source_target_pairs={{2,0},{4,2},{6,4},{8,6},{10,8},{12,10},{14,12},{3,1},{5,3},{7,5},{... | collective-permute-start | bytes 786440 | tf_op jit(solution)/shard_map/ppermute | solution.py:55
  134.8 5.3 %collective-permute-done.23 = f32[4,128,128]{2,1,0:T(8,128)S(1)} collective-permute-done((f32[4,128,128]{2,1,0:T(8,128)S(1)}, f32[4,128,128]{2,1,0:T(8,128)S(1)}, u32[]{:S(2)}, u32[]{:S(2)}) %collective-permute-start.23) | collective-permute-done | bytes 262176 | tf_op jit(solution)/shard_map/ppermute | solution.py:55
  140.1 1.9 %collective-permute-start.24 = (f32[4,128,128]{2,1,0:T(8,128)S(1)}, f32[4,128,128]{2,1,0:T(8,128)S(1)}, u32[]{:S(2)}, u32[]{:S(2)}) collective-permute-start(f32[4,128,128]{2,1,0:T(8,128)S(1)} %fusion.119), channel_id=1, source_target_pairs={{4,0},{6,2},{8,4},{10,6},{12,8},{14,10},{5,1},{7,3},{9,5},{11,7},{... | collective-permute-start | bytes 786440 | tf_op jit(solution)/shard_map/ppermute | solution.py:55
  142.4 4.9 %collective-permute-done.24 = f32[4,128,128]{2,1,0:T(8,128)S(1)} collective-permute-done((f32[4,128,128]{2,1,0:T(8,128)S(1)}, f32[4,128,128]{2,1,0:T(8,128)S(1)}, u32[]{:S(2)}, u32[]{:S(2)}) %collective-permute-start.24) | collective-permute-done | bytes 262176 | tf_op jit(solution)/shard_map/ppermute | solution.py:55
  150.1 7.5 %collective-permute-done.25 = f32[4,128,128]{2,1,0:T(8,128)S(1)} collective-permute-done((f32[4,128,128]{2,1,0:T(8,128)S(1)}, f32[4,128,128]{2,1,0:T(8,128)S(1)}, u32[]{:S(2)}, u32[]{:S(2)}) %collective-permute-start.25) | collective-permute-done | bytes 262176 | tf_op jit(solution)/shard_map/ppermute | solution.py:55
  159.2 3.5 %fusion.82 = f32[256,2048]{1,0:T(8,128)S(1)} fusion(bf16[256,1024]{0,1:T(8,128)(2,1)S(1)} %bitcast.146, bf16[2048,1024]{1,0:T(8,128)(2,1)} %constant_dynamic-update-slice_fusion.15), kind=kOutput, calls=%fused_computation.151 | convolution fusion | flops 1073741824 | bytes 6815744 | tf_op jit(solution)/shard_map/dot_general | solution.py:170
  162.7 2.4 %convolution_add_fusion = f32[256,2048]{1,0:T(8,128)S(1)} fusion(f32[256,2048]{1,0:T(8,128)S(1)} %fusion.82, bf16[256,512]{0,1:T(8,128)(2,1)S(1)} %bitcast.141, bf16[2048,512]{1,0:T(8,128)(2,1)} %constant_dynamic-update-slice_fusion.7), kind=kOutput, calls=%fused_computation.16 | convolution fusion | flops 537395200 | bytes 6553600 | tf_op jit(solution)/shard_map/dot_general | solution.py:169
  165.1 12.1 %collective-permute-start.26 = (f32[256,2048]{1,0:T(8,128)S(1)}, f32[256,2048]{1,0:T(8,128)}, u32[]{:S(2)}, u32[]{:S(2)}) collective-permute-start(f32[256,2048]{1,0:T(8,128)S(1)} %convolution_add_fusion), channel_id=1, source_target_pairs={{0,1},{1,0},{2,3},{3,2},{4,5},{5,4},{6,7},{7,6},{8,9},{9,8},{10,11... | collective-permute-start | bytes 6291464 | tf_op jit(solution)/shard_map/ppermute | solution.py:17
  177.7 3.7 %collective-permute-done.21 = bf16[256,512]{1,0:T(8,128)(2,1)S(1)} collective-permute-done((bf16[256,512]{1,0:T(8,128)(2,1)S(1)}, bf16[256,512]{1,0:T(8,128)(2,1)S(1)}, u32[]{:S(2)}, u32[]{:S(2)}) %collective-permute-start.21) | collective-permute-done | bytes 262176 | tf_op jit(solution)/shard_map/ppermute | solution.py:17
  182.3 3.7 %fusion.81 = f32[256,2048]{1,0:T(8,128)S(1)} fusion(bf16[256,1024]{0,1:T(8,128)(2,1)} %bitcast.145, bf16[2048,1024]{1,0:T(8,128)(2,1)} %constant_dynamic-update-slice_fusion.15), kind=kOutput, calls=%fused_computation.150 | convolution fusion | flops 1073741824 | bytes 6815744 | tf_op jit(solution)/shard_map/dot_general | solution.py:170
  186.0 4.0 %fusion.1 = bf16[256,2048]{1,0:T(8,128)(2,1)} fusion(f32[256,2048]{1,0:T(8,128)} %collective-permute-done.26, f32[256,2048]{1,0:T(8,128)S(1)} %fusion.81, bf16[256,512]{0,1:T(8,128)(2,1)S(1)} %bitcast.144, bf16[2048,512]{1,0:T(8,128)(2,1)} %constant_dynamic-update-slice_fusion.7), kind=kOutput, calls=%fused_computation.19 | convolution fusion | flops 538443776 | bytes 7602176 | tf_op jit(solution)/shard_map/dot_general | solution.py:169
  (145 shorter events, 56.4 us)
Async XLA Ops:
  2.6 16.1 %collective-permute-start.1 = (bf16[128,1024]{1,0:T(8,128)(2,1)}, bf16[128,1024]{1,0:T(8,128)(2,1)}, u32[]{:S(2)}, u32[]{:S(2)}) collective-permute-start(bf16[128,1024]{1,0:T(8,128)(2,1)} %pad_maximum_fusion.2), channel_id=1, source_target_pairs={{0,1},{1,0},{2,3},{3,2},{4,5},{5,4},{6,7},{7,6},{8,9},{9,8},{10,11... | collective-permute-start | bytes 786440 | tf_op jit(solution)/shard_map/ppermute | solution.py:17
  4.9 8.5 %copy-start.13 = (s32[8]{0:T(128)S(1)}, s32[8]{0:T(128)}, u32[]{:S(2)}) copy-start(s32[8]{0:T(128)} %constant.150.clone) | copy-start | bytes 100
  4.9 33.6 %collective-permute-start = (bf16[256,2048]{1,0:T(8,128)(2,1)S(1)}, bf16[256,2048]{1,0:T(8,128)(2,1)S(1)}, u32[]{:S(2)}, u32[]{:S(2)}) collective-permute-start(bf16[256,2048]{1,0:T(8,128)(2,1)S(1)} %add_convert_fusion.1), channel_id=1, source_target_pairs={{0,1},{1,0},{2,3},{3,2},{4,5},{5,4},{6,7},{7,6},{8,9},{9,8},{10,11... | collective-permute-start | bytes 3145736 | tf_op jit(solution)/shard_map/ppermute | solution.py:17
  5.1 21.3 %collective-permute-start.9 = (bf16[128,512]{1,0:T(8,128)(2,1)S(1)}, bf16[128,512]{1,0:T(8,128)(2,1)}, u32[]{:S(2)}, u32[]{:S(2)}) collective-permute-start(bf16[128,512]{1,0:T(8,128)(2,1)S(1)} %get-tuple-element.24), channel_id=1, source_target_pairs={{0,1},{1,0},{2,3},{3,2},{4,5},{5,4},{6,7},{7,6},{8,9},{9,8},{10,11... | collective-permute-start | bytes 393224 | tf_op jit(solution)/shard_map/ppermute | solution.py:17
  5.7 14.3 %collective-permute-start.17 = (s32[2,2]{1,0:T(2,128)S(1)}, s32[2,2]{1,0:T(2,128)S(1)}, u32[]{:S(2)}, u32[]{:S(2)}) collective-permute-start(s32[2,2]{1,0:T(2,128)S(1)} %bitcast.147), channel_id=1, source_target_pairs={{0,1},{1,0},{2,3},{3,2},{4,5},{5,4},{6,7},{7,6},{8,9},{9,8},{10,11... | collective-permute-start | bytes 56 | tf_op jit(solution)/shard_map/ppermute | solution.py:17
  7.7 120.5 %collective-permute-start.22 = (bf16[256,512]{0,1:T(8,128)(2,1)}, bf16[256,512]{0,1:T(8,128)(2,1)}, u32[]{:S(2)}, u32[]{:S(2)}) collective-permute-start(bf16[256,512]{0,1:T(8,128)(2,1)} %get-tuple-element.17), channel_id=1, source_target_pairs={{0,1},{1,0},{2,3},{3,2},{4,5},{5,4},{6,7},{7,6},{8,9},{9,8},{10,11... | collective-permute-start | bytes 786440 | tf_op jit(solution)/shard_map/ppermute | solution.py:17
  19.7 13.6 %collective-permute-start.2 = (bf16[256,1024]{1,0:T(8,128)(2,1)S(1)}, bf16[256,1024]{1,0:T(8,128)(2,1)}, u32[]{:S(2)}, u32[]{:S(2)}) collective-permute-start(bf16[256,1024]{1,0:T(8,128)(2,1)S(1)} %constant_dynamic-update-slice_fusion.17), channel_id=1, source_target_pairs={{0,4},{4,8},{8,12},{12,14},{14,10},{10,6},{6,2},{2,0},{1,5},{5,9},... | collective-permute-start | bytes 1572872 | tf_op jit(solution)/shard_map/ppermute | solution.py:38
  19.9 13.6 %collective-permute-start.3 = (bf16[256,1024]{1,0:T(8,128)(2,1)S(1)}, bf16[256,1024]{1,0:T(8,128)(2,1)}, u32[]{:S(2)}, u32[]{:S(2)}) collective-permute-start(bf16[256,1024]{1,0:T(8,128)(2,1)S(1)} %constant_dynamic-update-slice_fusion.17), channel_id=1, source_target_pairs={{0,2},{4,0},{8,4},{12,8},{14,12},{10,14},{6,10},{2,6},{1,3},{5,1},... | collective-permute-start | bytes 1572872 | tf_op jit(solution)/shard_map/ppermute | solution.py:41
  33.3 12.8 %collective-permute-start.4 = (bf16[256,1024]{1,0:T(8,128)(2,1)}, bf16[256,1024]{1,0:T(8,128)(2,1)S(1)}, u32[]{:S(2)}, u32[]{:S(2)}) collective-permute-start(bf16[256,1024]{1,0:T(8,128)(2,1)} %collective-permute-done.2), channel_id=1, source_target_pairs={{0,4},{4,8},{8,12},{12,14},{14,10},{10,6},{6,2},{2,0},{1,5},{5,9},... | collective-permute-start | bytes 1572872 | tf_op jit(solution)/shard_map/ppermute | solution.py:38
  33.5 12.8 %collective-permute-start.5 = (bf16[256,1024]{1,0:T(8,128)(2,1)}, bf16[256,1024]{1,0:T(8,128)(2,1)S(1)}, u32[]{:S(2)}, u32[]{:S(2)}) collective-permute-start(bf16[256,1024]{1,0:T(8,128)(2,1)} %collective-permute-done.3), channel_id=1, source_target_pairs={{0,2},{4,0},{8,4},{12,8},{14,12},{10,14},{6,10},{2,6},{1,3},{5,1},... | collective-permute-start | bytes 1572872 | tf_op jit(solution)/shard_map/ppermute | solution.py:41
  46.1 11.7 %collective-permute-start.6 = (bf16[256,1024]{1,0:T(8,128)(2,1)S(1)}, bf16[256,1024]{1,0:T(8,128)(2,1)S(1)}, u32[]{:S(2)}, u32[]{:S(2)}) collective-permute-start(bf16[256,1024]{1,0:T(8,128)(2,1)S(1)} %collective-permute-done.4), channel_id=1, source_target_pairs={{0,4},{4,8},{8,12},{12,14},{14,10},{10,6},{6,2},{2,0},{1,5},{5,9},... | collective-permute-start | bytes 1572872 | tf_op jit(solution)/shard_map/ppermute | solution.py:38
  46.3 12.9 %collective-permute-start.7 = (bf16[256,1024]{1,0:T(8,128)(2,1)S(1)}, bf16[256,1024]{1,0:T(8,128)(2,1)S(1)}, u32[]{:S(2)}, u32[]{:S(2)}) collective-permute-start(bf16[256,1024]{1,0:T(8,128)(2,1)S(1)} %collective-permute-done.5), channel_id=1, source_target_pairs={{0,2},{4,0},{8,4},{12,8},{14,12},{10,14},{6,10},{2,6},{1,3},{5,1},... | collective-permute-start | bytes 1572872 | tf_op jit(solution)/shard_map/ppermute | solution.py:41
  57.8 10.7 %collective-permute-start.8 = (bf16[256,1024]{1,0:T(8,128)(2,1)S(1)}, bf16[256,1024]{1,0:T(8,128)(2,1)S(1)}, u32[]{:S(2)}, u32[]{:S(2)}) collective-permute-start(bf16[256,1024]{1,0:T(8,128)(2,1)S(1)} %collective-permute-done.6), channel_id=1, source_target_pairs={{0,4},{4,8},{8,12},{12,14},{14,10},{10,6},{6,2},{2,0},{1,5},{5,9},... | collective-permute-start | bytes 1572872 | tf_op jit(solution)/shard_map/ppermute | solution.py:38
  75.4 4.4 %copy-start.2 = (bf16[256,512]{1,0:T(8,128)(2,1)S(1)}, bf16[256,512]{1,0:T(8,128)(2,1)}, u32[]{:S(2)}) copy-start(bf16[256,512]{1,0:T(8,128)(2,1)} %copy-done.1) | copy-start | bytes 786436
  75.4 5.9 %copy-start.6 = (bf16[256,1024]{1,0:T(8,128)(2,1)S(1)}, bf16[256,1024]{1,0:T(8,128)(2,1)}, u32[]{:S(2)}) copy-start(bf16[256,1024]{1,0:T(8,128)(2,1)} %copy-done.5) | copy-start | bytes 1572868
  75.8 8.6 %collective-permute-start.18 = (f32[4,128,128]{2,1,0:T(8,128)S(1)}, f32[4,128,128]{2,1,0:T(8,128)S(1)}, u32[]{:S(2)}, u32[]{:S(2)}) collective-permute-start(f32[4,128,128]{2,1,0:T(8,128)S(1)} %fusion.36), channel_id=1, source_target_pairs={{0,2},{2,4},{4,6},{6,8},{8,10},{10,12},{12,14},{1,3},{3,5},{5,7},{... | collective-permute-start | bytes 786440 | tf_op jit(solution)/shard_map/ppermute | solution.py:55
  79.8 9.2 %collective-permute-start.10 = (bf16[256,512]{1,0:T(8,128)(2,1)S(1)}, bf16[256,512]{1,0:T(8,128)(2,1)S(1)}, u32[]{:S(2)}, u32[]{:S(2)}) collective-permute-start(bf16[256,512]{1,0:T(8,128)(2,1)S(1)} %copy-done.2), channel_id=1, source_target_pairs={{0,4},{4,8},{8,12},{12,14},{14,10},{10,6},{6,2},{2,0},{1,5},{5,9},... | collective-permute-start | bytes 786440 | tf_op jit(solution)/shard_map/ppermute | solution.py:38
  80.0 7.7 %collective-permute-start.11 = (bf16[256,512]{1,0:T(8,128)(2,1)S(1)}, bf16[256,512]{1,0:T(8,128)(2,1)S(1)}, u32[]{:S(2)}, u32[]{:S(2)}) collective-permute-start(bf16[256,512]{1,0:T(8,128)(2,1)S(1)} %copy-done.2), channel_id=1, source_target_pairs={{0,2},{4,0},{8,4},{12,8},{14,12},{10,14},{6,10},{2,6},{1,3},{5,1},... | collective-permute-start | bytes 786440 | tf_op jit(solution)/shard_map/ppermute | solution.py:41
  84.4 10.3 %collective-permute-start.19 = (f32[4,128,128]{2,1,0:T(8,128)S(1)}, f32[4,128,128]{2,1,0:T(8,128)S(1)}, u32[]{:S(2)}, u32[]{:S(2)}) collective-permute-start(f32[4,128,128]{2,1,0:T(8,128)S(1)} %fusion.120), channel_id=1, source_target_pairs={{0,4},{2,6},{4,8},{6,10},{8,12},{10,14},{1,5},{3,7},{5,9},{7,11},{... | collective-permute-start | bytes 786440 | tf_op jit(solution)/shard_map/ppermute | solution.py:55
  87.7 12.6 %collective-permute-start.13 = (bf16[256,512]{1,0:T(8,128)(2,1)S(1)}, bf16[256,512]{1,0:T(8,128)(2,1)S(1)}, u32[]{:S(2)}, u32[]{:S(2)}) collective-permute-start(bf16[256,512]{1,0:T(8,128)(2,1)S(1)} %collective-permute-done.11), channel_id=1, source_target_pairs={{0,2},{4,0},{8,4},{12,8},{14,12},{10,14},{6,10},{2,6},{1,3},{5,1},... | collective-permute-start | bytes 786440 | tf_op jit(solution)/shard_map/ppermute | solution.py:41
  89.3 12.3 %collective-permute-start.12 = (bf16[256,512]{1,0:T(8,128)(2,1)S(1)}, bf16[256,512]{1,0:T(8,128)(2,1)S(1)}, u32[]{:S(2)}, u32[]{:S(2)}) collective-permute-start(bf16[256,512]{1,0:T(8,128)(2,1)S(1)} %collective-permute-done.10), channel_id=1, source_target_pairs={{0,4},{4,8},{8,12},{12,14},{14,10},{10,6},{6,2},{2,0},{1,5},{5,9},... | collective-permute-start | bytes 786440 | tf_op jit(solution)/shard_map/ppermute | solution.py:38
  94.7 23.5 %collective-permute-start.20 = (f32[4,128,128]{2,1,0:T(8,128)S(1)}, f32[4,128,128]{2,1,0:T(8,128)S(1)}, u32[]{:S(2)}, u32[]{:S(2)}) collective-permute-start(f32[4,128,128]{2,1,0:T(8,128)S(1)} %add.428), channel_id=1, source_target_pairs={{0,8},{2,10},{4,12},{6,14},{1,9},{3,11},{5,13},{7,15},{16,24},{18,... | collective-permute-start | bytes 786440 | tf_op jit(solution)/shard_map/ppermute | solution.py:55
  100.3 15.7 %collective-permute-start.15 = (bf16[256,512]{1,0:T(8,128)(2,1)S(1)}, bf16[256,512]{1,0:T(8,128)(2,1)S(1)}, u32[]{:S(2)}, u32[]{:S(2)}) collective-permute-start(bf16[256,512]{1,0:T(8,128)(2,1)S(1)} %collective-permute-done.13), channel_id=1, source_target_pairs={{0,2},{4,0},{8,4},{12,8},{14,12},{10,14},{6,10},{2,6},{1,3},{5,1},... | collective-permute-start | bytes 786440 | tf_op jit(solution)/shard_map/ppermute | solution.py:41
  101.6 14.6 %collective-permute-start.14 = (bf16[256,512]{1,0:T(8,128)(2,1)S(1)}, bf16[256,512]{1,0:T(8,128)(2,1)S(1)}, u32[]{:S(2)}, u32[]{:S(2)}) collective-permute-start(bf16[256,512]{1,0:T(8,128)(2,1)S(1)} %collective-permute-done.12), channel_id=1, source_target_pairs={{0,4},{4,8},{8,12},{12,14},{14,10},{10,6},{6,2},{2,0},{1,5},{5,9},... | collective-permute-start | bytes 786440 | tf_op jit(solution)/shard_map/ppermute | solution.py:38
  116.3 6.2 %collective-permute-start.16 = (bf16[256,512]{1,0:T(8,128)(2,1)S(1)}, bf16[256,512]{1,0:T(8,128)(2,1)S(1)}, u32[]{:S(2)}, u32[]{:S(2)}) collective-permute-start(bf16[256,512]{1,0:T(8,128)(2,1)S(1)} %collective-permute-done.14), channel_id=1, source_target_pairs={{0,4},{4,8},{8,12},{12,14},{14,10},{10,6},{6,2},{2,0},{1,5},{5,9},... | collective-permute-start | bytes 786440 | tf_op jit(solution)/shard_map/ppermute | solution.py:38
  132.1 8.0 %collective-permute-start.23 = (f32[4,128,128]{2,1,0:T(8,128)S(1)}, f32[4,128,128]{2,1,0:T(8,128)S(1)}, u32[]{:S(2)}, u32[]{:S(2)}) collective-permute-start(f32[4,128,128]{2,1,0:T(8,128)S(1)} %fusion.37), channel_id=1, source_target_pairs={{2,0},{4,2},{6,4},{8,6},{10,8},{12,10},{14,12},{3,1},{5,3},{7,5},{... | collective-permute-start | bytes 786440 | tf_op jit(solution)/shard_map/ppermute | solution.py:55
  134.8 13.8 %copy-start.10 = (bf16[256,512]{1,0:T(8,128)(2,1)S(1)}, bf16[256,512]{1,0:T(8,128)(2,1)}, u32[]{:S(2)}) copy-start(bf16[256,512]{1,0:T(8,128)(2,1)} %copy-done.9) | copy-start | bytes 786436
  140.1 7.1 %collective-permute-start.24 = (f32[4,128,128]{2,1,0:T(8,128)S(1)}, f32[4,128,128]{2,1,0:T(8,128)S(1)}, u32[]{:S(2)}, u32[]{:S(2)}) collective-permute-start(f32[4,128,128]{2,1,0:T(8,128)S(1)} %fusion.119), channel_id=1, source_target_pairs={{4,0},{6,2},{8,4},{10,6},{12,8},{14,10},{5,1},{7,3},{9,5},{11,7},{... | collective-permute-start | bytes 786440 | tf_op jit(solution)/shard_map/ppermute | solution.py:55
  147.3 10.3 %collective-permute-start.25 = (f32[4,128,128]{2,1,0:T(8,128)S(1)}, f32[4,128,128]{2,1,0:T(8,128)S(1)}, u32[]{:S(2)}, u32[]{:S(2)}) collective-permute-start(f32[4,128,128]{2,1,0:T(8,128)S(1)} %add.440), channel_id=1, source_target_pairs={{8,0},{10,2},{12,4},{14,6},{9,1},{11,3},{13,5},{15,7},{24,16},{26,... | collective-permute-start | bytes 786440 | tf_op jit(solution)/shard_map/ppermute | solution.py:55
  165.1 20.9 %collective-permute-start.26 = (f32[256,2048]{1,0:T(8,128)S(1)}, f32[256,2048]{1,0:T(8,128)}, u32[]{:S(2)}, u32[]{:S(2)}) collective-permute-start(f32[256,2048]{1,0:T(8,128)S(1)} %convolution_add_fusion), channel_id=1, source_target_pairs={{0,1},{1,0},{2,3},{3,2},{4,5},{5,4},{6,7},{7,6},{8,9},{9,8},{10,11... | collective-permute-start | bytes 6291464 | tf_op jit(solution)/shard_map/ppermute | solution.py:17
  177.4 4.0 %collective-permute-start.21 = (bf16[256,512]{1,0:T(8,128)(2,1)S(1)}, bf16[256,512]{1,0:T(8,128)(2,1)S(1)}, u32[]{:S(2)}, u32[]{:S(2)}) collective-permute-start(bf16[256,512]{1,0:T(8,128)(2,1)S(1)} %copy.20), channel_id=1, source_target_pairs={{0,1},{1,0},{2,3},{3,2},{4,5},{5,4},{6,7},{7,6},{8,9},{9,8},{10,11... | collective-permute-start | bytes 786440 | tf_op jit(solution)/shard_map/ppermute | solution.py:17
  182.3 3.7 %copy-start.11 = (bf16[1,256,4,128]{1,3,2,0:T(8,128)(2,1)S(1)}, bf16[1,256,4,128]{1,3,2,0:T(8,128)(2,1)}, u32[]{:S(2)}) copy-start(bf16[1,256,4,128]{1,3,2,0:T(8,128)(2,1)} %get-tuple-element.14) | copy-start | bytes 786436
  (11 other events, 23.7 us)

commit v4 on v3

--- a/solution.py
+++ b/solution.py
@@ -23,23 +23,33 @@
     return list(range(0, chips, 2)) + list(range(chips - 1, 0, -2))
 
 
-def ring_gather(block, chips, c):
+def ring_gather(block, chips, c, p):
     order = ring_order(chips)
     place = np.zeros(chips, np.int32)
     place[np.asarray(order)] = np.arange(chips)
     order_t = jnp.asarray(order, jnp.int32)
     here = jnp.asarray(place)[c]
-    ahead = [(order[p], order[(p + 1) % chips]) for p in range(chips)]
-    behind = [(order[p], order[(p - 1) % chips]) for p in range(chips)]
-    got = [(c, block)]
-    fwd = block
-    bwd = block
+    ahead = [(order[p_], order[(p_ + 1) % chips]) for p_ in range(chips)]
+    behind = [(order[p_], order[(p_ - 1) % chips]) for p_ in range(chips)]
+    share = block.shape[1] // 3
+    width = block.shape[1] - share
+    groups = lax.axis_size("groups")
+    partner = [(g, g ^ 1) for g in range(groups)]
+
+    def land(piece):
+        sent = lax.dynamic_slice_in_dim(piece, p * share, share, axis=1)
+        other = lax.ppermute(sent, "groups", partner)
+        return [(piece, p * share), (other, (1 - p) * width)]
+
+    got = [(c, [(block, 0)])]
+    fwd = lax.dynamic_slice_in_dim(block, p * share, width, axis=1)
+    bwd = fwd
     for step in range(1, chips // 2 + 1):
         fwd = lax.ppermute(fwd, "chip", ahead)
-        got.append((order_t[(here - step) % chips], fwd))
+        got.append((order_t[(here - step) % chips], land(fwd)))
         if step <= (chips - 1) // 2:
             bwd = lax.ppermute(bwd, "chip", behind)
-            got.append((order_t[(here + step) % chips], bwd))
+            got.append((order_t[(here + step) % chips], land(bwd)))
     return got
 
 
@@ -95,26 +105,16 @@
         return lax.dynamic_update_slice_in_dim(block, recv, (1 - k) * rows_dev, axis=0)
 
     span = 2 * rows_dev
-
-    def project(pieces):
-        out = None
-        full = jnp.zeros((chips * span, pieces[0][1].shape[1]), bf16)
-        for src, piece in pieces:
-            x_cols = lax.dynamic_slice_in_dim(x_pair, src * span, span, axis=1)
-            term = jnp.dot(x_cols, piece, preferred_element_type=f32)
-            out = term if out is None else out + term
-            full = lax.dynamic_update_slice_in_dim(full, piece, src * span, axis=0)
-        return out.astype(bf16), full
-
-    kv_pieces = ring_gather(chip_block((w_key, w_value)), chips, c)
-    q_block, _ = lax.optimization_barrier((chip_block((w_query,)), kv_pieces[-1][1]))
-    q_pieces = ring_gather(q_block, chips, c)
-    kv_proj, w_kv = project(kv_pieces)
-    q_proj, w_q = project(q_pieces)
-    kv_proj = kv_proj.reshape(2, tok, 2, heads, DH)
-    query = q_proj.reshape(2, tok, heads, DH)
-    key = kv_proj[:, :, 0]
-    value = kv_proj[:, :, 1]
+    block = chip_block((w_query, w_key, w_value))
+    w_half = jnp.zeros((chips * span, block.shape[1]), bf16)
+    for src, parts in ring_gather(block, chips, c, lax.axis_index("groups") % 2):
+        for piece, col in parts:
+            w_half = lax.dynamic_update_slice(w_half, piece, (src * span, col))
+    projected = jnp.dot(x_pair, w_half, preferred_element_type=f32).astype(bf16)
+    projected = projected.reshape(2, tok, 3, heads, DH)
+    query = projected[:, :, 0]
+    key = projected[:, :, 1]
+    value = projected[:, :, 2]
 
     local = jnp.einsum("jthd,jthe->jhde", key, value, preferred_element_type=f32)
     state0 = exclusive_scan(local[0] + local[1], chips, False)
@@ -162,12 +162,10 @@
     d_key = d_key + jnp.einsum("jshe,jhde->jshd", value, later_b, preferred_element_type=f32)
     d_value = jnp.einsum("jhts,jthe->jshe", attn, d_mixed_b, preferred_element_type=f32)
     d_value = d_value + jnp.einsum("jshd,jhde->jshe", key, later_b, preferred_element_type=f32)
-    dq_b = d_query.astype(bf16).reshape(2, tok, half)
-    dkv_b = jnp.stack([d_key, d_value], axis=2).astype(bf16).reshape(2, tok, 2 * half)
+    d_proj = jnp.stack([d_query, d_key, d_value], axis=2).astype(bf16).reshape(2, tok, 3 * half)
 
     def grad_rows(j):
-        g = lax.dot_general(dq_b[j], w_q, (((1,), (1,)), ((), ())), preferred_element_type=f32)
-        return g + lax.dot_general(dkv_b[j], w_kv, (((1,), (1,)), ((), ())), preferred_element_type=f32)
+        return lax.dot_general(d_proj[j], w_half, (((1,), (1,)), ((), ())), preferred_element_type=f32)
 
     received = swap(grad_rows(1))
     grad_input = (grad_rows(0) + received).astype(bf16)

time: 191 us -> 252 us (1.32)
  the two profiles are of different devices: /device:TPU:15 before, /device:TPU:0 now
where the time goes in v4:
time: 252 us; the launch traced here: 251 us
  local copies, waits for them, and re-layouts  91.4 us (36%)
  waiting for transfers between devices  84.7 us (34%)
  starting transfers between devices  36.8 us (15%)
  matrix products  18.9 us (7%)
  between operations  10.3 us (4%)
  other arithmetic  8.78 us (3%)
    dynamic_update_slice x15, local copies, waits for them, and re-layouts, on_device(): w_half = lax.dynamic_update_slice(w_half, piece, (src * span, col))  72.9 us
    ppermute x6, waiting for transfers between devices, exclusive_scan(): got = lax.ppermute(incl, 'chip', perm)  46.4 us
    ppermute x4, waiting for transfers between devices, ring_gather(): fwd = lax.ppermute(fwd, 'chip', ahead)  33.3 us
    ppermute x6, starting transfers between devices, exclusive_scan(): got = lax.ppermute(incl, 'chip', perm)  18.9 us
    dot_general x2, matrix products, grad_rows(): lax.dot_general(d_proj[j], w_half, (((1,), (1,)), ((), ())), preferred_el...  9.4 us
    ppermute x7, starting transfers between devices, land(): other = lax.ppermute(sent, 'groups', partner)  8.04 us
    ppermute x4, starting transfers between devices, ring_gather(): fwd = lax.ppermute(fwd, 'chip', ahead)  7.41 us
    unnamed x35, local copies, waits for them, and re-layouts  6.37 us
  transfers between devices with their start and end apart: 26, of which 13 were waited for; matrix products, arithmetic and copies ran while one was open for 39% of the time, Pallas kernels for 0%

profile of v4, /device:TPU:0, one launch (start us, length us, event | category | flops | bytes accessed | tf_op | source)
XLA Modules:
  0.0 250.9 jit_solution(8420271556066928891)
XLA Ops:
  4.8 3.0 %collective-permute-start.2 = (bf16[256,1024]{1,0:T(8,128)(2,1)S(1)}, bf16[256,1024]{1,0:T(8,128)(2,1)S(1)}, u32[]{:S(2)}, u32[]{:S(2)}) collective-permute-start(bf16[256,1024]{1,0:T(8,128)(2,1)S(1)} %constant_dynamic-slice_fusion.7), channel_id=1, source_target_pairs={{0,4},{4,8},{8,12},{12,14},{14,10},{10,6},{6,2},{2,0},{1,5},{5,9},... | collective-permute-start | bytes 1572872 | tf_op jit(solution)/shard_map/ppermute | solution.py:48
  7.8 12.2 %collective-permute-done.2 = bf16[256,1024]{1,0:T(8,128)(2,1)S(1)} collective-permute-done((bf16[256,1024]{1,0:T(8,128)(2,1)S(1)}, bf16[256,1024]{1,0:T(8,128)(2,1)S(1)}, u32[]{:S(2)}, u32[]{:S(2)}) %collective-permute-start.2) | collective-permute-done | bytes 524320 | tf_op jit(solution)/shard_map/ppermute | solution.py:48
  22.0 11.5 %collective-permute-done.6 = bf16[256,1024]{1,0:T(8,128)(2,1)} collective-permute-done((bf16[256,1024]{1,0:T(8,128)(2,1)S(1)}, bf16[256,1024]{1,0:T(8,128)(2,1)}, u32[]{:S(2)}, u32[]{:S(2)}) %collective-permute-start.6) | collective-permute-done | bytes 524320 | tf_op jit(solution)/shard_map/ppermute | solution.py:48
  40.4 5.9 %collective-permute-done.10 = bf16[256,1024]{1,0:T(8,128)(2,1)S(1)} collective-permute-done((bf16[256,1024]{1,0:T(8,128)(2,1)}, bf16[256,1024]{1,0:T(8,128)(2,1)S(1)}, u32[]{:S(2)}, u32[]{:S(2)}) %collective-permute-start.10) | collective-permute-done | bytes 524320 | tf_op jit(solution)/shard_map/ppermute | solution.py:48
  54.1 3.8 %collective-permute-done.14 = bf16[256,1024]{1,0:T(8,128)(2,1)S(1)} collective-permute-done((bf16[256,1024]{1,0:T(8,128)(2,1)S(1)}, bf16[256,1024]{1,0:T(8,128)(2,1)S(1)}, u32[]{:S(2)}, u32[]{:S(2)}) %collective-permute-start.14) | collective-permute-done | bytes 524320 | tf_op jit(solution)/shard_map/ppermute | solution.py:48
  73.5 6.3 %dynamic_update_slice.54 = bf16[2048,1536]{1,0:T(8,128)(2,1)S(1)} dynamic-update-slice(bf16[2048,1536]{1,0:T(8,128)(2,1)S(1)} %constant_dynamic-update-slice_fusion, bf16[256,1024]{1,0:T(8,128)(2,1)S(1)} %copy-done.2, s32[]{:T(128)S(6)} %select_n.207, s32[]{:T(128)S(6)} %select_n.203) | dynamic-update-slice | bytes 1048580 | tf_op jit(solution)/shard_map/dynamic_update_slice | solution.py:112
  79.9 3.0 %dynamic_update_slice.55 = bf16[2048,1536]{1,0:T(8,128)(2,1)S(1)} dynamic-update-slice(bf16[2048,1536]{1,0:T(8,128)(2,1)S(1)} %dynamic_update_slice.54, bf16[256,512]{1,0:T(8,128)(2,1)S(1)} %copy-done.7, s32[]{:T(128)S(6)} %select_n.207, s32[]{:T(128)S(6)} %select_n.209) | dynamic-update-slice | bytes 524292 | tf_op jit(solution)/shard_map/dynamic_update_slice | solution.py:112
  82.9 6.4 %dynamic_update_slice.56 = bf16[2048,1536]{1,0:T(8,128)(2,1)S(1)} dynamic-update-slice(bf16[2048,1536]{1,0:T(8,128)(2,1)S(1)} %dynamic_update_slice.55, bf16[256,1024]{1,0:T(8,128)(2,1)S(1)} %collective-permute-done.4, s32[]{:T(128)S(6)} %select_n.212, s32[]{:T(128)S(6)} %select_n.203) | dynamic-update-slice | bytes 1048580 | tf_op jit(solution)/shard_map/dynamic_update_slice | solution.py:112
  89.3 3.0 %dynamic_update_slice.57 = bf16[2048,1536]{1,0:T(8,128)(2,1)S(1)} dynamic-update-slice(bf16[2048,1536]{1,0:T(8,128)(2,1)S(1)} %dynamic_update_slice.56, bf16[256,512]{1,0:T(8,128)(2,1)S(1)} %copy-done.9, s32[]{:T(128)S(6)} %select_n.212, s32[]{:T(128)S(6)} %select_n.209) | dynamic-update-slice | bytes 524292 | tf_op jit(solution)/shard_map/dynamic_update_slice | solution.py:112
  92.3 7.6 %dynamic_update_slice.58 = bf16[2048,1536]{1,0:T(8,128)(2,1)S(1)} dynamic-update-slice(bf16[2048,1536]{1,0:T(8,128)(2,1)S(1)} %dynamic_update_slice.57, bf16[256,1024]{1,0:T(8,128)(2,1)} %collective-permute-done.6, s32[]{:T(128)S(6)} %select_n.215, s32[]{:T(128)S(6)} %select_n.203) | dynamic-update-slice | bytes 1048580 | tf_op jit(solution)/shard_map/dynamic_update_slice | solution.py:112
  99.9 3.0 %dynamic_update_slice.59 = bf16[2048,1536]{1,0:T(8,128)(2,1)S(1)} dynamic-update-slice(bf16[2048,1536]{1,0:T(8,128)(2,1)S(1)} %dynamic_update_slice.58, bf16[256,512]{1,0:T(8,128)(2,1)S(1)} %copy-done.11, s32[]{:T(128)S(6)} %select_n.215, s32[]{:T(128)S(6)} %select_n.209) | dynamic-update-slice | bytes 524292 | tf_op jit(solution)/shard_map/dynamic_update_slice | solution.py:112
  103.0 7.6 %dynamic_update_slice.60 = bf16[2048,1536]{1,0:T(8,128)(2,1)S(1)} dynamic-update-slice(bf16[2048,1536]{1,0:T(8,128)(2,1)S(1)} %dynamic_update_slice.59, bf16[256,1024]{1,0:T(8,128)(2,1)} %collective-permute-done.8, s32[]{:T(128)S(6)} %select_n.218, s32[]{:T(128)S(6)} %select_n.203) | dynamic-update-slice | bytes 1048580 | tf_op jit(solution)/shard_map/dynamic_update_slice | solution.py:112
  110.7 4.5 %dynamic_update_slice.61 = bf16[2048,1536]{1,0:T(8,128)(2,1)S(1)} dynamic-update-slice(bf16[2048,1536]{1,0:T(8,128)(2,1)S(1)} %dynamic_update_slice.60, bf16[256,512]{1,0:T(8,128)(2,1)} %collective-permute-done.9, s32[]{:T(128)S(6)} %select_n.218, s32[]{:T(128)S(6)} %select_n.209) | dynamic-update-slice | bytes 524292 | tf_op jit(solution)/shard_map/dynamic_update_slice | solution.py:112
  115.2 6.4 %dynamic_update_slice.62 = bf16[2048,1536]{1,0:T(8,128)(2,1)S(1)} dynamic-update-slice(bf16[2048,1536]{1,0:T(8,128)(2,1)S(1)} %dynamic_update_slice.61, bf16[256,1024]{1,0:T(8,128)(2,1)S(1)} %collective-permute-done.10, s32[]{:T(128)S(6)} %select_n.221, s32[]{:T(128)S(6)} %select_n.203) | dynamic-update-slice | bytes 1048580 | tf_op jit(solution)/shard_map/dynamic_update_slice | solution.py:112
  122.1 4.4 %dynamic_update_slice.63 = bf16[2048,1536]{1,0:T(8,128)(2,1)S(1)} dynamic-update-slice(bf16[2048,1536]{1,0:T(8,128)(2,1)S(1)} %dynamic_update_slice.62, bf16[256,512]{1,0:T(8,128)(2,1)} %collective-permute-done.11, s32[]{:T(128)S(6)} %select_n.221, s32[]{:T(128)S(6)} %select_n.209) | dynamic-update-slice | bytes 524292 | tf_op jit(solution)/shard_map/dynamic_update_slice | solution.py:112
  126.5 6.4 %dynamic_update_slice.64 = bf16[2048,1536]{1,0:T(8,128)(2,1)S(1)} dynamic-update-slice(bf16[2048,1536]{1,0:T(8,128)(2,1)S(1)} %dynamic_update_slice.63, bf16[256,1024]{1,0:T(8,128)(2,1)S(1)} %collective-permute-done.12, s32[]{:T(128)S(6)} %select_n.224, s32[]{:T(128)S(6)} %select_n.203) | dynamic-update-slice | bytes 1048580 | tf_op jit(solution)/shard_map/dynamic_update_slice | solution.py:112
  132.9 4.5 %dynamic_update_slice.65 = bf16[2048,1536]{1,0:T(8,128)(2,1)S(1)} dynamic-update-slice(bf16[2048,1536]{1,0:T(8,128)(2,1)S(1)} %dynamic_update_slice.64, bf16[256,512]{1,0:T(8,128)(2,1)} %collective-permute-done.13, s32[]{:T(128)S(6)} %select_n.224, s32[]{:T(128)S(6)} %select_n.209) | dynamic-update-slice | bytes 524292 | tf_op jit(solution)/shard_map/dynamic_update_slice | solution.py:112
  137.5 5.6 %dynamic_update_slice.66 = bf16[2048,1536]{1,0:T(8,128)(2,1)S(1)} dynamic-update-slice(bf16[2048,1536]{1,0:T(8,128)(2,1)S(1)} %dynamic_update_slice.65, bf16[256,1024]{1,0:T(8,128)(2,1)S(1)} %collective-permute-done.14, s32[]{:T(128)S(6)} %select_n.227, s32[]{:T(128)S(6)} %select_n.203) | dynamic-update-slice | bytes 1048580 | tf_op jit(solution)/shard_map/dynamic_update_slice | solution.py:112
  143.1 4.0 %dynamic_update_slice.67 = bf16[2048,1536]{1,0:T(8,128)(2,1)S(1)} dynamic-update-slice(bf16[2048,1536]{1,0:T(8,128)(2,1)S(1)} %dynamic_update_slice.66, bf16[256,512]{1,0:T(8,128)(2,1)} %collective-permute-done.15, s32[]{:T(128)S(6)} %select_n.227, s32[]{:T(128)S(6)} %select_n.209) | dynamic-update-slice | bytes 524292 | tf_op jit(solution)/shard_map/dynamic_update_slice | solution.py:112
  149.8 4.9 %convolution_convert_fusion = bf16[512,1536]{1,0:T(8,128)(2,1)S(1)} fusion(bf16[2048,1536]{1,0:T(8,128)(2,1)S(1)} %dynamic_update_slice.67, bf16[256,2048]{1,0:T(8,128)(2,1)} %collective-permute-done, bf16[256,2048]{1,0:T(8,128)(2,1)} %add_convert_fusion), kind=kOutput, calls=%fused_computation | convolution fusion | flops 3226206208 | bytes 9961472 | tf_op jit(solution)/shard_map/dot_general | solution.py:113
  158.9 3.5 %collective-permute-start.17 = (f32[4,128,128]{2,1,0:T(8,128)}, f32[4,128,128]{2,1,0:T(8,128)}, u32[]{:S(2)}, u32[]{:S(2)}) collective-permute-start(f32[4,128,128]{2,1,0:T(8,128)} %fusion.27), channel_id=1, source_target_pairs={{0,2},{2,4},{4,6},{6,8},{8,10},{10,12},{12,14},{1,3},{3,5},{5,7},{... | collective-permute-start | bytes 786440 | tf_op jit(solution)/shard_map/ppermute | solution.py:65
  163.1 4.7 %collective-permute-done.17 = f32[4,128,128]{2,1,0:T(8,128)} collective-permute-done((f32[4,128,128]{2,1,0:T(8,128)}, f32[4,128,128]{2,1,0:T(8,128)}, u32[]{:S(2)}, u32[]{:S(2)}) %collective-permute-start.17) | collective-permute-done | bytes 262176 | tf_op jit(solution)/shard_map/ppermute | solution.py:65
  168.8 5.8 %collective-permute-start.18 = (f32[4,128,128]{2,1,0:T(8,128)S(1)}, f32[4,128,128]{2,1,0:T(8,128)S(1)}, u32[]{:S(2)}, u32[]{:S(2)}) collective-permute-start(f32[4,128,128]{2,1,0:T(8,128)S(1)} %fusion.59), channel_id=1, source_target_pairs={{0,4},{2,6},{4,8},{6,10},{8,12},{10,14},{1,5},{3,7},{5,9},{7,11},{... | collective-permute-start | bytes 786440 | tf_op jit(solution)/shard_map/ppermute | solution.py:65
  175.0 4.5 %collective-permute-done.18 = f32[4,128,128]{2,1,0:T(8,128)S(1)} collective-permute-done((f32[4,128,128]{2,1,0:T(8,128)S(1)}, f32[4,128,128]{2,1,0:T(8,128)S(1)}, u32[]{:S(2)}, u32[]{:S(2)}) %collective-permute-start.18) | collective-permute-done | bytes 262176 | tf_op jit(solution)/shard_map/ppermute | solution.py:65
  179.6 5.7 %collective-permute-start.19 = (f32[4,128,128]{2,1,0:T(8,128)S(1)}, f32[4,128,128]{2,1,0:T(8,128)S(1)}, u32[]{:S(2)}, u32[]{:S(2)}) collective-permute-start(f32[4,128,128]{2,1,0:T(8,128)S(1)} %add.274), channel_id=1, source_target_pairs={{0,8},{2,10},{4,12},{6,14},{1,9},{3,11},{5,13},{7,15},{16,24},{18,... | collective-permute-start | bytes 786440 | tf_op jit(solution)/shard_map/ppermute | solution.py:65
  185.8 3.6 %collective-permute-done.19 = f32[4,128,128]{2,1,0:T(8,128)S(1)} collective-permute-done((f32[4,128,128]{2,1,0:T(8,128)S(1)}, f32[4,128,128]{2,1,0:T(8,128)S(1)}, u32[]{:S(2)}, u32[]{:S(2)}) %collective-permute-start.19) | collective-permute-done | bytes 262176 | tf_op jit(solution)/shard_map/ppermute | solution.py:65
  196.1 6.2 %collective-permute-done.22 = f32[4,128,128]{2,1,0:T(8,128)S(1)} collective-permute-done((f32[4,128,128]{2,1,0:T(8,128)S(1)}, f32[4,128,128]{2,1,0:T(8,128)S(1)}, u32[]{:S(2)}, u32[]{:S(2)}) %collective-permute-start.22) | collective-permute-done | bytes 262176 | tf_op jit(solution)/shard_map/ppermute | solution.py:65
  204.0 14.1 %collective-permute-done.23 = f32[4,128,128]{2,1,0:T(8,128)S(1)} collective-permute-done((f32[4,128,128]{2,1,0:T(8,128)S(1)}, f32[4,128,128]{2,1,0:T(8,128)S(1)}, u32[]{:S(2)}, u32[]{:S(2)}) %collective-permute-start.23) | collective-permute-done | bytes 262176 | tf_op jit(solution)/shard_map/ppermute | solution.py:65
  219.8 13.3 %collective-permute-done.24 = f32[4,128,128]{2,1,0:T(8,128)S(1)} collective-permute-done((f32[4,128,128]{2,1,0:T(8,128)S(1)}, f32[4,128,128]{2,1,0:T(8,128)S(1)}, u32[]{:S(2)}, u32[]{:S(2)}) %collective-permute-start.24) | collective-permute-done | bytes 262176 | tf_op jit(solution)/shard_map/ppermute | solution.py:65
  236.0 3.2 %fusion.44 = f32[256,2048]{1,0:T(8,128)} fusion(bf16[256,1536]{0,1:T(8,128)(2,1)S(1)} %bitcast.131, bf16[2048,1536]{1,0:T(8,128)(2,1)S(1)} %bitcast.124), kind=kOutput, calls=%fused_computation.99 | convolution fusion | flops 1610612736 | bytes 9175040 | tf_op jit(solution)/shard_map/dot_general | solution.py:168
  240.1 3.6 %collective-permute-done.20 = bf16[256,512]{1,0:T(8,128)(2,1)S(1)} collective-permute-done((bf16[256,512]{1,0:T(8,128)(2,1)S(1)}, bf16[256,512]{1,0:T(8,128)(2,1)S(1)}, u32[]{:S(2)}, u32[]{:S(2)}) %collective-permute-start.20) | collective-permute-done | bytes 262176 | tf_op jit(solution)/shard_map/ppermute | solution.py:17
  244.6 6.2 %fusion = bf16[256,2048]{1,0:T(8,128)(2,1)} fusion(f32[256,2048]{1,0:T(8,128)} %collective-permute-done.25, bf16[256,1536]{0,1:T(8,128)(2,1)S(1)} %bitcast.130, bf16[2048,1536]{1,0:T(8,128)(2,1)} %copy-done), kind=kOutput, calls=%fused_computation.2 | convolution fusion | flops 1611661312 | bytes 10223616 | tf_op jit(solution)/shard_map/dot_general | solution.py:168
  (131 shorter events, 52.0 us)
Async XLA Ops:
  2.8 1.9 collective-permute-start.1
  3.3 31.7 %copy-start.3 = (bf16[256,2048]{1,0:T(8,128)(2,1)S(1)}, bf16[256,2048]{1,0:T(8,128)(2,1)}, u32[]{:S(2)}) copy-start(bf16[256,2048]{1,0:T(8,128)(2,1)} %param.10) | copy-start | bytes 3145732
  3.3 31.7 %copy-start.4 = (bf16[256,2048]{1,0:T(8,128)(2,1)S(1)}, bf16[256,2048]{1,0:T(8,128)(2,1)}, u32[]{:S(2)}) copy-start(bf16[256,2048]{1,0:T(8,128)(2,1)} %param.9) | copy-start | bytes 3145732
  3.3 33.1 %copy-start.5 = (bf16[256,1024]{1,0:T(8,128)(2,1)S(1)}, bf16[256,1024]{1,0:T(8,128)(2,1)}, u32[]{:S(2)}) copy-start(bf16[256,1024]{1,0:T(8,128)(2,1)} %param.11) | copy-start | bytes 1572868
  4.8 15.2 %collective-permute-start.2 = (bf16[256,1024]{1,0:T(8,128)(2,1)S(1)}, bf16[256,1024]{1,0:T(8,128)(2,1)S(1)}, u32[]{:S(2)}, u32[]{:S(2)}) collective-permute-start(bf16[256,1024]{1,0:T(8,128)(2,1)S(1)} %constant_dynamic-slice_fusion.7), channel_id=1, source_target_pairs={{0,4},{4,8},{8,12},{12,14},{14,10},{10,6},{6,2},{2,0},{1,5},{5,9},... | collective-permute-start | bytes 1572872 | tf_op jit(solution)/shard_map/ppermute | solution.py:48
  7.8 14.0 %collective-permute-start.4 = (bf16[256,1024]{1,0:T(8,128)(2,1)S(1)}, bf16[256,1024]{1,0:T(8,128)(2,1)S(1)}, u32[]{:S(2)}, u32[]{:S(2)}) collective-permute-start(bf16[256,1024]{1,0:T(8,128)(2,1)S(1)} %constant_dynamic-slice_fusion.7), channel_id=1, source_target_pairs={{0,2},{4,0},{8,4},{12,8},{14,12},{10,14},{6,10},{2,6},{1,3},{5,1},... | collective-permute-start | bytes 1572872 | tf_op jit(solution)/shard_map/ppermute | solution.py:51
  20.0 13.6 %collective-permute-start.6 = (bf16[256,1024]{1,0:T(8,128)(2,1)S(1)}, bf16[256,1024]{1,0:T(8,128)(2,1)}, u32[]{:S(2)}, u32[]{:S(2)}) collective-permute-start(bf16[256,1024]{1,0:T(8,128)(2,1)S(1)} %collective-permute-done.2), channel_id=1, source_target_pairs={{0,4},{4,8},{8,12},{12,14},{14,10},{10,6},{6,2},{2,0},{1,5},{5,9},... | collective-permute-start | bytes 1572872 | tf_op jit(solution)/shard_map/ppermute | solution.py:48
  21.8 14.8 %collective-permute-start.8 = (bf16[256,1024]{1,0:T(8,128)(2,1)S(1)}, bf16[256,1024]{1,0:T(8,128)(2,1)}, u32[]{:S(2)}, u32[]{:S(2)}) collective-permute-start(bf16[256,1024]{1,0:T(8,128)(2,1)S(1)} %collective-permute-done.4), channel_id=1, source_target_pairs={{0,2},{4,0},{8,4},{12,8},{14,12},{10,14},{6,10},{2,6},{1,3},{5,1},... | collective-permute-start | bytes 1572872 | tf_op jit(solution)/shard_map/ppermute | solution.py:51
  33.5 12.8 %collective-permute-start.10 = (bf16[256,1024]{1,0:T(8,128)(2,1)}, bf16[256,1024]{1,0:T(8,128)(2,1)S(1)}, u32[]{:S(2)}, u32[]{:S(2)}) collective-permute-start(bf16[256,1024]{1,0:T(8,128)(2,1)} %collective-permute-done.6), channel_id=1, source_target_pairs={{0,4},{4,8},{8,12},{12,14},{14,10},{10,6},{6,2},{2,0},{1,5},{5,9},... | collective-permute-start | bytes 1572872 | tf_op jit(solution)/shard_map/ppermute | solution.py:48
  36.4 30.9 %copy-start.12 = (s32[8]{0:T(128)S(1)}, s32[8]{0:T(128)}, u32[]{:S(2)}) copy-start(s32[8]{0:T(128)} %constant.116.clone) | copy-start | bytes 100
  36.4 110.8 %collective-permute-start = (bf16[256,2048]{1,0:T(8,128)(2,1)}, bf16[256,2048]{1,0:T(8,128)(2,1)}, u32[]{:S(2)}, u32[]{:S(2)}) collective-permute-start(bf16[256,2048]{1,0:T(8,128)(2,1)} %add_convert_fusion), channel_id=1, source_target_pairs={{0,1},{1,0},{2,3},{3,2},{4,5},{5,4},{6,7},{7,6},{8,9},{9,8},{10,11... | collective-permute-start | bytes 3145736 | tf_op jit(solution)/shard_map/ppermute | solution.py:17
  36.6 15.0 %collective-permute-start.12 = (bf16[256,1024]{1,0:T(8,128)(2,1)}, bf16[256,1024]{1,0:T(8,128)(2,1)S(1)}, u32[]{:S(2)}, u32[]{:S(2)}) collective-permute-start(bf16[256,1024]{1,0:T(8,128)(2,1)} %collective-permute-done.8), channel_id=1, source_target_pairs={{0,2},{4,0},{8,4},{12,8},{14,12},{10,14},{6,10},{2,6},{1,3},{5,1},... | collective-permute-start | bytes 1572872 | tf_op jit(solution)/shard_map/ppermute | solution.py:51
  39.0 19.7 %collective-permute-start.3 = (bf16[256,512]{1,0:T(8,128)(2,1)S(1)}, bf16[256,512]{1,0:T(8,128)(2,1)S(1)}, u32[]{:S(2)}, u32[]{:S(2)}) collective-permute-start(bf16[256,512]{1,0:T(8,128)(2,1)S(1)} %constant_dynamic-slice_fusion.6), channel_id=1, source_target_pairs={{0,16},{16,0},{1,17},{17,1},{2,18},{18,2},{3,19},{19,3},{4,20},{20... | collective-permute-start | bytes 786440 | tf_op jit(solution)/shard_map/ppermute | solution.py:41
  46.3 11.6 %collective-permute-start.14 = (bf16[256,1024]{1,0:T(8,128)(2,1)S(1)}, bf16[256,1024]{1,0:T(8,128)(2,1)S(1)}, u32[]{:S(2)}, u32[]{:S(2)}) collective-permute-start(bf16[256,1024]{1,0:T(8,128)(2,1)S(1)} %collective-permute-done.10), channel_id=1, source_target_pairs={{0,4},{4,8},{8,12},{12,14},{14,10},{10,6},{6,2},{2,0},{1,5},{5,9},... | collective-permute-start | bytes 1572872 | tf_op jit(solution)/shard_map/ppermute | solution.py:48
  47.4 12.6 %collective-permute-start.5 = (bf16[256,512]{1,0:T(8,128)(2,1)S(1)}, bf16[256,512]{1,0:T(8,128)(2,1)S(1)}, u32[]{:S(2)}, u32[]{:S(2)}) collective-permute-start(bf16[256,512]{1,0:T(8,128)(2,1)S(1)} %constant_dynamic-slice_fusion.5), channel_id=1, source_target_pairs={{0,16},{16,0},{1,17},{17,1},{2,18},{18,2},{3,19},{19,3},{4,20},{20... | collective-permute-start | bytes 786440 | tf_op jit(solution)/shard_map/ppermute | solution.py:41
  51.7 9.2 %collective-permute-start.7 = (bf16[256,512]{1,0:T(8,128)(2,1)S(1)}, bf16[256,512]{1,0:T(8,128)(2,1)S(1)}, u32[]{:S(2)}, u32[]{:S(2)}) collective-permute-start(bf16[256,512]{1,0:T(8,128)(2,1)S(1)} %constant_dynamic-slice_fusion.4), channel_id=1, source_target_pairs={{0,16},{16,0},{1,17},{17,1},{2,18},{18,2},{3,19},{19,3},{4,20},{20... | collective-permute-start | bytes 786440 | tf_op jit(solution)/shard_map/ppermute | solution.py:41
  57.9 52.7 %collective-permute-start.9 = (bf16[256,512]{1,0:T(8,128)(2,1)}, bf16[256,512]{1,0:T(8,128)(2,1)}, u32[]{:S(2)}, u32[]{:S(2)}) collective-permute-start(bf16[256,512]{1,0:T(8,128)(2,1)} %constant_dynamic-slice_fusion.3), channel_id=1, source_target_pairs={{0,16},{16,0},{1,17},{17,1},{2,18},{18,2},{3,19},{19,3},{4,20},{20... | collective-permute-start | bytes 786440 | tf_op jit(solution)/shard_map/ppermute | solution.py:41
  58.7 62.9 %collective-permute-start.11 = (bf16[256,512]{1,0:T(8,128)(2,1)}, bf16[256,512]{1,0:T(8,128)(2,1)}, u32[]{:S(2)}, u32[]{:S(2)}) collective-permute-start(bf16[256,512]{1,0:T(8,128)(2,1)} %constant_dynamic-slice_fusion.2), channel_id=1, source_target_pairs={{0,16},{16,0},{1,17},{17,1},{2,18},{18,2},{3,19},{19,3},{4,20},{20... | collective-permute-start | bytes 786440 | tf_op jit(solution)/shard_map/ppermute | solution.py:41
  60.1 72.9 %collective-permute-start.13 = (bf16[256,512]{1,0:T(8,128)(2,1)}, bf16[256,512]{1,0:T(8,128)(2,1)}, u32[]{:S(2)}, u32[]{:S(2)}) collective-permute-start(bf16[256,512]{1,0:T(8,128)(2,1)} %constant_dynamic-slice_fusion.1), channel_id=1, source_target_pairs={{0,16},{16,0},{1,17},{17,1},{2,18},{18,2},{3,19},{19,3},{4,20},{20... | collective-permute-start | bytes 786440 | tf_op jit(solution)/shard_map/ppermute | solution.py:41
  60.9 82.2 %collective-permute-start.15 = (bf16[256,512]{1,0:T(8,128)(2,1)S(1)}, bf16[256,512]{1,0:T(8,128)(2,1)}, u32[]{:S(2)}, u32[]{:S(2)}) collective-permute-start(bf16[256,512]{1,0:T(8,128)(2,1)S(1)} %constant_dynamic-slice_fusion), channel_id=1, source_target_pairs={{0,16},{16,0},{1,17},{17,1},{2,18},{18,2},{3,19},{19,3},{4,20},{20... | collective-permute-start | bytes 786440 | tf_op jit(solution)/shard_map/ppermute | solution.py:41
  72.9 27.0 %copy-start.11 = (bf16[256,512]{1,0:T(8,128)(2,1)S(1)}, bf16[256,512]{1,0:T(8,128)(2,1)}, u32[]{:S(2)}) copy-start(bf16[256,512]{1,0:T(8,128)(2,1)} %copy-done.10) | copy-start | bytes 786436
  73.5 37.1 %copy-start.13 = (s32[1,2,2]{2,1,0:T(2,128)S(1)}, s32[1,2,2]{2,1,0:T(2,128)}, u32[]{:S(2)}) copy-start(s32[1,2,2]{2,1,0:T(2,128)} %param.15) | copy-start | bytes 52
  110.6 51.8 %collective-permute-start.16 = (s32[2,2]{1,0:T(2,128)S(1)}, s32[2,2]{1,0:T(2,128)S(1)}, u32[]{:S(2)}, u32[]{:S(2)}) collective-permute-start(s32[2,2]{1,0:T(2,128)S(1)} %bitcast.132), channel_id=1, source_target_pairs={{0,1},{1,0},{2,3},{3,2},{4,5},{5,4},{6,7},{7,6},{8,9},{9,8},{10,11... | collective-permute-start | bytes 56 | tf_op jit(solution)/shard_map/ppermute | solution.py:17
  121.6 69.2 %collective-permute-start.21 = (bf16[256,512]{0,1:T(8,128)(2,1)}, bf16[256,512]{0,1:T(8,128)(2,1)}, u32[]{:S(2)}, u32[]{:S(2)}) collective-permute-start(bf16[256,512]{0,1:T(8,128)(2,1)} %get-tuple-element.14), channel_id=1, source_target_pairs={{0,1},{1,0},{2,3},{3,2},{4,5},{5,4},{6,7},{7,6},{8,9},{9,8},{10,11... | collective-permute-start | bytes 786440 | tf_op jit(solution)/shard_map/ppermute | solution.py:17
  158.9 8.9 %collective-permute-start.17 = (f32[4,128,128]{2,1,0:T(8,128)}, f32[4,128,128]{2,1,0:T(8,128)}, u32[]{:S(2)}, u32[]{:S(2)}) collective-permute-start(f32[4,128,128]{2,1,0:T(8,128)} %fusion.27), channel_id=1, source_target_pairs={{0,2},{2,4},{4,6},{6,8},{8,10},{10,12},{12,14},{1,3},{3,5},{5,7},{... | collective-permute-start | bytes 786440 | tf_op jit(solution)/shard_map/ppermute | solution.py:65
  168.8 10.8 %collective-permute-start.18 = (f32[4,128,128]{2,1,0:T(8,128)S(1)}, f32[4,128,128]{2,1,0:T(8,128)S(1)}, u32[]{:S(2)}, u32[]{:S(2)}) collective-permute-start(f32[4,128,128]{2,1,0:T(8,128)S(1)} %fusion.59), channel_id=1, source_target_pairs={{0,4},{2,6},{4,8},{6,10},{8,12},{10,14},{1,5},{3,7},{5,9},{7,11},{... | collective-permute-start | bytes 786440 | tf_op jit(solution)/shard_map/ppermute | solution.py:65
  179.6 9.8 %collective-permute-start.19 = (f32[4,128,128]{2,1,0:T(8,128)S(1)}, f32[4,128,128]{2,1,0:T(8,128)S(1)}, u32[]{:S(2)}, u32[]{:S(2)}) collective-permute-start(f32[4,128,128]{2,1,0:T(8,128)S(1)} %add.274), channel_id=1, source_target_pairs={{0,8},{2,10},{4,12},{6,14},{1,9},{3,11},{5,13},{7,15},{16,24},{18,... | collective-permute-start | bytes 786440 | tf_op jit(solution)/shard_map/ppermute | solution.py:65
  194.1 8.3 %collective-permute-start.22 = (f32[4,128,128]{2,1,0:T(8,128)S(1)}, f32[4,128,128]{2,1,0:T(8,128)S(1)}, u32[]{:S(2)}, u32[]{:S(2)}) collective-permute-start(f32[4,128,128]{2,1,0:T(8,128)S(1)} %fusion.28), channel_id=1, source_target_pairs={{2,0},{4,2},{6,4},{8,6},{10,8},{12,10},{14,12},{3,1},{5,3},{7,5},{... | collective-permute-start | bytes 786440 | tf_op jit(solution)/shard_map/ppermute | solution.py:65
  202.4 15.8 %collective-permute-start.23 = (f32[4,128,128]{2,1,0:T(8,128)S(1)}, f32[4,128,128]{2,1,0:T(8,128)S(1)}, u32[]{:S(2)}, u32[]{:S(2)}) collective-permute-start(f32[4,128,128]{2,1,0:T(8,128)S(1)} %fusion.58), channel_id=1, source_target_pairs={{4,0},{6,2},{8,4},{10,6},{12,8},{14,10},{5,1},{7,3},{9,5},{11,7},{... | collective-permute-start | bytes 786440 | tf_op jit(solution)/shard_map/ppermute | solution.py:65
  218.2 14.9 %collective-permute-start.24 = (f32[4,128,128]{2,1,0:T(8,128)S(1)}, f32[4,128,128]{2,1,0:T(8,128)S(1)}, u32[]{:S(2)}, u32[]{:S(2)}) collective-permute-start(f32[4,128,128]{2,1,0:T(8,128)S(1)} %add.287), channel_id=1, source_target_pairs={{8,0},{10,2},{12,4},{14,6},{9,1},{11,3},{13,5},{15,7},{24,16},{26,... | collective-permute-start | bytes 786440 | tf_op jit(solution)/shard_map/ppermute | solution.py:65
  239.2 5.4 %collective-permute-start.25 = (f32[256,2048]{1,0:T(8,128)}, f32[256,2048]{1,0:T(8,128)}, u32[]{:S(2)}, u32[]{:S(2)}) collective-permute-start(f32[256,2048]{1,0:T(8,128)} %fusion.44), channel_id=1, source_target_pairs={{0,1},{1,0},{2,3},{3,2},{4,5},{5,4},{6,7},{7,6},{8,9},{9,8},{10,11... | collective-permute-start | bytes 6291464 | tf_op jit(solution)/shard_map/ppermute | solution.py:17
  239.4 4.3 %collective-permute-start.20 = (bf16[256,512]{1,0:T(8,128)(2,1)S(1)}, bf16[256,512]{1,0:T(8,128)(2,1)S(1)}, u32[]{:S(2)}, u32[]{:S(2)}) collective-permute-start(bf16[256,512]{1,0:T(8,128)(2,1)S(1)} %copy.17), channel_id=1, source_target_pairs={{0,1},{1,0},{2,3},{3,2},{4,5},{5,4},{6,7},{7,6},{8,9},{9,8},{10,11... | collective-permute-start | bytes 786440 | tf_op jit(solution)/shard_map/ppermute | solution.py:17
  (11 other events, 81.0 us)

commit v5 on v4

--- a/solution.py
+++ b/solution.py
@@ -38,11 +38,10 @@
 
     def land(piece):
         sent = lax.dynamic_slice_in_dim(piece, p * share, share, axis=1)
-        other = lax.ppermute(sent, "groups", partner)
-        return [(piece, p * share), (other, (1 - p) * width)]
-
-    got = [(c, [(block, 0)])]
+        return (piece, lax.ppermute(sent, "groups", partner))
+
     fwd = lax.dynamic_slice_in_dim(block, p * share, width, axis=1)
+    got = [(c, (fwd, lax.dynamic_slice_in_dim(block, (1 - p) * width, share, axis=1)))]
     bwd = fwd
     for step in range(1, chips // 2 + 1):
         fwd = lax.ppermute(fwd, "chip", ahead)
@@ -106,11 +105,21 @@
 
     span = 2 * rows_dev
     block = chip_block((w_query, w_key, w_value))
-    w_half = jnp.zeros((chips * span, block.shape[1]), bf16)
-    for src, parts in ring_gather(block, chips, c, lax.axis_index("groups") % 2):
-        for piece, col in parts:
-            w_half = lax.dynamic_update_slice(w_half, piece, (src * span, col))
-    projected = jnp.dot(x_pair, w_half, preferred_element_type=f32).astype(bf16)
+    parity = lax.axis_index("groups") % 2
+    share = half
+    width = 2 * half
+    w_ring = jnp.zeros((chips * span, width), bf16)
+    w_x = jnp.zeros((chips * span, share), bf16)
+    for src, (ringed, swapped) in ring_gather(block, chips, c, parity):
+        w_ring = lax.dynamic_update_slice_in_dim(w_ring, ringed, src * span, axis=0)
+        w_x = lax.dynamic_update_slice_in_dim(w_x, swapped, src * span, axis=0)
+    p_ring = jnp.dot(x_pair, w_ring, preferred_element_type=f32).astype(bf16)
+    p_x = jnp.dot(x_pair, w_x, preferred_element_type=f32).astype(bf16)
+    projected = jnp.where(
+        parity == 0,
+        jnp.concatenate([p_ring, p_x], axis=1),
+        jnp.concatenate([p_x, p_ring], axis=1),
+    )
     projected = projected.reshape(2, tok, 3, heads, DH)
     query = projected[:, :, 0]
     key = projected[:, :, 1]
@@ -165,7 +174,10 @@
     d_proj = jnp.stack([d_query, d_key, d_value], axis=2).astype(bf16).reshape(2, tok, 3 * half)
 
     def grad_rows(j):
-        return lax.dot_general(d_proj[j], w_half, (((1,), (1,)), ((), ())), preferred_element_type=f32)
+        d_ring = lax.dynamic_slice_in_dim(d_proj[j], parity * share, width, axis=1)
+        d_x = lax.dynamic_slice_in_dim(d_proj[j], (1 - parity) * width, share, axis=1)
+        g = lax.dot_general(d_ring, w_ring, (((1,), (1,)), ((), ())), preferred_element_type=f32)
+        return g + lax.dot_general(d_x, w_x, (((1,), (1,)), ((), ())), preferred_element_type=f32)
 
     received = swap(grad_rows(1))
     grad_input = (grad_rows(0) + received).astype(bf16)

time: 252 us -> 175 us (0.69)
  the two profiles are of different devices: /device:TPU:0 before, /device:TPU:15 now
where the time goes in v5:
time: 175 us; the launch traced here: 172 us
  starting transfers between devices  52.8 us (30%)
  waiting for transfers between devices  41.2 us (24%)
  local copies, waits for them, and re-layouts  30.9 us (18%)
  matrix products  24.2 us (14%)
  other arithmetic  12.7 us (7%)
  between operations  10.2 us (6%)
    ppermute x6, starting transfers between devices, swap(): return lax.ppermute(x, 'core', [(0, 1), (1, 0)])  26.2 us
    ppermute x6, waiting for transfers between devices, exclusive_scan(): got = lax.ppermute(incl, 'chip', perm)  25.2 us
    ppermute x6, starting transfers between devices, exclusive_scan(): got = lax.ppermute(incl, 'chip', perm)  16.8 us
    dot_general x2, matrix products, grad_rows(): lax.dot_general(d_ring, w_ring, (((1,), (1,)), ((), ())), preferred_eleme...  10.2 us
    ppermute x7, waiting for transfers between devices, land(): return (piece, lax.ppermute(sent, 'groups', partner))  9.99 us
    dynamic_update_slice x8, local copies, waits for them, and re-layouts, on_device(): w_ring = lax.dynamic_update_slice_in_dim(w_ring, ringed, src * span, axis=0)  9 us
    ppermute x7, starting transfers between devices, land(): return (piece, lax.ppermute(sent, 'groups', partner))  5.21 us
    dot_general x1, matrix products, on_device(): p_ring = jnp.dot(x_pair, w_ring, preferred_element_type=f32).astype(bf16)  5.16 us
  transfers between devices with their start and end apart: 26, of which 14 were waited for; matrix products, arithmetic and copies ran while one was open for 27% of the time, Pallas kernels for 0%

profile of v5, /device:TPU:15, one launch (start us, length us, event | category | flops | bytes accessed | tf_op | source)
XLA Modules:
  0.0 172.0 jit_solution(3878152788648293858)
XLA Ops:
  5.0 2.5 %broadcast_in_dim.27 = bf16[2048,1024]{1,0:T(8,128)(2,1)} broadcast(bf16[]{:T(256)} %constant.96.clone.1), dimensions={} | broadcast | bytes 4194306 | tf_op jit(solution)/shard_map/broadcast_in_dim | solution.py:111
  8.8 1.4 add_convert_fusion
  28.6 1.9 %constant_dynamic-update-slice_fusion.13 = bf16[2048,1024]{1,0:T(8,128)(2,1)} fusion(bf16[2048,1024]{1,0:T(8,128)(2,1)} %get-tuple-element.2, bf16[256,1024]{1,0:T(8,128)(2,1)} %collective-permute-done.2, s32[]{:T(128)S(6)} %select_n.212), kind=kLoop, calls=%fused_computation.103 | loop fusion | bytes 1048580 | tf_op jit(solution)/shard_map/dynamic_update_slice | solution.py:114
  30.5 1.9 %constant_dynamic-update-slice_fusion.12 = bf16[2048,1024]{1,0:T(8,128)(2,1)} fusion(bf16[2048,1024]{1,0:T(8,128)(2,1)} %constant_dynamic-update-slice_fusion.13, bf16[256,1024]{1,0:T(8,128)(2,1)} %collective-permute-done.3, s32[]{:T(128)S(6)} %select_n.215), kind=kLoop, calls=%fused_computation.102 | loop fusion | bytes 1048580 | tf_op jit(solution)/shard_map/dynamic_update_slice | solution.py:114
  32.4 5.5 %collective-permute-done.10 = bf16[256,512]{1,0:T(8,128)(2,1)S(1)} collective-permute-done((bf16[256,512]{1,0:T(8,128)(2,1)S(1)}, bf16[256,512]{1,0:T(8,128)(2,1)S(1)}, u32[]{:S(2)}, u32[]{:S(2)}) %collective-permute-start.10) | collective-permute-done | bytes 262176 | tf_op jit(solution)/shard_map/ppermute | solution.py:41
  43.1 1.4 collective-permute-done.11
  44.5 4.3 %collective-permute-start.16 = (s32[2,2]{1,0:T(2,128)S(1)}, s32[2,2]{1,0:T(2,128)S(1)}, u32[]{:S(2)}, u32[]{:S(2)}) collective-permute-start(s32[2,2]{1,0:T(2,128)S(1)} %bitcast.133), channel_id=1, source_target_pairs={{0,1},{1,0},{2,3},{3,2},{4,5},{5,4},{6,7},{7,6},{8,9},{9,8},{10,11... | collective-permute-start | bytes 56 | tf_op jit(solution)/shard_map/ppermute | solution.py:17
  48.8 1.3 collective-permute-done.12
  54.5 1.8 %collective-permute-done.13 = bf16[256,512]{1,0:T(8,128)(2,1)S(1)} collective-permute-done((bf16[256,512]{1,0:T(8,128)(2,1)S(1)}, bf16[256,512]{1,0:T(8,128)(2,1)S(1)}, u32[]{:S(2)}, u32[]{:S(2)}) %collective-permute-start.13) | collective-permute-done | bytes 262176 | tf_op jit(solution)/shard_map/ppermute | solution.py:41
  56.4 6.3 %collective-permute-start.21 = (bf16[256,512]{0,1:T(8,128)(2,1)}, bf16[256,512]{0,1:T(8,128)(2,1)}, u32[]{:S(2)}, u32[]{:S(2)}) collective-permute-start(bf16[256,512]{0,1:T(8,128)(2,1)} %get-tuple-element.16), channel_id=1, source_target_pairs={{0,1},{1,0},{2,3},{3,2},{4,5},{5,4},{6,7},{7,6},{8,9},{9,8},{10,11... | collective-permute-start | bytes 786440 | tf_op jit(solution)/shard_map/ppermute | solution.py:17
  64.0 5.2 %convolution_convert_fusion = bf16[512,1024]{1,0:T(8,128)(2,1)S(1)} fusion(bf16[2048,1024]{1,0:T(8,128)(2,1)} %constant_dynamic-update-slice_fusion.7, bf16[256,2048]{1,0:T(8,128)(2,1)} %collective-permute-done, bf16[256,2048]{1,0:T(8,128)(2,1)} %add_convert_fusion), kind=kOutput, calls=%fused_computation.10 | convolution fusion | flops 2152202240 | bytes 7340032 | tf_op jit(solution)/shard_map/dot_general | solution.py:116
  69.3 2.8 %fusion.4 = bf16[512,512]{1,0:T(8,128)(2,1)S(1)} fusion(bf16[2048,512]{1,0:T(8,128)(2,1)S(1)} %constant_dynamic-update-slice_fusion, bf16[256,2048]{1,0:T(8,128)(2,1)} %collective-permute-done, bf16[256,2048]{1,0:T(8,128)(2,1)} %add_convert_fusion), kind=kOutput, calls=%fused_computation.19 | convolution fusion | flops 1078198272 | bytes 4718592 | tf_op jit(solution)/shard_map/dot_general | solution.py:117
  72.1 1.6 maximum_select_fusion
  73.7 3.9 %select_n.234 = bf16[2,256,3,4,128]{4,3,2,1,0:T(4,128)(2,1)} reshape(bf16[512,1536]{1,0:T(8,128)(2,1)} %maximum_select_fusion) | data formatting | bytes 3145728 | tf_op jit(solution)/shard_map/jit(_where)/select_n | solution.py:118
  77.6 2.9 %fusion.51 = (bf16[2,256,1,4,128]{4,3,2,1,0:T(4,128)(2,1)}, bf16[2,256,1,4,128]{4,3,2,1,0:T(4,128)(2,1)S(1)}, bf16[2,256,1,4,128]{4,3,2,1,0:T(4,128)(2,1)}) fusion(bf16[2,256,3,4,128]{4,3,2,1,0:T(4,128)(2,1)} %select_n.234), kind=kLoop, calls=%fused_computation.124 | loop fusion | bytes 3145728 | tf_op jit(solution)/shard_map/slice | solution.py:126
  83.6 3.1 %collective-permute-start.17 = (f32[4,128,128]{2,1,0:T(8,128)}, f32[4,128,128]{2,1,0:T(8,128)}, u32[]{:S(2)}, u32[]{:S(2)}) collective-permute-start(f32[4,128,128]{2,1,0:T(8,128)} %fusion.33), channel_id=1, source_target_pairs={{0,2},{2,4},{4,6},{6,8},{8,10},{10,12},{12,14},{1,3},{3,5},{5,7},{... | collective-permute-start | bytes 786440 | tf_op jit(solution)/shard_map/ppermute | solution.py:64
  87.8 2.3 %reshape.113 = f32[2,256,256]{2,1,0:T(8,128)} reshape(f32[2,2,128,2,128]{4,3,2,1,0:T(2,128)} %broadcast_in_dim.31) | data formatting | bytes 1048576 | tf_op jit(solution)/shard_map/vmap()/reshape | solution.py:75
  92.4 3.2 %collective-permute-start.18 = (f32[4,128,128]{2,1,0:T(8,128)S(1)}, f32[4,128,128]{2,1,0:T(8,128)S(1)}, u32[]{:S(2)}, u32[]{:S(2)}) collective-permute-start(f32[4,128,128]{2,1,0:T(8,128)S(1)} %fusion.70), channel_id=1, source_target_pairs={{0,4},{2,6},{4,8},{6,10},{8,12},{10,14},{1,5},{3,7},{5,9},{7,11},{... | collective-permute-start | bytes 786440 | tf_op jit(solution)/shard_map/ppermute | solution.py:64
  96.0 3.4 %collective-permute-done.18 = f32[4,128,128]{2,1,0:T(8,128)S(1)} collective-permute-done((f32[4,128,128]{2,1,0:T(8,128)S(1)}, f32[4,128,128]{2,1,0:T(8,128)S(1)}, u32[]{:S(2)}, u32[]{:S(2)}) %collective-permute-start.18) | collective-permute-done | bytes 262176 | tf_op jit(solution)/shard_map/ppermute | solution.py:64
  99.5 4.2 %collective-permute-start.19 = (f32[4,128,128]{2,1,0:T(8,128)S(1)}, f32[4,128,128]{2,1,0:T(8,128)S(1)}, u32[]{:S(2)}, u32[]{:S(2)}) collective-permute-start(f32[4,128,128]{2,1,0:T(8,128)S(1)} %add.272), channel_id=1, source_target_pairs={{0,8},{2,10},{4,12},{6,14},{1,9},{3,11},{5,13},{7,15},{16,24},{18,... | collective-permute-start | bytes 786440 | tf_op jit(solution)/shard_map/ppermute | solution.py:64
  104.2 5.8 %collective-permute-done.19 = f32[4,128,128]{2,1,0:T(8,128)S(1)} collective-permute-done((f32[4,128,128]{2,1,0:T(8,128)S(1)}, f32[4,128,128]{2,1,0:T(8,128)S(1)}, u32[]{:S(2)}, u32[]{:S(2)}) %collective-permute-start.19) | collective-permute-done | bytes 262176 | tf_op jit(solution)/shard_map/ppermute | solution.py:64
  114.7 3.1 %collective-permute-start.22 = (f32[4,128,128]{2,1,0:T(8,128)S(1)}, f32[4,128,128]{2,1,0:T(8,128)S(1)}, u32[]{:S(2)}, u32[]{:S(2)}) collective-permute-start(f32[4,128,128]{2,1,0:T(8,128)S(1)} %fusion.34), channel_id=1, source_target_pairs={{2,0},{4,2},{6,4},{8,6},{10,8},{12,10},{14,12},{3,1},{5,3},{7,5},{... | collective-permute-start | bytes 786440 | tf_op jit(solution)/shard_map/ppermute | solution.py:64
  118.6 4.1 %collective-permute-done.22 = f32[4,128,128]{2,1,0:T(8,128)S(1)} collective-permute-done((f32[4,128,128]{2,1,0:T(8,128)S(1)}, f32[4,128,128]{2,1,0:T(8,128)S(1)}, u32[]{:S(2)}, u32[]{:S(2)}) %collective-permute-start.22) | collective-permute-done | bytes 262176 | tf_op jit(solution)/shard_map/ppermute | solution.py:64
  122.8 1.9 %collective-permute-start.23 = (f32[4,128,128]{2,1,0:T(8,128)S(1)}, f32[4,128,128]{2,1,0:T(8,128)S(1)}, u32[]{:S(2)}, u32[]{:S(2)}) collective-permute-start(f32[4,128,128]{2,1,0:T(8,128)S(1)} %fusion.69), channel_id=1, source_target_pairs={{4,0},{6,2},{8,4},{10,6},{12,8},{14,10},{5,1},{7,3},{9,5},{11,7},{... | collective-permute-start | bytes 786440 | tf_op jit(solution)/shard_map/ppermute | solution.py:64
  125.1 5.3 %collective-permute-done.23 = f32[4,128,128]{2,1,0:T(8,128)S(1)} collective-permute-done((f32[4,128,128]{2,1,0:T(8,128)S(1)}, f32[4,128,128]{2,1,0:T(8,128)S(1)}, u32[]{:S(2)}, u32[]{:S(2)}) %collective-permute-start.23) | collective-permute-done | bytes 262176 | tf_op jit(solution)/shard_map/ppermute | solution.py:64
  130.4 1.3 collective-permute-start.24
  132.0 6.5 %collective-permute-done.24 = f32[4,128,128]{2,1,0:T(8,128)S(1)} collective-permute-done((f32[4,128,128]{2,1,0:T(8,128)S(1)}, f32[4,128,128]{2,1,0:T(8,128)S(1)}, u32[]{:S(2)}, u32[]{:S(2)}) %collective-permute-start.24) | collective-permute-done | bytes 262176 | tf_op jit(solution)/shard_map/ppermute | solution.py:64
  140.3 4.9 %convolution_add_fusion = f32[256,2048]{1,0:T(8,128)} fusion(f32[256,2048]{1,0:T(8,128)S(1)} %fusion.29, bf16[2048,1024]{1,0:T(8,128)(2,1)} %constant_dynamic-update-slice_fusion.7, bf16[256,1536]{0,1:T(8,128)(2,1)S(1)} %bitcast.127, s32[]{:T(128)S(6)} %select_n.207), kind=kOutput, calls=%fused_computation | convolution fusion | flops 1074266112 | bytes 8912900 | tf_op jit(solution)/shard_map/dot_general | solution.py:179
  145.3 14.2 %collective-permute-start.25 = (f32[256,2048]{1,0:T(8,128)}, f32[256,2048]{1,0:T(8,128)}, u32[]{:S(2)}, u32[]{:S(2)}) collective-permute-start(f32[256,2048]{1,0:T(8,128)} %convolution_add_fusion), channel_id=1, source_target_pairs={{0,1},{1,0},{2,3},{3,2},{4,5},{5,4},{6,7},{7,6},{8,9},{9,8},{10,11... | collective-permute-start | bytes 6291464 | tf_op jit(solution)/shard_map/ppermute | solution.py:17
  160.5 3.5 %collective-permute-done.20 = bf16[256,512]{1,0:T(8,128)(2,1)} collective-permute-done((bf16[256,512]{1,0:T(8,128)(2,1)}, bf16[256,512]{1,0:T(8,128)(2,1)}, u32[]{:S(2)}, u32[]{:S(2)}) %collective-permute-start.20) | collective-permute-done | bytes 262176 | tf_op jit(solution)/shard_map/ppermute | solution.py:17
  163.9 2.0 %maximum_select_fusion.1 = bf16[256,1024]{1,0:T(8,128)(2,1)} fusion(bf16[256,512]{1,0:T(8,128)(2,1)} %collective-permute-done.20, bf16[256,512]{1,0:T(8,128)(2,1)S(1)} %copy.19, pred[]{:T(512)S(6)} %eq.15), kind=kLoop, calls=%fused_computation.30 | loop fusion | flops 2359296 | bytes 1048577 | tf_op jit(solution)/shard_map/jit(_where)/select_n | solution.py:146
  166.7 5.3 %fusion.1 = bf16[256,2048]{1,0:T(8,128)(2,1)} fusion(f32[256,2048]{1,0:T(8,128)} %collective-permute-done.25, f32[256,2048]{1,0:T(8,128)S(1)} %fusion.31, bf16[2048,1024]{1,0:T(8,128)(2,1)} %constant_dynamic-update-slice_fusion.7, bf16[256,1536]{0,1:T(8,128)(2,1)S(1)} %bitcast.125, s32[]{:T(128)S(6)} %select_n.207), kind=kOutput, calls=%fused_computation.3 | convolution fusion | flops 1075314688 | bytes 9961476 | tf_op jit(solution)/shard_map/dot_general | solution.py:179
  (119 shorter events, 43.1 us)
Async XLA Ops:
  2.8 2.1 %collective-permute-start.1 = (bf16[128,1536]{1,0:T(8,128)(2,1)S(1)}, bf16[128,1536]{1,0:T(8,128)(2,1)S(1)}, u32[]{:S(2)}, u32[]{:S(2)}) collective-permute-start(bf16[128,1536]{1,0:T(8,128)(2,1)S(1)} %pad_maximum_fusion.7), channel_id=1, source_target_pairs={{0,1},{1,0},{2,3},{3,2},{4,5},{5,4},{6,7},{7,6},{8,9},{9,8},{10,11... | collective-permute-start | bytes 1179656 | tf_op jit(solution)/shard_map/ppermute | solution.py:17
  7.5 4.6 %copy-start.8 = (s32[8]{0:T(128)S(1)}, s32[8]{0:T(128)}, u32[]{:S(2)}) copy-start(s32[8]{0:T(128)} %constant.118.clone) | copy-start | bytes 100
  8.6 8.7 %copy-start.6 = (s32[8]{0:T(128)S(1)}, s32[8]{0:T(128)}, u32[]{:S(2)}) copy-start(s32[8]{0:T(128)} %constant.117.clone) | copy-start | bytes 100
  8.6 13.9 %copy-start.5 = (bf16[256,1024]{1,0:T(8,128)(2,1)S(1)}, bf16[256,1024]{1,0:T(8,128)(2,1)}, u32[]{:S(2)}) copy-start(bf16[256,1024]{1,0:T(8,128)(2,1)} %param.11) | copy-start | bytes 1572868
  8.6 15.0 %collective-permute-start.2 = (bf16[256,1024]{1,0:T(8,128)(2,1)}, bf16[256,1024]{1,0:T(8,128)(2,1)}, u32[]{:S(2)}, u32[]{:S(2)}) collective-permute-start(bf16[256,1024]{1,0:T(8,128)(2,1)} %get-tuple-element.3), channel_id=1, source_target_pairs={{0,4},{4,8},{8,12},{12,14},{14,10},{10,6},{6,2},{2,0},{1,5},{5,9},... | collective-permute-start | bytes 1572872 | tf_op jit(solution)/shard_map/ppermute | solution.py:47
  10.1 53.9 %collective-permute-start = (bf16[256,2048]{1,0:T(8,128)(2,1)}, bf16[256,2048]{1,0:T(8,128)(2,1)}, u32[]{:S(2)}, u32[]{:S(2)}) collective-permute-start(bf16[256,2048]{1,0:T(8,128)(2,1)} %add_convert_fusion), channel_id=1, source_target_pairs={{0,1},{1,0},{2,3},{3,2},{4,5},{5,4},{6,7},{7,6},{8,9},{9,8},{10,11... | collective-permute-start | bytes 3145736 | tf_op jit(solution)/shard_map/ppermute | solution.py:17
  10.8 14.3 %collective-permute-start.3 = (bf16[256,1024]{1,0:T(8,128)(2,1)}, bf16[256,1024]{1,0:T(8,128)(2,1)}, u32[]{:S(2)}, u32[]{:S(2)}) collective-permute-start(bf16[256,1024]{1,0:T(8,128)(2,1)} %get-tuple-element.3), channel_id=1, source_target_pairs={{0,2},{4,0},{8,4},{12,8},{14,12},{10,14},{6,10},{2,6},{1,3},{5,1},... | collective-permute-start | bytes 1572872 | tf_op jit(solution)/shard_map/ppermute | solution.py:50
  24.6 7.8 %collective-permute-start.9 = (bf16[256,512]{1,0:T(8,128)(2,1)S(1)}, bf16[256,512]{1,0:T(8,128)(2,1)S(1)}, u32[]{:S(2)}, u32[]{:S(2)}) collective-permute-start(bf16[256,512]{1,0:T(8,128)(2,1)S(1)} %constant_dynamic-slice_fusion.6), channel_id=1, source_target_pairs={{0,16},{16,0},{1,17},{17,1},{2,18},{18,2},{3,19},{19,3},{4,20},{20... | collective-permute-start | bytes 786440 | tf_op jit(solution)/shard_map/ppermute | solution.py:41
  24.9 13.1 %collective-permute-start.4 = (bf16[256,1024]{1,0:T(8,128)(2,1)}, bf16[256,1024]{1,0:T(8,128)(2,1)S(1)}, u32[]{:S(2)}, u32[]{:S(2)}) collective-permute-start(bf16[256,1024]{1,0:T(8,128)(2,1)} %collective-permute-done.2), channel_id=1, source_target_pairs={{0,4},{4,8},{8,12},{12,14},{14,10},{10,6},{6,2},{2,0},{1,5},{5,9},... | collective-permute-start | bytes 1572872 | tf_op jit(solution)/shard_map/ppermute | solution.py:47
  26.1 11.8 %collective-permute-start.10 = (bf16[256,512]{1,0:T(8,128)(2,1)S(1)}, bf16[256,512]{1,0:T(8,128)(2,1)S(1)}, u32[]{:S(2)}, u32[]{:S(2)}) collective-permute-start(bf16[256,512]{1,0:T(8,128)(2,1)S(1)} %constant_dynamic-slice_fusion.5), channel_id=1, source_target_pairs={{0,16},{16,0},{1,17},{17,1},{2,18},{18,2},{3,19},{19,3},{4,20},{20... | collective-permute-start | bytes 786440 | tf_op jit(solution)/shard_map/ppermute | solution.py:41
  27.3 12.5 %collective-permute-start.5 = (bf16[256,1024]{1,0:T(8,128)(2,1)}, bf16[256,1024]{1,0:T(8,128)(2,1)S(1)}, u32[]{:S(2)}, u32[]{:S(2)}) collective-permute-start(bf16[256,1024]{1,0:T(8,128)(2,1)} %collective-permute-done.3), channel_id=1, source_target_pairs={{0,2},{4,0},{8,4},{12,8},{14,12},{10,14},{6,10},{2,6},{1,3},{5,1},... | collective-permute-start | bytes 1572872 | tf_op jit(solution)/shard_map/ppermute | solution.py:50
  32.4 12.1 %copy-start.7 = (s32[1,2,2]{2,1,0:T(2,128)S(1)}, s32[1,2,2]{2,1,0:T(2,128)}, u32[]{:S(2)}) copy-start(s32[1,2,2]{2,1,0:T(2,128)} %param.15) | copy-start | bytes 52
  38.1 6.4 %collective-permute-start.11 = (bf16[256,512]{1,0:T(8,128)(2,1)S(1)}, bf16[256,512]{1,0:T(8,128)(2,1)S(1)}, u32[]{:S(2)}, u32[]{:S(2)}) collective-permute-start(bf16[256,512]{1,0:T(8,128)(2,1)S(1)} %constant_dynamic-slice_fusion.4), channel_id=1, source_target_pairs={{0,16},{16,0},{1,17},{17,1},{2,18},{18,2},{3,19},{19,3},{4,20},{20... | collective-permute-start | bytes 786440 | tf_op jit(solution)/shard_map/ppermute | solution.py:41
  39.3 11.7 %collective-permute-start.6 = (bf16[256,1024]{1,0:T(8,128)(2,1)S(1)}, bf16[256,1024]{1,0:T(8,128)(2,1)S(1)}, u32[]{:S(2)}, u32[]{:S(2)}) collective-permute-start(bf16[256,1024]{1,0:T(8,128)(2,1)S(1)} %collective-permute-done.4), channel_id=1, source_target_pairs={{0,4},{4,8},{8,12},{12,14},{14,10},{10,6},{6,2},{2,0},{1,5},{5,9},... | collective-permute-start | bytes 1572872 | tf_op jit(solution)/shard_map/ppermute | solution.py:47
  39.9 10.3 %collective-permute-start.12 = (bf16[256,512]{1,0:T(8,128)(2,1)S(1)}, bf16[256,512]{1,0:T(8,128)(2,1)S(1)}, u32[]{:S(2)}, u32[]{:S(2)}) collective-permute-start(bf16[256,512]{1,0:T(8,128)(2,1)S(1)} %constant_dynamic-slice_fusion.3), channel_id=1, source_target_pairs={{0,16},{16,0},{1,17},{17,1},{2,18},{18,2},{3,19},{19,3},{4,20},{20... | collective-permute-start | bytes 786440 | tf_op jit(solution)/shard_map/ppermute | solution.py:41
  40.2 11.5 %collective-permute-start.7 = (bf16[256,1024]{1,0:T(8,128)(2,1)S(1)}, bf16[256,1024]{1,0:T(8,128)(2,1)S(1)}, u32[]{:S(2)}, u32[]{:S(2)}) collective-permute-start(bf16[256,1024]{1,0:T(8,128)(2,1)S(1)} %collective-permute-done.5), channel_id=1, source_target_pairs={{0,2},{4,0},{8,4},{12,8},{14,12},{10,14},{6,10},{2,6},{1,3},{5,1},... | collective-permute-start | bytes 1572872 | tf_op jit(solution)/shard_map/ppermute | solution.py:50
  44.5 42.3 %collective-permute-start.16 = (s32[2,2]{1,0:T(2,128)S(1)}, s32[2,2]{1,0:T(2,128)S(1)}, u32[]{:S(2)}, u32[]{:S(2)}) collective-permute-start(s32[2,2]{1,0:T(2,128)S(1)} %bitcast.133), channel_id=1, source_target_pairs={{0,1},{1,0},{2,3},{3,2},{4,5},{5,4},{6,7},{7,6},{8,9},{9,8},{10,11... | collective-permute-start | bytes 56 | tf_op jit(solution)/shard_map/ppermute | solution.py:17
  51.1 5.3 %collective-permute-start.13 = (bf16[256,512]{1,0:T(8,128)(2,1)S(1)}, bf16[256,512]{1,0:T(8,128)(2,1)S(1)}, u32[]{:S(2)}, u32[]{:S(2)}) collective-permute-start(bf16[256,512]{1,0:T(8,128)(2,1)S(1)} %constant_dynamic-slice_fusion.2), channel_id=1, source_target_pairs={{0,16},{16,0},{1,17},{17,1},{2,18},{18,2},{3,19},{19,3},{4,20},{20... | collective-permute-start | bytes 786440 | tf_op jit(solution)/shard_map/ppermute | solution.py:41
  51.5 11.3 %collective-permute-start.8 = (bf16[256,1024]{1,0:T(8,128)(2,1)S(1)}, bf16[256,1024]{1,0:T(8,128)(2,1)S(1)}, u32[]{:S(2)}, u32[]{:S(2)}) collective-permute-start(bf16[256,1024]{1,0:T(8,128)(2,1)S(1)} %collective-permute-done.6), channel_id=1, source_target_pairs={{0,4},{4,8},{8,12},{12,14},{14,10},{10,6},{6,2},{2,0},{1,5},{5,9},... | collective-permute-start | bytes 1572872 | tf_op jit(solution)/shard_map/ppermute | solution.py:47
  51.7 11.0 %collective-permute-start.14 = (bf16[256,512]{1,0:T(8,128)(2,1)S(1)}, bf16[256,512]{1,0:T(8,128)(2,1)S(1)}, u32[]{:S(2)}, u32[]{:S(2)}) collective-permute-start(bf16[256,512]{1,0:T(8,128)(2,1)S(1)} %constant_dynamic-slice_fusion.1), channel_id=1, source_target_pairs={{0,16},{16,0},{1,17},{17,1},{2,18},{18,2},{3,19},{19,3},{4,20},{20... | collective-permute-start | bytes 786440 | tf_op jit(solution)/shard_map/ppermute | solution.py:41
  56.4 55.1 %collective-permute-start.21 = (bf16[256,512]{0,1:T(8,128)(2,1)}, bf16[256,512]{0,1:T(8,128)(2,1)}, u32[]{:S(2)}, u32[]{:S(2)}) collective-permute-start(bf16[256,512]{0,1:T(8,128)(2,1)} %get-tuple-element.16), channel_id=1, source_target_pairs={{0,1},{1,0},{2,3},{3,2},{4,5},{5,4},{6,7},{7,6},{8,9},{9,8},{10,11... | collective-permute-start | bytes 786440 | tf_op jit(solution)/shard_map/ppermute | solution.py:17
  62.8 6.4 %collective-permute-start.15 = (bf16[256,512]{1,0:T(8,128)(2,1)S(1)}, bf16[256,512]{1,0:T(8,128)(2,1)S(1)}, u32[]{:S(2)}, u32[]{:S(2)}) collective-permute-start(bf16[256,512]{1,0:T(8,128)(2,1)S(1)} %constant_dynamic-slice_fusion), channel_id=1, source_target_pairs={{0,16},{16,0},{1,17},{17,1},{2,18},{18,2},{3,19},{19,3},{4,20},{20... | collective-permute-start | bytes 786440 | tf_op jit(solution)/shard_map/ppermute | solution.py:41
  83.6 7.6 %collective-permute-start.17 = (f32[4,128,128]{2,1,0:T(8,128)}, f32[4,128,128]{2,1,0:T(8,128)}, u32[]{:S(2)}, u32[]{:S(2)}) collective-permute-start(f32[4,128,128]{2,1,0:T(8,128)} %fusion.33), channel_id=1, source_target_pairs={{0,2},{2,4},{4,6},{6,8},{8,10},{10,12},{12,14},{1,3},{3,5},{5,7},{... | collective-permute-start | bytes 786440 | tf_op jit(solution)/shard_map/ppermute | solution.py:64
  90.0 5.5 %copy-start = (bf16[2,256,1,4,128]{4,3,2,1,0:T(4,128)(2,1)S(1)}, bf16[2,256,1,4,128]{4,3,2,1,0:T(4,128)(2,1)}, u32[]{:S(2)}) copy-start(bf16[2,256,1,4,128]{4,3,2,1,0:T(4,128)(2,1)} %get-tuple-element.8) | copy-start | bytes 1572868
  92.4 7.1 %collective-permute-start.18 = (f32[4,128,128]{2,1,0:T(8,128)S(1)}, f32[4,128,128]{2,1,0:T(8,128)S(1)}, u32[]{:S(2)}, u32[]{:S(2)}) collective-permute-start(f32[4,128,128]{2,1,0:T(8,128)S(1)} %fusion.70), channel_id=1, source_target_pairs={{0,4},{2,6},{4,8},{6,10},{8,12},{10,14},{1,5},{3,7},{5,9},{7,11},{... | collective-permute-start | bytes 786440 | tf_op jit(solution)/shard_map/ppermute | solution.py:64
  96.0 14.0 %copy-start.2 = (f32[2,4,128,128]{3,2,1,0:T(8,128)S(1)}, f32[2,4,128,128]{3,2,1,0:T(8,128)}, u32[]{:S(2)}) copy-start(f32[2,4,128,128]{3,2,1,0:T(8,128)} %copy-done.1) | copy-start | bytes 1572868
  99.5 10.5 %collective-permute-start.19 = (f32[4,128,128]{2,1,0:T(8,128)S(1)}, f32[4,128,128]{2,1,0:T(8,128)S(1)}, u32[]{:S(2)}, u32[]{:S(2)}) collective-permute-start(f32[4,128,128]{2,1,0:T(8,128)S(1)} %add.272), channel_id=1, source_target_pairs={{0,8},{2,10},{4,12},{6,14},{1,9},{3,11},{5,13},{7,15},{16,24},{18,... | collective-permute-start | bytes 786440 | tf_op jit(solution)/shard_map/ppermute | solution.py:64
  114.7 8.0 %collective-permute-start.22 = (f32[4,128,128]{2,1,0:T(8,128)S(1)}, f32[4,128,128]{2,1,0:T(8,128)S(1)}, u32[]{:S(2)}, u32[]{:S(2)}) collective-permute-start(f32[4,128,128]{2,1,0:T(8,128)S(1)} %fusion.34), channel_id=1, source_target_pairs={{2,0},{4,2},{6,4},{8,6},{10,8},{12,10},{14,12},{3,1},{5,3},{7,5},{... | collective-permute-start | bytes 786440 | tf_op jit(solution)/shard_map/ppermute | solution.py:64
  122.8 7.6 %collective-permute-start.23 = (f32[4,128,128]{2,1,0:T(8,128)S(1)}, f32[4,128,128]{2,1,0:T(8,128)S(1)}, u32[]{:S(2)}, u32[]{:S(2)}) collective-permute-start(f32[4,128,128]{2,1,0:T(8,128)S(1)} %fusion.69), channel_id=1, source_target_pairs={{4,0},{6,2},{8,4},{10,6},{12,8},{14,10},{5,1},{7,3},{9,5},{11,7},{... | collective-permute-start | bytes 786440 | tf_op jit(solution)/shard_map/ppermute | solution.py:64
  130.4 8.1 %collective-permute-start.24 = (f32[4,128,128]{2,1,0:T(8,128)S(1)}, f32[4,128,128]{2,1,0:T(8,128)S(1)}, u32[]{:S(2)}, u32[]{:S(2)}) collective-permute-start(f32[4,128,128]{2,1,0:T(8,128)S(1)} %add.285), channel_id=1, source_target_pairs={{8,0},{10,2},{12,4},{14,6},{9,1},{11,3},{13,5},{15,7},{24,16},{26,... | collective-permute-start | bytes 786440 | tf_op jit(solution)/shard_map/ppermute | solution.py:64
  145.3 21.4 %collective-permute-start.25 = (f32[256,2048]{1,0:T(8,128)}, f32[256,2048]{1,0:T(8,128)}, u32[]{:S(2)}, u32[]{:S(2)}) collective-permute-start(f32[256,2048]{1,0:T(8,128)} %convolution_add_fusion), channel_id=1, source_target_pairs={{0,1},{1,0},{2,3},{3,2},{4,5},{5,4},{6,7},{7,6},{8,9},{9,8},{10,11... | collective-permute-start | bytes 6291464 | tf_op jit(solution)/shard_map/ppermute | solution.py:17
  160.3 3.6 %collective-permute-start.20 = (bf16[256,512]{1,0:T(8,128)(2,1)}, bf16[256,512]{1,0:T(8,128)(2,1)}, u32[]{:S(2)}, u32[]{:S(2)}) collective-permute-start(bf16[256,512]{1,0:T(8,128)(2,1)} %copy.18), channel_id=1, source_target_pairs={{0,1},{1,0},{2,3},{3,2},{4,5},{5,4},{6,7},{7,6},{8,9},{9,8},{10,11... | collective-permute-start | bytes 786440 | tf_op jit(solution)/shard_map/ppermute | solution.py:17
  (3 other events, 8.5 us)

commit v6 on v4

--- a/solution.py
+++ b/solution.py
@@ -29,27 +29,28 @@
     place[np.asarray(order)] = np.arange(chips)
     order_t = jnp.asarray(order, jnp.int32)
     here = jnp.asarray(place)[c]
-    ahead = [(order[p_], order[(p_ + 1) % chips]) for p_ in range(chips)]
-    behind = [(order[p_], order[(p_ - 1) % chips]) for p_ in range(chips)]
-    share = block.shape[1] // 3
-    width = block.shape[1] - share
+    ahead = [(order[i], order[(i + 1) % chips]) for i in range(chips)]
+    behind = [(order[i], order[(i - 1) % chips]) for i in range(chips)]
+    span = block.shape[0]
+    share = (span * 3 // 8) // 8 * 8
+    width = span - share
     groups = lax.axis_size("groups")
     partner = [(g, g ^ 1) for g in range(groups)]
 
-    def land(piece):
-        sent = lax.dynamic_slice_in_dim(piece, p * share, share, axis=1)
+    def land(src, piece):
+        sent = lax.dynamic_slice_in_dim(piece, p * (width - share), share, axis=0)
         other = lax.ppermute(sent, "groups", partner)
-        return [(piece, p * share), (other, (1 - p) * width)]
+        return [(src, p * share, piece), (src, (1 - p) * width, other)]
 
-    got = [(c, [(block, 0)])]
-    fwd = lax.dynamic_slice_in_dim(block, p * share, width, axis=1)
+    fwd = lax.dynamic_slice_in_dim(block, p * share, width, axis=0)
     bwd = fwd
+    got = [(c, 0, block)]
     for step in range(1, chips // 2 + 1):
         fwd = lax.ppermute(fwd, "chip", ahead)
-        got.append((order_t[(here - step) % chips], land(fwd)))
+        got += land(order_t[(here - step) % chips], fwd)
         if step <= (chips - 1) // 2:
             bwd = lax.ppermute(bwd, "chip", behind)
-            got.append((order_t[(here + step) % chips], land(bwd)))
+            got += land(order_t[(here + step) % chips], bwd)
     return got
 
 
@@ -106,10 +107,10 @@
 
     span = 2 * rows_dev
     block = chip_block((w_query, w_key, w_value))
+    parity = lax.axis_index("groups") % 2
     w_half = jnp.zeros((chips * span, block.shape[1]), bf16)
-    for src, parts in ring_gather(block, chips, c, lax.axis_index("groups") % 2):
-        for piece, col in parts:
-            w_half = lax.dynamic_update_slice(w_half, piece, (src * span, col))
+    for src, offset, piece in ring_gather(block, chips, c, parity):
+        w_half = lax.dynamic_update_slice_in_dim(w_half, piece, src * span + offset, axis=0)
     projected = jnp.dot(x_pair, w_half, preferred_element_type=f32).astype(bf16)
     projected = projected.reshape(2, tok, 3, heads, DH)
     query = projected[:, :, 0]

time: 252 us -> 186 us (0.74)
  the two profiles are of different devices: /device:TPU:0 before, /device:TPU:15 now
where the time goes in v6:
time: 186 us; the launch traced here: 183 us
  waiting for transfers between devices  87.3 us (47%)
  starting transfers between devices  41.9 us (23%)
  matrix products  18.6 us (10%)
  local copies, waits for them, and re-layouts  15.9 us (9%)
  other arithmetic  9.91 us (5%)
  between operations  9.71 us (5%)
    ppermute x7, waiting for transfers between devices, land(): other = lax.ppermute(sent, 'groups', partner)  29.4 us
    ppermute x6, waiting for transfers between devices, exclusive_scan(): got = lax.ppermute(incl, 'chip', perm)  28.2 us
    ppermute x4, waiting for transfers between devices, ring_gather(): fwd = lax.ppermute(fwd, 'chip', ahead)  18.3 us
    ppermute x6, starting transfers between devices, swap(): return lax.ppermute(x, 'core', [(0, 1), (1, 0)])  17.4 us
    ppermute x6, starting transfers between devices, exclusive_scan(): got = lax.ppermute(incl, 'chip', perm)  17 us
    dot_general x2, matrix products, grad_rows(): lax.dot_general(d_proj[j], w_half, (((1,), (1,)), ((), ())), preferred_el...  9.46 us
    ppermute x3, waiting for transfers between devices, ring_gather(): bwd = lax.ppermute(bwd, 'chip', behind)  7.75 us
    unnamed x13, local copies, waits for them, and re-layouts  4.81 us
  transfers between devices with their start and end apart: 26, of which 18 were waited for; matrix products, arithmetic and copies ran while one was open for 14% of the time, Pallas kernels for 0%

profile of v6, /device:TPU:15, one launch (start us, length us, event | category | flops | bytes accessed | tf_op | source)
XLA Modules:
  0.0 183.3 jit_solution(1215604040207120553)
XLA Ops:
  3.6 1.9 %add_convert_fusion = bf16[256,2048]{1,0:T(8,128)(2,1)S(1)} fusion(bf16[256,2048]{1,0:T(8,128)(2,1)} %param.10, bf16[256,2048]{1,0:T(8,128)(2,1)} %param.9), kind=kLoop, calls=%fused_computation.8 | loop fusion | flops 2097152 | bytes 3145728 | tf_op jit(solution)/shard_map/convert_element_type | solution.py:95
  14.9 1.3 collective-permute-start.4
  23.1 3.9 %collective-permute-done.2 = bf16[160,1536]{1,0:T(8,128)(2,1)S(1)} collective-permute-done((bf16[160,1536]{1,0:T(8,128)(2,1)}, bf16[160,1536]{1,0:T(8,128)(2,1)S(1)}, u32[]{:S(2)}, u32[]{:S(2)}) %collective-permute-start.2) | collective-permute-done | bytes 491552 | tf_op jit(solution)/shard_map/ppermute | solution.py:49
  28.9 5.9 %collective-permute-done.3 = bf16[96,1536]{1,0:T(8,128)(2,1)S(1)} collective-permute-done((bf16[96,1536]{1,0:T(8,128)(2,1)S(1)}, bf16[96,1536]{1,0:T(8,128)(2,1)S(1)}, u32[]{:S(2)}, u32[]{:S(2)}) %collective-permute-start.3) | collective-permute-done | bytes 294944 | tf_op jit(solution)/shard_map/ppermute | solution.py:42
  36.1 4.9 %collective-permute-done.5 = bf16[96,1536]{1,0:T(8,128)(2,1)S(1)} collective-permute-done((bf16[96,1536]{1,0:T(8,128)(2,1)S(1)}, bf16[96,1536]{1,0:T(8,128)(2,1)S(1)}, u32[]{:S(2)}, u32[]{:S(2)}) %collective-permute-start.5) | collective-permute-done | bytes 294944 | tf_op jit(solution)/shard_map/ppermute | solution.py:42
  41.1 1.7 collective-permute-start.21
  44.8 6.8 %collective-permute-done.7 = bf16[96,1536]{1,0:T(8,128)(2,1)S(1)} collective-permute-done((bf16[96,1536]{1,0:T(8,128)(2,1)S(1)}, bf16[96,1536]{1,0:T(8,128)(2,1)S(1)}, u32[]{:S(2)}, u32[]{:S(2)}) %collective-permute-start.7) | collective-permute-done | bytes 294944 | tf_op jit(solution)/shard_map/ppermute | solution.py:42
  51.9 6.1 %collective-permute-done.9 = bf16[96,1536]{1,0:T(8,128)(2,1)S(1)} collective-permute-done((bf16[96,1536]{1,0:T(8,128)(2,1)S(1)}, bf16[96,1536]{1,0:T(8,128)(2,1)S(1)}, u32[]{:S(2)}, u32[]{:S(2)}) %collective-permute-start.9) | collective-permute-done | bytes 294944 | tf_op jit(solution)/shard_map/ppermute | solution.py:42
  57.9 1.3 collective-permute-start.12
  59.3 3.9 %collective-permute-done.10 = bf16[160,1536]{1,0:T(8,128)(2,1)S(1)} collective-permute-done((bf16[160,1536]{1,0:T(8,128)(2,1)S(1)}, bf16[160,1536]{1,0:T(8,128)(2,1)S(1)}, u32[]{:S(2)}, u32[]{:S(2)}) %collective-permute-start.10) | collective-permute-done | bytes 491552 | tf_op jit(solution)/shard_map/ppermute | solution.py:49
  63.5 6.4 %collective-permute-done.12 = bf16[160,1536]{1,0:T(8,128)(2,1)S(1)} collective-permute-done((bf16[160,1536]{1,0:T(8,128)(2,1)S(1)}, bf16[160,1536]{1,0:T(8,128)(2,1)S(1)}, u32[]{:S(2)}, u32[]{:S(2)}) %collective-permute-start.12) | collective-permute-done | bytes 491552 | tf_op jit(solution)/shard_map/ppermute | solution.py:52
  70.5 10.4 %collective-permute-done.14 = bf16[160,1536]{1,0:T(8,128)(2,1)S(1)} collective-permute-done((bf16[160,1536]{1,0:T(8,128)(2,1)S(1)}, bf16[160,1536]{1,0:T(8,128)(2,1)S(1)}, u32[]{:S(2)}, u32[]{:S(2)}) %collective-permute-start.14) | collective-permute-done | bytes 491552 | tf_op jit(solution)/shard_map/ppermute | solution.py:49
  81.4 5.6 %collective-permute-done.15 = bf16[96,1536]{1,0:T(8,128)(2,1)S(1)} collective-permute-done((bf16[96,1536]{1,0:T(8,128)(2,1)S(1)}, bf16[96,1536]{1,0:T(8,128)(2,1)S(1)}, u32[]{:S(2)}, u32[]{:S(2)}) %collective-permute-start.15) | collective-permute-done | bytes 294944 | tf_op jit(solution)/shard_map/ppermute | solution.py:42
  87.0 2.6 %copy-done = bf16[2048,1536]{1,0:T(8,128)(2,1)} copy-done((bf16[2048,1536]{1,0:T(8,128)(2,1)}, bf16[2048,1536]{1,0:T(8,128)(2,1)S(1)}, u32[]{:S(2)}) %copy-start) | copy-done | bytes 6291480
  89.6 4.6 %convolution_convert_fusion = bf16[512,1536]{1,0:T(8,128)(2,1)S(1)} fusion(bf16[2048,1536]{1,0:T(8,128)(2,1)S(1)} %constant_dynamic-update-slice_fusion, bf16[256,2048]{1,0:T(8,128)(2,1)} %collective-permute-done, bf16[256,2048]{1,0:T(8,128)(2,1)S(1)} %add_convert_fusion), kind=kOutput, calls=%fused_computation | convolution fusion | flops 3226206208 | bytes 9961472 | tf_op jit(solution)/shard_map/dot_general | solution.py:114
  94.7 1.3 fusion.40
  98.4 3.1 %collective-permute-start.17 = (f32[4,128,128]{2,1,0:T(8,128)}, f32[4,128,128]{2,1,0:T(8,128)}, u32[]{:S(2)}, u32[]{:S(2)}) collective-permute-start(f32[4,128,128]{2,1,0:T(8,128)} %fusion.27), channel_id=1, source_target_pairs={{0,2},{2,4},{4,6},{6,8},{8,10},{10,12},{12,14},{1,3},{3,5},{5,7},{... | collective-permute-start | bytes 786440 | tf_op jit(solution)/shard_map/ppermute | solution.py:66
  102.2 3.5 %collective-permute-done.17 = f32[4,128,128]{2,1,0:T(8,128)} collective-permute-done((f32[4,128,128]{2,1,0:T(8,128)}, f32[4,128,128]{2,1,0:T(8,128)}, u32[]{:S(2)}, u32[]{:S(2)}) %collective-permute-start.17) | collective-permute-done | bytes 262176 | tf_op jit(solution)/shard_map/ppermute | solution.py:66
  106.8 3.2 %collective-permute-start.18 = (f32[4,128,128]{2,1,0:T(8,128)S(1)}, f32[4,128,128]{2,1,0:T(8,128)S(1)}, u32[]{:S(2)}, u32[]{:S(2)}) collective-permute-start(f32[4,128,128]{2,1,0:T(8,128)S(1)} %fusion.59), channel_id=1, source_target_pairs={{0,4},{2,6},{4,8},{6,10},{8,12},{10,14},{1,5},{3,7},{5,9},{7,11},{... | collective-permute-start | bytes 786440 | tf_op jit(solution)/shard_map/ppermute | solution.py:66
  110.4 3.5 %collective-permute-done.18 = f32[4,128,128]{2,1,0:T(8,128)S(1)} collective-permute-done((f32[4,128,128]{2,1,0:T(8,128)S(1)}, f32[4,128,128]{2,1,0:T(8,128)S(1)}, u32[]{:S(2)}, u32[]{:S(2)}) %collective-permute-start.18) | collective-permute-done | bytes 262176 | tf_op jit(solution)/shard_map/ppermute | solution.py:66
  113.9 4.2 %collective-permute-start.19 = (f32[4,128,128]{2,1,0:T(8,128)S(1)}, f32[4,128,128]{2,1,0:T(8,128)S(1)}, u32[]{:S(2)}, u32[]{:S(2)}) collective-permute-start(f32[4,128,128]{2,1,0:T(8,128)S(1)} %add.334), channel_id=1, source_target_pairs={{0,8},{2,10},{4,12},{6,14},{1,9},{3,11},{5,13},{7,15},{16,24},{18,... | collective-permute-start | bytes 786440 | tf_op jit(solution)/shard_map/ppermute | solution.py:66
  118.6 5.5 %collective-permute-done.19 = f32[4,128,128]{2,1,0:T(8,128)S(1)} collective-permute-done((f32[4,128,128]{2,1,0:T(8,128)S(1)}, f32[4,128,128]{2,1,0:T(8,128)S(1)}, u32[]{:S(2)}, u32[]{:S(2)}) %collective-permute-start.19) | collective-permute-done | bytes 262176 | tf_op jit(solution)/shard_map/ppermute | solution.py:66
  128.8 3.0 %collective-permute-start.22 = (f32[4,128,128]{2,1,0:T(8,128)S(1)}, f32[4,128,128]{2,1,0:T(8,128)S(1)}, u32[]{:S(2)}, u32[]{:S(2)}) collective-permute-start(f32[4,128,128]{2,1,0:T(8,128)S(1)} %fusion.28), channel_id=1, source_target_pairs={{2,0},{4,2},{6,4},{8,6},{10,8},{12,10},{14,12},{3,1},{5,3},{7,5},{... | collective-permute-start | bytes 786440 | tf_op jit(solution)/shard_map/ppermute | solution.py:66
  132.7 4.2 %collective-permute-done.22 = f32[4,128,128]{2,1,0:T(8,128)S(1)} collective-permute-done((f32[4,128,128]{2,1,0:T(8,128)S(1)}, f32[4,128,128]{2,1,0:T(8,128)S(1)}, u32[]{:S(2)}, u32[]{:S(2)}) %collective-permute-start.22) | collective-permute-done | bytes 262176 | tf_op jit(solution)/shard_map/ppermute | solution.py:66
  136.9 1.9 %collective-permute-start.23 = (f32[4,128,128]{2,1,0:T(8,128)S(1)}, f32[4,128,128]{2,1,0:T(8,128)S(1)}, u32[]{:S(2)}, u32[]{:S(2)}) collective-permute-start(f32[4,128,128]{2,1,0:T(8,128)S(1)} %fusion.58), channel_id=1, source_target_pairs={{4,0},{6,2},{8,4},{10,6},{12,8},{14,10},{5,1},{7,3},{9,5},{11,7},{... | collective-permute-start | bytes 786440 | tf_op jit(solution)/shard_map/ppermute | solution.py:66
  139.2 5.2 %collective-permute-done.23 = f32[4,128,128]{2,1,0:T(8,128)S(1)} collective-permute-done((f32[4,128,128]{2,1,0:T(8,128)S(1)}, f32[4,128,128]{2,1,0:T(8,128)S(1)}, u32[]{:S(2)}, u32[]{:S(2)}) %collective-permute-start.23) | collective-permute-done | bytes 262176 | tf_op jit(solution)/shard_map/ppermute | solution.py:66
  144.5 1.5 collective-permute-start.24
  146.3 6.3 %collective-permute-done.24 = f32[4,128,128]{2,1,0:T(8,128)S(1)} collective-permute-done((f32[4,128,128]{2,1,0:T(8,128)S(1)}, f32[4,128,128]{2,1,0:T(8,128)S(1)}, u32[]{:S(2)}, u32[]{:S(2)}) %collective-permute-start.24) | collective-permute-done | bytes 262176 | tf_op jit(solution)/shard_map/ppermute | solution.py:66
  154.6 3.2 %fusion.44 = f32[256,2048]{1,0:T(8,128)} fusion(bf16[256,1536]{0,1:T(8,128)(2,1)S(1)} %bitcast.131, bf16[2048,1536]{1,0:T(8,128)(2,1)S(1)} %bitcast.124), kind=kOutput, calls=%fused_computation.113 | convolution fusion | flops 1610612736 | bytes 9175040 | tf_op jit(solution)/shard_map/dot_general | solution.py:169
  157.8 14.2 %collective-permute-start.25 = (f32[256,2048]{1,0:T(8,128)}, f32[256,2048]{1,0:T(8,128)}, u32[]{:S(2)}, u32[]{:S(2)}) collective-permute-start(f32[256,2048]{1,0:T(8,128)} %fusion.44), channel_id=1, source_target_pairs={{0,1},{1,0},{2,3},{3,2},{4,5},{5,4},{6,7},{7,6},{8,9},{9,8},{10,11... | collective-permute-start | bytes 6291464 | tf_op jit(solution)/shard_map/ppermute | solution.py:17
  172.4 3.7 %collective-permute-done.20 = bf16[256,512]{1,0:T(8,128)(2,1)S(1)} collective-permute-done((bf16[256,512]{1,0:T(8,128)(2,1)S(1)}, bf16[256,512]{1,0:T(8,128)(2,1)S(1)}, u32[]{:S(2)}, u32[]{:S(2)}) %collective-permute-start.20) | collective-permute-done | bytes 262176 | tf_op jit(solution)/shard_map/ppermute | solution.py:17
  177.1 6.2 %fusion = bf16[256,2048]{1,0:T(8,128)(2,1)} fusion(f32[256,2048]{1,0:T(8,128)} %collective-permute-done.25, bf16[256,1536]{0,1:T(8,128)(2,1)S(1)} %bitcast.130, bf16[2048,1536]{1,0:T(8,128)(2,1)} %copy-done), kind=kOutput, calls=%fused_computation.2 | convolution fusion | flops 1611661312 | bytes 10223616 | tf_op jit(solution)/shard_map/dot_general | solution.py:169
  (109 shorter events, 32.2 us)
Async XLA Ops:
  0.6 16.8 %copy-start.2 = (s32[8]{0:T(128)S(1)}, s32[8]{0:T(128)}, u32[]{:S(2)}) copy-start(s32[8]{0:T(128)} %constant.120.clone) | copy-start | bytes 100
  2.8 9.3 %collective-permute-start.1 = (bf16[128,1536]{1,0:T(8,128)(2,1)S(1)}, bf16[128,1536]{1,0:T(8,128)(2,1)}, u32[]{:S(2)}, u32[]{:S(2)}) collective-permute-start(bf16[128,1536]{1,0:T(8,128)(2,1)S(1)} %pad_maximum_fusion.2), channel_id=1, source_target_pairs={{0,1},{1,0},{2,3},{3,2},{4,5},{5,4},{6,7},{7,6},{8,9},{9,8},{10,11... | collective-permute-start | bytes 1179656 | tf_op jit(solution)/shard_map/ppermute | solution.py:17
  5.5 81.5 %collective-permute-start = (bf16[256,2048]{1,0:T(8,128)(2,1)S(1)}, bf16[256,2048]{1,0:T(8,128)(2,1)}, u32[]{:S(2)}, u32[]{:S(2)}) collective-permute-start(bf16[256,2048]{1,0:T(8,128)(2,1)S(1)} %add_convert_fusion), channel_id=1, source_target_pairs={{0,1},{1,0},{2,3},{3,2},{4,5},{5,4},{6,7},{7,6},{8,9},{9,8},{10,11... | collective-permute-start | bytes 3145736 | tf_op jit(solution)/shard_map/ppermute | solution.py:17
  5.6 95.9 %collective-permute-start.16 = (s32[2,2]{1,0:T(2,128)}, s32[2,2]{1,0:T(2,128)S(1)}, u32[]{:S(2)}, u32[]{:S(2)}) collective-permute-start(s32[2,2]{1,0:T(2,128)} %bitcast.132), channel_id=1, source_target_pairs={{0,1},{1,0},{2,3},{3,2},{4,5},{5,4},{6,7},{7,6},{8,9},{9,8},{10,11... | collective-permute-start | bytes 56 | tf_op jit(solution)/shard_map/ppermute | solution.py:17
  14.0 13.0 %collective-permute-start.2 = (bf16[160,1536]{1,0:T(8,128)(2,1)}, bf16[160,1536]{1,0:T(8,128)(2,1)S(1)}, u32[]{:S(2)}, u32[]{:S(2)}) collective-permute-start(bf16[160,1536]{1,0:T(8,128)(2,1)} %constant_dynamic-slice_fusion.7), channel_id=1, source_target_pairs={{0,4},{4,8},{8,12},{12,14},{14,10},{10,6},{6,2},{2,0},{1,5},{5,9},... | collective-permute-start | bytes 1474568 | tf_op jit(solution)/shard_map/ppermute | solution.py:49
  14.9 12.7 %collective-permute-start.4 = (bf16[160,1536]{1,0:T(8,128)(2,1)}, bf16[160,1536]{1,0:T(8,128)(2,1)S(1)}, u32[]{:S(2)}, u32[]{:S(2)}) collective-permute-start(bf16[160,1536]{1,0:T(8,128)(2,1)} %constant_dynamic-slice_fusion.7), channel_id=1, source_target_pairs={{0,2},{4,0},{8,4},{12,8},{14,12},{10,14},{6,10},{2,6},{1,3},{5,1},... | collective-permute-start | bytes 1474568 | tf_op jit(solution)/shard_map/ppermute | solution.py:52
  27.0 7.7 %collective-permute-start.3 = (bf16[96,1536]{1,0:T(8,128)(2,1)S(1)}, bf16[96,1536]{1,0:T(8,128)(2,1)S(1)}, u32[]{:S(2)}, u32[]{:S(2)}) collective-permute-start(bf16[96,1536]{1,0:T(8,128)(2,1)S(1)} %constant_dynamic-slice_fusion.6), channel_id=1, source_target_pairs={{0,16},{16,0},{1,17},{17,1},{2,18},{18,2},{3,19},{19,3},{4,20},{20... | collective-permute-start | bytes 884744 | tf_op jit(solution)/shard_map/ppermute | solution.py:42
  27.6 13.5 %collective-permute-start.5 = (bf16[96,1536]{1,0:T(8,128)(2,1)S(1)}, bf16[96,1536]{1,0:T(8,128)(2,1)S(1)}, u32[]{:S(2)}, u32[]{:S(2)}) collective-permute-start(bf16[96,1536]{1,0:T(8,128)(2,1)S(1)} %constant_dynamic-slice_fusion.5), channel_id=1, source_target_pairs={{0,16},{16,0},{1,17},{17,1},{2,18},{18,2},{3,19},{19,3},{4,20},{20... | collective-permute-start | bytes 884744 | tf_op jit(solution)/shard_map/ppermute | solution.py:42
  28.7 14.2 %collective-permute-start.6 = (bf16[160,1536]{1,0:T(8,128)(2,1)S(1)}, bf16[160,1536]{1,0:T(8,128)(2,1)S(1)}, u32[]{:S(2)}, u32[]{:S(2)}) collective-permute-start(bf16[160,1536]{1,0:T(8,128)(2,1)S(1)} %collective-permute-done.2), channel_id=1, source_target_pairs={{0,4},{4,8},{8,12},{12,14},{14,10},{10,6},{6,2},{2,0},{1,5},{5,9},... | collective-permute-start | bytes 1474568 | tf_op jit(solution)/shard_map/ppermute | solution.py:49
  34.8 9.6 %collective-permute-start.8 = (bf16[160,1536]{1,0:T(8,128)(2,1)S(1)}, bf16[160,1536]{1,0:T(8,128)(2,1)S(1)}, u32[]{:S(2)}, u32[]{:S(2)}) collective-permute-start(bf16[160,1536]{1,0:T(8,128)(2,1)S(1)} %collective-permute-done.4), channel_id=1, source_target_pairs={{0,2},{4,0},{8,4},{12,8},{14,12},{10,14},{6,10},{2,6},{1,3},{5,1},... | collective-permute-start | bytes 1474568 | tf_op jit(solution)/shard_map/ppermute | solution.py:52
  41.1 84.5 %collective-permute-start.21 = (bf16[256,512]{0,1:T(8,128)(2,1)}, bf16[256,512]{0,1:T(8,128)(2,1)}, u32[]{:S(2)}, u32[]{:S(2)}) collective-permute-start(bf16[256,512]{0,1:T(8,128)(2,1)} %get-tuple-element.14), channel_id=1, source_target_pairs={{0,1},{1,0},{2,3},{3,2},{4,5},{5,4},{6,7},{7,6},{8,9},{9,8},{10,11... | collective-permute-start | bytes 786440 | tf_op jit(solution)/shard_map/ppermute | solution.py:17
  42.9 8.7 %collective-permute-start.7 = (bf16[96,1536]{1,0:T(8,128)(2,1)S(1)}, bf16[96,1536]{1,0:T(8,128)(2,1)S(1)}, u32[]{:S(2)}, u32[]{:S(2)}) collective-permute-start(bf16[96,1536]{1,0:T(8,128)(2,1)S(1)} %constant_dynamic-slice_fusion.4), channel_id=1, source_target_pairs={{0,16},{16,0},{1,17},{17,1},{2,18},{18,2},{3,19},{19,3},{4,20},{20... | collective-permute-start | bytes 884744 | tf_op jit(solution)/shard_map/ppermute | solution.py:42
  44.4 13.5 %collective-permute-start.9 = (bf16[96,1536]{1,0:T(8,128)(2,1)S(1)}, bf16[96,1536]{1,0:T(8,128)(2,1)S(1)}, u32[]{:S(2)}, u32[]{:S(2)}) collective-permute-start(bf16[96,1536]{1,0:T(8,128)(2,1)S(1)} %constant_dynamic-slice_fusion.3), channel_id=1, source_target_pairs={{0,16},{16,0},{1,17},{17,1},{2,18},{18,2},{3,19},{19,3},{4,20},{20... | collective-permute-start | bytes 884744 | tf_op jit(solution)/shard_map/ppermute | solution.py:42
  51.6 11.5 %collective-permute-start.10 = (bf16[160,1536]{1,0:T(8,128)(2,1)S(1)}, bf16[160,1536]{1,0:T(8,128)(2,1)S(1)}, u32[]{:S(2)}, u32[]{:S(2)}) collective-permute-start(bf16[160,1536]{1,0:T(8,128)(2,1)S(1)} %collective-permute-done.6), channel_id=1, source_target_pairs={{0,4},{4,8},{8,12},{12,14},{14,10},{10,6},{6,2},{2,0},{1,5},{5,9},... | collective-permute-start | bytes 1474568 | tf_op jit(solution)/shard_map/ppermute | solution.py:49
  57.9 12.0 %collective-permute-start.12 = (bf16[160,1536]{1,0:T(8,128)(2,1)S(1)}, bf16[160,1536]{1,0:T(8,128)(2,1)S(1)}, u32[]{:S(2)}, u32[]{:S(2)}) collective-permute-start(bf16[160,1536]{1,0:T(8,128)(2,1)S(1)} %collective-permute-done.8), channel_id=1, source_target_pairs={{0,2},{4,0},{8,4},{12,8},{14,12},{10,14},{6,10},{2,6},{1,3},{5,1},... | collective-permute-start | bytes 1474568 | tf_op jit(solution)/shard_map/ppermute | solution.py:52
  63.2 6.9 %collective-permute-start.11 = (bf16[96,1536]{1,0:T(8,128)(2,1)S(1)}, bf16[96,1536]{1,0:T(8,128)(2,1)S(1)}, u32[]{:S(2)}, u32[]{:S(2)}) collective-permute-start(bf16[96,1536]{1,0:T(8,128)(2,1)S(1)} %constant_dynamic-slice_fusion.2), channel_id=1, source_target_pairs={{0,16},{16,0},{1,17},{17,1},{2,18},{18,2},{3,19},{19,3},{4,20},{20... | collective-permute-start | bytes 884744 | tf_op jit(solution)/shard_map/ppermute | solution.py:42
  69.9 11.0 %collective-permute-start.14 = (bf16[160,1536]{1,0:T(8,128)(2,1)S(1)}, bf16[160,1536]{1,0:T(8,128)(2,1)S(1)}, u32[]{:S(2)}, u32[]{:S(2)}) collective-permute-start(bf16[160,1536]{1,0:T(8,128)(2,1)S(1)} %collective-permute-done.10), channel_id=1, source_target_pairs={{0,4},{4,8},{8,12},{12,14},{14,10},{10,6},{6,2},{2,0},{1,5},{5,9},... | collective-permute-start | bytes 1474568 | tf_op jit(solution)/shard_map/ppermute | solution.py:49
  70.1 11.2 %collective-permute-start.13 = (bf16[96,1536]{1,0:T(8,128)(2,1)S(1)}, bf16[96,1536]{1,0:T(8,128)(2,1)S(1)}, u32[]{:S(2)}, u32[]{:S(2)}) collective-permute-start(bf16[96,1536]{1,0:T(8,128)(2,1)S(1)} %constant_dynamic-slice_fusion.1), channel_id=1, source_target_pairs={{0,16},{16,0},{1,17},{17,1},{2,18},{18,2},{3,19},{19,3},{4,20},{20... | collective-permute-start | bytes 884744 | tf_op jit(solution)/shard_map/ppermute | solution.py:42
  81.0 6.0 %collective-permute-start.15 = (bf16[96,1536]{1,0:T(8,128)(2,1)S(1)}, bf16[96,1536]{1,0:T(8,128)(2,1)S(1)}, u32[]{:S(2)}, u32[]{:S(2)}) collective-permute-start(bf16[96,1536]{1,0:T(8,128)(2,1)S(1)} %constant_dynamic-slice_fusion), channel_id=1, source_target_pairs={{0,16},{16,0},{1,17},{17,1},{2,18},{18,2},{3,19},{19,3},{4,20},{20... | collective-permute-start | bytes 884744 | tf_op jit(solution)/shard_map/ppermute | solution.py:42
  87.0 2.6 %copy-start = (bf16[2048,1536]{1,0:T(8,128)(2,1)}, bf16[2048,1536]{1,0:T(8,128)(2,1)S(1)}, u32[]{:S(2)}) copy-start(bf16[2048,1536]{1,0:T(8,128)(2,1)S(1)} %constant_dynamic-update-slice_fusion) | copy-start | bytes 18874372
  94.2 7.3 %copy-start.3 = (s32[1,2,2]{2,1,0:T(2,128)S(1)}, s32[1,2,2]{2,1,0:T(2,128)}, u32[]{:S(2)}) copy-start(s32[1,2,2]{2,1,0:T(2,128)} %param.15) | copy-start | bytes 52
  94.3 7.9 %copy-start.1 = (pred[256,256]{1,0:T(8,128)(4,1)S(1)}, pred[256,256]{1,0:T(8,128)(4,1)}, u32[]{:S(2)}) copy-start(pred[256,256]{1,0:T(8,128)(4,1)} %iota_compare_fusion) | copy-start | bytes 196612
  98.4 7.4 %collective-permute-start.17 = (f32[4,128,128]{2,1,0:T(8,128)}, f32[4,128,128]{2,1,0:T(8,128)}, u32[]{:S(2)}, u32[]{:S(2)}) collective-permute-start(f32[4,128,128]{2,1,0:T(8,128)} %fusion.27), channel_id=1, source_target_pairs={{0,2},{2,4},{4,6},{6,8},{8,10},{10,12},{12,14},{1,3},{3,5},{5,7},{... | collective-permute-start | bytes 786440 | tf_op jit(solution)/shard_map/ppermute | solution.py:66
  106.8 7.1 %collective-permute-start.18 = (f32[4,128,128]{2,1,0:T(8,128)S(1)}, f32[4,128,128]{2,1,0:T(8,128)S(1)}, u32[]{:S(2)}, u32[]{:S(2)}) collective-permute-start(f32[4,128,128]{2,1,0:T(8,128)S(1)} %fusion.59), channel_id=1, source_target_pairs={{0,4},{2,6},{4,8},{6,10},{8,12},{10,14},{1,5},{3,7},{5,9},{7,11},{... | collective-permute-start | bytes 786440 | tf_op jit(solution)/shard_map/ppermute | solution.py:66
  113.9 10.2 %collective-permute-start.19 = (f32[4,128,128]{2,1,0:T(8,128)S(1)}, f32[4,128,128]{2,1,0:T(8,128)S(1)}, u32[]{:S(2)}, u32[]{:S(2)}) collective-permute-start(f32[4,128,128]{2,1,0:T(8,128)S(1)} %add.334), channel_id=1, source_target_pairs={{0,8},{2,10},{4,12},{6,14},{1,9},{3,11},{5,13},{7,15},{16,24},{18,... | collective-permute-start | bytes 786440 | tf_op jit(solution)/shard_map/ppermute | solution.py:66
  128.8 8.0 %collective-permute-start.22 = (f32[4,128,128]{2,1,0:T(8,128)S(1)}, f32[4,128,128]{2,1,0:T(8,128)S(1)}, u32[]{:S(2)}, u32[]{:S(2)}) collective-permute-start(f32[4,128,128]{2,1,0:T(8,128)S(1)} %fusion.28), channel_id=1, source_target_pairs={{2,0},{4,2},{6,4},{8,6},{10,8},{12,10},{14,12},{3,1},{5,3},{7,5},{... | collective-permute-start | bytes 786440 | tf_op jit(solution)/shard_map/ppermute | solution.py:66
  136.9 7.5 %collective-permute-start.23 = (f32[4,128,128]{2,1,0:T(8,128)S(1)}, f32[4,128,128]{2,1,0:T(8,128)S(1)}, u32[]{:S(2)}, u32[]{:S(2)}) collective-permute-start(f32[4,128,128]{2,1,0:T(8,128)S(1)} %fusion.58), channel_id=1, source_target_pairs={{4,0},{6,2},{8,4},{10,6},{12,8},{14,10},{5,1},{7,3},{9,5},{11,7},{... | collective-permute-start | bytes 786440 | tf_op jit(solution)/shard_map/ppermute | solution.py:66
  144.5 8.1 %collective-permute-start.24 = (f32[4,128,128]{2,1,0:T(8,128)S(1)}, f32[4,128,128]{2,1,0:T(8,128)S(1)}, u32[]{:S(2)}, u32[]{:S(2)}) collective-permute-start(f32[4,128,128]{2,1,0:T(8,128)S(1)} %add.347), channel_id=1, source_target_pairs={{8,0},{10,2},{12,4},{14,6},{9,1},{11,3},{13,5},{15,7},{24,16},{26,... | collective-permute-start | bytes 786440 | tf_op jit(solution)/shard_map/ppermute | solution.py:66
  146.3 7.4 %slice-start = ((s8[6291456]{0:T(1024)(128)(4,1)}), s8[4194304]{0:T(1024)(128)(4,1)S(1)}, s32[]{:S(2)}) async-start(s8[6291456]{0:T(1024)(128)(4,1)} %bitcast.123), calls=%async_computation | async-start | bytes 8388608
  153.0 1.6 slice-start.1
  157.8 19.3 %collective-permute-start.25 = (f32[256,2048]{1,0:T(8,128)}, f32[256,2048]{1,0:T(8,128)}, u32[]{:S(2)}, u32[]{:S(2)}) collective-permute-start(f32[256,2048]{1,0:T(8,128)} %fusion.44), channel_id=1, source_target_pairs={{0,1},{1,0},{2,3},{3,2},{4,5},{5,4},{6,7},{7,6},{8,9},{9,8},{10,11... | collective-permute-start | bytes 6291464 | tf_op jit(solution)/shard_map/ppermute | solution.py:17
  172.2 3.9 %collective-permute-start.20 = (bf16[256,512]{1,0:T(8,128)(2,1)S(1)}, bf16[256,512]{1,0:T(8,128)(2,1)S(1)}, u32[]{:S(2)}, u32[]{:S(2)}) collective-permute-start(bf16[256,512]{1,0:T(8,128)(2,1)S(1)} %copy.17), channel_id=1, source_target_pairs={{0,1},{1,0},{2,3},{3,2},{4,5},{5,4},{6,7},{7,6},{8,9},{9,8},{10,11... | collective-permute-start | bytes 786440 | tf_op jit(solution)/shard_map/ppermute | solution.py:17

commit v7 on v5

--- a/solution.py
+++ b/solution.py
@@ -53,19 +53,16 @@
 
 
 def exclusive_scan(total, chips, reverse):
-    incl = total
-    excl = jnp.zeros_like(total)
-    d = 1
-    while d < chips:
-        if reverse:
-            perm = [(i, i - d) for i in range(d, chips)]
-        else:
-            perm = [(i, i + d) for i in range(chips - d)]
-        got = lax.ppermute(incl, "chip", perm)
-        incl = incl + got
-        excl = excl + got
-        d *= 2
-    return excl
+    flat = total.reshape(chips, -1)
+    got = lax.all_to_all(flat, "chip", 0, 0)
+    if reverse:
+        got = got[::-1]
+    run = jnp.cumsum(got[:-1], axis=0)
+    before = jnp.concatenate([jnp.zeros_like(got[:1]), run], axis=0)
+    if reverse:
+        before = before[::-1]
+    back = lax.all_to_all(before, "chip", 0, 0)
+    return back.reshape(total.shape)
 
 
 def dense_allow(block_masks, tokens):

time: 175 us -> 246 us (1.41)
  the two profiles are of different devices: /device:TPU:15 before, /device:TPU:0 now
where the time goes in v7:
time: 246 us; the launch traced here: 241 us
  local copies, waits for them, and re-layouts  97.9 us (40%)
  waiting for transfers between devices  43 us (17%)
  matrix products  36.6 us (15%)
  starting transfers between devices  34.8 us (14%)
  other arithmetic  18.8 us (8%)
  between operations  9.86 us (4%)
    slice x3, local copies, waits for them, and re-layouts, exclusive_scan(): run = jnp.cumsum(got[:-1], axis=0)  30 us
    rev x1, local copies, waits for them, and re-layouts, exclusive_scan(): before = before[::-1]  27.9 us
    ppermute x7, waiting for transfers between devices, land(): return (piece, lax.ppermute(sent, 'groups', partner))  19.6 us
    dot_general x2, matrix products, grad_rows(): lax.dot_general(d_ring, w_ring, (((1,), (1,)), ((), ())), preferred_eleme...  10.2 us
    all_to_all x2, starting transfers between devices, exclusive_scan(): got = lax.all_to_all(flat, 'chip', 0, 0)  9.59 us
    dynamic_update_slice x8, local copies, waits for them, and re-layouts, on_device(): w_ring = lax.dynamic_update_slice_in_dim(w_ring, ringed, src * span, axis=0)  9.07 us
    all_to_all x2, waiting for transfers between devices, exclusive_scan(): back = lax.all_to_all(before, 'chip', 0, 0)  8.43 us
    all_to_all x2, starting transfers between devices, exclusive_scan(): back = lax.all_to_all(before, 'chip', 0, 0)  8.28 us
  transfers between devices with their start and end apart: 24, of which 16 were waited for; matrix products, arithmetic and copies ran while one was open for 25% of the time, Pallas kernels for 0%

profile of v7, /device:TPU:0, one launch (start us, length us, event | category | flops | bytes accessed | tf_op | source)
XLA Modules:
  0.0 241.0 jit_solution(5167072302156598897)
XLA Ops:
  4.7 2.5 %broadcast_in_dim.27 = bf16[2048,1024]{1,0:T(8,128)(2,1)} broadcast(bf16[]{:T(256)} %constant.101.clone.1), dimensions={} | broadcast | bytes 4194306 | tf_op jit(solution)/shard_map/broadcast_in_dim | solution.py:108
  8.3 3.0 %collective-permute-start.2 = (bf16[256,1024]{1,0:T(8,128)(2,1)}, bf16[256,1024]{1,0:T(8,128)(2,1)}, u32[]{:S(2)}, u32[]{:S(2)}) collective-permute-start(bf16[256,1024]{1,0:T(8,128)(2,1)} %get-tuple-element.3), channel_id=1, source_target_pairs={{0,4},{4,8},{8,12},{12,14},{14,10},{10,6},{6,2},{2,0},{1,5},{5,9},... | collective-permute-start | bytes 1572872 | tf_op jit(solution)/shard_map/ppermute | solution.py:47
  24.8 2.0 collective-permute-start.9
  31.8 1.9 constant_dynamic-update-slice_fusion.12
  34.1 5.3 %collective-permute-done.10 = bf16[256,512]{1,0:T(8,128)(2,1)S(1)} collective-permute-done((bf16[256,512]{1,0:T(8,128)(2,1)S(1)}, bf16[256,512]{1,0:T(8,128)(2,1)S(1)}, u32[]{:S(2)}, u32[]{:S(2)}) %collective-permute-start.10) | collective-permute-done | bytes 262176 | tf_op jit(solution)/shard_map/ppermute | solution.py:41
  47.3 3.0 %collective-permute-done.11 = bf16[256,512]{1,0:T(8,128)(2,1)S(1)} collective-permute-done((bf16[256,512]{1,0:T(8,128)(2,1)S(1)}, bf16[256,512]{1,0:T(8,128)(2,1)S(1)}, u32[]{:S(2)}, u32[]{:S(2)}) %collective-permute-start.11) | collective-permute-done | bytes 262176 | tf_op jit(solution)/shard_map/ppermute | solution.py:41
  50.4 4.0 %collective-permute-done.12 = bf16[256,512]{1,0:T(8,128)(2,1)S(1)} collective-permute-done((bf16[256,512]{1,0:T(8,128)(2,1)S(1)}, bf16[256,512]{1,0:T(8,128)(2,1)S(1)}, u32[]{:S(2)}, u32[]{:S(2)}) %collective-permute-start.12) | collective-permute-done | bytes 262176 | tf_op jit(solution)/shard_map/ppermute | solution.py:41
  60.1 4.0 %collective-permute-done.13 = bf16[256,512]{1,0:T(8,128)(2,1)S(1)} collective-permute-done((bf16[256,512]{1,0:T(8,128)(2,1)S(1)}, bf16[256,512]{1,0:T(8,128)(2,1)S(1)}, u32[]{:S(2)}, u32[]{:S(2)}) %collective-permute-start.13) | collective-permute-done | bytes 262176 | tf_op jit(solution)/shard_map/ppermute | solution.py:41
  64.1 3.0 %collective-permute-done.14 = bf16[256,512]{1,0:T(8,128)(2,1)S(1)} collective-permute-done((bf16[256,512]{1,0:T(8,128)(2,1)S(1)}, bf16[256,512]{1,0:T(8,128)(2,1)S(1)}, u32[]{:S(2)}, u32[]{:S(2)}) %collective-permute-start.14) | collective-permute-done | bytes 262176 | tf_op jit(solution)/shard_map/ppermute | solution.py:41
  69.8 5.2 %convolution_convert_fusion = bf16[512,1024]{1,0:T(8,128)(2,1)S(1)} fusion(bf16[2048,1024]{1,0:T(8,128)(2,1)} %constant_dynamic-update-slice_fusion.7, bf16[256,2048]{1,0:T(8,128)(2,1)} %collective-permute-done, bf16[256,2048]{1,0:T(8,128)(2,1)} %add_convert_fusion), kind=kOutput, calls=%fused_computation.10 | convolution fusion | flops 2152202240 | bytes 7340032 | tf_op jit(solution)/shard_map/dot_general | solution.py:113
  75.0 2.8 %fusion.4 = bf16[512,512]{1,0:T(8,128)(2,1)S(1)} fusion(bf16[2048,512]{1,0:T(8,128)(2,1)S(1)} %constant_dynamic-update-slice_fusion, bf16[256,2048]{1,0:T(8,128)(2,1)} %collective-permute-done, bf16[256,2048]{1,0:T(8,128)(2,1)} %add_convert_fusion), kind=kOutput, calls=%fused_computation.19 | convolution fusion | flops 1078198272 | bytes 4718592 | tf_op jit(solution)/shard_map/dot_general | solution.py:114
  79.4 4.0 %select_n.238 = bf16[2,256,3,4,128]{4,3,2,1,0:T(4,128)(2,1)} reshape(bf16[512,1536]{1,0:T(8,128)(2,1)} %maximum_select_fusion) | data formatting | bytes 3145728 | tf_op jit(solution)/shard_map/jit(_where)/select_n | solution.py:115
  83.3 2.9 %fusion.45 = (bf16[2,256,1,4,128]{4,3,2,1,0:T(4,128)(2,1)}, bf16[2,256,1,4,128]{4,3,2,1,0:T(4,128)(2,1)S(1)}, bf16[2,256,1,4,128]{4,3,2,1,0:T(4,128)(2,1)}) fusion(bf16[2,256,3,4,128]{4,3,2,1,0:T(4,128)(2,1)} %select_n.238), kind=kLoop, calls=%fused_computation.117 | loop fusion | bytes 3145728 | tf_op jit(solution)/shard_map/slice | solution.py:123
  89.4 5.6 %all-to-all-start = ((f32[8,1,8192]{2,1,0:T(1,128)}), f32[8,1,8192]{2,1,0:T(1,128)}, u32[]{:S(2)}, u32[]{:S(2)}) async-start(f32[8,1,8192]{2,1,0:T(1,128)} %bitcast.96), calls=%async_computation | async-start | bytes 524288 | tf_op jit(solution)/shard_map/all_to_all | solution.py:57
  96.0 2.3 reshape.179
  100.1 3.1 %all-to-all-done = f32[8,1,8192]{2,1,0:T(1,128)} async-done(((f32[8,1,8192]{2,1,0:T(1,128)}), f32[8,1,8192]{2,1,0:T(1,128)}, u32[]{:S(2)}, u32[]{:S(2)}) %all-to-all-start) | async-done | bytes 262176 | tf_op jit(solution)/shard_map/all_to_all | solution.py:57
  108.9 4.2 %all-to-all-start.1 = ((f32[8,1,8192]{2,1,0:T(1,128)}), f32[8,1,8192]{2,1,0:T(1,128)}, u32[]{:S(2)}, u32[]{:S(2)}) async-start(f32[8,1,8192]{2,1,0:T(1,128)} %copy.39), calls=%async_computation.1 | async-start | bytes 524288 | tf_op jit(solution)/shard_map/all_to_all | solution.py:64
  117.2 4.0 %all-to-all-done.1 = f32[8,1,8192]{2,1,0:T(1,128)} async-done(((f32[8,1,8192]{2,1,0:T(1,128)}), f32[8,1,8192]{2,1,0:T(1,128)}, u32[]{:S(2)}, u32[]{:S(2)}) %all-to-all-start.1) | async-done | bytes 262176 | tf_op jit(solution)/shard_map/all_to_all | solution.py:64
  125.4 2.1 fusion.13
  130.9 4.0 %all-to-all-start.2 = ((f32[8,1,8192]{2,1,0:T(1,128)}), f32[8,1,8192]{2,1,0:T(1,128)}, u32[]{:S(2)}, u32[]{:S(2)}) async-start(f32[8,1,8192]{2,1,0:T(1,128)} %bitcast.30), calls=%async_computation.2 | async-start | bytes 524288 | tf_op jit(solution)/shard_map/all_to_all | solution.py:57
  134.9 2.8 %fusion.24 = f32[2,4,128,256]{3,2,1,0:T(8,128)} fusion(bf16[2,4,256,256]{3,2,1,0:T(8,128)(2,1)} %multiply_convert_fusion, bf16[2,256,1,4,128]{4,3,2,1,0:T(4,128)(2,1)S(1)} %get-tuple-element.7), kind=kOutput, calls=%fused_computation.51 | convolution fusion | flops 134217728 | bytes 2621440 | tf_op jit(solution)/shard_map/jhts,jshd->jthd/dot_general | solution.py:165
  139.1 4.1 %all-to-all-done.2 = f32[8,1,8192]{2,1,0:T(1,128)} async-done(((f32[8,1,8192]{2,1,0:T(1,128)}), f32[8,1,8192]{2,1,0:T(1,128)}, u32[]{:S(2)}, u32[]{:S(2)}) %all-to-all-start.2) | async-done | bytes 262176 | tf_op jit(solution)/shard_map/all_to_all | solution.py:57
  145.0 28.1 %slice.82 = f32[7,8192]{1,0:T(8,128)} reverse(f32[7,8192]{1,0:T(8,128)} %bitcast.99), dimensions={0} | reverse | bytes 458752 | tf_op jit(solution)/shard_map/slice | solution.py:60
  176.5 27.9 %rev.4 = f32[8,8192]{1,0:T(8,128)} reverse(f32[8,8192]{1,0:T(8,128)} %concatenate.40), dimensions={0} | reverse | bytes 524288 | tf_op jit(solution)/shard_map/rev | solution.py:63
  204.4 1.9 copy.54
  206.3 4.1 %all-to-all-start.3 = ((f32[8,1,8192]{2,1,0:T(1,128)}), f32[8,1,8192]{2,1,0:T(1,128)}, u32[]{:S(2)}, u32[]{:S(2)}) async-start(f32[8,1,8192]{2,1,0:T(1,128)} %copy.54), calls=%async_computation.3 | async-start | bytes 524288 | tf_op jit(solution)/shard_map/all_to_all | solution.py:64
  210.4 2.4 %fusion.10 = bf16[2,256,1,4,128]{1,4,3,0,2:T(8,128)(2,1)} fusion(f32[2,4,128,256]{3,2,1,0:T(8,128)} %fusion.24, bf16[2,256,4,128]{1,3,2,0:T(8,128)(2,1)S(1)} %get-tuple-element.9, bf16[1,4,128,128]{3,2,1,0:T(8,128)(2,1)S(1)} %copy-done.14, bf16[1,4,128,128]{3,2,1,0:T(8,128)(2,1)S(1)} %get-tuple-element.13), kind=kOutput, calls=%fused_computation.25 | convolution fusion | flops 67764224 | bytes 2359296 | tf_op jit(solution)/shard_map/jthe,jhde->jthd/dot_general | solution.py:166
  214.2 4.5 %all-to-all-done.3 = f32[8,1,8192]{2,1,0:T(1,128)} async-done(((f32[8,1,8192]{2,1,0:T(1,128)}), f32[8,1,8192]{2,1,0:T(1,128)}, u32[]{:S(2)}, u32[]{:S(2)}) %all-to-all-start.3) | async-done | bytes 262176 | tf_op jit(solution)/shard_map/all_to_all | solution.py:64
  223.1 5.0 %convolution_add_fusion = f32[256,2048]{1,0:T(8,128)} fusion(f32[256,2048]{1,0:T(8,128)S(1)} %fusion.29, bf16[2048,1024]{1,0:T(8,128)(2,1)} %constant_dynamic-update-slice_fusion.7, bf16[256,1536]{0,1:T(8,128)(2,1)S(1)} %bitcast.92, s32[]{:T(128)S(6)} %select_n.211), kind=kOutput, calls=%fused_computation | convolution fusion | flops 1074266112 | bytes 8912900 | tf_op jit(solution)/shard_map/dot_general | solution.py:176
  229.6 3.3 %collective-permute-done.17 = bf16[256,512]{1,0:T(8,128)(2,1)} collective-permute-done((bf16[256,512]{1,0:T(8,128)(2,1)}, bf16[256,512]{1,0:T(8,128)(2,1)}, u32[]{:S(2)}, u32[]{:S(2)}) %collective-permute-start.17) | collective-permute-done | bytes 262176 | tf_op jit(solution)/shard_map/ppermute | solution.py:17
  233.0 2.0 maximum_select_fusion.1
  235.8 5.3 %fusion.1 = bf16[256,2048]{1,0:T(8,128)(2,1)} fusion(f32[256,2048]{1,0:T(8,128)} %collective-permute-done.19, f32[256,2048]{1,0:T(8,128)S(1)} %fusion.31, bf16[2048,1024]{1,0:T(8,128)(2,1)} %constant_dynamic-update-slice_fusion.7, bf16[256,1536]{0,1:T(8,128)(2,1)S(1)} %bitcast.90, s32[]{:T(128)S(6)} %select_n.211), kind=kOutput, calls=%fused_computation.3 | convolution fusion | flops 1075314688 | bytes 9961476 | tf_op jit(solution)/shard_map/dot_general | solution.py:176
  (147 shorter events, 71.2 us)
Async XLA Ops:
  2.8 1.9 collective-permute-start.1
  4.7 6.6 %copy-start.15 = (bf16[256,2048]{1,0:T(8,128)(2,1)S(1)}, bf16[256,2048]{1,0:T(8,128)(2,1)}, u32[]{:S(2)}) copy-start(bf16[256,2048]{1,0:T(8,128)(2,1)} %param.10) | copy-start | bytes 3145732
  4.7 6.6 %copy-start.16 = (bf16[256,2048]{1,0:T(8,128)(2,1)S(1)}, bf16[256,2048]{1,0:T(8,128)(2,1)}, u32[]{:S(2)}) copy-start(bf16[256,2048]{1,0:T(8,128)(2,1)} %param.9) | copy-start | bytes 3145732
  7.2 5.5 %copy-start.20 = (s32[8]{0:T(128)S(1)}, s32[8]{0:T(128)}, u32[]{:S(2)}) copy-start(s32[8]{0:T(128)} %constant.123.clone) | copy-start | bytes 100
  7.2 10.2 %copy-start.18 = (s32[8]{0:T(128)S(1)}, s32[8]{0:T(128)}, u32[]{:S(2)}) copy-start(s32[8]{0:T(128)} %constant.122.clone) | copy-start | bytes 100
  8.3 14.3 %copy-start.17 = (bf16[256,1024]{1,0:T(8,128)(2,1)S(1)}, bf16[256,1024]{1,0:T(8,128)(2,1)}, u32[]{:S(2)}) copy-start(bf16[256,1024]{1,0:T(8,128)(2,1)} %param.11) | copy-start | bytes 1572868
  8.3 15.5 %collective-permute-start.2 = (bf16[256,1024]{1,0:T(8,128)(2,1)}, bf16[256,1024]{1,0:T(8,128)(2,1)}, u32[]{:S(2)}, u32[]{:S(2)}) collective-permute-start(bf16[256,1024]{1,0:T(8,128)(2,1)} %get-tuple-element.3), channel_id=1, source_target_pairs={{0,4},{4,8},{8,12},{12,14},{14,10},{10,6},{6,2},{2,0},{1,5},{5,9},... | collective-permute-start | bytes 1572872 | tf_op jit(solution)/shard_map/ppermute | solution.py:47
  11.3 17.1 %collective-permute-start.3 = (bf16[256,1024]{1,0:T(8,128)(2,1)}, bf16[256,1024]{1,0:T(8,128)(2,1)}, u32[]{:S(2)}, u32[]{:S(2)}) collective-permute-start(bf16[256,1024]{1,0:T(8,128)(2,1)} %get-tuple-element.3), channel_id=1, source_target_pairs={{0,2},{4,0},{8,4},{12,8},{14,12},{10,14},{6,10},{2,6},{1,3},{5,1},... | collective-permute-start | bytes 1572872 | tf_op jit(solution)/shard_map/ppermute | solution.py:50
  12.7 57.1 %collective-permute-start = (bf16[256,2048]{1,0:T(8,128)(2,1)}, bf16[256,2048]{1,0:T(8,128)(2,1)}, u32[]{:S(2)}, u32[]{:S(2)}) collective-permute-start(bf16[256,2048]{1,0:T(8,128)(2,1)} %add_convert_fusion), channel_id=1, source_target_pairs={{0,1},{1,0},{2,3},{3,2},{4,5},{5,4},{6,7},{7,6},{8,9},{9,8},{10,11... | collective-permute-start | bytes 3145736 | tf_op jit(solution)/shard_map/ppermute | solution.py:17
  24.8 9.2 %collective-permute-start.9 = (bf16[256,512]{1,0:T(8,128)(2,1)S(1)}, bf16[256,512]{1,0:T(8,128)(2,1)S(1)}, u32[]{:S(2)}, u32[]{:S(2)}) collective-permute-start(bf16[256,512]{1,0:T(8,128)(2,1)S(1)} %constant_dynamic-slice_fusion.6), channel_id=1, source_target_pairs={{0,16},{16,0},{1,17},{17,1},{2,18},{18,2},{3,19},{19,3},{4,20},{20... | collective-permute-start | bytes 786440 | tf_op jit(solution)/shard_map/ppermute | solution.py:41
  26.8 14.3 %collective-permute-start.4 = (bf16[256,1024]{1,0:T(8,128)(2,1)}, bf16[256,1024]{1,0:T(8,128)(2,1)S(1)}, u32[]{:S(2)}, u32[]{:S(2)}) collective-permute-start(bf16[256,1024]{1,0:T(8,128)(2,1)} %collective-permute-done.2), channel_id=1, source_target_pairs={{0,4},{4,8},{8,12},{12,14},{14,10},{10,6},{6,2},{2,0},{1,5},{5,9},... | collective-permute-start | bytes 1572872 | tf_op jit(solution)/shard_map/ppermute | solution.py:47
  29.3 10.0 %collective-permute-start.10 = (bf16[256,512]{1,0:T(8,128)(2,1)S(1)}, bf16[256,512]{1,0:T(8,128)(2,1)S(1)}, u32[]{:S(2)}, u32[]{:S(2)}) collective-permute-start(bf16[256,512]{1,0:T(8,128)(2,1)S(1)} %constant_dynamic-slice_fusion.5), channel_id=1, source_target_pairs={{0,16},{16,0},{1,17},{17,1},{2,18},{18,2},{3,19},{19,3},{4,20},{20... | collective-permute-start | bytes 786440 | tf_op jit(solution)/shard_map/ppermute | solution.py:41
  29.9 13.7 %collective-permute-start.5 = (bf16[256,1024]{1,0:T(8,128)(2,1)}, bf16[256,1024]{1,0:T(8,128)(2,1)S(1)}, u32[]{:S(2)}, u32[]{:S(2)}) collective-permute-start(bf16[256,1024]{1,0:T(8,128)(2,1)} %collective-permute-done.3), channel_id=1, source_target_pairs={{0,2},{4,0},{8,4},{12,8},{14,12},{10,14},{6,10},{2,6},{1,3},{5,1},... | collective-permute-start | bytes 1572872 | tf_op jit(solution)/shard_map/ppermute | solution.py:50
  33.7 16.6 %copy-start.19 = (s32[1,2,2]{2,1,0:T(2,128)S(1)}, s32[1,2,2]{2,1,0:T(2,128)}, u32[]{:S(2)}) copy-start(s32[1,2,2]{2,1,0:T(2,128)} %param.15) | copy-start | bytes 52
  41.1 9.3 %collective-permute-start.11 = (bf16[256,512]{1,0:T(8,128)(2,1)S(1)}, bf16[256,512]{1,0:T(8,128)(2,1)S(1)}, u32[]{:S(2)}, u32[]{:S(2)}) collective-permute-start(bf16[256,512]{1,0:T(8,128)(2,1)S(1)} %constant_dynamic-slice_fusion.4), channel_id=1, source_target_pairs={{0,16},{16,0},{1,17},{17,1},{2,18},{18,2},{3,19},{19,3},{4,20},{20... | collective-permute-start | bytes 786440 | tf_op jit(solution)/shard_map/ppermute | solution.py:41
  41.5 13.2 %collective-permute-start.6 = (bf16[256,1024]{1,0:T(8,128)(2,1)S(1)}, bf16[256,1024]{1,0:T(8,128)(2,1)S(1)}, u32[]{:S(2)}, u32[]{:S(2)}) collective-permute-start(bf16[256,1024]{1,0:T(8,128)(2,1)S(1)} %collective-permute-done.4), channel_id=1, source_target_pairs={{0,4},{4,8},{8,12},{12,14},{14,10},{10,6},{6,2},{2,0},{1,5},{5,9},... | collective-permute-start | bytes 1572872 | tf_op jit(solution)/shard_map/ppermute | solution.py:47
  43.7 10.7 %collective-permute-start.12 = (bf16[256,512]{1,0:T(8,128)(2,1)S(1)}, bf16[256,512]{1,0:T(8,128)(2,1)S(1)}, u32[]{:S(2)}, u32[]{:S(2)}) collective-permute-start(bf16[256,512]{1,0:T(8,128)(2,1)S(1)} %constant_dynamic-slice_fusion.3), channel_id=1, source_target_pairs={{0,16},{16,0},{1,17},{17,1},{2,18},{18,2},{3,19},{19,3},{4,20},{20... | collective-permute-start | bytes 786440 | tf_op jit(solution)/shard_map/ppermute | solution.py:41
  45.2 12.6 %collective-permute-start.7 = (bf16[256,1024]{1,0:T(8,128)(2,1)S(1)}, bf16[256,1024]{1,0:T(8,128)(2,1)S(1)}, u32[]{:S(2)}, u32[]{:S(2)}) collective-permute-start(bf16[256,1024]{1,0:T(8,128)(2,1)S(1)} %collective-permute-done.5), channel_id=1, source_target_pairs={{0,2},{4,0},{8,4},{12,8},{14,12},{10,14},{6,10},{2,6},{1,3},{5,1},... | collective-permute-start | bytes 1572872 | tf_op jit(solution)/shard_map/ppermute | solution.py:50
  50.4 44.6 %collective-permute-start.16 = (s32[2,2]{1,0:T(2,128)S(1)}, s32[2,2]{1,0:T(2,128)S(1)}, u32[]{:S(2)}, u32[]{:S(2)}) collective-permute-start(s32[2,2]{1,0:T(2,128)S(1)} %bitcast.102), channel_id=1, source_target_pairs={{0,1},{1,0},{2,3},{3,2},{4,5},{5,4},{6,7},{7,6},{8,9},{9,8},{10,11... | collective-permute-start | bytes 56 | tf_op jit(solution)/shard_map/ppermute | solution.py:17
  54.7 9.3 %collective-permute-start.13 = (bf16[256,512]{1,0:T(8,128)(2,1)S(1)}, bf16[256,512]{1,0:T(8,128)(2,1)S(1)}, u32[]{:S(2)}, u32[]{:S(2)}) collective-permute-start(bf16[256,512]{1,0:T(8,128)(2,1)S(1)} %constant_dynamic-slice_fusion.2), channel_id=1, source_target_pairs={{0,16},{16,0},{1,17},{17,1},{2,18},{18,2},{3,19},{19,3},{4,20},{20... | collective-permute-start | bytes 786440 | tf_op jit(solution)/shard_map/ppermute | solution.py:41
  56.2 11.8 %collective-permute-start.8 = (bf16[256,1024]{1,0:T(8,128)(2,1)S(1)}, bf16[256,1024]{1,0:T(8,128)(2,1)S(1)}, u32[]{:S(2)}, u32[]{:S(2)}) collective-permute-start(bf16[256,1024]{1,0:T(8,128)(2,1)S(1)} %collective-permute-done.6), channel_id=1, source_target_pairs={{0,4},{4,8},{8,12},{12,14},{14,10},{10,6},{6,2},{2,0},{1,5},{5,9},... | collective-permute-start | bytes 1572872 | tf_op jit(solution)/shard_map/ppermute | solution.py:47
  57.8 9.3 %collective-permute-start.14 = (bf16[256,512]{1,0:T(8,128)(2,1)S(1)}, bf16[256,512]{1,0:T(8,128)(2,1)S(1)}, u32[]{:S(2)}, u32[]{:S(2)}) collective-permute-start(bf16[256,512]{1,0:T(8,128)(2,1)S(1)} %constant_dynamic-slice_fusion.1), channel_id=1, source_target_pairs={{0,16},{16,0},{1,17},{17,1},{2,18},{18,2},{3,19},{19,3},{4,20},{20... | collective-permute-start | bytes 786440 | tf_op jit(solution)/shard_map/ppermute | solution.py:41
  64.0 60.1 %collective-permute-start.18 = (bf16[256,512]{0,1:T(8,128)(2,1)}, bf16[256,512]{0,1:T(8,128)(2,1)}, u32[]{:S(2)}, u32[]{:S(2)}) collective-permute-start(bf16[256,512]{0,1:T(8,128)(2,1)} %get-tuple-element.16), channel_id=1, source_target_pairs={{0,1},{1,0},{2,3},{3,2},{4,5},{5,4},{6,7},{7,6},{8,9},{9,8},{10,11... | collective-permute-start | bytes 786440 | tf_op jit(solution)/shard_map/ppermute | solution.py:17
  68.0 7.0 %collective-permute-start.15 = (bf16[256,512]{1,0:T(8,128)(2,1)S(1)}, bf16[256,512]{1,0:T(8,128)(2,1)S(1)}, u32[]{:S(2)}, u32[]{:S(2)}) collective-permute-start(bf16[256,512]{1,0:T(8,128)(2,1)S(1)} %constant_dynamic-slice_fusion), channel_id=1, source_target_pairs={{0,16},{16,0},{1,17},{17,1},{2,18},{18,2},{3,19},{19,3},{4,20},{20... | collective-permute-start | bytes 786440 | tf_op jit(solution)/shard_map/ppermute | solution.py:41
  87.5 27.3 %copy-start = (bf16[2,256,1,4,128]{1,4,3,0,2:T(8,128)(2,1)}, bf16[2,256,1,4,128]{1,4,3,0,2:T(8,128)(2,1)S(1)}, u32[]{:S(2)}) copy-start(bf16[2,256,1,4,128]{1,4,3,0,2:T(8,128)(2,1)S(1)} %copy.73) | copy-start | bytes 1572868
  89.4 13.9 %all-to-all-start = ((f32[8,1,8192]{2,1,0:T(1,128)}), f32[8,1,8192]{2,1,0:T(1,128)}, u32[]{:S(2)}, u32[]{:S(2)}) async-start(f32[8,1,8192]{2,1,0:T(1,128)} %bitcast.96), calls=%async_computation | async-start | bytes 524288 | tf_op jit(solution)/shard_map/all_to_all | solution.py:57
  108.9 12.3 %all-to-all-start.1 = ((f32[8,1,8192]{2,1,0:T(1,128)}), f32[8,1,8192]{2,1,0:T(1,128)}, u32[]{:S(2)}, u32[]{:S(2)}) async-start(f32[8,1,8192]{2,1,0:T(1,128)} %copy.39), calls=%async_computation.1 | async-start | bytes 524288 | tf_op jit(solution)/shard_map/all_to_all | solution.py:64
  130.9 12.3 %all-to-all-start.2 = ((f32[8,1,8192]{2,1,0:T(1,128)}), f32[8,1,8192]{2,1,0:T(1,128)}, u32[]{:S(2)}, u32[]{:S(2)}) async-start(f32[8,1,8192]{2,1,0:T(1,128)} %bitcast.30), calls=%async_computation.2 | async-start | bytes 524288 | tf_op jit(solution)/shard_map/all_to_all | solution.py:57
  139.1 71.3 %copy-start.14 = (bf16[1,4,128,128]{3,2,1,0:T(8,128)(2,1)S(1)}, bf16[1,4,128,128]{3,2,1,0:T(8,128)(2,1)}, u32[]{:S(2)}) copy-start(bf16[1,4,128,128]{3,2,1,0:T(8,128)(2,1)} %copy-done.13) | copy-start | bytes 393220
  206.3 12.3 %all-to-all-start.3 = ((f32[8,1,8192]{2,1,0:T(1,128)}), f32[8,1,8192]{2,1,0:T(1,128)}, u32[]{:S(2)}, u32[]{:S(2)}) async-start(f32[8,1,8192]{2,1,0:T(1,128)} %copy.54), calls=%async_computation.3 | async-start | bytes 524288 | tf_op jit(solution)/shard_map/all_to_all | solution.py:64
  228.1 7.7 %collective-permute-start.19 = (f32[256,2048]{1,0:T(8,128)}, f32[256,2048]{1,0:T(8,128)}, u32[]{:S(2)}, u32[]{:S(2)}) collective-permute-start(f32[256,2048]{1,0:T(8,128)} %convolution_add_fusion), channel_id=1, source_target_pairs={{0,1},{1,0},{2,3},{3,2},{4,5},{5,4},{6,7},{7,6},{8,9},{9,8},{10,11... | collective-permute-start | bytes 6291464 | tf_op jit(solution)/shard_map/ppermute | solution.py:17
  229.0 4.0 %collective-permute-start.17 = (bf16[256,512]{1,0:T(8,128)(2,1)}, bf16[256,512]{1,0:T(8,128)(2,1)}, u32[]{:S(2)}, u32[]{:S(2)}) collective-permute-start(bf16[256,512]{1,0:T(8,128)(2,1)} %copy.41), channel_id=1, source_target_pairs={{0,1},{1,0},{2,3},{3,2},{4,5},{5,4},{6,7},{7,6},{8,9},{9,8},{10,11... | collective-permute-start | bytes 786440 | tf_op jit(solution)/shard_map/ppermute | solution.py:17
  (13 other events, 34.1 us)

commit v8 on v5

--- a/solution.py
+++ b/solution.py
@@ -110,20 +110,21 @@
     width = 2 * half
     w_ring = jnp.zeros((chips * span, width), bf16)
     w_x = jnp.zeros((chips * span, share), bf16)
+    p_ring = None
+    p_x = None
     for src, (ringed, swapped) in ring_gather(block, chips, c, parity):
         w_ring = lax.dynamic_update_slice_in_dim(w_ring, ringed, src * span, axis=0)
         w_x = lax.dynamic_update_slice_in_dim(w_x, swapped, src * span, axis=0)
-    p_ring = jnp.dot(x_pair, w_ring, preferred_element_type=f32).astype(bf16)
-    p_x = jnp.dot(x_pair, w_x, preferred_element_type=f32).astype(bf16)
-    projected = jnp.where(
-        parity == 0,
-        jnp.concatenate([p_ring, p_x], axis=1),
-        jnp.concatenate([p_x, p_ring], axis=1),
-    )
-    projected = projected.reshape(2, tok, 3, heads, DH)
-    query = projected[:, :, 0]
-    key = projected[:, :, 1]
-    value = projected[:, :, 2]
+        x_cols = lax.dynamic_slice_in_dim(x_pair, src * span, span, axis=1)
+        t_ring = jnp.dot(x_cols, ringed, preferred_element_type=f32)
+        t_x = jnp.dot(x_cols, swapped, preferred_element_type=f32)
+        p_ring = t_ring if p_ring is None else p_ring + t_ring
+        p_x = t_x if p_x is None else p_x + t_x
+    p_ring = p_ring.astype(bf16).reshape(2, tok, 2, heads, DH)
+    p_x = p_x.astype(bf16).reshape(2, tok, heads, DH)
+    query = jnp.where(parity == 0, p_ring[:, :, 0], p_x)
+    key = jnp.where(parity == 0, p_ring[:, :, 1], p_ring[:, :, 0])
+    value = jnp.where(parity == 0, p_x, p_ring[:, :, 1])
 
     local = jnp.einsum("jthd,jthe->jhde", key, value, preferred_element_type=f32)
     state0 = exclusive_scan(local[0] + local[1], chips, False)

time: 175 us -> 189 us (1.080)
  the two profiles are of different devices: /device:TPU:15 before, /device:TPU:0 now
where the time goes in v8:
time: 189 us; the launch traced here: 188 us
  waiting for transfers between devices  59.5 us (31%)
  starting transfers between devices  40 us (21%)
  matrix products  36.3 us (19%)
  local copies, waits for them, and re-layouts  30.8 us (16%)
  other arithmetic  11.1 us (6%)
  between operations  10.3 us (5%)
    ppermute x6, waiting for transfers between devices, exclusive_scan(): got = lax.ppermute(incl, 'chip', perm)  36.4 us
    ppermute x6, starting transfers between devices, exclusive_scan(): got = lax.ppermute(incl, 'chip', perm)  21 us
    ppermute x4, waiting for transfers between devices, ring_gather(): fwd = lax.ppermute(fwd, 'chip', ahead)  12.4 us
    dot_general x8, matrix products, on_device(): t_x = jnp.dot(x_cols, swapped, preferred_element_type=f32)  12 us
    dot_general x2, matrix products, grad_rows(): lax.dot_general(d_ring, w_ring, (((1,), (1,)), ((), ())), preferred_eleme...  10.2 us
    ppermute x7, starting transfers between devices, land(): return (piece, lax.ppermute(sent, 'groups', partner))  9.74 us
    dynamic_update_slice x8, local copies, waits for them, and re-layouts, on_device(): w_ring = lax.dynamic_update_slice_in_dim(w_ring, ringed, src * span, axis=0)  9.08 us
    dot_general x8, matrix products, on_device(): t_ring = jnp.dot(x_cols, ringed, preferred_element_type=f32)  8.08 us
  transfers between devices with their start and end apart: 26, of which 12 were waited for; matrix products, arithmetic and copies ran while one was open for 33% of the time, Pallas kernels for 0%

profile of v8, /device:TPU:0, one launch (start us, length us, event | category | flops | bytes accessed | tf_op | source)
XLA Modules:
  0.0 188.0 jit_solution(11501983186395981068)
XLA Ops:
  5.7 1.6 add_convert_fusion.1
  8.7 2.5 %broadcast_in_dim.31 = bf16[2048,1024]{1,0:T(8,128)(2,1)} broadcast(bf16[]{:T(256)} %constant.99.clone.1), dimensions={} | broadcast | bytes 4194306 | tf_op jit(solution)/shard_map/broadcast_in_dim | solution.py:111
  12.3 3.0 %collective-permute-start.4 = (bf16[256,1024]{1,0:T(8,128)(2,1)}, bf16[256,1024]{1,0:T(8,128)(2,1)}, u32[]{:S(2)}, u32[]{:S(2)}) collective-permute-start(bf16[256,1024]{1,0:T(8,128)(2,1)} %get-tuple-element.3), channel_id=1, source_target_pairs={{0,2},{4,0},{8,4},{12,8},{14,12},{10,14},{6,10},{2,6},{1,3},{5,1},... | collective-permute-start | bytes 1572872 | tf_op jit(solution)/shard_map/ppermute | solution.py:50
  29.4 2.0 %collective-permute-start.5 = (bf16[256,512]{1,0:T(8,128)(2,1)S(1)}, bf16[256,512]{1,0:T(8,128)(2,1)S(1)}, u32[]{:S(2)}, u32[]{:S(2)}) collective-permute-start(bf16[256,512]{1,0:T(8,128)(2,1)S(1)} %constant_dynamic-slice_fusion.5), channel_id=1, source_target_pairs={{0,16},{16,0},{1,17},{17,1},{2,18},{18,2},{3,19},{19,3},{4,20},{20... | collective-permute-start | bytes 786440 | tf_op jit(solution)/shard_map/ppermute | solution.py:41
  31.4 8.2 %collective-permute-done.2 = bf16[256,1024]{1,0:T(8,128)(2,1)} collective-permute-done((bf16[256,1024]{1,0:T(8,128)(2,1)}, bf16[256,1024]{1,0:T(8,128)(2,1)}, u32[]{:S(2)}, u32[]{:S(2)}) %collective-permute-start.2) | collective-permute-done | bytes 524320 | tf_op jit(solution)/shard_map/ppermute | solution.py:47
  42.1 1.6 collective-permute-start.8
  43.7 1.9 %constant_dynamic-update-slice_fusion.13 = bf16[2048,1024]{1,0:T(8,128)(2,1)} fusion(bf16[2048,1024]{1,0:T(8,128)(2,1)} %get-tuple-element.2, bf16[256,1024]{1,0:T(8,128)(2,1)} %collective-permute-done.2, s32[]{:T(128)S(6)} %select_n.224), kind=kLoop, calls=%fused_computation.118 | loop fusion | bytes 1048580 | tf_op jit(solution)/shard_map/dynamic_update_slice | solution.py:116
  45.6 1.9 %constant_dynamic-update-slice_fusion.12 = bf16[2048,1024]{1,0:T(8,128)(2,1)} fusion(bf16[2048,1024]{1,0:T(8,128)(2,1)} %constant_dynamic-update-slice_fusion.13, bf16[256,1024]{1,0:T(8,128)(2,1)} %collective-permute-done.4, s32[]{:T(128)S(6)} %select_n.229), kind=kLoop, calls=%fused_computation.117 | loop fusion | bytes 1048580 | tf_op jit(solution)/shard_map/dynamic_update_slice | solution.py:116
  55.7 4.2 %collective-permute-done.6 = bf16[256,1024]{1,0:T(8,128)(2,1)S(1)} collective-permute-done((bf16[256,1024]{1,0:T(8,128)(2,1)}, bf16[256,1024]{1,0:T(8,128)(2,1)S(1)}, u32[]{:S(2)}, u32[]{:S(2)}) %collective-permute-start.6) | collective-permute-done | bytes 524320 | tf_op jit(solution)/shard_map/ppermute | solution.py:47
  68.5 3.0 %collective-permute-done.12 = bf16[256,1024]{1,0:T(8,128)(2,1)S(1)} collective-permute-done((bf16[256,1024]{1,0:T(8,128)(2,1)S(1)}, bf16[256,1024]{1,0:T(8,128)(2,1)S(1)}, u32[]{:S(2)}, u32[]{:S(2)}) %collective-permute-start.12) | collective-permute-done | bytes 524320 | tf_op jit(solution)/shard_map/ppermute | solution.py:50
  73.1 1.9 %collective-permute-start.11 = (bf16[256,512]{1,0:T(8,128)(2,1)S(1)}, bf16[256,512]{1,0:T(8,128)(2,1)S(1)}, u32[]{:S(2)}, u32[]{:S(2)}) collective-permute-start(bf16[256,512]{1,0:T(8,128)(2,1)S(1)} %constant_dynamic-slice_fusion.2), channel_id=1, source_target_pairs={{0,16},{16,0},{1,17},{17,1},{2,18},{18,2},{3,19},{19,3},{4,20},{20... | collective-permute-start | bytes 786440 | tf_op jit(solution)/shard_map/ppermute | solution.py:41
  78.1 3.5 %collective-permute-done.11 = bf16[256,512]{1,0:T(8,128)(2,1)S(1)} collective-permute-done((bf16[256,512]{1,0:T(8,128)(2,1)S(1)}, bf16[256,512]{1,0:T(8,128)(2,1)S(1)}, u32[]{:S(2)}, u32[]{:S(2)}) %collective-permute-start.11) | collective-permute-done | bytes 262176 | tf_op jit(solution)/shard_map/ppermute | solution.py:41
  81.7 1.6 fusion.63
  86.8 1.9 add_convert_fusion
  88.7 2.6 %reshape.115 = bf16[2,256,2,4,128]{4,3,2,1,0:T(4,128)(2,1)} reshape(bf16[512,1024]{1,0:T(8,128)(2,1)} %add_convert_fusion) | data formatting | bytes 2097152 | tf_op jit(solution)/shard_map/reshape | solution.py:123
  91.3 2.7 %fusion.85 = (bf16[2,256,1,4,128]{4,3,2,1,0:T(4,128)(2,1)}, bf16[2,256,1,4,128]{4,3,2,1,0:T(4,128)(2,1)}) fusion(bf16[2,256,2,4,128]{4,3,2,1,0:T(4,128)(2,1)} %reshape.115), kind=kLoop, calls=%fused_computation.160 | loop fusion | bytes 2097152 | tf_op jit(solution)/shard_map/slice | solution.py:125
  95.9 2.6 %fusion.9 = bf16[512,512]{1,0:T(8,128)(2,1)} fusion(f32[512,512]{1,0:T(8,128)S(1)} %fusion.81, f32[512,512]{1,0:T(8,128)} %fusion.59, f32[512,512]{1,0:T(8,128)S(1)} %copy-done.6, f32[512,512]{1,0:T(8,128)S(1)} %copy-done.4, f32[512,512]{1,0:T(8,128)S(1)} %copy-done.5, f32[512,512]{1,0:T(8,128)S(1)} %copy-done.2, f32[512,512]{1,0:T(8,128)S(1)} %copy-done.3, ...), kind=kOutput, calls=%fused_computation.39 | convolution fusion | flops 136839168 | bytes 10223624 | tf_op jit(solution)/shard_map/dot_general | solution.py:120
  98.5 2.0 %reshape.114 = bf16[2,256,4,128]{3,2,1,0:T(4,128)(2,1)} reshape(bf16[512,512]{1,0:T(8,128)(2,1)} %fusion.9) | data formatting | bytes 1048576 | tf_op jit(solution)/shard_map/reshape | solution.py:124
  100.5 1.7 broadcast_select_fusion
  102.7 3.5 %collective-permute-start.17 = (f32[4,128,128]{2,1,0:T(8,128)S(1)}, f32[4,128,128]{2,1,0:T(8,128)S(1)}, u32[]{:S(2)}, u32[]{:S(2)}) collective-permute-start(f32[4,128,128]{2,1,0:T(8,128)S(1)} %fusion.37), channel_id=1, source_target_pairs={{0,2},{2,4},{4,6},{6,8},{8,10},{10,12},{12,14},{1,3},{3,5},{5,7},{... | collective-permute-start | bytes 786440 | tf_op jit(solution)/shard_map/ppermute | solution.py:64
  108.0 2.0 %collective-permute-done.17 = f32[4,128,128]{2,1,0:T(8,128)S(1)} collective-permute-done((f32[4,128,128]{2,1,0:T(8,128)S(1)}, f32[4,128,128]{2,1,0:T(8,128)S(1)}, u32[]{:S(2)}, u32[]{:S(2)}) %collective-permute-start.17) | collective-permute-done | bytes 262176 | tf_op jit(solution)/shard_map/ppermute | solution.py:64
  110.1 4.6 %collective-permute-start.18 = (f32[4,128,128]{2,1,0:T(8,128)S(1)}, f32[4,128,128]{2,1,0:T(8,128)S(1)}, u32[]{:S(2)}, u32[]{:S(2)}) collective-permute-start(f32[4,128,128]{2,1,0:T(8,128)S(1)} %fusion.134), channel_id=1, source_target_pairs={{0,4},{2,6},{4,8},{6,10},{8,12},{10,14},{1,5},{3,7},{5,9},{7,11},{... | collective-permute-start | bytes 786440 | tf_op jit(solution)/shard_map/ppermute | solution.py:64
  115.1 5.3 %collective-permute-done.18 = f32[4,128,128]{2,1,0:T(8,128)S(1)} collective-permute-done((f32[4,128,128]{2,1,0:T(8,128)S(1)}, f32[4,128,128]{2,1,0:T(8,128)S(1)}, u32[]{:S(2)}, u32[]{:S(2)}) %collective-permute-start.18) | collective-permute-done | bytes 262176 | tf_op jit(solution)/shard_map/ppermute | solution.py:64
  120.5 9.0 %collective-permute-start.19 = (f32[4,128,128]{2,1,0:T(8,128)S(1)}, f32[4,128,128]{2,1,0:T(8,128)S(1)}, u32[]{:S(2)}, u32[]{:S(2)}) collective-permute-start(f32[4,128,128]{2,1,0:T(8,128)S(1)} %add.336), channel_id=1, source_target_pairs={{0,8},{2,10},{4,12},{6,14},{1,9},{3,11},{5,13},{7,15},{16,24},{18,... | collective-permute-start | bytes 786440 | tf_op jit(solution)/shard_map/ppermute | solution.py:64
  130.0 3.4 %collective-permute-done.19 = f32[4,128,128]{2,1,0:T(8,128)S(1)} collective-permute-done((f32[4,128,128]{2,1,0:T(8,128)S(1)}, f32[4,128,128]{2,1,0:T(8,128)S(1)}, u32[]{:S(2)}, u32[]{:S(2)}) %collective-permute-start.19) | collective-permute-done | bytes 262176 | tf_op jit(solution)/shard_map/ppermute | solution.py:64
  139.2 6.2 %collective-permute-done.22 = f32[4,128,128]{2,1,0:T(8,128)S(1)} collective-permute-done((f32[4,128,128]{2,1,0:T(8,128)S(1)}, f32[4,128,128]{2,1,0:T(8,128)S(1)}, u32[]{:S(2)}, u32[]{:S(2)}) %collective-permute-start.22) | collective-permute-done | bytes 262176 | tf_op jit(solution)/shard_map/ppermute | solution.py:64
  147.0 9.3 %collective-permute-done.23 = f32[4,128,128]{2,1,0:T(8,128)S(1)} collective-permute-done((f32[4,128,128]{2,1,0:T(8,128)S(1)}, f32[4,128,128]{2,1,0:T(8,128)S(1)}, u32[]{:S(2)}, u32[]{:S(2)}) %collective-permute-start.23) | collective-permute-done | bytes 262176 | tf_op jit(solution)/shard_map/ppermute | solution.py:64
  158.0 10.3 %collective-permute-done.24 = f32[4,128,128]{2,1,0:T(8,128)S(1)} collective-permute-done((f32[4,128,128]{2,1,0:T(8,128)S(1)}, f32[4,128,128]{2,1,0:T(8,128)S(1)}, u32[]{:S(2)}, u32[]{:S(2)}) %collective-permute-start.24) | collective-permute-done | bytes 262176 | tf_op jit(solution)/shard_map/ppermute | solution.py:64
  170.1 4.9 %convolution_add_fusion = f32[256,2048]{1,0:T(8,128)} fusion(f32[256,2048]{1,0:T(8,128)S(1)} %fusion.33, bf16[2048,1024]{1,0:T(8,128)(2,1)} %constant_dynamic-update-slice_fusion.7, bf16[256,1536]{0,1:T(8,128)(2,1)S(1)} %bitcast.141, s32[]{:T(128)S(6)} %select_n.225), kind=kOutput, calls=%fused_computation.16 | convolution fusion | flops 1074266112 | bytes 8912900 | tf_op jit(solution)/shard_map/dot_general | solution.py:180
  176.6 3.3 %collective-permute-done.20 = bf16[256,512]{1,0:T(8,128)(2,1)} collective-permute-done((bf16[256,512]{1,0:T(8,128)(2,1)}, bf16[256,512]{1,0:T(8,128)(2,1)}, u32[]{:S(2)}, u32[]{:S(2)}) %collective-permute-start.20) | collective-permute-done | bytes 262176 | tf_op jit(solution)/shard_map/ppermute | solution.py:17
  179.9 2.0 %maximum_select_fusion = bf16[256,1024]{1,0:T(8,128)(2,1)} fusion(bf16[256,512]{1,0:T(8,128)(2,1)} %collective-permute-done.20, bf16[256,512]{1,0:T(8,128)(2,1)S(1)} %copy.19, pred[]{:T(512)S(6)} %eq.17), kind=kLoop, calls=%fused_computation.50 | loop fusion | flops 2359296 | bytes 1048577 | tf_op jit(solution)/shard_map/jit(_where)/select_n | solution.py:147
  182.7 5.3 %fusion.1 = bf16[256,2048]{1,0:T(8,128)(2,1)} fusion(f32[256,2048]{1,0:T(8,128)} %collective-permute-done.25, f32[256,2048]{1,0:T(8,128)S(1)} %fusion.35, bf16[2048,1024]{1,0:T(8,128)(2,1)} %constant_dynamic-update-slice_fusion.7, bf16[256,1536]{0,1:T(8,128)(2,1)S(1)} %bitcast.139, s32[]{:T(128)S(6)} %select_n.225), kind=kOutput, calls=%fused_computation.19 | convolution fusion | flops 1075314688 | bytes 9961476 | tf_op jit(solution)/shard_map/dot_general | solution.py:180
  (149 shorter events, 58.4 us)
Async XLA Ops:
  0.6 25.1 %collective-permute-start.16 = (s32[2,2]{1,0:T(2,128)}, s32[2,2]{1,0:T(2,128)S(1)}, u32[]{:S(2)}, u32[]{:S(2)}) collective-permute-start(s32[2,2]{1,0:T(2,128)} %bitcast.147), channel_id=1, source_target_pairs={{0,1},{1,0},{2,3},{3,2},{4,5},{5,4},{6,7},{7,6},{8,9},{9,8},{10,11... | collective-permute-start | bytes 56 | tf_op jit(solution)/shard_map/ppermute | solution.py:17
  4.2 3.4 %collective-permute-start.1 = (bf16[128,1536]{1,0:T(8,128)(2,1)}, bf16[128,1536]{1,0:T(8,128)(2,1)}, u32[]{:S(2)}, u32[]{:S(2)}) collective-permute-start(bf16[128,1536]{1,0:T(8,128)(2,1)} %pad_maximum_fusion.2), channel_id=1, source_target_pairs={{0,1},{1,0},{2,3},{3,2},{4,5},{5,4},{6,7},{7,6},{8,9},{9,8},{10,11... | collective-permute-start | bytes 1179656 | tf_op jit(solution)/shard_map/ppermute | solution.py:17
  5.3 128.5 %collective-permute-start.21 = (bf16[256,512]{0,1:T(8,128)(2,1)}, bf16[256,512]{0,1:T(8,128)(2,1)}, u32[]{:S(2)}, u32[]{:S(2)}) collective-permute-start(bf16[256,512]{0,1:T(8,128)(2,1)} %get-tuple-element.15), channel_id=1, source_target_pairs={{0,1},{1,0},{2,3},{3,2},{4,5},{5,4},{6,7},{7,6},{8,9},{9,8},{10,11... | collective-permute-start | bytes 786440 | tf_op jit(solution)/shard_map/ppermute | solution.py:17
  7.3 40.1 %collective-permute-start = (bf16[256,2048]{1,0:T(8,128)(2,1)S(1)}, bf16[256,2048]{1,0:T(8,128)(2,1)S(1)}, u32[]{:S(2)}, u32[]{:S(2)}) collective-permute-start(bf16[256,2048]{1,0:T(8,128)(2,1)S(1)} %add_convert_fusion.1), channel_id=1, source_target_pairs={{0,1},{1,0},{2,3},{3,2},{4,5},{5,4},{6,7},{7,6},{8,9},{9,8},{10,11... | collective-permute-start | bytes 3145736 | tf_op jit(solution)/shard_map/ppermute | solution.py:17
  8.6 6.6 %copy-start.16 = (s32[8]{0:T(128)S(1)}, s32[8]{0:T(128)}, u32[]{:S(2)}) copy-start(s32[8]{0:T(128)} %constant.118.clone) | copy-start | bytes 100
  8.7 11.9 %copy-start.14 = (s32[8]{0:T(128)S(1)}, s32[8]{0:T(128)}, u32[]{:S(2)}) copy-start(s32[8]{0:T(128)} %constant.117.clone) | copy-start | bytes 100
  8.7 17.0 %copy-start.15 = (s32[1,2,2]{2,1,0:T(2,128)S(1)}, s32[1,2,2]{2,1,0:T(2,128)}, u32[]{:S(2)}) copy-start(s32[1,2,2]{2,1,0:T(2,128)} %param.15) | copy-start | bytes 52
  12.3 16.1 %collective-permute-start.4 = (bf16[256,1024]{1,0:T(8,128)(2,1)}, bf16[256,1024]{1,0:T(8,128)(2,1)}, u32[]{:S(2)}, u32[]{:S(2)}) collective-permute-start(bf16[256,1024]{1,0:T(8,128)(2,1)} %get-tuple-element.3), channel_id=1, source_target_pairs={{0,2},{4,0},{8,4},{12,8},{14,12},{10,14},{6,10},{2,6},{1,3},{5,1},... | collective-permute-start | bytes 1572872 | tf_op jit(solution)/shard_map/ppermute | solution.py:50
  25.6 14.0 %collective-permute-start.2 = (bf16[256,1024]{1,0:T(8,128)(2,1)}, bf16[256,1024]{1,0:T(8,128)(2,1)}, u32[]{:S(2)}, u32[]{:S(2)}) collective-permute-start(bf16[256,1024]{1,0:T(8,128)(2,1)} %get-tuple-element.3), channel_id=1, source_target_pairs={{0,4},{4,8},{8,12},{12,14},{14,10},{10,6},{6,2},{2,0},{1,5},{5,9},... | collective-permute-start | bytes 1572872 | tf_op jit(solution)/shard_map/ppermute | solution.py:47
  29.4 23.0 %collective-permute-start.5 = (bf16[256,512]{1,0:T(8,128)(2,1)S(1)}, bf16[256,512]{1,0:T(8,128)(2,1)S(1)}, u32[]{:S(2)}, u32[]{:S(2)}) collective-permute-start(bf16[256,512]{1,0:T(8,128)(2,1)S(1)} %constant_dynamic-slice_fusion.5), channel_id=1, source_target_pairs={{0,16},{16,0},{1,17},{17,1},{2,18},{18,2},{3,19},{19,3},{4,20},{20... | collective-permute-start | bytes 786440 | tf_op jit(solution)/shard_map/ppermute | solution.py:41
  40.6 13.1 %collective-permute-start.3 = (bf16[256,512]{1,0:T(8,128)(2,1)S(1)}, bf16[256,512]{1,0:T(8,128)(2,1)S(1)}, u32[]{:S(2)}, u32[]{:S(2)}) collective-permute-start(bf16[256,512]{1,0:T(8,128)(2,1)S(1)} %constant_dynamic-slice_fusion.6), channel_id=1, source_target_pairs={{0,16},{16,0},{1,17},{17,1},{2,18},{18,2},{3,19},{19,3},{4,20},{20... | collective-permute-start | bytes 786440 | tf_op jit(solution)/shard_map/ppermute | solution.py:41
  42.1 13.0 %collective-permute-start.8 = (bf16[256,1024]{1,0:T(8,128)(2,1)}, bf16[256,1024]{1,0:T(8,128)(2,1)S(1)}, u32[]{:S(2)}, u32[]{:S(2)}) collective-permute-start(bf16[256,1024]{1,0:T(8,128)(2,1)} %collective-permute-done.4), channel_id=1, source_target_pairs={{0,2},{4,0},{8,4},{12,8},{14,12},{10,14},{6,10},{2,6},{1,3},{5,1},... | collective-permute-start | bytes 1572872 | tf_op jit(solution)/shard_map/ppermute | solution.py:50
  47.5 12.4 %collective-permute-start.6 = (bf16[256,1024]{1,0:T(8,128)(2,1)}, bf16[256,1024]{1,0:T(8,128)(2,1)S(1)}, u32[]{:S(2)}, u32[]{:S(2)}) collective-permute-start(bf16[256,1024]{1,0:T(8,128)(2,1)} %collective-permute-done.2), channel_id=1, source_target_pairs={{0,4},{4,8},{8,12},{12,14},{14,10},{10,6},{6,2},{2,0},{1,5},{5,9},... | collective-permute-start | bytes 1572872 | tf_op jit(solution)/shard_map/ppermute | solution.py:47
  55.1 10.0 %collective-permute-start.9 = (bf16[256,512]{1,0:T(8,128)(2,1)S(1)}, bf16[256,512]{1,0:T(8,128)(2,1)S(1)}, u32[]{:S(2)}, u32[]{:S(2)}) collective-permute-start(bf16[256,512]{1,0:T(8,128)(2,1)S(1)} %constant_dynamic-slice_fusion.3), channel_id=1, source_target_pairs={{0,16},{16,0},{1,17},{17,1},{2,18},{18,2},{3,19},{19,3},{4,20},{20... | collective-permute-start | bytes 786440 | tf_op jit(solution)/shard_map/ppermute | solution.py:41
  59.9 7.3 %collective-permute-start.7 = (bf16[256,512]{1,0:T(8,128)(2,1)S(1)}, bf16[256,512]{1,0:T(8,128)(2,1)S(1)}, u32[]{:S(2)}, u32[]{:S(2)}) collective-permute-start(bf16[256,512]{1,0:T(8,128)(2,1)S(1)} %constant_dynamic-slice_fusion.4), channel_id=1, source_target_pairs={{0,16},{16,0},{1,17},{17,1},{2,18},{18,2},{3,19},{19,3},{4,20},{20... | collective-permute-start | bytes 786440 | tf_op jit(solution)/shard_map/ppermute | solution.py:41
  60.5 11.0 %collective-permute-start.12 = (bf16[256,1024]{1,0:T(8,128)(2,1)S(1)}, bf16[256,1024]{1,0:T(8,128)(2,1)S(1)}, u32[]{:S(2)}, u32[]{:S(2)}) collective-permute-start(bf16[256,1024]{1,0:T(8,128)(2,1)S(1)} %collective-permute-done.8), channel_id=1, source_target_pairs={{0,2},{4,0},{8,4},{12,8},{14,12},{10,14},{6,10},{2,6},{1,3},{5,1},... | collective-permute-start | bytes 1572872 | tf_op jit(solution)/shard_map/ppermute | solution.py:50
  62.0 11.0 %collective-permute-start.10 = (bf16[256,1024]{1,0:T(8,128)(2,1)S(1)}, bf16[256,1024]{1,0:T(8,128)(2,1)S(1)}, u32[]{:S(2)}, u32[]{:S(2)}) collective-permute-start(bf16[256,1024]{1,0:T(8,128)(2,1)S(1)} %collective-permute-done.6), channel_id=1, source_target_pairs={{0,4},{4,8},{8,12},{12,14},{14,10},{10,6},{6,2},{2,0},{1,5},{5,9},... | collective-permute-start | bytes 1572872 | tf_op jit(solution)/shard_map/ppermute | solution.py:47
  71.5 11.7 %collective-permute-start.13 = (bf16[256,512]{1,0:T(8,128)(2,1)S(1)}, bf16[256,512]{1,0:T(8,128)(2,1)S(1)}, u32[]{:S(2)}, u32[]{:S(2)}) collective-permute-start(bf16[256,512]{1,0:T(8,128)(2,1)S(1)} %constant_dynamic-slice_fusion.1), channel_id=1, source_target_pairs={{0,16},{16,0},{1,17},{17,1},{2,18},{18,2},{3,19},{19,3},{4,20},{20... | collective-permute-start | bytes 786440 | tf_op jit(solution)/shard_map/ppermute | solution.py:41
  73.1 8.6 %collective-permute-start.11 = (bf16[256,512]{1,0:T(8,128)(2,1)S(1)}, bf16[256,512]{1,0:T(8,128)(2,1)S(1)}, u32[]{:S(2)}, u32[]{:S(2)}) collective-permute-start(bf16[256,512]{1,0:T(8,128)(2,1)S(1)} %constant_dynamic-slice_fusion.2), channel_id=1, source_target_pairs={{0,16},{16,0},{1,17},{17,1},{2,18},{18,2},{3,19},{19,3},{4,20},{20... | collective-permute-start | bytes 786440 | tf_op jit(solution)/shard_map/ppermute | solution.py:41
  75.0 9.5 %collective-permute-start.14 = (bf16[256,1024]{1,0:T(8,128)(2,1)S(1)}, bf16[256,1024]{1,0:T(8,128)(2,1)S(1)}, u32[]{:S(2)}, u32[]{:S(2)}) collective-permute-start(bf16[256,1024]{1,0:T(8,128)(2,1)S(1)} %collective-permute-done.10), channel_id=1, source_target_pairs={{0,4},{4,8},{8,12},{12,14},{14,10},{10,6},{6,2},{2,0},{1,5},{5,9},... | collective-permute-start | bytes 1572872 | tf_op jit(solution)/shard_map/ppermute | solution.py:47
  85.4 8.6 %collective-permute-start.15 = (bf16[256,512]{1,0:T(8,128)(2,1)}, bf16[256,512]{1,0:T(8,128)(2,1)}, u32[]{:S(2)}, u32[]{:S(2)}) collective-permute-start(bf16[256,512]{1,0:T(8,128)(2,1)} %constant_dynamic-slice_fusion), channel_id=1, source_target_pairs={{0,16},{16,0},{1,17},{17,1},{2,18},{18,2},{3,19},{19,3},{4,20},{20... | collective-permute-start | bytes 786440 | tf_op jit(solution)/shard_map/ppermute | solution.py:41
  91.3 4.1 %copy-start.6 = (f32[512,512]{1,0:T(8,128)S(1)}, f32[512,512]{1,0:T(8,128)}, u32[]{:S(2)}) copy-start(f32[512,512]{1,0:T(8,128)} %fusion.63) | copy-start | bytes 3145732
  100.5 5.6 %copy-start.1 = (bf16[2048,512]{1,0:T(8,128)(2,1)S(1)}, bf16[2048,512]{1,0:T(8,128)(2,1)}, u32[]{:S(2)}) copy-start(bf16[2048,512]{1,0:T(8,128)(2,1)} %copy-done) | copy-start | bytes 6291460
  100.5 5.6 %copy-start.12 = (bf16[256,512]{1,0:T(8,128)(2,1)S(1)}, bf16[256,512]{1,0:T(8,128)(2,1)}, u32[]{:S(2)}) copy-start(bf16[256,512]{1,0:T(8,128)(2,1)} %copy-done.11) | copy-start | bytes 786436
  102.7 7.4 %collective-permute-start.17 = (f32[4,128,128]{2,1,0:T(8,128)S(1)}, f32[4,128,128]{2,1,0:T(8,128)S(1)}, u32[]{:S(2)}, u32[]{:S(2)}) collective-permute-start(f32[4,128,128]{2,1,0:T(8,128)S(1)} %fusion.37), channel_id=1, source_target_pairs={{0,2},{2,4},{4,6},{6,8},{8,10},{10,12},{12,14},{1,3},{3,5},{5,7},{... | collective-permute-start | bytes 786440 | tf_op jit(solution)/shard_map/ppermute | solution.py:64
  110.1 10.4 %collective-permute-start.18 = (f32[4,128,128]{2,1,0:T(8,128)S(1)}, f32[4,128,128]{2,1,0:T(8,128)S(1)}, u32[]{:S(2)}, u32[]{:S(2)}) collective-permute-start(f32[4,128,128]{2,1,0:T(8,128)S(1)} %fusion.134), channel_id=1, source_target_pairs={{0,4},{2,6},{4,8},{6,10},{8,12},{10,14},{1,5},{3,7},{5,9},{7,11},{... | collective-permute-start | bytes 786440 | tf_op jit(solution)/shard_map/ppermute | solution.py:64
  120.5 12.9 %collective-permute-start.19 = (f32[4,128,128]{2,1,0:T(8,128)S(1)}, f32[4,128,128]{2,1,0:T(8,128)S(1)}, u32[]{:S(2)}, u32[]{:S(2)}) collective-permute-start(f32[4,128,128]{2,1,0:T(8,128)S(1)} %add.336), channel_id=1, source_target_pairs={{0,8},{2,10},{4,12},{6,14},{1,9},{3,11},{5,13},{7,15},{16,24},{18,... | collective-permute-start | bytes 786440 | tf_op jit(solution)/shard_map/ppermute | solution.py:64
  137.1 8.3 %collective-permute-start.22 = (f32[4,128,128]{2,1,0:T(8,128)S(1)}, f32[4,128,128]{2,1,0:T(8,128)S(1)}, u32[]{:S(2)}, u32[]{:S(2)}) collective-permute-start(f32[4,128,128]{2,1,0:T(8,128)S(1)} %fusion.38), channel_id=1, source_target_pairs={{2,0},{4,2},{6,4},{8,6},{10,8},{12,10},{14,12},{3,1},{5,3},{7,5},{... | collective-permute-start | bytes 786440 | tf_op jit(solution)/shard_map/ppermute | solution.py:64
  145.4 10.9 %collective-permute-start.23 = (f32[4,128,128]{2,1,0:T(8,128)S(1)}, f32[4,128,128]{2,1,0:T(8,128)S(1)}, u32[]{:S(2)}, u32[]{:S(2)}) collective-permute-start(f32[4,128,128]{2,1,0:T(8,128)S(1)} %fusion.133), channel_id=1, source_target_pairs={{4,0},{6,2},{8,4},{10,6},{12,8},{14,10},{5,1},{7,3},{9,5},{11,7},{... | collective-permute-start | bytes 786440 | tf_op jit(solution)/shard_map/ppermute | solution.py:64
  156.3 12.0 %collective-permute-start.24 = (f32[4,128,128]{2,1,0:T(8,128)S(1)}, f32[4,128,128]{2,1,0:T(8,128)S(1)}, u32[]{:S(2)}, u32[]{:S(2)}) collective-permute-start(f32[4,128,128]{2,1,0:T(8,128)S(1)} %add.349), channel_id=1, source_target_pairs={{8,0},{10,2},{12,4},{14,6},{9,1},{11,3},{13,5},{15,7},{24,16},{26,... | collective-permute-start | bytes 786440 | tf_op jit(solution)/shard_map/ppermute | solution.py:64
  175.0 7.7 %collective-permute-start.25 = (f32[256,2048]{1,0:T(8,128)}, f32[256,2048]{1,0:T(8,128)}, u32[]{:S(2)}, u32[]{:S(2)}) collective-permute-start(f32[256,2048]{1,0:T(8,128)} %convolution_add_fusion), channel_id=1, source_target_pairs={{0,1},{1,0},{2,3},{3,2},{4,5},{5,4},{6,7},{7,6},{8,9},{9,8},{10,11... | collective-permute-start | bytes 6291464 | tf_op jit(solution)/shard_map/ppermute | solution.py:17
  175.9 4.0 %collective-permute-start.20 = (bf16[256,512]{1,0:T(8,128)(2,1)}, bf16[256,512]{1,0:T(8,128)(2,1)}, u32[]{:S(2)}, u32[]{:S(2)}) collective-permute-start(bf16[256,512]{1,0:T(8,128)(2,1)} %copy.18), channel_id=1, source_target_pairs={{0,1},{1,0},{2,3},{3,2},{4,5},{5,4},{6,7},{7,6},{8,9},{9,8},{10,11... | collective-permute-start | bytes 786440 | tf_op jit(solution)/shard_map/ppermute | solution.py:17
  (11 other events, 30.6 us)

commit v9 on v5

--- a/solution.py
+++ b/solution.py
@@ -180,7 +180,8 @@
         return g + lax.dot_general(d_x, w_x, (((1,), (1,)), ((), ())), preferred_element_type=f32)
 
     received = swap(grad_rows(1))
-    grad_input = (grad_rows(0) + received).astype(bf16)
+    own, received = lax.optimization_barrier((grad_rows(0), received))
+    grad_input = (own + received).astype(bf16)
     return (output, grad_input)
 
 

time: 175 us -> 176 us (level)
  other arithmetic: 12.7 us -> 15.5 us
  matrix products: 24.2 us -> 22.4 us
    convert_element_type x0 -> x1, other arithmetic: none -> 2.83 us  [on_device(): grad_input = (own + received).astype(bf16)]
    dot_general x2, matrix products: 10.2 us -> 8.39 us  [grad_rows(): lax.dot_general(d_ring, w_ring, (((1,), (1,)), ((), ())), preferred_eleme...]
  transfers between devices with their start and end apart: 26 -> 26, of which waited for: 14 -> 14; matrix products, arithmetic and copies ran while one was open for 27% -> 29% of each run, Pallas kernels for 0% -> 0%
where the time goes in v9:
time: 176 us; the launch traced here: 173 us
  starting transfers between devices  52.8 us (30%)
  waiting for transfers between devices  41.2 us (23%)
  local copies, waits for them, and re-layouts  30.9 us (18%)
  matrix products  22.4 us (13%)
  other arithmetic  15.5 us (9%)
  between operations  10.2 us (6%)
    ppermute x6, starting transfers between devices, swap(): return lax.ppermute(x, 'core', [(0, 1), (1, 0)])  26.2 us
    ppermute x6, waiting for transfers between devices, exclusive_scan(): got = lax.ppermute(incl, 'chip', perm)  25.2 us
    ppermute x6, starting transfers between devices, exclusive_scan(): got = lax.ppermute(incl, 'chip', perm)  16.8 us
    ppermute x7, waiting for transfers between devices, land(): return (piece, lax.ppermute(sent, 'groups', partner))  9.99 us
    dynamic_update_slice x8, local copies, waits for them, and re-layouts, on_device(): w_ring = lax.dynamic_update_slice_in_dim(w_ring, ringed, src * span, axis=0)  9 us
    dot_general x2, matrix products, grad_rows(): lax.dot_general(d_ring, w_ring, (((1,), (1,)), ((), ())), preferred_eleme...  8.39 us
    ppermute x7, starting transfers between devices, land(): return (piece, lax.ppermute(sent, 'groups', partner))  5.21 us
    dot_general x1, matrix products, on_device(): p_ring = jnp.dot(x_pair, w_ring, preferred_element_type=f32).astype(bf16)  5.16 us
  transfers between devices with their start and end apart: 26, of which 14 were waited for; matrix products, arithmetic and copies ran while one was open for 29% of the time, Pallas kernels for 0%

profile of v9, /device:TPU:15, one launch (start us, length us, event | category | flops | bytes accessed | tf_op | source)
XLA Modules:
  0.0 173.0 jit_solution(4770533352452543432)
XLA Ops:
  5.0 2.5 %broadcast_in_dim.27 = bf16[2048,1024]{1,0:T(8,128)(2,1)} broadcast(bf16[]{:T(256)} %constant.96.clone.1), dimensions={} | broadcast | bytes 4194306 | tf_op jit(solution)/shard_map/broadcast_in_dim | solution.py:111
  8.8 1.4 add_convert_fusion.1
  28.6 1.9 %constant_dynamic-update-slice_fusion.13 = bf16[2048,1024]{1,0:T(8,128)(2,1)} fusion(bf16[2048,1024]{1,0:T(8,128)(2,1)} %get-tuple-element.6, bf16[256,1024]{1,0:T(8,128)(2,1)} %collective-permute-done.2, s32[]{:T(128)S(6)} %select_n.212), kind=kLoop, calls=%fused_computation.102 | loop fusion | bytes 1048580 | tf_op jit(solution)/shard_map/dynamic_update_slice | solution.py:114
  30.5 1.9 %constant_dynamic-update-slice_fusion.12 = bf16[2048,1024]{1,0:T(8,128)(2,1)} fusion(bf16[2048,1024]{1,0:T(8,128)(2,1)} %constant_dynamic-update-slice_fusion.13, bf16[256,1024]{1,0:T(8,128)(2,1)} %collective-permute-done.3, s32[]{:T(128)S(6)} %select_n.215), kind=kLoop, calls=%fused_computation.101 | loop fusion | bytes 1048580 | tf_op jit(solution)/shard_map/dynamic_update_slice | solution.py:114
  32.4 5.5 %collective-permute-done.10 = bf16[256,512]{1,0:T(8,128)(2,1)S(1)} collective-permute-done((bf16[256,512]{1,0:T(8,128)(2,1)S(1)}, bf16[256,512]{1,0:T(8,128)(2,1)S(1)}, u32[]{:S(2)}, u32[]{:S(2)}) %collective-permute-start.10) | collective-permute-done | bytes 262176 | tf_op jit(solution)/shard_map/ppermute | solution.py:41
  43.1 1.4 collective-permute-done.11
  44.5 4.3 %collective-permute-start.16 = (s32[2,2]{1,0:T(2,128)S(1)}, s32[2,2]{1,0:T(2,128)S(1)}, u32[]{:S(2)}, u32[]{:S(2)}) collective-permute-start(s32[2,2]{1,0:T(2,128)S(1)} %bitcast.133), channel_id=1, source_target_pairs={{0,1},{1,0},{2,3},{3,2},{4,5},{5,4},{6,7},{7,6},{8,9},{9,8},{10,11... | collective-permute-start | bytes 56 | tf_op jit(solution)/shard_map/ppermute | solution.py:17
  48.8 1.3 collective-permute-done.12
  54.5 1.8 %collective-permute-done.13 = bf16[256,512]{1,0:T(8,128)(2,1)S(1)} collective-permute-done((bf16[256,512]{1,0:T(8,128)(2,1)S(1)}, bf16[256,512]{1,0:T(8,128)(2,1)S(1)}, u32[]{:S(2)}, u32[]{:S(2)}) %collective-permute-start.13) | collective-permute-done | bytes 262176 | tf_op jit(solution)/shard_map/ppermute | solution.py:41
  56.4 6.3 %collective-permute-start.21 = (bf16[256,512]{0,1:T(8,128)(2,1)}, bf16[256,512]{0,1:T(8,128)(2,1)}, u32[]{:S(2)}, u32[]{:S(2)}) collective-permute-start(bf16[256,512]{0,1:T(8,128)(2,1)} %get-tuple-element.20), channel_id=1, source_target_pairs={{0,1},{1,0},{2,3},{3,2},{4,5},{5,4},{6,7},{7,6},{8,9},{9,8},{10,11... | collective-permute-start | bytes 786440 | tf_op jit(solution)/shard_map/ppermute | solution.py:17
  64.0 5.2 %convolution_convert_fusion = bf16[512,1024]{1,0:T(8,128)(2,1)S(1)} fusion(bf16[2048,1024]{1,0:T(8,128)(2,1)} %constant_dynamic-update-slice_fusion.7, bf16[256,2048]{1,0:T(8,128)(2,1)} %collective-permute-done, bf16[256,2048]{1,0:T(8,128)(2,1)} %add_convert_fusion.1), kind=kOutput, calls=%fused_computation.9 | convolution fusion | flops 2152202240 | bytes 7340032 | tf_op jit(solution)/shard_map/dot_general | solution.py:116
  69.3 2.8 %fusion.2 = bf16[512,512]{1,0:T(8,128)(2,1)S(1)} fusion(bf16[2048,512]{1,0:T(8,128)(2,1)S(1)} %constant_dynamic-update-slice_fusion, bf16[256,2048]{1,0:T(8,128)(2,1)} %collective-permute-done, bf16[256,2048]{1,0:T(8,128)(2,1)} %add_convert_fusion.1), kind=kOutput, calls=%fused_computation.18 | convolution fusion | flops 1078198272 | bytes 4718592 | tf_op jit(solution)/shard_map/dot_general | solution.py:117
  72.1 1.6 maximum_select_fusion
  73.7 3.9 %select_n.234 = bf16[2,256,3,4,128]{4,3,2,1,0:T(4,128)(2,1)} reshape(bf16[512,1536]{1,0:T(8,128)(2,1)} %maximum_select_fusion) | data formatting | bytes 3145728 | tf_op jit(solution)/shard_map/jit(_where)/select_n | solution.py:118
  77.6 2.9 %fusion.49 = (bf16[2,256,1,4,128]{4,3,2,1,0:T(4,128)(2,1)}, bf16[2,256,1,4,128]{4,3,2,1,0:T(4,128)(2,1)S(1)}, bf16[2,256,1,4,128]{4,3,2,1,0:T(4,128)(2,1)}) fusion(bf16[2,256,3,4,128]{4,3,2,1,0:T(4,128)(2,1)} %select_n.234), kind=kLoop, calls=%fused_computation.123 | loop fusion | bytes 3145728 | tf_op jit(solution)/shard_map/slice | solution.py:126
  83.6 3.1 %collective-permute-start.17 = (f32[4,128,128]{2,1,0:T(8,128)}, f32[4,128,128]{2,1,0:T(8,128)}, u32[]{:S(2)}, u32[]{:S(2)}) collective-permute-start(f32[4,128,128]{2,1,0:T(8,128)} %fusion.31), channel_id=1, source_target_pairs={{0,2},{2,4},{4,6},{6,8},{8,10},{10,12},{12,14},{1,3},{3,5},{5,7},{... | collective-permute-start | bytes 786440 | tf_op jit(solution)/shard_map/ppermute | solution.py:64
  87.8 2.3 %reshape.113 = f32[2,256,256]{2,1,0:T(8,128)} reshape(f32[2,2,128,2,128]{4,3,2,1,0:T(2,128)} %broadcast_in_dim.31) | data formatting | bytes 1048576 | tf_op jit(solution)/shard_map/vmap()/reshape | solution.py:75
  92.4 3.2 %collective-permute-start.18 = (f32[4,128,128]{2,1,0:T(8,128)S(1)}, f32[4,128,128]{2,1,0:T(8,128)S(1)}, u32[]{:S(2)}, u32[]{:S(2)}) collective-permute-start(f32[4,128,128]{2,1,0:T(8,128)S(1)} %fusion.68), channel_id=1, source_target_pairs={{0,4},{2,6},{4,8},{6,10},{8,12},{10,14},{1,5},{3,7},{5,9},{7,11},{... | collective-permute-start | bytes 786440 | tf_op jit(solution)/shard_map/ppermute | solution.py:64
  96.0 3.4 %collective-permute-done.18 = f32[4,128,128]{2,1,0:T(8,128)S(1)} collective-permute-done((f32[4,128,128]{2,1,0:T(8,128)S(1)}, f32[4,128,128]{2,1,0:T(8,128)S(1)}, u32[]{:S(2)}, u32[]{:S(2)}) %collective-permute-start.18) | collective-permute-done | bytes 262176 | tf_op jit(solution)/shard_map/ppermute | solution.py:64
  99.5 4.2 %collective-permute-start.19 = (f32[4,128,128]{2,1,0:T(8,128)S(1)}, f32[4,128,128]{2,1,0:T(8,128)S(1)}, u32[]{:S(2)}, u32[]{:S(2)}) collective-permute-start(f32[4,128,128]{2,1,0:T(8,128)S(1)} %add.272), channel_id=1, source_target_pairs={{0,8},{2,10},{4,12},{6,14},{1,9},{3,11},{5,13},{7,15},{16,24},{18,... | collective-permute-start | bytes 786440 | tf_op jit(solution)/shard_map/ppermute | solution.py:64
  104.2 5.8 %collective-permute-done.19 = f32[4,128,128]{2,1,0:T(8,128)S(1)} collective-permute-done((f32[4,128,128]{2,1,0:T(8,128)S(1)}, f32[4,128,128]{2,1,0:T(8,128)S(1)}, u32[]{:S(2)}, u32[]{:S(2)}) %collective-permute-start.19) | collective-permute-done | bytes 262176 | tf_op jit(solution)/shard_map/ppermute | solution.py:64
  114.7 3.1 %collective-permute-start.22 = (f32[4,128,128]{2,1,0:T(8,128)S(1)}, f32[4,128,128]{2,1,0:T(8,128)S(1)}, u32[]{:S(2)}, u32[]{:S(2)}) collective-permute-start(f32[4,128,128]{2,1,0:T(8,128)S(1)} %fusion.32), channel_id=1, source_target_pairs={{2,0},{4,2},{6,4},{8,6},{10,8},{12,10},{14,12},{3,1},{5,3},{7,5},{... | collective-permute-start | bytes 786440 | tf_op jit(solution)/shard_map/ppermute | solution.py:64
  118.6 4.1 %collective-permute-done.22 = f32[4,128,128]{2,1,0:T(8,128)S(1)} collective-permute-done((f32[4,128,128]{2,1,0:T(8,128)S(1)}, f32[4,128,128]{2,1,0:T(8,128)S(1)}, u32[]{:S(2)}, u32[]{:S(2)}) %collective-permute-start.22) | collective-permute-done | bytes 262176 | tf_op jit(solution)/shard_map/ppermute | solution.py:64
  122.8 1.9 %collective-permute-start.23 = (f32[4,128,128]{2,1,0:T(8,128)S(1)}, f32[4,128,128]{2,1,0:T(8,128)S(1)}, u32[]{:S(2)}, u32[]{:S(2)}) collective-permute-start(f32[4,128,128]{2,1,0:T(8,128)S(1)} %fusion.67), channel_id=1, source_target_pairs={{4,0},{6,2},{8,4},{10,6},{12,8},{14,10},{5,1},{7,3},{9,5},{11,7},{... | collective-permute-start | bytes 786440 | tf_op jit(solution)/shard_map/ppermute | solution.py:64
  125.1 5.3 %collective-permute-done.23 = f32[4,128,128]{2,1,0:T(8,128)S(1)} collective-permute-done((f32[4,128,128]{2,1,0:T(8,128)S(1)}, f32[4,128,128]{2,1,0:T(8,128)S(1)}, u32[]{:S(2)}, u32[]{:S(2)}) %collective-permute-start.23) | collective-permute-done | bytes 262176 | tf_op jit(solution)/shard_map/ppermute | solution.py:64
  132.0 6.5 %collective-permute-done.24 = f32[4,128,128]{2,1,0:T(8,128)S(1)} collective-permute-done((f32[4,128,128]{2,1,0:T(8,128)S(1)}, f32[4,128,128]{2,1,0:T(8,128)S(1)}, u32[]{:S(2)}, u32[]{:S(2)}) %collective-permute-start.24) | collective-permute-done | bytes 262176 | tf_op jit(solution)/shard_map/ppermute | solution.py:64
  140.3 4.9 %convolution_add_fusion = f32[256,2048]{1,0:T(8,128)} fusion(f32[256,2048]{1,0:T(8,128)S(1)} %fusion.27, bf16[2048,1024]{1,0:T(8,128)(2,1)} %constant_dynamic-update-slice_fusion.7, bf16[256,1536]{0,1:T(8,128)(2,1)S(1)} %bitcast.127, s32[]{:T(128)S(6)} %select_n.207), kind=kOutput, calls=%fused_computation | convolution fusion | flops 1074266112 | bytes 8912900 | tf_op jit(solution)/shard_map/dot_general | solution.py:179
  145.2 14.2 %collective-permute-start.25 = (f32[256,2048]{1,0:T(8,128)}, f32[256,2048]{1,0:T(8,128)}, u32[]{:S(2)}, u32[]{:S(2)}) collective-permute-start(f32[256,2048]{1,0:T(8,128)} %convolution_add_fusion), channel_id=1, source_target_pairs={{0,1},{1,0},{2,3},{3,2},{4,5},{5,4},{6,7},{7,6},{8,9},{9,8},{10,11... | collective-permute-start | bytes 6291464 | tf_op jit(solution)/shard_map/ppermute | solution.py:17
  160.4 3.5 %collective-permute-done.20 = bf16[256,512]{1,0:T(8,128)(2,1)} collective-permute-done((bf16[256,512]{1,0:T(8,128)(2,1)}, bf16[256,512]{1,0:T(8,128)(2,1)}, u32[]{:S(2)}, u32[]{:S(2)}) %collective-permute-start.20) | collective-permute-done | bytes 262176 | tf_op jit(solution)/shard_map/ppermute | solution.py:17
  163.9 2.0 %maximum_select_fusion.1 = bf16[256,1024]{1,0:T(8,128)(2,1)} fusion(bf16[256,512]{1,0:T(8,128)(2,1)} %collective-permute-done.20, bf16[256,512]{1,0:T(8,128)(2,1)S(1)} %copy.19, pred[]{:T(512)S(6)} %eq.15), kind=kLoop, calls=%fused_computation.29 | loop fusion | flops 2359296 | bytes 1048577 | tf_op jit(solution)/shard_map/jit(_where)/select_n | solution.py:146
  166.6 3.5 %convolution_add_fusion.1 = f32[256,2048]{1,0:T(8,128)S(1)} fusion(f32[256,2048]{1,0:T(8,128)S(1)} %fusion.29, bf16[2048,1024]{1,0:T(8,128)(2,1)} %constant_dynamic-update-slice_fusion.7, bf16[256,1536]{0,1:T(8,128)(2,1)S(1)} %bitcast.125, s32[]{:T(128)S(6)} %select_n.207), kind=kOutput, calls=%fused_computation.1 | convolution fusion | flops 1074266112 | bytes 8912900 | tf_op jit(solution)/shard_map/dot_general | solution.py:179
  170.2 2.8 %add_convert_fusion = bf16[256,2048]{1,0:T(8,128)(2,1)} fusion(f32[256,2048]{1,0:T(8,128)S(1)} %convolution_add_fusion.1, f32[256,2048]{1,0:T(8,128)} %collective-permute-done.25), kind=kLoop, calls=%fused_computation.3 | loop fusion | flops 1048576 | bytes 5242880 | tf_op jit(solution)/shard_map/convert_element_type | solution.py:184
  (120 shorter events, 44.4 us)
Async XLA Ops:
  2.8 2.1 %collective-permute-start.1 = (bf16[128,1536]{1,0:T(8,128)(2,1)S(1)}, bf16[128,1536]{1,0:T(8,128)(2,1)S(1)}, u32[]{:S(2)}, u32[]{:S(2)}) collective-permute-start(bf16[128,1536]{1,0:T(8,128)(2,1)S(1)} %pad_maximum_fusion.7), channel_id=1, source_target_pairs={{0,1},{1,0},{2,3},{3,2},{4,5},{5,4},{6,7},{7,6},{8,9},{9,8},{10,11... | collective-permute-start | bytes 1179656 | tf_op jit(solution)/shard_map/ppermute | solution.py:17
  7.5 4.6 %copy-start.8 = (s32[8]{0:T(128)S(1)}, s32[8]{0:T(128)}, u32[]{:S(2)}) copy-start(s32[8]{0:T(128)} %constant.118.clone) | copy-start | bytes 100
  8.6 8.7 %copy-start.6 = (s32[8]{0:T(128)S(1)}, s32[8]{0:T(128)}, u32[]{:S(2)}) copy-start(s32[8]{0:T(128)} %constant.117.clone) | copy-start | bytes 100
  8.6 13.9 %copy-start.5 = (bf16[256,1024]{1,0:T(8,128)(2,1)S(1)}, bf16[256,1024]{1,0:T(8,128)(2,1)}, u32[]{:S(2)}) copy-start(bf16[256,1024]{1,0:T(8,128)(2,1)} %param.11) | copy-start | bytes 1572868
  8.6 15.0 %collective-permute-start.2 = (bf16[256,1024]{1,0:T(8,128)(2,1)}, bf16[256,1024]{1,0:T(8,128)(2,1)}, u32[]{:S(2)}, u32[]{:S(2)}) collective-permute-start(bf16[256,1024]{1,0:T(8,128)(2,1)} %get-tuple-element.7), channel_id=1, source_target_pairs={{0,4},{4,8},{8,12},{12,14},{14,10},{10,6},{6,2},{2,0},{1,5},{5,9},... | collective-permute-start | bytes 1572872 | tf_op jit(solution)/shard_map/ppermute | solution.py:47
  10.1 53.9 %collective-permute-start = (bf16[256,2048]{1,0:T(8,128)(2,1)}, bf16[256,2048]{1,0:T(8,128)(2,1)}, u32[]{:S(2)}, u32[]{:S(2)}) collective-permute-start(bf16[256,2048]{1,0:T(8,128)(2,1)} %add_convert_fusion.1), channel_id=1, source_target_pairs={{0,1},{1,0},{2,3},{3,2},{4,5},{5,4},{6,7},{7,6},{8,9},{9,8},{10,11... | collective-permute-start | bytes 3145736 | tf_op jit(solution)/shard_map/ppermute | solution.py:17
  10.8 14.3 %collective-permute-start.3 = (bf16[256,1024]{1,0:T(8,128)(2,1)}, bf16[256,1024]{1,0:T(8,128)(2,1)}, u32[]{:S(2)}, u32[]{:S(2)}) collective-permute-start(bf16[256,1024]{1,0:T(8,128)(2,1)} %get-tuple-element.7), channel_id=1, source_target_pairs={{0,2},{4,0},{8,4},{12,8},{14,12},{10,14},{6,10},{2,6},{1,3},{5,1},... | collective-permute-start | bytes 1572872 | tf_op jit(solution)/shard_map/ppermute | solution.py:50
  24.6 7.8 %collective-permute-start.9 = (bf16[256,512]{1,0:T(8,128)(2,1)S(1)}, bf16[256,512]{1,0:T(8,128)(2,1)S(1)}, u32[]{:S(2)}, u32[]{:S(2)}) collective-permute-start(bf16[256,512]{1,0:T(8,128)(2,1)S(1)} %constant_dynamic-slice_fusion.6), channel_id=1, source_target_pairs={{0,16},{16,0},{1,17},{17,1},{2,18},{18,2},{3,19},{19,3},{4,20},{20... | collective-permute-start | bytes 786440 | tf_op jit(solution)/shard_map/ppermute | solution.py:41
  24.9 13.1 %collective-permute-start.4 = (bf16[256,1024]{1,0:T(8,128)(2,1)}, bf16[256,1024]{1,0:T(8,128)(2,1)S(1)}, u32[]{:S(2)}, u32[]{:S(2)}) collective-permute-start(bf16[256,1024]{1,0:T(8,128)(2,1)} %collective-permute-done.2), channel_id=1, source_target_pairs={{0,4},{4,8},{8,12},{12,14},{14,10},{10,6},{6,2},{2,0},{1,5},{5,9},... | collective-permute-start | bytes 1572872 | tf_op jit(solution)/shard_map/ppermute | solution.py:47
  26.1 11.8 %collective-permute-start.10 = (bf16[256,512]{1,0:T(8,128)(2,1)S(1)}, bf16[256,512]{1,0:T(8,128)(2,1)S(1)}, u32[]{:S(2)}, u32[]{:S(2)}) collective-permute-start(bf16[256,512]{1,0:T(8,128)(2,1)S(1)} %constant_dynamic-slice_fusion.5), channel_id=1, source_target_pairs={{0,16},{16,0},{1,17},{17,1},{2,18},{18,2},{3,19},{19,3},{4,20},{20... | collective-permute-start | bytes 786440 | tf_op jit(solution)/shard_map/ppermute | solution.py:41
  27.3 12.5 %collective-permute-start.5 = (bf16[256,1024]{1,0:T(8,128)(2,1)}, bf16[256,1024]{1,0:T(8,128)(2,1)S(1)}, u32[]{:S(2)}, u32[]{:S(2)}) collective-permute-start(bf16[256,1024]{1,0:T(8,128)(2,1)} %collective-permute-done.3), channel_id=1, source_target_pairs={{0,2},{4,0},{8,4},{12,8},{14,12},{10,14},{6,10},{2,6},{1,3},{5,1},... | collective-permute-start | bytes 1572872 | tf_op jit(solution)/shard_map/ppermute | solution.py:50
  32.4 12.1 %copy-start.7 = (s32[1,2,2]{2,1,0:T(2,128)S(1)}, s32[1,2,2]{2,1,0:T(2,128)}, u32[]{:S(2)}) copy-start(s32[1,2,2]{2,1,0:T(2,128)} %param.15) | copy-start | bytes 52
  38.1 6.4 %collective-permute-start.11 = (bf16[256,512]{1,0:T(8,128)(2,1)S(1)}, bf16[256,512]{1,0:T(8,128)(2,1)S(1)}, u32[]{:S(2)}, u32[]{:S(2)}) collective-permute-start(bf16[256,512]{1,0:T(8,128)(2,1)S(1)} %constant_dynamic-slice_fusion.4), channel_id=1, source_target_pairs={{0,16},{16,0},{1,17},{17,1},{2,18},{18,2},{3,19},{19,3},{4,20},{20... | collective-permute-start | bytes 786440 | tf_op jit(solution)/shard_map/ppermute | solution.py:41
  39.3 11.7 %collective-permute-start.6 = (bf16[256,1024]{1,0:T(8,128)(2,1)S(1)}, bf16[256,1024]{1,0:T(8,128)(2,1)S(1)}, u32[]{:S(2)}, u32[]{:S(2)}) collective-permute-start(bf16[256,1024]{1,0:T(8,128)(2,1)S(1)} %collective-permute-done.4), channel_id=1, source_target_pairs={{0,4},{4,8},{8,12},{12,14},{14,10},{10,6},{6,2},{2,0},{1,5},{5,9},... | collective-permute-start | bytes 1572872 | tf_op jit(solution)/shard_map/ppermute | solution.py:47
  39.9 10.3 %collective-permute-start.12 = (bf16[256,512]{1,0:T(8,128)(2,1)S(1)}, bf16[256,512]{1,0:T(8,128)(2,1)S(1)}, u32[]{:S(2)}, u32[]{:S(2)}) collective-permute-start(bf16[256,512]{1,0:T(8,128)(2,1)S(1)} %constant_dynamic-slice_fusion.3), channel_id=1, source_target_pairs={{0,16},{16,0},{1,17},{17,1},{2,18},{18,2},{3,19},{19,3},{4,20},{20... | collective-permute-start | bytes 786440 | tf_op jit(solution)/shard_map/ppermute | solution.py:41
  40.2 11.5 %collective-permute-start.7 = (bf16[256,1024]{1,0:T(8,128)(2,1)S(1)}, bf16[256,1024]{1,0:T(8,128)(2,1)S(1)}, u32[]{:S(2)}, u32[]{:S(2)}) collective-permute-start(bf16[256,1024]{1,0:T(8,128)(2,1)S(1)} %collective-permute-done.5), channel_id=1, source_target_pairs={{0,2},{4,0},{8,4},{12,8},{14,12},{10,14},{6,10},{2,6},{1,3},{5,1},... | collective-permute-start | bytes 1572872 | tf_op jit(solution)/shard_map/ppermute | solution.py:50
  44.5 42.3 %collective-permute-start.16 = (s32[2,2]{1,0:T(2,128)S(1)}, s32[2,2]{1,0:T(2,128)S(1)}, u32[]{:S(2)}, u32[]{:S(2)}) collective-permute-start(s32[2,2]{1,0:T(2,128)S(1)} %bitcast.133), channel_id=1, source_target_pairs={{0,1},{1,0},{2,3},{3,2},{4,5},{5,4},{6,7},{7,6},{8,9},{9,8},{10,11... | collective-permute-start | bytes 56 | tf_op jit(solution)/shard_map/ppermute | solution.py:17
  51.1 5.3 %collective-permute-start.13 = (bf16[256,512]{1,0:T(8,128)(2,1)S(1)}, bf16[256,512]{1,0:T(8,128)(2,1)S(1)}, u32[]{:S(2)}, u32[]{:S(2)}) collective-permute-start(bf16[256,512]{1,0:T(8,128)(2,1)S(1)} %constant_dynamic-slice_fusion.2), channel_id=1, source_target_pairs={{0,16},{16,0},{1,17},{17,1},{2,18},{18,2},{3,19},{19,3},{4,20},{20... | collective-permute-start | bytes 786440 | tf_op jit(solution)/shard_map/ppermute | solution.py:41
  51.5 11.3 %collective-permute-start.8 = (bf16[256,1024]{1,0:T(8,128)(2,1)S(1)}, bf16[256,1024]{1,0:T(8,128)(2,1)S(1)}, u32[]{:S(2)}, u32[]{:S(2)}) collective-permute-start(bf16[256,1024]{1,0:T(8,128)(2,1)S(1)} %collective-permute-done.6), channel_id=1, source_target_pairs={{0,4},{4,8},{8,12},{12,14},{14,10},{10,6},{6,2},{2,0},{1,5},{5,9},... | collective-permute-start | bytes 1572872 | tf_op jit(solution)/shard_map/ppermute | solution.py:47
  51.7 11.0 %collective-permute-start.14 = (bf16[256,512]{1,0:T(8,128)(2,1)S(1)}, bf16[256,512]{1,0:T(8,128)(2,1)S(1)}, u32[]{:S(2)}, u32[]{:S(2)}) collective-permute-start(bf16[256,512]{1,0:T(8,128)(2,1)S(1)} %constant_dynamic-slice_fusion.1), channel_id=1, source_target_pairs={{0,16},{16,0},{1,17},{17,1},{2,18},{18,2},{3,19},{19,3},{4,20},{20... | collective-permute-start | bytes 786440 | tf_op jit(solution)/shard_map/ppermute | solution.py:41
  56.4 55.1 %collective-permute-start.21 = (bf16[256,512]{0,1:T(8,128)(2,1)}, bf16[256,512]{0,1:T(8,128)(2,1)}, u32[]{:S(2)}, u32[]{:S(2)}) collective-permute-start(bf16[256,512]{0,1:T(8,128)(2,1)} %get-tuple-element.20), channel_id=1, source_target_pairs={{0,1},{1,0},{2,3},{3,2},{4,5},{5,4},{6,7},{7,6},{8,9},{9,8},{10,11... | collective-permute-start | bytes 786440 | tf_op jit(solution)/shard_map/ppermute | solution.py:17
  62.8 6.4 %collective-permute-start.15 = (bf16[256,512]{1,0:T(8,128)(2,1)S(1)}, bf16[256,512]{1,0:T(8,128)(2,1)S(1)}, u32[]{:S(2)}, u32[]{:S(2)}) collective-permute-start(bf16[256,512]{1,0:T(8,128)(2,1)S(1)} %constant_dynamic-slice_fusion), channel_id=1, source_target_pairs={{0,16},{16,0},{1,17},{17,1},{2,18},{18,2},{3,19},{19,3},{4,20},{20... | collective-permute-start | bytes 786440 | tf_op jit(solution)/shard_map/ppermute | solution.py:41
  83.6 7.6 %collective-permute-start.17 = (f32[4,128,128]{2,1,0:T(8,128)}, f32[4,128,128]{2,1,0:T(8,128)}, u32[]{:S(2)}, u32[]{:S(2)}) collective-permute-start(f32[4,128,128]{2,1,0:T(8,128)} %fusion.31), channel_id=1, source_target_pairs={{0,2},{2,4},{4,6},{6,8},{8,10},{10,12},{12,14},{1,3},{3,5},{5,7},{... | collective-permute-start | bytes 786440 | tf_op jit(solution)/shard_map/ppermute | solution.py:64
  90.0 5.5 %copy-start = (bf16[2,256,1,4,128]{4,3,2,1,0:T(4,128)(2,1)S(1)}, bf16[2,256,1,4,128]{4,3,2,1,0:T(4,128)(2,1)}, u32[]{:S(2)}) copy-start(bf16[2,256,1,4,128]{4,3,2,1,0:T(4,128)(2,1)} %get-tuple-element.12) | copy-start | bytes 1572868
  92.4 7.1 %collective-permute-start.18 = (f32[4,128,128]{2,1,0:T(8,128)S(1)}, f32[4,128,128]{2,1,0:T(8,128)S(1)}, u32[]{:S(2)}, u32[]{:S(2)}) collective-permute-start(f32[4,128,128]{2,1,0:T(8,128)S(1)} %fusion.68), channel_id=1, source_target_pairs={{0,4},{2,6},{4,8},{6,10},{8,12},{10,14},{1,5},{3,7},{5,9},{7,11},{... | collective-permute-start | bytes 786440 | tf_op jit(solution)/shard_map/ppermute | solution.py:64
  96.0 14.0 %copy-start.2 = (f32[2,4,128,128]{3,2,1,0:T(8,128)S(1)}, f32[2,4,128,128]{3,2,1,0:T(8,128)}, u32[]{:S(2)}) copy-start(f32[2,4,128,128]{3,2,1,0:T(8,128)} %copy-done.1) | copy-start | bytes 1572868
  99.5 10.5 %collective-permute-start.19 = (f32[4,128,128]{2,1,0:T(8,128)S(1)}, f32[4,128,128]{2,1,0:T(8,128)S(1)}, u32[]{:S(2)}, u32[]{:S(2)}) collective-permute-start(f32[4,128,128]{2,1,0:T(8,128)S(1)} %add.272), channel_id=1, source_target_pairs={{0,8},{2,10},{4,12},{6,14},{1,9},{3,11},{5,13},{7,15},{16,24},{18,... | collective-permute-start | bytes 786440 | tf_op jit(solution)/shard_map/ppermute | solution.py:64
  114.7 8.0 %collective-permute-start.22 = (f32[4,128,128]{2,1,0:T(8,128)S(1)}, f32[4,128,128]{2,1,0:T(8,128)S(1)}, u32[]{:S(2)}, u32[]{:S(2)}) collective-permute-start(f32[4,128,128]{2,1,0:T(8,128)S(1)} %fusion.32), channel_id=1, source_target_pairs={{2,0},{4,2},{6,4},{8,6},{10,8},{12,10},{14,12},{3,1},{5,3},{7,5},{... | collective-permute-start | bytes 786440 | tf_op jit(solution)/shard_map/ppermute | solution.py:64
  122.8 7.6 %collective-permute-start.23 = (f32[4,128,128]{2,1,0:T(8,128)S(1)}, f32[4,128,128]{2,1,0:T(8,128)S(1)}, u32[]{:S(2)}, u32[]{:S(2)}) collective-permute-start(f32[4,128,128]{2,1,0:T(8,128)S(1)} %fusion.67), channel_id=1, source_target_pairs={{4,0},{6,2},{8,4},{10,6},{12,8},{14,10},{5,1},{7,3},{9,5},{11,7},{... | collective-permute-start | bytes 786440 | tf_op jit(solution)/shard_map/ppermute | solution.py:64
  130.4 8.1 %collective-permute-start.24 = (f32[4,128,128]{2,1,0:T(8,128)S(1)}, f32[4,128,128]{2,1,0:T(8,128)S(1)}, u32[]{:S(2)}, u32[]{:S(2)}) collective-permute-start(f32[4,128,128]{2,1,0:T(8,128)S(1)} %add.285), channel_id=1, source_target_pairs={{8,0},{10,2},{12,4},{14,6},{9,1},{11,3},{13,5},{15,7},{24,16},{26,... | collective-permute-start | bytes 786440 | tf_op jit(solution)/shard_map/ppermute | solution.py:64
  145.2 24.9 %collective-permute-start.25 = (f32[256,2048]{1,0:T(8,128)}, f32[256,2048]{1,0:T(8,128)}, u32[]{:S(2)}, u32[]{:S(2)}) collective-permute-start(f32[256,2048]{1,0:T(8,128)} %convolution_add_fusion), channel_id=1, source_target_pairs={{0,1},{1,0},{2,3},{3,2},{4,5},{5,4},{6,7},{7,6},{8,9},{9,8},{10,11... | collective-permute-start | bytes 6291464 | tf_op jit(solution)/shard_map/ppermute | solution.py:17
  160.3 3.6 %collective-permute-start.20 = (bf16[256,512]{1,0:T(8,128)(2,1)}, bf16[256,512]{1,0:T(8,128)(2,1)}, u32[]{:S(2)}, u32[]{:S(2)}) collective-permute-start(bf16[256,512]{1,0:T(8,128)(2,1)} %copy.18), channel_id=1, source_target_pairs={{0,1},{1,0},{2,3},{3,2},{4,5},{5,4},{6,7},{7,6},{8,9},{9,8},{10,11... | collective-permute-start | bytes 786440 | tf_op jit(solution)/shard_map/ppermute | solution.py:17
  (3 other events, 8.5 us)

commit v10 on v9

--- a/solution.py
+++ b/solution.py
@@ -156,6 +156,7 @@
     d_mixed = (grad_out - normed * jnp.mean(grad_out * normed, axis=-1, keepdims=True)) / root
     d_mixed_b = d_mixed.astype(bf16)
     grad_local = jnp.einsum("jthd,jthe->jhde", query, d_mixed_b, preferred_element_type=f32)
+    output, grad_local = lax.optimization_barrier((output, grad_local))
 
     later1 = exclusive_scan(grad_local[0] + grad_local[1], chips, True)
     later_mine = jnp.where(first, later1 + grad_local[1], later1)

time: 176 us -> 181 us (1.028)
  the two profiles are of different devices: /device:TPU:15 before, /device:TPU:7 now
where the time goes in v10:
time: 181 us; the launch traced here: 180 us
  starting transfers between devices  50.4 us (28%)
  waiting for transfers between devices  47.7 us (26%)
  local copies, waits for them, and re-layouts  33.4 us (18%)
  matrix products  23.1 us (13%)
  other arithmetic  14.2 us (8%)
  between operations  10.8 us (6%)
    ppermute x6, waiting for transfers between devices, exclusive_scan(): got = lax.ppermute(incl, 'chip', perm)  35.1 us
    ppermute x6, starting transfers between devices, swap(): return lax.ppermute(x, 'core', [(0, 1), (1, 0)])  23.4 us
    ppermute x6, starting transfers between devices, exclusive_scan(): got = lax.ppermute(incl, 'chip', perm)  17.1 us
    ppermute x7, waiting for transfers between devices, land(): return (piece, lax.ppermute(sent, 'groups', partner))  9.93 us
    dynamic_update_slice x8, local copies, waits for them, and re-layouts, on_device(): w_ring = lax.dynamic_update_slice_in_dim(w_ring, ringed, src * span, axis=0)  9.05 us
    dot_general x2, matrix products, grad_rows(): lax.dot_general(d_ring, w_ring, (((1,), (1,)), ((), ())), preferred_eleme...  7 us
    ppermute x7, starting transfers between devices, land(): return (piece, lax.ppermute(sent, 'groups', partner))  5.17 us
    dot_general x1, matrix products, on_device(): p_ring = jnp.dot(x_pair, w_ring, preferred_element_type=f32).astype(bf16)  5.16 us
  transfers between devices with their start and end apart: 26, of which 13 were waited for; matrix products, arithmetic and copies ran while one was open for 27% of the time, Pallas kernels for 0%

profile of v10, /device:TPU:7, one launch (start us, length us, event | category | flops | bytes accessed | tf_op | source)
XLA Modules:
  0.0 179.5 jit_solution(9653401655086629797)
XLA Ops:
  5.0 2.5 %broadcast_in_dim.27 = bf16[2048,1024]{1,0:T(8,128)(2,1)} broadcast(bf16[]{:T(256)} %constant.96.clone.1), dimensions={} | broadcast | bytes 4194306 | tf_op jit(solution)/shard_map/broadcast_in_dim | solution.py:111
  26.6 1.4 collective-permute-start.10
  29.2 1.9 %constant_dynamic-update-slice_fusion.13 = bf16[2048,1024]{1,0:T(8,128)(2,1)} fusion(bf16[2048,1024]{1,0:T(8,128)(2,1)} %get-tuple-element.10, bf16[256,1024]{1,0:T(8,128)(2,1)} %collective-permute-done.2, s32[]{:T(128)S(6)} %select_n.212), kind=kLoop, calls=%fused_computation.100 | loop fusion | bytes 1048580 | tf_op jit(solution)/shard_map/dynamic_update_slice | solution.py:114
  31.1 1.9 %constant_dynamic-update-slice_fusion.12 = bf16[2048,1024]{1,0:T(8,128)(2,1)} fusion(bf16[2048,1024]{1,0:T(8,128)(2,1)} %constant_dynamic-update-slice_fusion.13, bf16[256,1024]{1,0:T(8,128)(2,1)} %collective-permute-done.3, s32[]{:T(128)S(6)} %select_n.215), kind=kLoop, calls=%fused_computation.99 | loop fusion | bytes 1048580 | tf_op jit(solution)/shard_map/dynamic_update_slice | solution.py:114
  33.0 5.5 %collective-permute-done.10 = bf16[256,512]{1,0:T(8,128)(2,1)S(1)} collective-permute-done((bf16[256,512]{1,0:T(8,128)(2,1)S(1)}, bf16[256,512]{1,0:T(8,128)(2,1)S(1)}, u32[]{:S(2)}, u32[]{:S(2)}) %collective-permute-start.10) | collective-permute-done | bytes 262176 | tf_op jit(solution)/shard_map/ppermute | solution.py:41
  45.1 4.3 %collective-permute-start.16 = (s32[2,2]{1,0:T(2,128)S(1)}, s32[2,2]{1,0:T(2,128)S(1)}, u32[]{:S(2)}, u32[]{:S(2)}) collective-permute-start(s32[2,2]{1,0:T(2,128)S(1)} %bitcast.127), channel_id=1, source_target_pairs={{0,1},{1,0},{2,3},{3,2},{4,5},{5,4},{6,7},{7,6},{8,9},{9,8},{10,11... | collective-permute-start | bytes 56 | tf_op jit(solution)/shard_map/ppermute | solution.py:17
  55.2 1.8 collective-permute-done.13
  57.0 6.3 %collective-permute-start.21 = (bf16[256,512]{0,1:T(8,128)(2,1)}, bf16[256,512]{0,1:T(8,128)(2,1)}, u32[]{:S(2)}, u32[]{:S(2)}) collective-permute-start(bf16[256,512]{0,1:T(8,128)(2,1)} %get-tuple-element.24), channel_id=1, source_target_pairs={{0,1},{1,0},{2,3},{3,2},{4,5},{5,4},{6,7},{7,6},{8,9},{9,8},{10,11... | collective-permute-start | bytes 786440 | tf_op jit(solution)/shard_map/ppermute | solution.py:17
  64.7 5.2 %convolution_convert_fusion = bf16[512,1024]{1,0:T(8,128)(2,1)S(1)} fusion(bf16[2048,1024]{1,0:T(8,128)(2,1)} %constant_dynamic-update-slice_fusion.7, bf16[256,2048]{1,0:T(8,128)(2,1)} %collective-permute-done, bf16[256,2048]{1,0:T(8,128)(2,1)} %add_convert_fusion.1), kind=kOutput, calls=%fused_computation.9 | convolution fusion | flops 2152202240 | bytes 7340032 | tf_op jit(solution)/shard_map/dot_general | solution.py:116
  69.9 2.8 %fusion.2 = bf16[512,512]{1,0:T(8,128)(2,1)S(1)} fusion(bf16[2048,512]{1,0:T(8,128)(2,1)S(1)} %constant_dynamic-update-slice_fusion, bf16[256,2048]{1,0:T(8,128)(2,1)} %collective-permute-done, bf16[256,2048]{1,0:T(8,128)(2,1)} %add_convert_fusion.1), kind=kOutput, calls=%fused_computation.18 | convolution fusion | flops 1078198272 | bytes 4718592 | tf_op jit(solution)/shard_map/dot_general | solution.py:117
  72.7 1.6 maximum_select_fusion
  74.3 4.0 %select_n.234 = bf16[2,256,3,4,128]{4,3,2,1,0:T(4,128)(2,1)} reshape(bf16[512,1536]{1,0:T(8,128)(2,1)} %maximum_select_fusion) | data formatting | bytes 3145728 | tf_op jit(solution)/shard_map/jit(_where)/select_n | solution.py:118
  78.2 2.9 %fusion.48 = (bf16[2,256,1,4,128]{4,3,2,1,0:T(4,128)(2,1)}, bf16[2,256,1,4,128]{4,3,2,1,0:T(4,128)(2,1)S(1)}, bf16[2,256,1,4,128]{4,3,2,1,0:T(4,128)(2,1)}) fusion(bf16[2,256,3,4,128]{4,3,2,1,0:T(4,128)(2,1)} %select_n.234), kind=kLoop, calls=%fused_computation.121 | loop fusion | bytes 3145728 | tf_op jit(solution)/shard_map/slice | solution.py:126
  84.3 3.1 %collective-permute-start.17 = (f32[4,128,128]{2,1,0:T(8,128)}, f32[4,128,128]{2,1,0:T(8,128)}, u32[]{:S(2)}, u32[]{:S(2)}) collective-permute-start(f32[4,128,128]{2,1,0:T(8,128)} %fusion.31), channel_id=1, source_target_pairs={{0,2},{2,4},{4,6},{6,8},{8,10},{10,12},{12,14},{1,3},{3,5},{5,7},{... | collective-permute-start | bytes 786440 | tf_op jit(solution)/shard_map/ppermute | solution.py:64
  88.4 2.3 %reshape.113 = f32[2,256,256]{2,1,0:T(8,128)} reshape(f32[2,2,128,2,128]{4,3,2,1,0:T(2,128)} %broadcast_in_dim.31) | data formatting | bytes 1048576 | tf_op jit(solution)/shard_map/vmap()/reshape | solution.py:75
  93.0 3.2 %collective-permute-start.18 = (f32[4,128,128]{2,1,0:T(8,128)S(1)}, f32[4,128,128]{2,1,0:T(8,128)S(1)}, u32[]{:S(2)}, u32[]{:S(2)}) collective-permute-start(f32[4,128,128]{2,1,0:T(8,128)S(1)} %fusion.67), channel_id=1, source_target_pairs={{0,4},{2,6},{4,8},{6,10},{8,12},{10,14},{1,5},{3,7},{5,9},{7,11},{... | collective-permute-start | bytes 786440 | tf_op jit(solution)/shard_map/ppermute | solution.py:64
  96.7 2.8 %collective-permute-done.18 = f32[4,128,128]{2,1,0:T(8,128)S(1)} collective-permute-done((f32[4,128,128]{2,1,0:T(8,128)S(1)}, f32[4,128,128]{2,1,0:T(8,128)S(1)}, u32[]{:S(2)}, u32[]{:S(2)}) %collective-permute-start.18) | collective-permute-done | bytes 262176 | tf_op jit(solution)/shard_map/ppermute | solution.py:64
  99.5 5.0 %collective-permute-start.19 = (f32[4,128,128]{2,1,0:T(8,128)S(1)}, f32[4,128,128]{2,1,0:T(8,128)S(1)}, u32[]{:S(2)}, u32[]{:S(2)}) collective-permute-start(f32[4,128,128]{2,1,0:T(8,128)S(1)} %add.272), channel_id=1, source_target_pairs={{0,8},{2,10},{4,12},{6,14},{1,9},{3,11},{5,13},{7,15},{16,24},{18,... | collective-permute-start | bytes 786440 | tf_op jit(solution)/shard_map/ppermute | solution.py:64
  105.1 2.9 %collective-permute-done.19 = f32[4,128,128]{2,1,0:T(8,128)S(1)} collective-permute-done((f32[4,128,128]{2,1,0:T(8,128)S(1)}, f32[4,128,128]{2,1,0:T(8,128)S(1)}, u32[]{:S(2)}, u32[]{:S(2)}) %collective-permute-start.19) | collective-permute-done | bytes 262176 | tf_op jit(solution)/shard_map/ppermute | solution.py:64
  111.9 1.5 multiply_convert_fusion
  114.1 1.8 %copy.18 = bf16[256,512]{1,0:T(8,128)(2,1)} copy(bf16[256,512]{0,1:T(8,128)(2,1)} %bitcast.126) | data formatting | bytes 524288 | tf_op jit(solution)/shard_map/squeeze | solution.py:145
  115.9 10.0 %collective-permute-start.20 = (bf16[256,512]{1,0:T(8,128)(2,1)}, bf16[256,512]{1,0:T(8,128)(2,1)}, u32[]{:S(2)}, u32[]{:S(2)}) collective-permute-start(bf16[256,512]{1,0:T(8,128)(2,1)} %copy.18), channel_id=1, source_target_pairs={{0,1},{1,0},{2,3},{3,2},{4,5},{5,4},{6,7},{7,6},{8,9},{9,8},{10,11... | collective-permute-start | bytes 786440 | tf_op jit(solution)/shard_map/ppermute | solution.py:17
  126.7 1.5 fusion.21
  128.2 2.2 %maximum_select_fusion.1 = bf16[256,1024]{1,0:T(8,128)(2,1)} fusion(bf16[256,512]{1,0:T(8,128)(2,1)} %collective-permute-done.20, bf16[256,512]{1,0:T(8,128)(2,1)} %copy.19, pred[]{:T(512)S(6)} %eq.15), kind=kLoop, calls=%fused_computation.29 | loop fusion | flops 2359296 | bytes 1048577 | tf_op jit(solution)/shard_map/jit(_where)/select_n | solution.py:146
  130.4 3.0 %collective-permute-start.22 = (f32[4,128,128]{2,1,0:T(8,128)S(1)}, f32[4,128,128]{2,1,0:T(8,128)S(1)}, u32[]{:S(2)}, u32[]{:S(2)}) collective-permute-start(f32[4,128,128]{2,1,0:T(8,128)S(1)} %bitcast_add_fusion), channel_id=1, source_target_pairs={{2,0},{4,2},{6,4},{8,6},{10,8},{12,10},{14,12},{3,1},{5,3},{7,5},{... | collective-permute-start | bytes 786440 | tf_op jit(solution)/shard_map/ppermute | solution.py:64
  134.3 6.9 %collective-permute-done.22 = f32[4,128,128]{2,1,0:T(8,128)S(1)} collective-permute-done((f32[4,128,128]{2,1,0:T(8,128)S(1)}, f32[4,128,128]{2,1,0:T(8,128)S(1)}, u32[]{:S(2)}, u32[]{:S(2)}) %collective-permute-start.22) | collective-permute-done | bytes 262176 | tf_op jit(solution)/shard_map/ppermute | solution.py:64
  142.9 8.5 %collective-permute-done.23 = f32[4,128,128]{2,1,0:T(8,128)S(1)} collective-permute-done((f32[4,128,128]{2,1,0:T(8,128)S(1)}, f32[4,128,128]{2,1,0:T(8,128)S(1)}, u32[]{:S(2)}, u32[]{:S(2)}) %collective-permute-start.23) | collective-permute-done | bytes 262176 | tf_op jit(solution)/shard_map/ppermute | solution.py:64
  151.4 1.4 collective-permute-start.24
  153.1 14.1 %collective-permute-done.24 = f32[4,128,128]{2,1,0:T(8,128)S(1)} collective-permute-done((f32[4,128,128]{2,1,0:T(8,128)S(1)}, f32[4,128,128]{2,1,0:T(8,128)S(1)}, u32[]{:S(2)}, u32[]{:S(2)}) %collective-permute-start.24) | collective-permute-done | bytes 262176 | tf_op jit(solution)/shard_map/ppermute | solution.py:64
  169.0 3.5 %convolution_add_fusion = f32[256,2048]{1,0:T(8,128)S(1)} fusion(f32[256,2048]{1,0:T(8,128)S(1)} %fusion.27, bf16[2048,1024]{1,0:T(8,128)(2,1)} %constant_dynamic-update-slice_fusion.7, bf16[256,1536]{0,1:T(8,128)(2,1)S(1)} %bitcast.121, s32[]{:T(128)S(6)} %select_n.207), kind=kOutput, calls=%fused_computation | convolution fusion | flops 1074266112 | bytes 8912900 | tf_op jit(solution)/shard_map/dot_general | solution.py:180
  172.5 1.5 collective-permute-start.25
  174.8 3.5 %convolution_add_fusion.1 = f32[256,2048]{1,0:T(8,128)S(1)} fusion(f32[256,2048]{1,0:T(8,128)S(1)} %fusion.29, bf16[2048,1024]{1,0:T(8,128)(2,1)} %constant_dynamic-update-slice_fusion.7, bf16[256,1536]{0,1:T(8,128)(2,1)S(1)} %bitcast.119, s32[]{:T(128)S(6)} %select_n.207), kind=kOutput, calls=%fused_computation.1 | convolution fusion | flops 1074266112 | bytes 8912900 | tf_op jit(solution)/shard_map/dot_general | solution.py:180
  (138 shorter events, 48.2 us)
Async XLA Ops:
  2.8 2.1 %collective-permute-start.1 = (bf16[128,1536]{1,0:T(8,128)(2,1)S(1)}, bf16[128,1536]{1,0:T(8,128)(2,1)S(1)}, u32[]{:S(2)}, u32[]{:S(2)}) collective-permute-start(bf16[128,1536]{1,0:T(8,128)(2,1)S(1)} %pad_maximum_fusion.7), channel_id=1, source_target_pairs={{0,1},{1,0},{2,3},{3,2},{4,5},{5,4},{6,7},{7,6},{8,9},{9,8},{10,11... | collective-permute-start | bytes 1179656 | tf_op jit(solution)/shard_map/ppermute | solution.py:17
  8.6 14.4 %copy-start.14 = (bf16[256,1024]{1,0:T(8,128)(2,1)S(1)}, bf16[256,1024]{1,0:T(8,128)(2,1)}, u32[]{:S(2)}) copy-start(bf16[256,1024]{1,0:T(8,128)(2,1)} %param.11) | copy-start | bytes 1572868
  8.6 15.6 %collective-permute-start.2 = (bf16[256,1024]{1,0:T(8,128)(2,1)}, bf16[256,1024]{1,0:T(8,128)(2,1)}, u32[]{:S(2)}, u32[]{:S(2)}) collective-permute-start(bf16[256,1024]{1,0:T(8,128)(2,1)} %get-tuple-element.11), channel_id=1, source_target_pairs={{0,4},{4,8},{8,12},{12,14},{14,10},{10,6},{6,2},{2,0},{1,5},{5,9},... | collective-permute-start | bytes 1572872 | tf_op jit(solution)/shard_map/ppermute | solution.py:47
  10.2 54.5 %collective-permute-start = (bf16[256,2048]{1,0:T(8,128)(2,1)}, bf16[256,2048]{1,0:T(8,128)(2,1)}, u32[]{:S(2)}, u32[]{:S(2)}) collective-permute-start(bf16[256,2048]{1,0:T(8,128)(2,1)} %add_convert_fusion.1), channel_id=1, source_target_pairs={{0,1},{1,0},{2,3},{3,2},{4,5},{5,4},{6,7},{7,6},{8,9},{9,8},{10,11... | collective-permute-start | bytes 3145736 | tf_op jit(solution)/shard_map/ppermute | solution.py:17
  10.8 14.8 %collective-permute-start.3 = (bf16[256,1024]{1,0:T(8,128)(2,1)}, bf16[256,1024]{1,0:T(8,128)(2,1)}, u32[]{:S(2)}, u32[]{:S(2)}) collective-permute-start(bf16[256,1024]{1,0:T(8,128)(2,1)} %get-tuple-element.11), channel_id=1, source_target_pairs={{0,2},{4,0},{8,4},{12,8},{14,12},{10,14},{6,10},{2,6},{1,3},{5,1},... | collective-permute-start | bytes 1572872 | tf_op jit(solution)/shard_map/ppermute | solution.py:50
  25.2 7.8 %collective-permute-start.9 = (bf16[256,512]{1,0:T(8,128)(2,1)S(1)}, bf16[256,512]{1,0:T(8,128)(2,1)S(1)}, u32[]{:S(2)}, u32[]{:S(2)}) collective-permute-start(bf16[256,512]{1,0:T(8,128)(2,1)S(1)} %constant_dynamic-slice_fusion.6), channel_id=1, source_target_pairs={{0,16},{16,0},{1,17},{17,1},{2,18},{18,2},{3,19},{19,3},{4,20},{20... | collective-permute-start | bytes 786440 | tf_op jit(solution)/shard_map/ppermute | solution.py:41
  25.5 13.1 %collective-permute-start.4 = (bf16[256,1024]{1,0:T(8,128)(2,1)}, bf16[256,1024]{1,0:T(8,128)(2,1)S(1)}, u32[]{:S(2)}, u32[]{:S(2)}) collective-permute-start(bf16[256,1024]{1,0:T(8,128)(2,1)} %collective-permute-done.2), channel_id=1, source_target_pairs={{0,4},{4,8},{8,12},{12,14},{14,10},{10,6},{6,2},{2,0},{1,5},{5,9},... | collective-permute-start | bytes 1572872 | tf_op jit(solution)/shard_map/ppermute | solution.py:47
  26.6 11.9 %collective-permute-start.10 = (bf16[256,512]{1,0:T(8,128)(2,1)S(1)}, bf16[256,512]{1,0:T(8,128)(2,1)S(1)}, u32[]{:S(2)}, u32[]{:S(2)}) collective-permute-start(bf16[256,512]{1,0:T(8,128)(2,1)S(1)} %constant_dynamic-slice_fusion.5), channel_id=1, source_target_pairs={{0,16},{16,0},{1,17},{17,1},{2,18},{18,2},{3,19},{19,3},{4,20},{20... | collective-permute-start | bytes 786440 | tf_op jit(solution)/shard_map/ppermute | solution.py:41
  28.0 12.5 %collective-permute-start.5 = (bf16[256,1024]{1,0:T(8,128)(2,1)}, bf16[256,1024]{1,0:T(8,128)(2,1)S(1)}, u32[]{:S(2)}, u32[]{:S(2)}) collective-permute-start(bf16[256,1024]{1,0:T(8,128)(2,1)} %collective-permute-done.3), channel_id=1, source_target_pairs={{0,2},{4,0},{8,4},{12,8},{14,12},{10,14},{6,10},{2,6},{1,3},{5,1},... | collective-permute-start | bytes 1572872 | tf_op jit(solution)/shard_map/ppermute | solution.py:50
  33.0 12.1 %copy-start.16 = (s32[1,2,2]{2,1,0:T(2,128)S(1)}, s32[1,2,2]{2,1,0:T(2,128)}, u32[]{:S(2)}) copy-start(s32[1,2,2]{2,1,0:T(2,128)} %param.15) | copy-start | bytes 52
  38.7 6.4 %collective-permute-start.11 = (bf16[256,512]{1,0:T(8,128)(2,1)S(1)}, bf16[256,512]{1,0:T(8,128)(2,1)S(1)}, u32[]{:S(2)}, u32[]{:S(2)}) collective-permute-start(bf16[256,512]{1,0:T(8,128)(2,1)S(1)} %constant_dynamic-slice_fusion.4), channel_id=1, source_target_pairs={{0,16},{16,0},{1,17},{17,1},{2,18},{18,2},{3,19},{19,3},{4,20},{20... | collective-permute-start | bytes 786440 | tf_op jit(solution)/shard_map/ppermute | solution.py:41
  40.0 11.7 %collective-permute-start.6 = (bf16[256,1024]{1,0:T(8,128)(2,1)S(1)}, bf16[256,1024]{1,0:T(8,128)(2,1)S(1)}, u32[]{:S(2)}, u32[]{:S(2)}) collective-permute-start(bf16[256,1024]{1,0:T(8,128)(2,1)S(1)} %collective-permute-done.4), channel_id=1, source_target_pairs={{0,4},{4,8},{8,12},{12,14},{14,10},{10,6},{6,2},{2,0},{1,5},{5,9},... | collective-permute-start | bytes 1572872 | tf_op jit(solution)/shard_map/ppermute | solution.py:47
  40.5 10.2 %collective-permute-start.12 = (bf16[256,512]{1,0:T(8,128)(2,1)S(1)}, bf16[256,512]{1,0:T(8,128)(2,1)S(1)}, u32[]{:S(2)}, u32[]{:S(2)}) collective-permute-start(bf16[256,512]{1,0:T(8,128)(2,1)S(1)} %constant_dynamic-slice_fusion.3), channel_id=1, source_target_pairs={{0,16},{16,0},{1,17},{17,1},{2,18},{18,2},{3,19},{19,3},{4,20},{20... | collective-permute-start | bytes 786440 | tf_op jit(solution)/shard_map/ppermute | solution.py:41
  40.9 11.6 %collective-permute-start.7 = (bf16[256,1024]{1,0:T(8,128)(2,1)S(1)}, bf16[256,1024]{1,0:T(8,128)(2,1)S(1)}, u32[]{:S(2)}, u32[]{:S(2)}) collective-permute-start(bf16[256,1024]{1,0:T(8,128)(2,1)S(1)} %collective-permute-done.5), channel_id=1, source_target_pairs={{0,2},{4,0},{8,4},{12,8},{14,12},{10,14},{6,10},{2,6},{1,3},{5,1},... | collective-permute-start | bytes 1572872 | tf_op jit(solution)/shard_map/ppermute | solution.py:50
  45.1 42.3 %collective-permute-start.16 = (s32[2,2]{1,0:T(2,128)S(1)}, s32[2,2]{1,0:T(2,128)S(1)}, u32[]{:S(2)}, u32[]{:S(2)}) collective-permute-start(s32[2,2]{1,0:T(2,128)S(1)} %bitcast.127), channel_id=1, source_target_pairs={{0,1},{1,0},{2,3},{3,2},{4,5},{5,4},{6,7},{7,6},{8,9},{9,8},{10,11... | collective-permute-start | bytes 56 | tf_op jit(solution)/shard_map/ppermute | solution.py:17
  51.7 5.3 %collective-permute-start.13 = (bf16[256,512]{1,0:T(8,128)(2,1)S(1)}, bf16[256,512]{1,0:T(8,128)(2,1)S(1)}, u32[]{:S(2)}, u32[]{:S(2)}) collective-permute-start(bf16[256,512]{1,0:T(8,128)(2,1)S(1)} %constant_dynamic-slice_fusion.2), channel_id=1, source_target_pairs={{0,16},{16,0},{1,17},{17,1},{2,18},{18,2},{3,19},{19,3},{4,20},{20... | collective-permute-start | bytes 786440 | tf_op jit(solution)/shard_map/ppermute | solution.py:41
  52.1 11.3 %collective-permute-start.8 = (bf16[256,1024]{1,0:T(8,128)(2,1)S(1)}, bf16[256,1024]{1,0:T(8,128)(2,1)S(1)}, u32[]{:S(2)}, u32[]{:S(2)}) collective-permute-start(bf16[256,1024]{1,0:T(8,128)(2,1)S(1)} %collective-permute-done.6), channel_id=1, source_target_pairs={{0,4},{4,8},{8,12},{12,14},{14,10},{10,6},{6,2},{2,0},{1,5},{5,9},... | collective-permute-start | bytes 1572872 | tf_op jit(solution)/shard_map/ppermute | solution.py:47
  52.6 10.7 %collective-permute-start.14 = (bf16[256,512]{1,0:T(8,128)(2,1)S(1)}, bf16[256,512]{1,0:T(8,128)(2,1)S(1)}, u32[]{:S(2)}, u32[]{:S(2)}) collective-permute-start(bf16[256,512]{1,0:T(8,128)(2,1)S(1)} %constant_dynamic-slice_fusion.1), channel_id=1, source_target_pairs={{0,16},{16,0},{1,17},{17,1},{2,18},{18,2},{3,19},{19,3},{4,20},{20... | collective-permute-start | bytes 786440 | tf_op jit(solution)/shard_map/ppermute | solution.py:41
  57.0 52.4 %collective-permute-start.21 = (bf16[256,512]{0,1:T(8,128)(2,1)}, bf16[256,512]{0,1:T(8,128)(2,1)}, u32[]{:S(2)}, u32[]{:S(2)}) collective-permute-start(bf16[256,512]{0,1:T(8,128)(2,1)} %get-tuple-element.24), channel_id=1, source_target_pairs={{0,1},{1,0},{2,3},{3,2},{4,5},{5,4},{6,7},{7,6},{8,9},{9,8},{10,11... | collective-permute-start | bytes 786440 | tf_op jit(solution)/shard_map/ppermute | solution.py:17
  63.4 6.4 %collective-permute-start.15 = (bf16[256,512]{1,0:T(8,128)(2,1)S(1)}, bf16[256,512]{1,0:T(8,128)(2,1)S(1)}, u32[]{:S(2)}, u32[]{:S(2)}) collective-permute-start(bf16[256,512]{1,0:T(8,128)(2,1)S(1)} %constant_dynamic-slice_fusion), channel_id=1, source_target_pairs={{0,16},{16,0},{1,17},{17,1},{2,18},{18,2},{3,19},{19,3},{4,20},{20... | collective-permute-start | bytes 786440 | tf_op jit(solution)/shard_map/ppermute | solution.py:41
  82.4 22.2 %copy-start = (bf16[2,256,1,4,128]{1,4,3,0,2:T(8,128)(2,1)}, bf16[2,256,1,4,128]{1,4,3,0,2:T(8,128)(2,1)S(1)}, u32[]{:S(2)}) copy-start(bf16[2,256,1,4,128]{1,4,3,0,2:T(8,128)(2,1)S(1)} %copy.46) | copy-start | bytes 1572868
  84.3 7.6 %collective-permute-start.17 = (f32[4,128,128]{2,1,0:T(8,128)}, f32[4,128,128]{2,1,0:T(8,128)}, u32[]{:S(2)}, u32[]{:S(2)}) collective-permute-start(f32[4,128,128]{2,1,0:T(8,128)} %fusion.31), channel_id=1, source_target_pairs={{0,2},{2,4},{4,6},{6,8},{8,10},{10,12},{12,14},{1,3},{3,5},{5,7},{... | collective-permute-start | bytes 786440 | tf_op jit(solution)/shard_map/ppermute | solution.py:64
  93.0 6.5 %collective-permute-start.18 = (f32[4,128,128]{2,1,0:T(8,128)S(1)}, f32[4,128,128]{2,1,0:T(8,128)S(1)}, u32[]{:S(2)}, u32[]{:S(2)}) collective-permute-start(f32[4,128,128]{2,1,0:T(8,128)S(1)} %fusion.67), channel_id=1, source_target_pairs={{0,4},{2,6},{4,8},{6,10},{8,12},{10,14},{1,5},{3,7},{5,9},{7,11},{... | collective-permute-start | bytes 786440 | tf_op jit(solution)/shard_map/ppermute | solution.py:64
  96.7 12.3 %copy-start.5 = (bf16[2,4,256,256]{3,2,1,0:T(8,128)(2,1)}, bf16[2,4,256,256]{3,2,1,0:T(8,128)(2,1)S(1)}, u32[]{:S(2)}) copy-start(bf16[2,4,256,256]{3,2,1,0:T(8,128)(2,1)S(1)} %multiply_convert_fusion.1) | copy-start | bytes 3145732
  99.5 8.4 %collective-permute-start.19 = (f32[4,128,128]{2,1,0:T(8,128)S(1)}, f32[4,128,128]{2,1,0:T(8,128)S(1)}, u32[]{:S(2)}, u32[]{:S(2)}) collective-permute-start(f32[4,128,128]{2,1,0:T(8,128)S(1)} %add.272), channel_id=1, source_target_pairs={{0,8},{2,10},{4,12},{6,14},{1,9},{3,11},{5,13},{7,15},{16,24},{18,... | collective-permute-start | bytes 786440 | tf_op jit(solution)/shard_map/ppermute | solution.py:64
  115.9 12.3 %collective-permute-start.20 = (bf16[256,512]{1,0:T(8,128)(2,1)}, bf16[256,512]{1,0:T(8,128)(2,1)}, u32[]{:S(2)}, u32[]{:S(2)}) collective-permute-start(bf16[256,512]{1,0:T(8,128)(2,1)} %copy.18), channel_id=1, source_target_pairs={{0,1},{1,0},{2,3},{3,2},{4,5},{5,4},{6,7},{7,6},{8,9},{9,8},{10,11... | collective-permute-start | bytes 786440 | tf_op jit(solution)/shard_map/ppermute | solution.py:17
  130.4 10.7 %collective-permute-start.22 = (f32[4,128,128]{2,1,0:T(8,128)S(1)}, f32[4,128,128]{2,1,0:T(8,128)S(1)}, u32[]{:S(2)}, u32[]{:S(2)}) collective-permute-start(f32[4,128,128]{2,1,0:T(8,128)S(1)} %bitcast_add_fusion), channel_id=1, source_target_pairs={{2,0},{4,2},{6,4},{8,6},{10,8},{12,10},{14,12},{3,1},{5,3},{7,5},{... | collective-permute-start | bytes 786440 | tf_op jit(solution)/shard_map/ppermute | solution.py:64
  134.3 18.5 %copy-start.6 = (bf16[2,4,256,256]{3,2,1,0:T(8,128)(2,1)S(1)}, bf16[2,4,256,256]{3,2,1,0:T(8,128)(2,1)}, u32[]{:S(2)}) copy-start(bf16[2,4,256,256]{3,2,1,0:T(8,128)(2,1)} %copy-done.5) | copy-start | bytes 3145732
  141.2 10.1 %collective-permute-start.23 = (f32[4,128,128]{2,1,0:T(8,128)S(1)}, f32[4,128,128]{2,1,0:T(8,128)S(1)}, u32[]{:S(2)}, u32[]{:S(2)}) collective-permute-start(f32[4,128,128]{2,1,0:T(8,128)S(1)} %fusion.66), channel_id=1, source_target_pairs={{4,0},{6,2},{8,4},{10,6},{12,8},{14,10},{5,1},{7,3},{9,5},{11,7},{... | collective-permute-start | bytes 786440 | tf_op jit(solution)/shard_map/ppermute | solution.py:64
  151.3 15.9 %copy-start.2 = (bf16[2,256,1,4,128]{1,4,3,0,2:T(8,128)(2,1)S(1)}, bf16[2,256,1,4,128]{1,4,3,0,2:T(8,128)(2,1)}, u32[]{:S(2)}) copy-start(bf16[2,256,1,4,128]{1,4,3,0,2:T(8,128)(2,1)} %copy-done) | copy-start | bytes 1572868
  151.4 15.8 %collective-permute-start.24 = (f32[4,128,128]{2,1,0:T(8,128)S(1)}, f32[4,128,128]{2,1,0:T(8,128)S(1)}, u32[]{:S(2)}, u32[]{:S(2)}) collective-permute-start(f32[4,128,128]{2,1,0:T(8,128)S(1)} %add.285), channel_id=1, source_target_pairs={{8,0},{10,2},{12,4},{14,6},{9,1},{11,3},{13,5},{15,7},{24,16},{26,... | collective-permute-start | bytes 786440 | tf_op jit(solution)/shard_map/ppermute | solution.py:64
  172.5 5.8 %collective-permute-start.25 = (f32[256,2048]{1,0:T(8,128)S(1)}, f32[256,2048]{1,0:T(8,128)S(1)}, u32[]{:S(2)}, u32[]{:S(2)}) collective-permute-start(f32[256,2048]{1,0:T(8,128)S(1)} %convolution_add_fusion), channel_id=1, source_target_pairs={{0,1},{1,0},{2,3},{3,2},{4,5},{5,4},{6,7},{7,6},{8,9},{9,8},{10,11... | collective-permute-start | bytes 6291464 | tf_op jit(solution)/shard_map/ppermute | solution.py:17
  (12 other events, 64.2 us)

commit v11 on v10

--- a/solution.py
+++ b/solution.py
@@ -108,22 +108,23 @@
     parity = lax.axis_index("groups") % 2
     share = half
     width = 2 * half
-    w_ring = jnp.zeros((chips * span, width), bf16)
-    w_x = jnp.zeros((chips * span, share), bf16)
+    mats = [jnp.zeros((chips * span, share), bf16) for _ in range(3)]
     for src, (ringed, swapped) in ring_gather(block, chips, c, parity):
-        w_ring = lax.dynamic_update_slice_in_dim(w_ring, ringed, src * span, axis=0)
-        w_x = lax.dynamic_update_slice_in_dim(w_x, swapped, src * span, axis=0)
-    p_ring = jnp.dot(x_pair, w_ring, preferred_element_type=f32).astype(bf16)
-    p_x = jnp.dot(x_pair, w_x, preferred_element_type=f32).astype(bf16)
-    projected = jnp.where(
-        parity == 0,
-        jnp.concatenate([p_ring, p_x], axis=1),
-        jnp.concatenate([p_x, p_ring], axis=1),
-    )
-    projected = projected.reshape(2, tok, 3, heads, DH)
-    query = projected[:, :, 0]
-    key = projected[:, :, 1]
-    value = projected[:, :, 2]
+        lower, upper = ringed[:, :share], ringed[:, share:]
+        parts = (
+            jnp.where(parity == 0, lower, swapped),
+            jnp.where(parity == 0, upper, lower),
+            jnp.where(parity == 0, swapped, upper),
+        )
+        mats = [lax.dynamic_update_slice_in_dim(m, part, src * span, axis=0) for m, part in zip(mats, parts)]
+    w_q, w_k, w_v = mats
+
+    def project(w):
+        return jnp.dot(x_pair, w, preferred_element_type=f32).astype(bf16).reshape(2, tok, heads, DH)
+
+    key = project(w_k)
+    value = project(w_v)
+    query = project(w_q)
 
     local = jnp.einsum("jthd,jthe->jhde", key, value, preferred_element_type=f32)
     state0 = exclusive_scan(local[0] + local[1], chips, False)
@@ -172,13 +173,15 @@
     d_key = d_key + jnp.einsum("jshe,jhde->jshd", value, later_b, preferred_element_type=f32)
     d_value = jnp.einsum("jhts,jthe->jshe", attn, d_mixed_b, preferred_element_type=f32)
     d_value = d_value + jnp.einsum("jshd,jhde->jshe", key, later_b, preferred_element_type=f32)
-    d_proj = jnp.stack([d_query, d_key, d_value], axis=2).astype(bf16).reshape(2, tok, 3 * half)
+    dq_b = d_query.astype(bf16).reshape(2, tok, half)
+    dk_b = d_key.astype(bf16).reshape(2, tok, half)
+    dv_b = d_value.astype(bf16).reshape(2, tok, half)
 
     def grad_rows(j):
-        d_ring = lax.dynamic_slice_in_dim(d_proj[j], parity * share, width, axis=1)
-        d_x = lax.dynamic_slice_in_dim(d_proj[j], (1 - parity) * width, share, axis=1)
-        g = lax.dot_general(d_ring, w_ring, (((1,), (1,)), ((), ())), preferred_element_type=f32)
-        return g + lax.dot_general(d_x, w_x, (((1,), (1,)), ((), ())), preferred_element_type=f32)
+        dims = (((1,), (1,)), ((), ()))
+        g = lax.dot_general(dq_b[j], w_q, dims, preferred_element_type=f32)
+        g = g + lax.dot_general(dk_b[j], w_k, dims, preferred_element_type=f32)
+        return g + lax.dot_general(dv_b[j], w_v, dims, preferred_element_type=f32)
 
     received = swap(grad_rows(1))
     own, received = lax.optimization_barrier((grad_rows(0), received))

time: 181 us -> 179 us (0.989)
  the two profiles are of different devices: /device:TPU:7 before, /device:TPU:0 now
where the time goes in v11:
time: 179 us; the launch traced here: 178 us
  waiting for transfers between devices  77.2 us (43%)
  starting transfers between devices  35.2 us (20%)
  matrix products  21.9 us (12%)
  local copies, waits for them, and re-layouts  20 us (11%)
  other arithmetic  13.5 us (8%)
  between operations  9.91 us (6%)
    ppermute x6, waiting for transfers between devices, exclusive_scan(): got = lax.ppermute(incl, 'chip', perm)  38.7 us
    ppermute x3, waiting for transfers between devices, ring_gather(): bwd = lax.ppermute(bwd, 'chip', behind)  18.5 us
    ppermute x7, waiting for transfers between devices, land(): return (piece, lax.ppermute(sent, 'groups', partner))  17.7 us
    ppermute x6, starting transfers between devices, exclusive_scan(): got = lax.ppermute(incl, 'chip', perm)  17.2 us
    dot_general x3, matrix products, project(): jnp.dot(x_pair, w, preferred_element_type=f32).astype(bf16)  9.37 us
    ppermute x4, starting transfers between devices, ring_gather(): fwd = lax.ppermute(fwd, 'chip', ahead)  7.95 us
    ppermute x7, starting transfers between devices, land(): return (piece, lax.ppermute(sent, 'groups', partner))  7.9 us
    unnamed x48, local copies, waits for them, and re-layouts  5.11 us
  transfers between devices with their start and end apart: 26, of which 15 were waited for; matrix products, arithmetic and copies ran while one was open for 21% of the time, Pallas kernels for 0%

profile of v11, /device:TPU:0, one launch (start us, length us, event | category | flops | bytes accessed | tf_op | source)
XLA Modules:
  0.0 177.7 jit_solution(9359118022713126477)
XLA Ops:
  7.7 2.9 %collective-permute-start.2 = (bf16[256,1024]{1,0:T(8,128)(2,1)}, bf16[256,1024]{1,0:T(8,128)(2,1)S(1)}, u32[]{:S(2)}, u32[]{:S(2)}) collective-permute-start(bf16[256,1024]{1,0:T(8,128)(2,1)} %constant_dynamic-slice_fusion.7), channel_id=1, source_target_pairs={{0,4},{4,8},{8,12},{12,14},{14,10},{10,6},{6,2},{2,0},{1,5},{5,9},... | collective-permute-start | bytes 1572872 | tf_op jit(solution)/shard_map/ppermute | solution.py:47
  24.0 2.0 %collective-permute-start.6 = (bf16[256,1024]{1,0:T(8,128)(2,1)S(1)}, bf16[256,1024]{1,0:T(8,128)(2,1)S(1)}, u32[]{:S(2)}, u32[]{:S(2)}) collective-permute-start(bf16[256,1024]{1,0:T(8,128)(2,1)S(1)} %collective-permute-done.2), channel_id=1, source_target_pairs={{0,4},{4,8},{8,12},{12,14},{14,10},{10,6},{6,2},{2,0},{1,5},{5,9},... | collective-permute-start | bytes 1572872 | tf_op jit(solution)/shard_map/ppermute | solution.py:47
  26.3 1.6 collective-permute-start.3
  28.3 8.9 %collective-permute-done.4 = bf16[256,1024]{1,0:T(8,128)(2,1)S(1)} collective-permute-done((bf16[256,1024]{1,0:T(8,128)(2,1)}, bf16[256,1024]{1,0:T(8,128)(2,1)S(1)}, u32[]{:S(2)}, u32[]{:S(2)}) %collective-permute-start.4) | collective-permute-done | bytes 524320 | tf_op jit(solution)/shard_map/ppermute | solution.py:50
  37.2 1.6 collective-permute-start.5
  39.2 1.6 collective-permute-start.10
  41.0 3.6 %collective-permute-done.5 = bf16[256,512]{1,0:T(8,128)(2,1)S(1)} collective-permute-done((bf16[256,512]{1,0:T(8,128)(2,1)S(1)}, bf16[256,512]{1,0:T(8,128)(2,1)S(1)}, u32[]{:S(2)}, u32[]{:S(2)}) %collective-permute-start.5) | collective-permute-done | bytes 262176 | tf_op jit(solution)/shard_map/ppermute | solution.py:41
  44.6 1.5 collective-permute-start.7
  46.3 5.2 %collective-permute-done.8 = bf16[256,1024]{1,0:T(8,128)(2,1)S(1)} collective-permute-done((bf16[256,1024]{1,0:T(8,128)(2,1)S(1)}, bf16[256,1024]{1,0:T(8,128)(2,1)S(1)}, u32[]{:S(2)}, u32[]{:S(2)}) %collective-permute-start.8) | collective-permute-done | bytes 524320 | tf_op jit(solution)/shard_map/ppermute | solution.py:50
  54.3 4.1 %collective-permute-done.9 = bf16[256,512]{1,0:T(8,128)(2,1)S(1)} collective-permute-done((bf16[256,512]{1,0:T(8,128)(2,1)S(1)}, bf16[256,512]{1,0:T(8,128)(2,1)S(1)}, u32[]{:S(2)}, u32[]{:S(2)}) %collective-permute-start.9) | collective-permute-done | bytes 262176 | tf_op jit(solution)/shard_map/ppermute | solution.py:41
  59.1 4.4 %collective-permute-done.12 = bf16[256,1024]{1,0:T(8,128)(2,1)S(1)} collective-permute-done((bf16[256,1024]{1,0:T(8,128)(2,1)S(1)}, bf16[256,1024]{1,0:T(8,128)(2,1)S(1)}, u32[]{:S(2)}, u32[]{:S(2)}) %collective-permute-start.12) | collective-permute-done | bytes 524320 | tf_op jit(solution)/shard_map/ppermute | solution.py:50
  63.6 1.6 collective-permute-start.13
  66.8 6.1 %collective-permute-done.13 = bf16[256,512]{1,0:T(8,128)(2,1)S(1)} collective-permute-done((bf16[256,512]{1,0:T(8,128)(2,1)S(1)}, bf16[256,512]{1,0:T(8,128)(2,1)S(1)}, u32[]{:S(2)}, u32[]{:S(2)}) %collective-permute-start.13) | collective-permute-done | bytes 262176 | tf_op jit(solution)/shard_map/ppermute | solution.py:41
  73.1 3.0 %collective-permute-done.15 = bf16[256,512]{1,0:T(8,128)(2,1)S(1)} collective-permute-done((bf16[256,512]{1,0:T(8,128)(2,1)S(1)}, bf16[256,512]{1,0:T(8,128)(2,1)S(1)}, u32[]{:S(2)}, u32[]{:S(2)}) %collective-permute-start.15) | collective-permute-done | bytes 262176 | tf_op jit(solution)/shard_map/ppermute | solution.py:41
  78.9 2.8 %convolution_convert_fusion = bf16[512,512]{1,0:T(8,128)(2,1)S(1)} fusion(bf16[2048,512]{1,0:T(8,128)(2,1)S(1)} %get-tuple-element.40, bf16[256,2048]{1,0:T(8,128)(2,1)} %collective-permute-done, bf16[256,2048]{1,0:T(8,128)(2,1)} %add_convert_fusion.1), kind=kOutput, calls=%fused_computation.16 | convolution fusion | flops 1078198272 | bytes 4718592 | tf_op jit(solution)/shard_map/dot_general | solution.py:123
  81.9 3.8 %convolution_convert_fusion.2 = bf16[512,512]{1,0:T(8,128)(2,1)} fusion(bf16[2048,512]{1,0:T(8,128)(2,1)S(1)} %get-tuple-element.16, bf16[256,2048]{1,0:T(8,128)(2,1)} %collective-permute-done, bf16[256,2048]{1,0:T(8,128)(2,1)} %add_convert_fusion.1), kind=kOutput, calls=%fused_computation.18 | convolution fusion | flops 1078198272 | bytes 4718592 | tf_op jit(solution)/shard_map/dot_general | solution.py:123
  87.9 1.5 fusion.18
  90.2 3.1 %collective-permute-start.17 = (f32[4,128,128]{2,1,0:T(8,128)S(1)}, f32[4,128,128]{2,1,0:T(8,128)}, u32[]{:S(2)}, u32[]{:S(2)}) collective-permute-start(f32[4,128,128]{2,1,0:T(8,128)S(1)} %fusion.24), channel_id=1, source_target_pairs={{0,2},{2,4},{4,6},{6,8},{8,10},{10,12},{12,14},{1,3},{3,5},{5,7},{... | collective-permute-start | bytes 786440 | tf_op jit(solution)/shard_map/ppermute | solution.py:64
  93.3 2.8 %convolution_convert_fusion.1 = bf16[512,512]{1,0:T(8,128)(2,1)S(1)} fusion(bf16[2048,512]{1,0:T(8,128)(2,1)S(1)} %copy-done.1, bf16[256,2048]{1,0:T(8,128)(2,1)} %collective-permute-done, bf16[256,2048]{1,0:T(8,128)(2,1)} %add_convert_fusion.1), kind=kOutput, calls=%fused_computation.17 | convolution fusion | flops 1078198272 | bytes 4718592 | tf_op jit(solution)/shard_map/dot_general | solution.py:123
  99.7 4.5 %collective-permute-start.18 = (f32[4,128,128]{2,1,0:T(8,128)S(1)}, f32[4,128,128]{2,1,0:T(8,128)S(1)}, u32[]{:S(2)}, u32[]{:S(2)}) collective-permute-start(f32[4,128,128]{2,1,0:T(8,128)S(1)} %fusion.80), channel_id=1, source_target_pairs={{0,4},{2,6},{4,8},{6,10},{8,12},{10,14},{1,5},{3,7},{5,9},{7,11},{... | collective-permute-start | bytes 786440 | tf_op jit(solution)/shard_map/ppermute | solution.py:64
  104.2 1.7 multiply_convert_fusion.1
  105.9 2.1 %collective-permute-done.18 = f32[4,128,128]{2,1,0:T(8,128)S(1)} collective-permute-done((f32[4,128,128]{2,1,0:T(8,128)S(1)}, f32[4,128,128]{2,1,0:T(8,128)S(1)}, u32[]{:S(2)}, u32[]{:S(2)}) %collective-permute-start.18) | collective-permute-done | bytes 262176 | tf_op jit(solution)/shard_map/ppermute | solution.py:64
  108.1 5.6 %collective-permute-start.19 = (f32[4,128,128]{2,1,0:T(8,128)S(1)}, f32[4,128,128]{2,1,0:T(8,128)S(1)}, u32[]{:S(2)}, u32[]{:S(2)}) collective-permute-start(f32[4,128,128]{2,1,0:T(8,128)S(1)} %add.276), channel_id=1, source_target_pairs={{0,8},{2,10},{4,12},{6,14},{1,9},{3,11},{5,13},{7,15},{16,24},{18,... | collective-permute-start | bytes 786440 | tf_op jit(solution)/shard_map/ppermute | solution.py:64
  114.2 3.2 %collective-permute-done.19 = f32[4,128,128]{2,1,0:T(8,128)S(1)} collective-permute-done((f32[4,128,128]{2,1,0:T(8,128)S(1)}, f32[4,128,128]{2,1,0:T(8,128)S(1)}, u32[]{:S(2)}, u32[]{:S(2)}) %collective-permute-start.19) | collective-permute-done | bytes 262176 | tf_op jit(solution)/shard_map/ppermute | solution.py:64
  122.0 1.8 %copy.18 = bf16[256,512]{1,0:T(8,128)(2,1)} copy(bf16[256,512]{0,1:T(8,128)(2,1)} %bitcast.118) | data formatting | bytes 524288 | tf_op jit(solution)/shard_map/squeeze | solution.py:146
  124.7 1.6 multiply_convert_fusion
  128.1 2.0 %maximum_select_fusion = bf16[256,1024]{1,0:T(8,128)(2,1)} fusion(bf16[256,512]{1,0:T(8,128)(2,1)} %collective-permute-done.20, bf16[256,512]{1,0:T(8,128)(2,1)S(1)} %copy-done.19, pred[]{:T(512)S(6)} %eq.13), kind=kLoop, calls=%fused_computation.29 | loop fusion | flops 2359296 | bytes 1048577 | tf_op jit(solution)/shard_map/jit(_where)/select_n | solution.py:147
  132.2 8.5 %collective-permute-done.22 = f32[4,128,128]{2,1,0:T(8,128)S(1)} collective-permute-done((f32[4,128,128]{2,1,0:T(8,128)S(1)}, f32[4,128,128]{2,1,0:T(8,128)S(1)}, u32[]{:S(2)}, u32[]{:S(2)}) %collective-permute-start.22) | collective-permute-done | bytes 262176 | tf_op jit(solution)/shard_map/ppermute | solution.py:64
  142.4 10.7 %collective-permute-done.23 = f32[4,128,128]{2,1,0:T(8,128)S(1)} collective-permute-done((f32[4,128,128]{2,1,0:T(8,128)S(1)}, f32[4,128,128]{2,1,0:T(8,128)S(1)}, u32[]{:S(2)}, u32[]{:S(2)}) %collective-permute-start.23) | collective-permute-done | bytes 262176 | tf_op jit(solution)/shard_map/ppermute | solution.py:64
  153.2 1.4 collective-permute-start.24
  154.9 14.2 %collective-permute-done.24 = f32[4,128,128]{2,1,0:T(8,128)S(1)} collective-permute-done((f32[4,128,128]{2,1,0:T(8,128)S(1)}, f32[4,128,128]{2,1,0:T(8,128)S(1)}, u32[]{:S(2)}, u32[]{:S(2)}) %collective-permute-start.24) | collective-permute-done | bytes 262176 | tf_op jit(solution)/shard_map/ppermute | solution.py:64
  174.7 1.8 %collective-permute-done.25 = f32[256,2048]{1,0:T(8,128)S(1)} collective-permute-done((f32[256,2048]{1,0:T(8,128)S(1)}, f32[256,2048]{1,0:T(8,128)S(1)}, u32[]{:S(2)}, u32[]{:S(2)}) %collective-permute-start.25) | collective-permute-done | bytes 2097184 | tf_op jit(solution)/shard_map/ppermute | solution.py:17
  (151 shorter events, 46.7 us)
Async XLA Ops:
  3.6 2.1 %collective-permute-start.1 = (bf16[128,1536]{1,0:T(8,128)(2,1)}, bf16[128,1536]{1,0:T(8,128)(2,1)}, u32[]{:S(2)}, u32[]{:S(2)}) collective-permute-start(bf16[128,1536]{1,0:T(8,128)(2,1)} %pad_maximum_fusion.5), channel_id=1, source_target_pairs={{0,1},{1,0},{2,3},{3,2},{4,5},{5,4},{6,7},{7,6},{8,9},{9,8},{10,11... | collective-permute-start | bytes 1179656 | tf_op jit(solution)/shard_map/ppermute | solution.py:17
  5.2 113.7 %collective-permute-start.21 = (bf16[256,512]{0,1:T(8,128)(2,1)}, bf16[256,512]{0,1:T(8,128)(2,1)}, u32[]{:S(2)}, u32[]{:S(2)}) collective-permute-start(bf16[256,512]{0,1:T(8,128)(2,1)} %get-tuple-element.37), channel_id=1, source_target_pairs={{0,1},{1,0},{2,3},{3,2},{4,5},{5,4},{6,7},{7,6},{8,9},{9,8},{10,11... | collective-permute-start | bytes 786440 | tf_op jit(solution)/shard_map/ppermute | solution.py:17
  6.8 10.5 %copy-start.21 = (s32[8]{0:T(128)S(1)}, s32[8]{0:T(128)}, u32[]{:S(2)}) copy-start(s32[8]{0:T(128)} %constant.116.clone) | copy-start | bytes 100
  7.7 16.3 %collective-permute-start.2 = (bf16[256,1024]{1,0:T(8,128)(2,1)}, bf16[256,1024]{1,0:T(8,128)(2,1)S(1)}, u32[]{:S(2)}, u32[]{:S(2)}) collective-permute-start(bf16[256,1024]{1,0:T(8,128)(2,1)} %constant_dynamic-slice_fusion.7), channel_id=1, source_target_pairs={{0,4},{4,8},{8,12},{12,14},{14,10},{10,6},{6,2},{2,0},{1,5},{5,9},... | collective-permute-start | bytes 1572872 | tf_op jit(solution)/shard_map/ppermute | solution.py:47
  12.0 65.6 %collective-permute-start = (bf16[256,2048]{1,0:T(8,128)(2,1)}, bf16[256,2048]{1,0:T(8,128)(2,1)}, u32[]{:S(2)}, u32[]{:S(2)}) collective-permute-start(bf16[256,2048]{1,0:T(8,128)(2,1)} %add_convert_fusion.1), channel_id=1, source_target_pairs={{0,1},{1,0},{2,3},{3,2},{4,5},{5,4},{6,7},{7,6},{8,9},{9,8},{10,11... | collective-permute-start | bytes 3145736 | tf_op jit(solution)/shard_map/ppermute | solution.py:17
  12.0 10.4 %collective-permute-start.16 = (s32[2,2]{1,0:T(2,128)S(1)}, s32[2,2]{1,0:T(2,128)S(1)}, u32[]{:S(2)}, u32[]{:S(2)}) collective-permute-start(s32[2,2]{1,0:T(2,128)S(1)} %bitcast.119), channel_id=1, source_target_pairs={{0,1},{1,0},{2,3},{3,2},{4,5},{5,4},{6,7},{7,6},{8,9},{9,8},{10,11... | collective-permute-start | bytes 56 | tf_op jit(solution)/shard_map/ppermute | solution.py:17
  23.1 14.1 %collective-permute-start.4 = (bf16[256,1024]{1,0:T(8,128)(2,1)}, bf16[256,1024]{1,0:T(8,128)(2,1)S(1)}, u32[]{:S(2)}, u32[]{:S(2)}) collective-permute-start(bf16[256,1024]{1,0:T(8,128)(2,1)} %constant_dynamic-slice_fusion.7), channel_id=1, source_target_pairs={{0,2},{4,0},{8,4},{12,8},{14,12},{10,14},{6,10},{2,6},{1,3},{5,1},... | collective-permute-start | bytes 1572872 | tf_op jit(solution)/shard_map/ppermute | solution.py:50
  24.0 15.2 %collective-permute-start.6 = (bf16[256,1024]{1,0:T(8,128)(2,1)S(1)}, bf16[256,1024]{1,0:T(8,128)(2,1)S(1)}, u32[]{:S(2)}, u32[]{:S(2)}) collective-permute-start(bf16[256,1024]{1,0:T(8,128)(2,1)S(1)} %collective-permute-done.2), channel_id=1, source_target_pairs={{0,4},{4,8},{8,12},{12,14},{14,10},{10,6},{6,2},{2,0},{1,5},{5,9},... | collective-permute-start | bytes 1572872 | tf_op jit(solution)/shard_map/ppermute | solution.py:47
  26.3 12.5 %collective-permute-start.3 = (bf16[256,512]{1,0:T(8,128)(2,1)S(1)}, bf16[256,512]{1,0:T(8,128)(2,1)S(1)}, u32[]{:S(2)}, u32[]{:S(2)}) collective-permute-start(bf16[256,512]{1,0:T(8,128)(2,1)S(1)} %constant_dynamic-slice_fusion.6), channel_id=1, source_target_pairs={{0,16},{16,0},{1,17},{17,1},{2,18},{18,2},{3,19},{19,3},{4,20},{20... | collective-permute-start | bytes 786440 | tf_op jit(solution)/shard_map/ppermute | solution.py:41
  37.2 7.4 %collective-permute-start.5 = (bf16[256,512]{1,0:T(8,128)(2,1)S(1)}, bf16[256,512]{1,0:T(8,128)(2,1)S(1)}, u32[]{:S(2)}, u32[]{:S(2)}) collective-permute-start(bf16[256,512]{1,0:T(8,128)(2,1)S(1)} %constant_dynamic-slice_fusion.5), channel_id=1, source_target_pairs={{0,16},{16,0},{1,17},{17,1},{2,18},{18,2},{3,19},{19,3},{4,20},{20... | collective-permute-start | bytes 786440 | tf_op jit(solution)/shard_map/ppermute | solution.py:41
  38.7 12.7 %collective-permute-start.8 = (bf16[256,1024]{1,0:T(8,128)(2,1)S(1)}, bf16[256,1024]{1,0:T(8,128)(2,1)S(1)}, u32[]{:S(2)}, u32[]{:S(2)}) collective-permute-start(bf16[256,1024]{1,0:T(8,128)(2,1)S(1)} %collective-permute-done.4), channel_id=1, source_target_pairs={{0,2},{4,0},{8,4},{12,8},{14,12},{10,14},{6,10},{2,6},{1,3},{5,1},... | collective-permute-start | bytes 1572872 | tf_op jit(solution)/shard_map/ppermute | solution.py:50
  39.2 13.5 %collective-permute-start.10 = (bf16[256,1024]{1,0:T(8,128)(2,1)S(1)}, bf16[256,1024]{1,0:T(8,128)(2,1)S(1)}, u32[]{:S(2)}, u32[]{:S(2)}) collective-permute-start(bf16[256,1024]{1,0:T(8,128)(2,1)S(1)} %collective-permute-done.6), channel_id=1, source_target_pairs={{0,4},{4,8},{8,12},{12,14},{14,10},{10,6},{6,2},{2,0},{1,5},{5,9},... | collective-permute-start | bytes 1572872 | tf_op jit(solution)/shard_map/ppermute | solution.py:47
  44.6 7.5 %collective-permute-start.7 = (bf16[256,512]{1,0:T(8,128)(2,1)S(1)}, bf16[256,512]{1,0:T(8,128)(2,1)S(1)}, u32[]{:S(2)}, u32[]{:S(2)}) collective-permute-start(bf16[256,512]{1,0:T(8,128)(2,1)S(1)} %constant_dynamic-slice_fusion.4), channel_id=1, source_target_pairs={{0,16},{16,0},{1,17},{17,1},{2,18},{18,2},{3,19},{19,3},{4,20},{20... | collective-permute-start | bytes 786440 | tf_op jit(solution)/shard_map/ppermute | solution.py:41
  51.5 7.0 %collective-permute-start.9 = (bf16[256,512]{1,0:T(8,128)(2,1)S(1)}, bf16[256,512]{1,0:T(8,128)(2,1)S(1)}, u32[]{:S(2)}, u32[]{:S(2)}) collective-permute-start(bf16[256,512]{1,0:T(8,128)(2,1)S(1)} %constant_dynamic-slice_fusion.3), channel_id=1, source_target_pairs={{0,16},{16,0},{1,17},{17,1},{2,18},{18,2},{3,19},{19,3},{4,20},{20... | collective-permute-start | bytes 786440 | tf_op jit(solution)/shard_map/ppermute | solution.py:41
  52.1 11.5 %collective-permute-start.12 = (bf16[256,1024]{1,0:T(8,128)(2,1)S(1)}, bf16[256,1024]{1,0:T(8,128)(2,1)S(1)}, u32[]{:S(2)}, u32[]{:S(2)}) collective-permute-start(bf16[256,1024]{1,0:T(8,128)(2,1)S(1)} %collective-permute-done.8), channel_id=1, source_target_pairs={{0,2},{4,0},{8,4},{12,8},{14,12},{10,14},{6,10},{2,6},{1,3},{5,1},... | collective-permute-start | bytes 1572872 | tf_op jit(solution)/shard_map/ppermute | solution.py:50
  52.7 12.5 %collective-permute-start.14 = (bf16[256,1024]{1,0:T(8,128)(2,1)S(1)}, bf16[256,1024]{1,0:T(8,128)(2,1)S(1)}, u32[]{:S(2)}, u32[]{:S(2)}) collective-permute-start(bf16[256,1024]{1,0:T(8,128)(2,1)S(1)} %collective-permute-done.10), channel_id=1, source_target_pairs={{0,4},{4,8},{8,12},{12,14},{14,10},{10,6},{6,2},{2,0},{1,5},{5,9},... | collective-permute-start | bytes 1572872 | tf_op jit(solution)/shard_map/ppermute | solution.py:47
  58.4 8.2 %collective-permute-start.11 = (bf16[256,512]{1,0:T(8,128)(2,1)S(1)}, bf16[256,512]{1,0:T(8,128)(2,1)S(1)}, u32[]{:S(2)}, u32[]{:S(2)}) collective-permute-start(bf16[256,512]{1,0:T(8,128)(2,1)S(1)} %constant_dynamic-slice_fusion.2), channel_id=1, source_target_pairs={{0,16},{16,0},{1,17},{17,1},{2,18},{18,2},{3,19},{19,3},{4,20},{20... | collective-permute-start | bytes 786440 | tf_op jit(solution)/shard_map/ppermute | solution.py:41
  63.6 9.3 %collective-permute-start.13 = (bf16[256,512]{1,0:T(8,128)(2,1)S(1)}, bf16[256,512]{1,0:T(8,128)(2,1)S(1)}, u32[]{:S(2)}, u32[]{:S(2)}) collective-permute-start(bf16[256,512]{1,0:T(8,128)(2,1)S(1)} %constant_dynamic-slice_fusion.1), channel_id=1, source_target_pairs={{0,16},{16,0},{1,17},{17,1},{2,18},{18,2},{3,19},{19,3},{4,20},{20... | collective-permute-start | bytes 786440 | tf_op jit(solution)/shard_map/ppermute | solution.py:41
  65.2 10.9 %collective-permute-start.15 = (bf16[256,512]{1,0:T(8,128)(2,1)S(1)}, bf16[256,512]{1,0:T(8,128)(2,1)S(1)}, u32[]{:S(2)}, u32[]{:S(2)}) collective-permute-start(bf16[256,512]{1,0:T(8,128)(2,1)S(1)} %constant_dynamic-slice_fusion), channel_id=1, source_target_pairs={{0,16},{16,0},{1,17},{17,1},{2,18},{18,2},{3,19},{19,3},{4,20},{20... | collective-permute-start | bytes 786440 | tf_op jit(solution)/shard_map/ppermute | solution.py:41
  90.2 8.1 %collective-permute-start.17 = (f32[4,128,128]{2,1,0:T(8,128)S(1)}, f32[4,128,128]{2,1,0:T(8,128)}, u32[]{:S(2)}, u32[]{:S(2)}) collective-permute-start(f32[4,128,128]{2,1,0:T(8,128)S(1)} %fusion.24), channel_id=1, source_target_pairs={{0,2},{2,4},{4,6},{6,8},{8,10},{10,12},{12,14},{1,3},{3,5},{5,7},{... | collective-permute-start | bytes 786440 | tf_op jit(solution)/shard_map/ppermute | solution.py:64
  98.3 20.2 %copy-start.5 = (bf16[2,256,4,128]{1,3,2,0:T(8,128)(2,1)}, bf16[2,256,4,128]{1,3,2,0:T(8,128)(2,1)S(1)}, u32[]{:S(2)}) copy-start(bf16[2,256,4,128]{1,3,2,0:T(8,128)(2,1)S(1)} %copy.23) | copy-start | bytes 1572868
  99.7 8.4 %collective-permute-start.18 = (f32[4,128,128]{2,1,0:T(8,128)S(1)}, f32[4,128,128]{2,1,0:T(8,128)S(1)}, u32[]{:S(2)}, u32[]{:S(2)}) collective-permute-start(f32[4,128,128]{2,1,0:T(8,128)S(1)} %fusion.80), channel_id=1, source_target_pairs={{0,4},{2,6},{4,8},{6,10},{8,12},{10,14},{1,5},{3,7},{5,9},{7,11},{... | collective-permute-start | bytes 786440 | tf_op jit(solution)/shard_map/ppermute | solution.py:64
  105.9 12.6 %copy-start.7 = (bf16[2,4,256,256]{3,2,1,0:T(8,128)(2,1)}, bf16[2,4,256,256]{3,2,1,0:T(8,128)(2,1)S(1)}, u32[]{:S(2)}) copy-start(bf16[2,4,256,256]{3,2,1,0:T(8,128)(2,1)S(1)} %multiply_convert_fusion.1) | copy-start | bytes 3145732
  105.9 11.5 %copy-start.10 = (f32[2,4,128,128]{3,2,1,0:T(8,128)S(1)}, f32[2,4,128,128]{3,2,1,0:T(8,128)}, u32[]{:S(2)}) copy-start(f32[2,4,128,128]{3,2,1,0:T(8,128)} %copy-done.9) | copy-start | bytes 1572868
  108.1 9.3 %collective-permute-start.19 = (f32[4,128,128]{2,1,0:T(8,128)S(1)}, f32[4,128,128]{2,1,0:T(8,128)S(1)}, u32[]{:S(2)}, u32[]{:S(2)}) collective-permute-start(f32[4,128,128]{2,1,0:T(8,128)S(1)} %add.276), channel_id=1, source_target_pairs={{0,8},{2,10},{4,12},{6,14},{1,9},{3,11},{5,13},{7,15},{16,24},{18,... | collective-permute-start | bytes 786440 | tf_op jit(solution)/shard_map/ppermute | solution.py:64
  123.8 4.3 %collective-permute-start.20 = (bf16[256,512]{1,0:T(8,128)(2,1)}, bf16[256,512]{1,0:T(8,128)(2,1)}, u32[]{:S(2)}, u32[]{:S(2)}) collective-permute-start(bf16[256,512]{1,0:T(8,128)(2,1)} %copy.18), channel_id=1, source_target_pairs={{0,1},{1,0},{2,3},{3,2},{4,5},{5,4},{6,7},{7,6},{8,9},{9,8},{10,11... | collective-permute-start | bytes 786440 | tf_op jit(solution)/shard_map/ppermute | solution.py:17
  130.1 10.6 %collective-permute-start.22 = (f32[4,128,128]{2,1,0:T(8,128)S(1)}, f32[4,128,128]{2,1,0:T(8,128)S(1)}, u32[]{:S(2)}, u32[]{:S(2)}) collective-permute-start(f32[4,128,128]{2,1,0:T(8,128)S(1)} %bitcast_add_fusion), channel_id=1, source_target_pairs={{2,0},{4,2},{6,4},{8,6},{10,8},{12,10},{14,12},{3,1},{5,3},{7,5},{... | collective-permute-start | bytes 786440 | tf_op jit(solution)/shard_map/ppermute | solution.py:64
  131.4 10.6 %copy-start.8 = (bf16[2,4,256,256]{3,2,1,0:T(8,128)(2,1)S(1)}, bf16[2,4,256,256]{3,2,1,0:T(8,128)(2,1)}, u32[]{:S(2)}) copy-start(bf16[2,4,256,256]{3,2,1,0:T(8,128)(2,1)} %copy-done.7) | copy-start | bytes 3145732
  140.8 12.3 %collective-permute-start.23 = (f32[4,128,128]{2,1,0:T(8,128)S(1)}, f32[4,128,128]{2,1,0:T(8,128)S(1)}, u32[]{:S(2)}, u32[]{:S(2)}) collective-permute-start(f32[4,128,128]{2,1,0:T(8,128)S(1)} %fusion.79), channel_id=1, source_target_pairs={{4,0},{6,2},{8,4},{10,6},{12,8},{14,10},{5,1},{7,3},{9,5},{11,7},{... | collective-permute-start | bytes 786440 | tf_op jit(solution)/shard_map/ppermute | solution.py:64
  153.2 16.0 %copy-start.12 = (bf16[2,256,4,128]{3,2,1,0:T(4,128)(2,1)S(1)}, bf16[2,256,4,128]{3,2,1,0:T(4,128)(2,1)}, u32[]{:S(2)}) copy-start(bf16[2,256,4,128]{3,2,1,0:T(4,128)(2,1)} %copy-done.11) | copy-start | bytes 1572868
  153.2 15.9 %collective-permute-start.24 = (f32[4,128,128]{2,1,0:T(8,128)S(1)}, f32[4,128,128]{2,1,0:T(8,128)S(1)}, u32[]{:S(2)}, u32[]{:S(2)}) collective-permute-start(f32[4,128,128]{2,1,0:T(8,128)S(1)} %add.288), channel_id=1, source_target_pairs={{8,0},{10,2},{12,4},{14,6},{9,1},{11,3},{13,5},{15,7},{24,16},{26,... | collective-permute-start | bytes 786440 | tf_op jit(solution)/shard_map/ppermute | solution.py:64
  172.3 4.2 %collective-permute-start.25 = (f32[256,2048]{1,0:T(8,128)S(1)}, f32[256,2048]{1,0:T(8,128)S(1)}, u32[]{:S(2)}, u32[]{:S(2)}) collective-permute-start(f32[256,2048]{1,0:T(8,128)S(1)} %fusion), channel_id=1, source_target_pairs={{0,1},{1,0},{2,3},{3,2},{4,5},{5,4},{6,7},{7,6},{8,9},{9,8},{10,11... | collective-permute-start | bytes 6291464 | tf_op jit(solution)/shard_map/ppermute | solution.py:17
  (18 other events, 59.4 us)

commit v12 on v11

--- a/solution.py
+++ b/solution.py
@@ -143,13 +143,6 @@
     normed = mixed / root
 
     out_b = normed.astype(bf16).reshape(2, tok, half)
-    out_recv = swap(out_b[1])
-    output = jnp.where(
-        first,
-        jnp.concatenate([out_b[0], out_recv], axis=1),
-        jnp.concatenate([out_recv, out_b[0]], axis=1),
-    )
-
     cot = cotangent.reshape(tok, 2, half)
     cot_mine = jnp.where(first, cot[:, 0], cot[:, 1])
     cot_other = jnp.where(first, cot[:, 1], cot[:, 0])
@@ -157,12 +150,18 @@
     d_mixed = (grad_out - normed * jnp.mean(grad_out * normed, axis=-1, keepdims=True)) / root
     d_mixed_b = d_mixed.astype(bf16)
     grad_local = jnp.einsum("jthd,jthe->jhde", query, d_mixed_b, preferred_element_type=f32)
-    output, grad_local = lax.optimization_barrier((output, grad_local))
 
     later1 = exclusive_scan(grad_local[0] + grad_local[1], chips, True)
     later_mine = jnp.where(first, later1 + grad_local[1], later1)
     later_other = jnp.where(first, later1, later1 + grad_local[0])
     later_b = jnp.stack([later_mine, later_other]).astype(bf16)
+    out_send, later_b = lax.optimization_barrier((out_b[1], later_b))
+    out_recv = swap(out_send)
+    output = jnp.where(
+        first,
+        jnp.concatenate([out_b[0], out_recv], axis=1),
+        jnp.concatenate([out_recv, out_b[0]], axis=1),
+    )
 
     d_attn = (
         jnp.einsum("jthe,jshe->jhts", d_mixed_b, value, preferred_element_type=f32) * allow[:, None]

time: 179 us -> 173 us (0.966)
  the two profiles are of different devices: /device:TPU:0 before, /device:TPU:15 now
where the time goes in v12:
time: 173 us; the launch traced here: 170 us
  waiting for transfers between devices  60.2 us (35%)
  starting transfers between devices  39.8 us (23%)
  matrix products  25.1 us (15%)
  local copies, waits for them, and re-layouts  20.7 us (12%)
  other arithmetic  14 us (8%)
  between operations  10.2 us (6%)
    ppermute x6, waiting for transfers between devices, exclusive_scan(): got = lax.ppermute(incl, 'chip', perm)  22.5 us
    ppermute x3, waiting for transfers between devices, ring_gather(): bwd = lax.ppermute(bwd, 'chip', behind)  20.2 us
    ppermute x6, starting transfers between devices, exclusive_scan(): got = lax.ppermute(incl, 'chip', perm)  16.7 us
    ppermute x7, waiting for transfers between devices, land(): return (piece, lax.ppermute(sent, 'groups', partner))  16.3 us
    ppermute x6, starting transfers between devices, swap(): return lax.ppermute(x, 'core', [(0, 1), (1, 0)])  14.2 us
    dot_general x3, matrix products, project(): jnp.dot(x_pair, w, preferred_element_type=f32).astype(bf16)  9.38 us
    unnamed x42, local copies, waits for them, and re-layouts  6.5 us
    reshape x5, local copies, waits for them, and re-layouts, project(): jnp.dot(x_pair, w, preferred_element_type=f32).astype(bf16)  4.54 us
  transfers between devices with their start and end apart: 26, of which 14 were waited for; matrix products, arithmetic and copies ran while one was open for 24% of the time, Pallas kernels for 0%

profile of v12, /device:TPU:15, one launch (start us, length us, event | category | flops | bytes accessed | tf_op | source)
XLA Modules:
  0.0 170.0 jit_solution(12636661515863624020)
XLA Ops:
  8.1 1.4 add_convert_fusion.1
  21.1 1.3 collective-permute-start.4
  24.5 9.8 %collective-permute-done.4 = bf16[256,1024]{1,0:T(8,128)(2,1)S(1)} collective-permute-done((bf16[256,1024]{1,0:T(8,128)(2,1)}, bf16[256,1024]{1,0:T(8,128)(2,1)S(1)}, u32[]{:S(2)}, u32[]{:S(2)}) %collective-permute-start.4) | collective-permute-done | bytes 524320 | tf_op jit(solution)/shard_map/ppermute | solution.py:50
  34.7 1.3 collective-permute-start.8
  36.3 4.5 %collective-permute-done.5 = bf16[256,512]{1,0:T(8,128)(2,1)S(1)} collective-permute-done((bf16[256,512]{1,0:T(8,128)(2,1)S(1)}, bf16[256,512]{1,0:T(8,128)(2,1)S(1)}, u32[]{:S(2)}, u32[]{:S(2)}) %collective-permute-start.5) | collective-permute-done | bytes 262176 | tf_op jit(solution)/shard_map/ppermute | solution.py:41
  41.3 5.2 %collective-permute-done.8 = bf16[256,1024]{1,0:T(8,128)(2,1)S(1)} collective-permute-done((bf16[256,1024]{1,0:T(8,128)(2,1)S(1)}, bf16[256,1024]{1,0:T(8,128)(2,1)S(1)}, u32[]{:S(2)}, u32[]{:S(2)}) %collective-permute-start.8) | collective-permute-done | bytes 524320 | tf_op jit(solution)/shard_map/ppermute | solution.py:50
  47.8 1.3 collective-permute-start.12
  49.4 2.3 %collective-permute-done.9 = bf16[256,512]{1,0:T(8,128)(2,1)S(1)} collective-permute-done((bf16[256,512]{1,0:T(8,128)(2,1)S(1)}, bf16[256,512]{1,0:T(8,128)(2,1)S(1)}, u32[]{:S(2)}, u32[]{:S(2)}) %collective-permute-start.9) | collective-permute-done | bytes 262176 | tf_op jit(solution)/shard_map/ppermute | solution.py:41
  53.1 5.2 %collective-permute-done.12 = bf16[256,1024]{1,0:T(8,128)(2,1)S(1)} collective-permute-done((bf16[256,1024]{1,0:T(8,128)(2,1)S(1)}, bf16[256,1024]{1,0:T(8,128)(2,1)S(1)}, u32[]{:S(2)}, u32[]{:S(2)}) %collective-permute-start.12) | collective-permute-done | bytes 524320 | tf_op jit(solution)/shard_map/ppermute | solution.py:50
  60.2 4.3 %collective-permute-done.13 = bf16[256,512]{1,0:T(8,128)(2,1)S(1)} collective-permute-done((bf16[256,512]{1,0:T(8,128)(2,1)S(1)}, bf16[256,512]{1,0:T(8,128)(2,1)S(1)}, u32[]{:S(2)}, u32[]{:S(2)}) %collective-permute-start.13) | collective-permute-done | bytes 262176 | tf_op jit(solution)/shard_map/ppermute | solution.py:41
  64.7 5.1 %collective-permute-done.15 = bf16[256,512]{1,0:T(8,128)(2,1)S(1)} collective-permute-done((bf16[256,512]{1,0:T(8,128)(2,1)S(1)}, bf16[256,512]{1,0:T(8,128)(2,1)S(1)}, u32[]{:S(2)}, u32[]{:S(2)}) %collective-permute-start.15) | collective-permute-done | bytes 262176 | tf_op jit(solution)/shard_map/ppermute | solution.py:41
  69.9 1.3 copy-done
  71.3 1.4 copy-done.3
  72.7 2.8 %convolution_convert_fusion = bf16[512,512]{1,0:T(8,128)(2,1)S(1)} fusion(bf16[2048,512]{1,0:T(8,128)(2,1)S(1)} %get-tuple-element.40, bf16[256,2048]{1,0:T(8,128)(2,1)} %collective-permute-done, bf16[256,2048]{1,0:T(8,128)(2,1)} %add_convert_fusion.1), kind=kOutput, calls=%fused_computation.16 | convolution fusion | flops 1078198272 | bytes 4718592 | tf_op jit(solution)/shard_map/dot_general | solution.py:123
  75.6 3.8 %convolution_convert_fusion.2 = bf16[512,512]{1,0:T(8,128)(2,1)} fusion(bf16[2048,512]{1,0:T(8,128)(2,1)S(1)} %get-tuple-element.16, bf16[256,2048]{1,0:T(8,128)(2,1)} %collective-permute-done, bf16[256,2048]{1,0:T(8,128)(2,1)} %add_convert_fusion.1), kind=kOutput, calls=%fused_computation.18 | convolution fusion | flops 1078198272 | bytes 4718592 | tf_op jit(solution)/shard_map/dot_general | solution.py:123
  81.6 1.5 fusion.18
  84.0 4.3 %collective-permute-start.17 = (f32[4,128,128]{2,1,0:T(8,128)S(1)}, f32[4,128,128]{2,1,0:T(8,128)}, u32[]{:S(2)}, u32[]{:S(2)}) collective-permute-start(f32[4,128,128]{2,1,0:T(8,128)S(1)} %fusion.24), channel_id=1, source_target_pairs={{0,2},{2,4},{4,6},{6,8},{8,10},{10,12},{12,14},{1,3},{3,5},{5,7},{... | collective-permute-start | bytes 786440 | tf_op jit(solution)/shard_map/ppermute | solution.py:64
  88.3 2.8 %convolution_convert_fusion.1 = bf16[512,512]{1,0:T(8,128)(2,1)S(1)} fusion(bf16[2048,512]{1,0:T(8,128)(2,1)S(1)} %copy-done.1, bf16[256,2048]{1,0:T(8,128)(2,1)} %collective-permute-done, bf16[256,2048]{1,0:T(8,128)(2,1)} %add_convert_fusion.1), kind=kOutput, calls=%fused_computation.17 | convolution fusion | flops 1078198272 | bytes 4718592 | tf_op jit(solution)/shard_map/dot_general | solution.py:123
  94.4 3.1 %collective-permute-start.18 = (f32[4,128,128]{2,1,0:T(8,128)S(1)}, f32[4,128,128]{2,1,0:T(8,128)S(1)}, u32[]{:S(2)}, u32[]{:S(2)}) collective-permute-start(f32[4,128,128]{2,1,0:T(8,128)S(1)} %fusion.81), channel_id=1, source_target_pairs={{0,4},{2,6},{4,8},{6,10},{8,12},{10,14},{1,5},{3,7},{5,9},{7,11},{... | collective-permute-start | bytes 786440 | tf_op jit(solution)/shard_map/ppermute | solution.py:64
  97.6 1.7 multiply_convert_fusion.1
  99.3 2.3 %collective-permute-done.18 = f32[4,128,128]{2,1,0:T(8,128)S(1)} collective-permute-done((f32[4,128,128]{2,1,0:T(8,128)S(1)}, f32[4,128,128]{2,1,0:T(8,128)S(1)}, u32[]{:S(2)}, u32[]{:S(2)}) %collective-permute-start.18) | collective-permute-done | bytes 262176 | tf_op jit(solution)/shard_map/ppermute | solution.py:64
  101.6 2.9 %collective-permute-start.19 = (f32[4,128,128]{2,1,0:T(8,128)S(1)}, f32[4,128,128]{2,1,0:T(8,128)S(1)}, u32[]{:S(2)}, u32[]{:S(2)}) collective-permute-start(f32[4,128,128]{2,1,0:T(8,128)S(1)} %add.276), channel_id=1, source_target_pairs={{0,8},{2,10},{4,12},{6,14},{1,9},{3,11},{5,13},{7,15},{16,24},{18,... | collective-permute-start | bytes 786440 | tf_op jit(solution)/shard_map/ppermute | solution.py:64
  105.0 6.1 %collective-permute-done.19 = f32[4,128,128]{2,1,0:T(8,128)S(1)} collective-permute-done((f32[4,128,128]{2,1,0:T(8,128)S(1)}, f32[4,128,128]{2,1,0:T(8,128)S(1)}, u32[]{:S(2)}, u32[]{:S(2)}) %collective-permute-start.19) | collective-permute-done | bytes 262176 | tf_op jit(solution)/shard_map/ppermute | solution.py:64
  115.8 3.2 %collective-permute-start.21 = (f32[4,128,128]{2,1,0:T(8,128)S(1)}, f32[4,128,128]{2,1,0:T(8,128)S(1)}, u32[]{:S(2)}, u32[]{:S(2)}) collective-permute-start(f32[4,128,128]{2,1,0:T(8,128)S(1)} %fusion.25), channel_id=1, source_target_pairs={{2,0},{4,2},{6,4},{8,6},{10,8},{12,10},{14,12},{3,1},{5,3},{7,5},{... | collective-permute-start | bytes 786440 | tf_op jit(solution)/shard_map/ppermute | solution.py:64
  122.0 1.9 %collective-permute-done.21 = f32[4,128,128]{2,1,0:T(8,128)S(1)} collective-permute-done((f32[4,128,128]{2,1,0:T(8,128)S(1)}, f32[4,128,128]{2,1,0:T(8,128)S(1)}, u32[]{:S(2)}, u32[]{:S(2)}) %collective-permute-start.21) | collective-permute-done | bytes 262176 | tf_op jit(solution)/shard_map/ppermute | solution.py:64
  123.9 1.9 %collective-permute-start.22 = (f32[4,128,128]{2,1,0:T(8,128)S(1)}, f32[4,128,128]{2,1,0:T(8,128)S(1)}, u32[]{:S(2)}, u32[]{:S(2)}) collective-permute-start(f32[4,128,128]{2,1,0:T(8,128)S(1)} %fusion.80), channel_id=1, source_target_pairs={{4,0},{6,2},{8,4},{10,6},{12,8},{14,10},{5,1},{7,3},{9,5},{11,7},{... | collective-permute-start | bytes 786440 | tf_op jit(solution)/shard_map/ppermute | solution.py:64
  126.1 5.3 %collective-permute-done.22 = f32[4,128,128]{2,1,0:T(8,128)S(1)} collective-permute-done((f32[4,128,128]{2,1,0:T(8,128)S(1)}, f32[4,128,128]{2,1,0:T(8,128)S(1)}, u32[]{:S(2)}, u32[]{:S(2)}) %collective-permute-start.22) | collective-permute-done | bytes 262176 | tf_op jit(solution)/shard_map/ppermute | solution.py:64
  133.8 7.0 %collective-permute-done.23 = f32[4,128,128]{2,1,0:T(8,128)S(1)} collective-permute-done((f32[4,128,128]{2,1,0:T(8,128)S(1)}, f32[4,128,128]{2,1,0:T(8,128)S(1)}, u32[]{:S(2)}, u32[]{:S(2)}) %collective-permute-start.23) | collective-permute-done | bytes 262176 | tf_op jit(solution)/shard_map/ppermute | solution.py:64
  143.3 2.1 %fusion = f32[256,2048]{1,0:T(8,128)} fusion(f32[256,2048]{1,0:T(8,128)S(1)} %fusion.48, f32[256,2048]{1,0:T(8,128)S(1)} %fusion.47, bf16[256,512]{0,1:T(8,128)(2,1)S(1)} %bitcast.123, bf16[2048,512]{1,0:T(8,128)(2,1)S(1)} %copy-done.4), kind=kOutput, calls=%fused_computation.1 | convolution fusion | flops 537919488 | bytes 8650752 | tf_op jit(solution)/shard_map/dot_general | solution.py:182
  145.4 12.8 %collective-permute-start.25 = (f32[256,2048]{1,0:T(8,128)}, f32[256,2048]{1,0:T(8,128)}, u32[]{:S(2)}, u32[]{:S(2)}) collective-permute-start(f32[256,2048]{1,0:T(8,128)} %fusion), channel_id=1, source_target_pairs={{0,1},{1,0},{2,3},{3,2},{4,5},{5,4},{6,7},{7,6},{8,9},{9,8},{10,11... | collective-permute-start | bytes 6291464 | tf_op jit(solution)/shard_map/ppermute | solution.py:17
  159.3 3.7 %fusion.43 = f32[256,2048]{1,0:T(8,128)} fusion(bf16[256,512]{0,1:T(8,128)(2,1)S(1)} %bitcast.119, bf16[2048,512]{1,0:T(8,128)(2,1)} %copy-done), kind=kOutput, calls=%fused_computation.123 | convolution fusion | flops 536870912 | bytes 4456448 | tf_op jit(solution)/shard_map/dot_general | solution.py:181
  167.2 2.8 %add_convert_fusion = bf16[256,2048]{1,0:T(8,128)(2,1)} fusion(f32[256,2048]{1,0:T(8,128)S(1)} %fusion.1, f32[256,2048]{1,0:T(8,128)} %collective-permute-done.25), kind=kLoop, calls=%fused_computation.5 | loop fusion | flops 1048576 | bytes 5242880 | tf_op jit(solution)/shard_map/convert_element_type | solution.py:187
  (146 shorter events, 43.4 us)
Async XLA Ops:
  3.6 2.4 %collective-permute-start.1 = (bf16[128,1536]{1,0:T(8,128)(2,1)}, bf16[128,1536]{1,0:T(8,128)(2,1)}, u32[]{:S(2)}, u32[]{:S(2)}) collective-permute-start(bf16[128,1536]{1,0:T(8,128)(2,1)} %pad_maximum_fusion.5), channel_id=1, source_target_pairs={{0,1},{1,0},{2,3},{3,2},{4,5},{5,4},{6,7},{7,6},{8,9},{9,8},{10,11... | collective-permute-start | bytes 1179656 | tf_op jit(solution)/shard_map/ppermute | solution.py:17
  5.4 107.1 %collective-permute-start.20 = (bf16[256,512]{0,1:T(8,128)(2,1)}, bf16[256,512]{0,1:T(8,128)(2,1)}, u32[]{:S(2)}, u32[]{:S(2)}) collective-permute-start(bf16[256,512]{0,1:T(8,128)(2,1)} %get-tuple-element.39), channel_id=1, source_target_pairs={{0,1},{1,0},{2,3},{3,2},{4,5},{5,4},{6,7},{7,6},{8,9},{9,8},{10,11... | collective-permute-start | bytes 786440 | tf_op jit(solution)/shard_map/ppermute | solution.py:17
  7.0 8.3 %copy-start.18 = (s32[8]{0:T(128)S(1)}, s32[8]{0:T(128)}, u32[]{:S(2)}) copy-start(s32[8]{0:T(128)} %constant.116.clone) | copy-start | bytes 100
  7.9 15.4 %collective-permute-start.2 = (bf16[256,1024]{1,0:T(8,128)(2,1)}, bf16[256,1024]{1,0:T(8,128)(2,1)S(1)}, u32[]{:S(2)}, u32[]{:S(2)}) collective-permute-start(bf16[256,1024]{1,0:T(8,128)(2,1)} %constant_dynamic-slice_fusion.7), channel_id=1, source_target_pairs={{0,4},{4,8},{8,12},{12,14},{14,10},{10,6},{6,2},{2,0},{1,5},{5,9},... | collective-permute-start | bytes 1572872 | tf_op jit(solution)/shard_map/ppermute | solution.py:47
  9.5 61.8 %collective-permute-start = (bf16[256,2048]{1,0:T(8,128)(2,1)}, bf16[256,2048]{1,0:T(8,128)(2,1)}, u32[]{:S(2)}, u32[]{:S(2)}) collective-permute-start(bf16[256,2048]{1,0:T(8,128)(2,1)} %add_convert_fusion.1), channel_id=1, source_target_pairs={{0,1},{1,0},{2,3},{3,2},{4,5},{5,4},{6,7},{7,6},{8,9},{9,8},{10,11... | collective-permute-start | bytes 3145736 | tf_op jit(solution)/shard_map/ppermute | solution.py:17
  10.1 10.3 %collective-permute-start.16 = (s32[2,2]{1,0:T(2,128)S(1)}, s32[2,2]{1,0:T(2,128)S(1)}, u32[]{:S(2)}, u32[]{:S(2)}) collective-permute-start(s32[2,2]{1,0:T(2,128)S(1)} %bitcast.127), channel_id=1, source_target_pairs={{0,1},{1,0},{2,3},{3,2},{4,5},{5,4},{6,7},{7,6},{8,9},{9,8},{10,11... | collective-permute-start | bytes 56 | tf_op jit(solution)/shard_map/ppermute | solution.py:17
  21.1 13.2 %collective-permute-start.4 = (bf16[256,1024]{1,0:T(8,128)(2,1)}, bf16[256,1024]{1,0:T(8,128)(2,1)S(1)}, u32[]{:S(2)}, u32[]{:S(2)}) collective-permute-start(bf16[256,1024]{1,0:T(8,128)(2,1)} %constant_dynamic-slice_fusion.7), channel_id=1, source_target_pairs={{0,2},{4,0},{8,4},{12,8},{14,12},{10,14},{6,10},{2,6},{1,3},{5,1},... | collective-permute-start | bytes 1572872 | tf_op jit(solution)/shard_map/ppermute | solution.py:50
  23.3 12.7 %collective-permute-start.6 = (bf16[256,1024]{1,0:T(8,128)(2,1)S(1)}, bf16[256,1024]{1,0:T(8,128)(2,1)S(1)}, u32[]{:S(2)}, u32[]{:S(2)}) collective-permute-start(bf16[256,1024]{1,0:T(8,128)(2,1)S(1)} %collective-permute-done.2), channel_id=1, source_target_pairs={{0,4},{4,8},{8,12},{12,14},{14,10},{10,6},{6,2},{2,0},{1,5},{5,9},... | collective-permute-start | bytes 1572872 | tf_op jit(solution)/shard_map/ppermute | solution.py:47
  23.7 10.9 %collective-permute-start.3 = (bf16[256,512]{1,0:T(8,128)(2,1)S(1)}, bf16[256,512]{1,0:T(8,128)(2,1)S(1)}, u32[]{:S(2)}, u32[]{:S(2)}) collective-permute-start(bf16[256,512]{1,0:T(8,128)(2,1)S(1)} %constant_dynamic-slice_fusion.6), channel_id=1, source_target_pairs={{0,16},{16,0},{1,17},{17,1},{2,18},{18,2},{3,19},{19,3},{4,20},{20... | collective-permute-start | bytes 786440 | tf_op jit(solution)/shard_map/ppermute | solution.py:41
  34.4 6.5 %collective-permute-start.5 = (bf16[256,512]{1,0:T(8,128)(2,1)S(1)}, bf16[256,512]{1,0:T(8,128)(2,1)S(1)}, u32[]{:S(2)}, u32[]{:S(2)}) collective-permute-start(bf16[256,512]{1,0:T(8,128)(2,1)S(1)} %constant_dynamic-slice_fusion.5), channel_id=1, source_target_pairs={{0,16},{16,0},{1,17},{17,1},{2,18},{18,2},{3,19},{19,3},{4,20},{20... | collective-permute-start | bytes 786440 | tf_op jit(solution)/shard_map/ppermute | solution.py:41
  34.7 11.8 %collective-permute-start.8 = (bf16[256,1024]{1,0:T(8,128)(2,1)S(1)}, bf16[256,1024]{1,0:T(8,128)(2,1)S(1)}, u32[]{:S(2)}, u32[]{:S(2)}) collective-permute-start(bf16[256,1024]{1,0:T(8,128)(2,1)S(1)} %collective-permute-done.4), channel_id=1, source_target_pairs={{0,2},{4,0},{8,4},{12,8},{14,12},{10,14},{6,10},{2,6},{1,3},{5,1},... | collective-permute-start | bytes 1572872 | tf_op jit(solution)/shard_map/ppermute | solution.py:50
  36.0 13.1 %collective-permute-start.10 = (bf16[256,1024]{1,0:T(8,128)(2,1)S(1)}, bf16[256,1024]{1,0:T(8,128)(2,1)S(1)}, u32[]{:S(2)}, u32[]{:S(2)}) collective-permute-start(bf16[256,1024]{1,0:T(8,128)(2,1)S(1)} %collective-permute-done.6), channel_id=1, source_target_pairs={{0,4},{4,8},{8,12},{12,14},{14,10},{10,6},{6,2},{2,0},{1,5},{5,9},... | collective-permute-start | bytes 1572872 | tf_op jit(solution)/shard_map/ppermute | solution.py:47
  40.9 6.9 %collective-permute-start.7 = (bf16[256,512]{1,0:T(8,128)(2,1)S(1)}, bf16[256,512]{1,0:T(8,128)(2,1)S(1)}, u32[]{:S(2)}, u32[]{:S(2)}) collective-permute-start(bf16[256,512]{1,0:T(8,128)(2,1)S(1)} %constant_dynamic-slice_fusion.4), channel_id=1, source_target_pairs={{0,16},{16,0},{1,17},{17,1},{2,18},{18,2},{3,19},{19,3},{4,20},{20... | collective-permute-start | bytes 786440 | tf_op jit(solution)/shard_map/ppermute | solution.py:41
  46.5 5.3 %collective-permute-start.9 = (bf16[256,512]{1,0:T(8,128)(2,1)S(1)}, bf16[256,512]{1,0:T(8,128)(2,1)S(1)}, u32[]{:S(2)}, u32[]{:S(2)}) collective-permute-start(bf16[256,512]{1,0:T(8,128)(2,1)S(1)} %constant_dynamic-slice_fusion.3), channel_id=1, source_target_pairs={{0,16},{16,0},{1,17},{17,1},{2,18},{18,2},{3,19},{19,3},{4,20},{20... | collective-permute-start | bytes 786440 | tf_op jit(solution)/shard_map/ppermute | solution.py:41
  47.8 10.6 %collective-permute-start.12 = (bf16[256,1024]{1,0:T(8,128)(2,1)S(1)}, bf16[256,1024]{1,0:T(8,128)(2,1)S(1)}, u32[]{:S(2)}, u32[]{:S(2)}) collective-permute-start(bf16[256,1024]{1,0:T(8,128)(2,1)S(1)} %collective-permute-done.8), channel_id=1, source_target_pairs={{0,2},{4,0},{8,4},{12,8},{14,12},{10,14},{6,10},{2,6},{1,3},{5,1},... | collective-permute-start | bytes 1572872 | tf_op jit(solution)/shard_map/ppermute | solution.py:50
  49.1 10.3 %collective-permute-start.14 = (bf16[256,1024]{1,0:T(8,128)(2,1)S(1)}, bf16[256,1024]{1,0:T(8,128)(2,1)S(1)}, u32[]{:S(2)}, u32[]{:S(2)}) collective-permute-start(bf16[256,1024]{1,0:T(8,128)(2,1)S(1)} %collective-permute-done.10), channel_id=1, source_target_pairs={{0,4},{4,8},{8,12},{12,14},{14,10},{10,6},{6,2},{2,0},{1,5},{5,9},... | collective-permute-start | bytes 1572872 | tf_op jit(solution)/shard_map/ppermute | solution.py:47
  51.8 8.2 %collective-permute-start.11 = (bf16[256,512]{1,0:T(8,128)(2,1)S(1)}, bf16[256,512]{1,0:T(8,128)(2,1)S(1)}, u32[]{:S(2)}, u32[]{:S(2)}) collective-permute-start(bf16[256,512]{1,0:T(8,128)(2,1)S(1)} %constant_dynamic-slice_fusion.2), channel_id=1, source_target_pairs={{0,16},{16,0},{1,17},{17,1},{2,18},{18,2},{3,19},{19,3},{4,20},{20... | collective-permute-start | bytes 786440 | tf_op jit(solution)/shard_map/ppermute | solution.py:41
  58.4 6.1 %collective-permute-start.13 = (bf16[256,512]{1,0:T(8,128)(2,1)S(1)}, bf16[256,512]{1,0:T(8,128)(2,1)S(1)}, u32[]{:S(2)}, u32[]{:S(2)}) collective-permute-start(bf16[256,512]{1,0:T(8,128)(2,1)S(1)} %constant_dynamic-slice_fusion.1), channel_id=1, source_target_pairs={{0,16},{16,0},{1,17},{17,1},{2,18},{18,2},{3,19},{19,3},{4,20},{20... | collective-permute-start | bytes 786440 | tf_op jit(solution)/shard_map/ppermute | solution.py:41
  59.4 10.4 %collective-permute-start.15 = (bf16[256,512]{1,0:T(8,128)(2,1)S(1)}, bf16[256,512]{1,0:T(8,128)(2,1)S(1)}, u32[]{:S(2)}, u32[]{:S(2)}) collective-permute-start(bf16[256,512]{1,0:T(8,128)(2,1)S(1)} %constant_dynamic-slice_fusion), channel_id=1, source_target_pairs={{0,16},{16,0},{1,17},{17,1},{2,18},{18,2},{3,19},{19,3},{4,20},{20... | collective-permute-start | bytes 786440 | tf_op jit(solution)/shard_map/ppermute | solution.py:41
  81.6 6.6 %copy-start.1 = (bf16[2048,512]{1,0:T(8,128)(2,1)S(1)}, bf16[2048,512]{1,0:T(8,128)(2,1)}, u32[]{:S(2)}) copy-start(bf16[2048,512]{1,0:T(8,128)(2,1)} %copy-done) | copy-start | bytes 6291460
  84.0 9.3 %collective-permute-start.17 = (f32[4,128,128]{2,1,0:T(8,128)S(1)}, f32[4,128,128]{2,1,0:T(8,128)}, u32[]{:S(2)}, u32[]{:S(2)}) collective-permute-start(f32[4,128,128]{2,1,0:T(8,128)S(1)} %fusion.24), channel_id=1, source_target_pairs={{0,2},{2,4},{4,6},{6,8},{8,10},{10,12},{12,14},{1,3},{3,5},{5,7},{... | collective-permute-start | bytes 786440 | tf_op jit(solution)/shard_map/ppermute | solution.py:64
  94.4 7.1 %collective-permute-start.18 = (f32[4,128,128]{2,1,0:T(8,128)S(1)}, f32[4,128,128]{2,1,0:T(8,128)S(1)}, u32[]{:S(2)}, u32[]{:S(2)}) collective-permute-start(f32[4,128,128]{2,1,0:T(8,128)S(1)} %fusion.81), channel_id=1, source_target_pairs={{0,4},{2,6},{4,8},{6,10},{8,12},{10,14},{1,5},{3,7},{5,9},{7,11},{... | collective-permute-start | bytes 786440 | tf_op jit(solution)/shard_map/ppermute | solution.py:64
  99.3 11.8 %copy-start.7 = (f32[2,4,128,128]{3,2,1,0:T(8,128)S(1)}, f32[2,4,128,128]{3,2,1,0:T(8,128)}, u32[]{:S(2)}) copy-start(f32[2,4,128,128]{3,2,1,0:T(8,128)} %copy-done.6) | copy-start | bytes 1572868
  101.6 9.5 %collective-permute-start.19 = (f32[4,128,128]{2,1,0:T(8,128)S(1)}, f32[4,128,128]{2,1,0:T(8,128)S(1)}, u32[]{:S(2)}, u32[]{:S(2)}) collective-permute-start(f32[4,128,128]{2,1,0:T(8,128)S(1)} %add.276), channel_id=1, source_target_pairs={{0,8},{2,10},{4,12},{6,14},{1,9},{3,11},{5,13},{7,15},{16,24},{18,... | collective-permute-start | bytes 786440 | tf_op jit(solution)/shard_map/ppermute | solution.py:64
  105.0 7.6 %copy-start.13 = (bf16[256,1,512]{0,2,1:T(8,128)(2,1)S(1)}, bf16[256,1,512]{0,2,1:T(8,128)(2,1)}, u32[]{:S(2)}) copy-start(bf16[256,1,512]{0,2,1:T(8,128)(2,1)} %get-tuple-element.38) | copy-start | bytes 786436
  115.8 8.0 %collective-permute-start.21 = (f32[4,128,128]{2,1,0:T(8,128)S(1)}, f32[4,128,128]{2,1,0:T(8,128)S(1)}, u32[]{:S(2)}, u32[]{:S(2)}) collective-permute-start(f32[4,128,128]{2,1,0:T(8,128)S(1)} %fusion.25), channel_id=1, source_target_pairs={{2,0},{4,2},{6,4},{8,6},{10,8},{12,10},{14,12},{3,1},{5,3},{7,5},{... | collective-permute-start | bytes 786440 | tf_op jit(solution)/shard_map/ppermute | solution.py:64
  123.9 7.5 %collective-permute-start.22 = (f32[4,128,128]{2,1,0:T(8,128)S(1)}, f32[4,128,128]{2,1,0:T(8,128)S(1)}, u32[]{:S(2)}, u32[]{:S(2)}) collective-permute-start(f32[4,128,128]{2,1,0:T(8,128)S(1)} %fusion.80), channel_id=1, source_target_pairs={{4,0},{6,2},{8,4},{10,6},{12,8},{14,10},{5,1},{7,3},{9,5},{11,7},{... | collective-permute-start | bytes 786440 | tf_op jit(solution)/shard_map/ppermute | solution.py:64
  131.4 9.3 %collective-permute-start.23 = (f32[4,128,128]{2,1,0:T(8,128)S(1)}, f32[4,128,128]{2,1,0:T(8,128)S(1)}, u32[]{:S(2)}, u32[]{:S(2)}) collective-permute-start(f32[4,128,128]{2,1,0:T(8,128)S(1)} %add.287), channel_id=1, source_target_pairs={{8,0},{10,2},{12,4},{14,6},{9,1},{11,3},{13,5},{15,7},{24,16},{26,... | collective-permute-start | bytes 786440 | tf_op jit(solution)/shard_map/ppermute | solution.py:64
  133.1 7.8 %copy-start.9 = (bf16[2,256,4,128]{3,2,1,0:T(4,128)(2,1)S(1)}, bf16[2,256,4,128]{3,2,1,0:T(4,128)(2,1)}, u32[]{:S(2)}) copy-start(bf16[2,256,4,128]{3,2,1,0:T(4,128)(2,1)} %copy-done.8) | copy-start | bytes 1572868
  143.3 16.0 %copy-start.16 = (bf16[1,256,4,128]{1,3,2,0:T(8,128)(2,1)S(1)}, bf16[1,256,4,128]{1,3,2,0:T(8,128)(2,1)}, u32[]{:S(2)}) copy-start(bf16[1,256,4,128]{1,3,2,0:T(8,128)(2,1)} %get-tuple-element.33) | copy-start | bytes 786436
  145.4 21.7 %collective-permute-start.25 = (f32[256,2048]{1,0:T(8,128)}, f32[256,2048]{1,0:T(8,128)}, u32[]{:S(2)}, u32[]{:S(2)}) collective-permute-start(f32[256,2048]{1,0:T(8,128)} %fusion), channel_id=1, source_target_pairs={{0,1},{1,0},{2,3},{3,2},{4,5},{5,4},{6,7},{7,6},{8,9},{9,8},{10,11... | collective-permute-start | bytes 6291464 | tf_op jit(solution)/shard_map/ppermute | solution.py:17
  163.1 3.1 %collective-permute-start.24 = (bf16[256,512]{1,0:T(8,128)(2,1)S(1)}, bf16[256,512]{1,0:T(8,128)(2,1)S(1)}, u32[]{:S(2)}, u32[]{:S(2)}) collective-permute-start(bf16[256,512]{1,0:T(8,128)(2,1)S(1)} %copy.22), channel_id=1, source_target_pairs={{0,1},{1,0},{2,3},{3,2},{4,5},{5,4},{6,7},{7,6},{8,9},{9,8},{10,11... | collective-permute-start | bytes 786440 | tf_op jit(solution)/shard_map/ppermute | solution.py:17
  (15 other events, 37.9 us)

commit v13 on v12

--- a/solution.py
+++ b/solution.py
@@ -108,23 +108,22 @@
     parity = lax.axis_index("groups") % 2
     share = half
     width = 2 * half
-    mats = [jnp.zeros((chips * span, share), bf16) for _ in range(3)]
+    w_ring = jnp.zeros((chips * span, width), bf16)
+    w_x = jnp.zeros((chips * span, share), bf16)
     for src, (ringed, swapped) in ring_gather(block, chips, c, parity):
-        lower, upper = ringed[:, :share], ringed[:, share:]
-        parts = (
-            jnp.where(parity == 0, lower, swapped),
-            jnp.where(parity == 0, upper, lower),
-            jnp.where(parity == 0, swapped, upper),
-        )
-        mats = [lax.dynamic_update_slice_in_dim(m, part, src * span, axis=0) for m, part in zip(mats, parts)]
-    w_q, w_k, w_v = mats
+        w_ring = lax.dynamic_update_slice_in_dim(w_ring, ringed, src * span, axis=0)
+        w_x = lax.dynamic_update_slice_in_dim(w_x, swapped, src * span, axis=0)
+    even = parity == 0
 
     def project(w):
         return jnp.dot(x_pair, w, preferred_element_type=f32).astype(bf16).reshape(2, tok, heads, DH)
 
-    key = project(w_k)
-    value = project(w_v)
-    query = project(w_q)
+    p_lo = project(w_ring[:, :share])
+    p_hi = project(w_ring[:, share:])
+    p_x = project(w_x)
+    query = jnp.where(even, p_lo, p_x)
+    key = jnp.where(even, p_hi, p_lo)
+    value = jnp.where(even, p_x, p_hi)
 
     local = jnp.einsum("jthd,jthe->jhde", key, value, preferred_element_type=f32)
     state0 = exclusive_scan(local[0] + local[1], chips, False)
@@ -178,9 +177,12 @@
 
     def grad_rows(j):
         dims = (((1,), (1,)), ((), ()))
-        g = lax.dot_general(dq_b[j], w_q, dims, preferred_element_type=f32)
-        g = g + lax.dot_general(dk_b[j], w_k, dims, preferred_element_type=f32)
-        return g + lax.dot_general(dv_b[j], w_v, dims, preferred_element_type=f32)
+        d_lo = jnp.where(even, dq_b[j], dk_b[j])
+        d_hi = jnp.where(even, dk_b[j], dv_b[j])
+        d_x = jnp.where(even, dv_b[j], dq_b[j])
+        g = lax.dot_general(d_lo, w_ring[:, :share], dims, preferred_element_type=f32)
+        g = g + lax.dot_general(d_hi, w_ring[:, share:], dims, preferred_element_type=f32)
+        return g + lax.dot_general(d_x, w_x, dims, preferred_element_type=f32)
 
     received = swap(grad_rows(1))
     own, received = lax.optimization_barrier((grad_rows(0), received))

time: 173 us -> 172 us (level); the launches traced: 170 us -> 171 us
  waiting for transfers between devices: 60.2 us -> 38.7 us
  starting transfers between devices: 39.8 us -> 51.1 us
  local copies, waits for them, and re-layouts: 20.7 us -> 28 us
  matrix products: 25.1 us -> 28.9 us
    ppermute x3, waiting for transfers between devices: 20.2 us -> 0.33 us  [ring_gather(): bwd = lax.ppermute(bwd, 'chip', behind)]
    ppermute x6, starting transfers between devices: 14.2 us -> 26.5 us  [swap(): return lax.ppermute(x, 'core', [(0, 1), (1, 0)])]
    dynamic_update_slice x0 -> x16, local copies, waits for them, and re-layouts: none -> 9.22 us  [the longest x8 9.03 us: on_device(): w_ring = lax.dynamic_update_slice_in_dim(w_ring, ringed, src * span, axis=0)]
    ppermute x7, waiting for transfers between devices: 16.3 us -> 9.94 us  [land(): return (piece, lax.ppermute(sent, 'groups', partner))]
    select_n x0 -> x5, local copies, waits for them, and re-layouts: none -> 4.96 us  [the longest x2 3.22 us: on_device(): query = jnp.where(even, p_lo, p_x)]
    unnamed x42 -> x26, local copies, waits for them, and re-layouts: 6.5 us -> 1.77 us
    reshape x5 -> x0, local copies, waits for them, and re-layouts: 4.54 us -> none  [project(): jnp.dot(x_pair, w, preferred_element_type=f32).astype(bf16)]
    dot_general x6, matrix products: 8.87 us -> 12.5 us  [the longest x2 6.23 us: grad_rows(): lax.dot_general(d_lo, w_ring[:, :share], dims, preferred_element_type=f32)]
  transfers between devices with their start and end apart: 26 -> 26, of which waited for: 14 -> 13; matrix products, arithmetic and copies ran while one was open for 24% -> 28% of each run, Pallas kernels for 0% -> 0%
where the time goes in v13:
time: 172 us; the launch traced here: 171 us
  starting transfers between devices  51.1 us (30%)
  waiting for transfers between devices  38.7 us (23%)
  matrix products  28.9 us (17%)
  local copies, waits for them, and re-layouts  28 us (16%)
  other arithmetic  14.2 us (8%)
  between operations  10.3 us (6%)
    ppermute x6, starting transfers between devices, swap(): return lax.ppermute(x, 'core', [(0, 1), (1, 0)])  26.5 us
    ppermute x6, waiting for transfers between devices, exclusive_scan(): got = lax.ppermute(incl, 'chip', perm)  26.1 us
    ppermute x6, starting transfers between devices, exclusive_scan(): got = lax.ppermute(incl, 'chip', perm)  14.8 us
    dot_general x3, matrix products, project(): jnp.dot(x_pair, w, preferred_element_type=f32).astype(bf16)  10.7 us
    ppermute x7, waiting for transfers between devices, land(): return (piece, lax.ppermute(sent, 'groups', partner))  9.94 us
    dynamic_update_slice x8, local copies, waits for them, and re-layouts, on_device(): w_ring = lax.dynamic_update_slice_in_dim(w_ring, ringed, src * span, axis=0)  9.03 us
    dot_general x2, matrix products, grad_rows(): lax.dot_general(d_lo, w_ring[:, :share], dims, preferred_element_type=f32)  6.23 us
    ppermute x7, starting transfers between devices, land(): return (piece, lax.ppermute(sent, 'groups', partner))  5.21 us
  transfers between devices with their start and end apart: 26, of which 13 were waited for; matrix products, arithmetic and copies ran while one was open for 28% of the time, Pallas kernels for 0%

profile of v13, /device:TPU:15, one launch (start us, length us, event | category | flops | bytes accessed | tf_op | source)
XLA Modules:
  0.0 171.2 jit_solution(5313744420312924101)
XLA Ops:
  5.0 2.5 %broadcast_in_dim.29 = bf16[2048,1024]{1,0:T(8,128)(2,1)} broadcast(bf16[]{:T(256)} %constant.96.clone.1), dimensions={} | broadcast | bytes 4194306 | tf_op jit(solution)/shard_map/broadcast_in_dim | solution.py:111
  28.7 1.9 %constant_dynamic-update-slice_fusion.6 = bf16[2048,1024]{1,0:T(8,128)(2,1)} fusion(bf16[2048,1024]{1,0:T(8,128)(2,1)} %get-tuple-element.10, bf16[256,1024]{1,0:T(8,128)(2,1)} %collective-permute-done.2, s32[]{:T(128)S(6)} %select_n.267), kind=kLoop, calls=%fused_computation.94 | loop fusion | bytes 1048580 | tf_op jit(solution)/shard_map/dynamic_update_slice | solution.py:114
  30.6 1.9 %constant_dynamic-update-slice_fusion.5 = bf16[2048,1024]{1,0:T(8,128)(2,1)} fusion(bf16[2048,1024]{1,0:T(8,128)(2,1)} %constant_dynamic-update-slice_fusion.6, bf16[256,1024]{1,0:T(8,128)(2,1)} %collective-permute-done.4, s32[]{:T(128)S(6)} %select_n.270), kind=kLoop, calls=%fused_computation.93 | loop fusion | bytes 1048580 | tf_op jit(solution)/shard_map/dynamic_update_slice | solution.py:114
  32.5 5.4 %collective-permute-done.5 = bf16[256,512]{1,0:T(8,128)(2,1)S(1)} collective-permute-done((bf16[256,512]{1,0:T(8,128)(2,1)S(1)}, bf16[256,512]{1,0:T(8,128)(2,1)S(1)}, u32[]{:S(2)}, u32[]{:S(2)}) %collective-permute-start.5) | collective-permute-done | bytes 262176 | tf_op jit(solution)/shard_map/ppermute | solution.py:41
  43.2 1.4 collective-permute-done.7
  44.6 4.3 %collective-permute-start.16 = (s32[2,2]{1,0:T(2,128)S(1)}, s32[2,2]{1,0:T(2,128)S(1)}, u32[]{:S(2)}, u32[]{:S(2)}) collective-permute-start(s32[2,2]{1,0:T(2,128)S(1)} %bitcast.121), channel_id=1, source_target_pairs={{0,1},{1,0},{2,3},{3,2},{4,5},{5,4},{6,7},{7,6},{8,9},{9,8},{10,11... | collective-permute-start | bytes 56 | tf_op jit(solution)/shard_map/ppermute | solution.py:17
  54.6 1.8 %collective-permute-done.11 = bf16[256,512]{1,0:T(8,128)(2,1)S(1)} collective-permute-done((bf16[256,512]{1,0:T(8,128)(2,1)S(1)}, bf16[256,512]{1,0:T(8,128)(2,1)S(1)}, u32[]{:S(2)}, u32[]{:S(2)}) %collective-permute-start.11) | collective-permute-done | bytes 262176 | tf_op jit(solution)/shard_map/ppermute | solution.py:41
  56.5 6.3 %collective-permute-start.20 = (bf16[256,512]{0,1:T(8,128)(2,1)}, bf16[256,512]{0,1:T(8,128)(2,1)}, u32[]{:S(2)}, u32[]{:S(2)}) collective-permute-start(bf16[256,512]{0,1:T(8,128)(2,1)} %get-tuple-element.31), channel_id=1, source_target_pairs={{0,1},{1,0},{2,3},{3,2},{4,5},{5,4},{6,7},{7,6},{8,9},{9,8},{10,11... | collective-permute-start | bytes 786440 | tf_op jit(solution)/shard_map/ppermute | solution.py:17
  64.1 3.5 %fusion.16 = bf16[512,512]{1,0:T(8,128)(2,1)S(1)} fusion(bf16[2048,1024]{1,0:T(8,128)(2,1)} %constant_dynamic-update-slice_fusion, bf16[256,2048]{1,0:T(8,128)(2,1)} %collective-permute-done, bf16[256,2048]{1,0:T(8,128)(2,1)} %add_convert_fusion.1), kind=kOutput, calls=%fused_computation.27 | convolution fusion | flops 1078198272 | bytes 4718592 | tf_op jit(solution)/shard_map/dot_general | solution.py:119
  67.6 3.5 %fusion.13 = bf16[512,512]{1,0:T(8,128)(2,1)S(1)} fusion(bf16[2048,1024]{1,0:T(8,128)(2,1)} %constant_dynamic-update-slice_fusion, bf16[256,2048]{1,0:T(8,128)(2,1)} %collective-permute-done, bf16[256,2048]{1,0:T(8,128)(2,1)} %add_convert_fusion.1), kind=kOutput, calls=%fused_computation.26 | convolution fusion | flops 1078198272 | bytes 4718592 | tf_op jit(solution)/shard_map/dot_general | solution.py:119
  71.2 3.8 %broadcast_select_fusion.2 = (bf16[512,512]{1,0:T(8,128)(2,1)}, bf16[512,512]{1,0:T(8,128)(2,1)S(1)}, bf16[512,512]{1,0:T(8,128)(2,1)}) fusion(bf16[512,512]{1,0:T(8,128)(2,1)S(1)} %fusion.13, pred[]{:T(512)S(6)} %eq.16, bf16[512,512]{1,0:T(8,128)(2,1)S(1)} %fusion.16, bf16[2048,512]{1,0:T(8,128)(2,1)S(1)} %constant_dynamic-update-slice_fusion.8, ...), kind=kOutput, calls=%fused_computation.44 | convolution fusion | flops 1078984704 | bytes 6815745 | tf_op jit(solution)/shard_map/dot_general | solution.py:119
  79.0 3.1 %collective-permute-start.17 = (f32[4,128,128]{2,1,0:T(8,128)}, f32[4,128,128]{2,1,0:T(8,128)}, u32[]{:S(2)}, u32[]{:S(2)}) collective-permute-start(f32[4,128,128]{2,1,0:T(8,128)} %fusion.40), channel_id=1, source_target_pairs={{0,2},{2,4},{4,6},{6,8},{8,10},{10,12},{12,14},{1,3},{3,5},{5,7},{... | collective-permute-start | bytes 786440 | tf_op jit(solution)/shard_map/ppermute | solution.py:64
  83.2 2.3 %reshape.139 = f32[2,256,256]{2,1,0:T(8,128)} reshape(f32[2,2,128,2,128]{4,3,2,1,0:T(2,128)} %broadcast_in_dim.31) | data formatting | bytes 1048576 | tf_op jit(solution)/shard_map/vmap()/reshape | solution.py:75
  85.5 1.9 %broadcast_select_fusion.3 = f32[2,256,256]{2,1,0:T(8,128)} fusion(f32[2,256,256]{2,1,0:T(8,128)} %reshape.139, pred[256,256]{1,0:T(8,128)(4,1)S(1)} %iota_compare_fusion), kind=kLoop, calls=%fused_computation.72 | loop fusion | flops 131072 | bytes 1114112 | tf_op jit(solution)/shard_map/vmap(jit(_where))/select_n | solution.py:78
  87.3 2.0 %select_n.289 = bf16[2,256,4,128]{3,2,1,0:T(4,128)(2,1)} reshape(bf16[512,512]{1,0:T(8,128)(2,1)} %get-tuple-element.34) | data formatting | bytes 1048576 | tf_op jit(solution)/shard_map/jit(_where)/select_n | solution.py:124
  91.7 3.2 %collective-permute-start.18 = (f32[4,128,128]{2,1,0:T(8,128)S(1)}, f32[4,128,128]{2,1,0:T(8,128)S(1)}, u32[]{:S(2)}, u32[]{:S(2)}) collective-permute-start(f32[4,128,128]{2,1,0:T(8,128)S(1)} %fusion.86), channel_id=1, source_target_pairs={{0,4},{2,6},{4,8},{6,10},{8,12},{10,14},{1,5},{3,7},{5,9},{7,11},{... | collective-permute-start | bytes 786440 | tf_op jit(solution)/shard_map/ppermute | solution.py:64
  95.0 1.7 multiply_convert_fusion.1
  96.7 2.2 %collective-permute-done.18 = f32[4,128,128]{2,1,0:T(8,128)S(1)} collective-permute-done((f32[4,128,128]{2,1,0:T(8,128)S(1)}, f32[4,128,128]{2,1,0:T(8,128)S(1)}, u32[]{:S(2)}, u32[]{:S(2)}) %collective-permute-start.18) | collective-permute-done | bytes 262176 | tf_op jit(solution)/shard_map/ppermute | solution.py:64
  98.9 3.0 %collective-permute-start.19 = (f32[4,128,128]{2,1,0:T(8,128)S(1)}, f32[4,128,128]{2,1,0:T(8,128)S(1)}, u32[]{:S(2)}, u32[]{:S(2)}) collective-permute-start(f32[4,128,128]{2,1,0:T(8,128)S(1)} %add.268), channel_id=1, source_target_pairs={{0,8},{2,10},{4,12},{6,14},{1,9},{3,11},{5,13},{7,15},{16,24},{18,... | collective-permute-start | bytes 786440 | tf_op jit(solution)/shard_map/ppermute | solution.py:64
  102.4 7.0 %collective-permute-done.19 = f32[4,128,128]{2,1,0:T(8,128)S(1)} collective-permute-done((f32[4,128,128]{2,1,0:T(8,128)S(1)}, f32[4,128,128]{2,1,0:T(8,128)S(1)}, u32[]{:S(2)}, u32[]{:S(2)}) %collective-permute-start.19) | collective-permute-done | bytes 262176 | tf_op jit(solution)/shard_map/ppermute | solution.py:64
  114.7 1.9 %collective-permute-start.21 = (f32[4,128,128]{2,1,0:T(8,128)S(1)}, f32[4,128,128]{2,1,0:T(8,128)S(1)}, u32[]{:S(2)}, u32[]{:S(2)}) collective-permute-start(f32[4,128,128]{2,1,0:T(8,128)S(1)} %fusion.41), channel_id=1, source_target_pairs={{2,0},{4,2},{6,4},{8,6},{10,8},{12,10},{14,12},{3,1},{5,3},{7,5},{... | collective-permute-start | bytes 786440 | tf_op jit(solution)/shard_map/ppermute | solution.py:64
  117.2 5.6 %collective-permute-done.21 = f32[4,128,128]{2,1,0:T(8,128)S(1)} collective-permute-done((f32[4,128,128]{2,1,0:T(8,128)S(1)}, f32[4,128,128]{2,1,0:T(8,128)S(1)}, u32[]{:S(2)}, u32[]{:S(2)}) %collective-permute-start.21) | collective-permute-done | bytes 262176 | tf_op jit(solution)/shard_map/ppermute | solution.py:64
  122.8 2.1 %collective-permute-start.22 = (f32[4,128,128]{2,1,0:T(8,128)S(1)}, f32[4,128,128]{2,1,0:T(8,128)S(1)}, u32[]{:S(2)}, u32[]{:S(2)}) collective-permute-start(f32[4,128,128]{2,1,0:T(8,128)S(1)} %fusion.85), channel_id=1, source_target_pairs={{4,0},{6,2},{8,4},{10,6},{12,8},{14,10},{5,1},{7,3},{9,5},{11,7},{... | collective-permute-start | bytes 786440 | tf_op jit(solution)/shard_map/ppermute | solution.py:64
  125.3 4.6 %collective-permute-done.22 = f32[4,128,128]{2,1,0:T(8,128)S(1)} collective-permute-done((f32[4,128,128]{2,1,0:T(8,128)S(1)}, f32[4,128,128]{2,1,0:T(8,128)S(1)}, u32[]{:S(2)}, u32[]{:S(2)}) %collective-permute-start.22) | collective-permute-done | bytes 262176 | tf_op jit(solution)/shard_map/ppermute | solution.py:64
  130.0 1.4 collective-permute-start.23
  131.7 6.8 %collective-permute-done.23 = f32[4,128,128]{2,1,0:T(8,128)S(1)} collective-permute-done((f32[4,128,128]{2,1,0:T(8,128)S(1)}, f32[4,128,128]{2,1,0:T(8,128)S(1)}, u32[]{:S(2)}, u32[]{:S(2)}) %collective-permute-start.23) | collective-permute-done | bytes 262176 | tf_op jit(solution)/shard_map/ppermute | solution.py:64
  140.0 2.3 %fusion.6 = f32[256,2048]{1,0:T(8,128)S(1)} fusion(bf16[256,512]{0,1:T(8,128)(2,1)S(1)} %bitcast.120, bf16[2048,1024]{1,0:T(8,128)(2,1)} %constant_dynamic-update-slice_fusion), kind=kOutput, calls=%fused_computation.13 | convolution fusion | flops 536870912 | bytes 4456448 | tf_op jit(solution)/shard_map/dot_general | solution.py:184
  143.2 3.8 %fusion = f32[256,2048]{1,0:T(8,128)} fusion(f32[256,2048]{1,0:T(8,128)S(1)} %fusion.59, f32[256,2048]{1,0:T(8,128)S(1)} %fusion.6, bf16[256,512]{0,1:T(8,128)(2,1)S(1)} %bitcast.118, bf16[2048,1024]{1,0:T(8,128)(2,1)} %constant_dynamic-update-slice_fusion), kind=kOutput, calls=%fused_computation.1 | convolution fusion | flops 537919488 | bytes 8650752 | tf_op jit(solution)/shard_map/dot_general | solution.py:183
  147.0 14.4 %collective-permute-start.25 = (f32[256,2048]{1,0:T(8,128)}, f32[256,2048]{1,0:T(8,128)}, u32[]{:S(2)}, u32[]{:S(2)}) collective-permute-start(f32[256,2048]{1,0:T(8,128)} %fusion), channel_id=1, source_target_pairs={{0,1},{1,0},{2,3},{3,2},{4,5},{5,4},{6,7},{7,6},{8,9},{9,8},{10,11... | collective-permute-start | bytes 6291464 | tf_op jit(solution)/shard_map/ppermute | solution.py:17
  161.8 2.4 %fusion.8 = f32[256,2048]{1,0:T(8,128)S(1)} fusion(bf16[256,512]{0,1:T(8,128)(2,1)} %bitcast.117, bf16[2048,1024]{1,0:T(8,128)(2,1)} %constant_dynamic-update-slice_fusion), kind=kOutput, calls=%fused_computation.15 | convolution fusion | flops 536870912 | bytes 4456448 | tf_op jit(solution)/shard_map/dot_general | solution.py:184
  165.0 2.4 %fusion.1 = f32[256,2048]{1,0:T(8,128)S(1)} fusion(f32[256,2048]{1,0:T(8,128)S(1)} %fusion.58, f32[256,2048]{1,0:T(8,128)S(1)} %fusion.8, bf16[256,512]{0,1:T(8,128)(2,1)S(1)} %bitcast.115, bf16[2048,1024]{1,0:T(8,128)(2,1)} %constant_dynamic-update-slice_fusion), kind=kOutput, calls=%fused_computation.3 | convolution fusion | flops 537919488 | bytes 8650752 | tf_op jit(solution)/shard_map/dot_general | solution.py:183
  168.4 2.8 %add_convert_fusion = bf16[256,2048]{1,0:T(8,128)(2,1)} fusion(f32[256,2048]{1,0:T(8,128)S(1)} %fusion.1, f32[256,2048]{1,0:T(8,128)} %collective-permute-done.25), kind=kLoop, calls=%fused_computation.5 | loop fusion | flops 1048576 | bytes 5242880 | tf_op jit(solution)/shard_map/convert_element_type | solution.py:189
  (132 shorter events, 47.7 us)
Async XLA Ops:
  2.8 2.1 %collective-permute-start.1 = (bf16[128,1536]{1,0:T(8,128)(2,1)S(1)}, bf16[128,1536]{1,0:T(8,128)(2,1)S(1)}, u32[]{:S(2)}, u32[]{:S(2)}) collective-permute-start(bf16[128,1536]{1,0:T(8,128)(2,1)S(1)} %pad_maximum_fusion.5), channel_id=1, source_target_pairs={{0,1},{1,0},{2,3},{3,2},{4,5},{5,4},{6,7},{7,6},{8,9},{9,8},{10,11... | collective-permute-start | bytes 1179656 | tf_op jit(solution)/shard_map/ppermute | solution.py:17
  8.6 8.7 %copy-start.10 = (s32[8]{0:T(128)S(1)}, s32[8]{0:T(128)}, u32[]{:S(2)}) copy-start(s32[8]{0:T(128)} %constant.117.clone) | copy-start | bytes 100
  8.6 13.9 %copy-start.9 = (bf16[256,1024]{1,0:T(8,128)(2,1)S(1)}, bf16[256,1024]{1,0:T(8,128)(2,1)}, u32[]{:S(2)}) copy-start(bf16[256,1024]{1,0:T(8,128)(2,1)} %param.11) | copy-start | bytes 1572868
  8.6 15.1 %collective-permute-start.2 = (bf16[256,1024]{1,0:T(8,128)(2,1)}, bf16[256,1024]{1,0:T(8,128)(2,1)}, u32[]{:S(2)}, u32[]{:S(2)}) collective-permute-start(bf16[256,1024]{1,0:T(8,128)(2,1)} %get-tuple-element.11), channel_id=1, source_target_pairs={{0,4},{4,8},{8,12},{12,14},{14,10},{10,6},{6,2},{2,0},{1,5},{5,9},... | collective-permute-start | bytes 1572872 | tf_op jit(solution)/shard_map/ppermute | solution.py:47
  10.1 54.0 %collective-permute-start = (bf16[256,2048]{1,0:T(8,128)(2,1)}, bf16[256,2048]{1,0:T(8,128)(2,1)}, u32[]{:S(2)}, u32[]{:S(2)}) collective-permute-start(bf16[256,2048]{1,0:T(8,128)(2,1)} %add_convert_fusion.1), channel_id=1, source_target_pairs={{0,1},{1,0},{2,3},{3,2},{4,5},{5,4},{6,7},{7,6},{8,9},{9,8},{10,11... | collective-permute-start | bytes 3145736 | tf_op jit(solution)/shard_map/ppermute | solution.py:17
  10.8 14.4 %collective-permute-start.4 = (bf16[256,1024]{1,0:T(8,128)(2,1)}, bf16[256,1024]{1,0:T(8,128)(2,1)}, u32[]{:S(2)}, u32[]{:S(2)}) collective-permute-start(bf16[256,1024]{1,0:T(8,128)(2,1)} %get-tuple-element.11), channel_id=1, source_target_pairs={{0,2},{4,0},{8,4},{12,8},{14,12},{10,14},{6,10},{2,6},{1,3},{5,1},... | collective-permute-start | bytes 1572872 | tf_op jit(solution)/shard_map/ppermute | solution.py:50
  24.7 7.8 %collective-permute-start.3 = (bf16[256,512]{1,0:T(8,128)(2,1)S(1)}, bf16[256,512]{1,0:T(8,128)(2,1)S(1)}, u32[]{:S(2)}, u32[]{:S(2)}) collective-permute-start(bf16[256,512]{1,0:T(8,128)(2,1)S(1)} %constant_dynamic-slice_fusion.6), channel_id=1, source_target_pairs={{0,16},{16,0},{1,17},{17,1},{2,18},{18,2},{3,19},{19,3},{4,20},{20... | collective-permute-start | bytes 786440 | tf_op jit(solution)/shard_map/ppermute | solution.py:41
  25.0 13.1 %collective-permute-start.6 = (bf16[256,1024]{1,0:T(8,128)(2,1)}, bf16[256,1024]{1,0:T(8,128)(2,1)S(1)}, u32[]{:S(2)}, u32[]{:S(2)}) collective-permute-start(bf16[256,1024]{1,0:T(8,128)(2,1)} %collective-permute-done.2), channel_id=1, source_target_pairs={{0,4},{4,8},{8,12},{12,14},{14,10},{10,6},{6,2},{2,0},{1,5},{5,9},... | collective-permute-start | bytes 1572872 | tf_op jit(solution)/shard_map/ppermute | solution.py:47
  26.2 11.8 %collective-permute-start.5 = (bf16[256,512]{1,0:T(8,128)(2,1)S(1)}, bf16[256,512]{1,0:T(8,128)(2,1)S(1)}, u32[]{:S(2)}, u32[]{:S(2)}) collective-permute-start(bf16[256,512]{1,0:T(8,128)(2,1)S(1)} %constant_dynamic-slice_fusion.5), channel_id=1, source_target_pairs={{0,16},{16,0},{1,17},{17,1},{2,18},{18,2},{3,19},{19,3},{4,20},{20... | collective-permute-start | bytes 786440 | tf_op jit(solution)/shard_map/ppermute | solution.py:41
  27.4 12.5 %collective-permute-start.8 = (bf16[256,1024]{1,0:T(8,128)(2,1)}, bf16[256,1024]{1,0:T(8,128)(2,1)S(1)}, u32[]{:S(2)}, u32[]{:S(2)}) collective-permute-start(bf16[256,1024]{1,0:T(8,128)(2,1)} %collective-permute-done.4), channel_id=1, source_target_pairs={{0,2},{4,0},{8,4},{12,8},{14,12},{10,14},{6,10},{2,6},{1,3},{5,1},... | collective-permute-start | bytes 1572872 | tf_op jit(solution)/shard_map/ppermute | solution.py:50
  32.5 12.1 %copy-start.11 = (s32[1,2,2]{2,1,0:T(2,128)S(1)}, s32[1,2,2]{2,1,0:T(2,128)}, u32[]{:S(2)}) copy-start(s32[1,2,2]{2,1,0:T(2,128)} %param.15) | copy-start | bytes 52
  38.1 6.4 %collective-permute-start.7 = (bf16[256,512]{1,0:T(8,128)(2,1)S(1)}, bf16[256,512]{1,0:T(8,128)(2,1)S(1)}, u32[]{:S(2)}, u32[]{:S(2)}) collective-permute-start(bf16[256,512]{1,0:T(8,128)(2,1)S(1)} %constant_dynamic-slice_fusion.4), channel_id=1, source_target_pairs={{0,16},{16,0},{1,17},{17,1},{2,18},{18,2},{3,19},{19,3},{4,20},{20... | collective-permute-start | bytes 786440 | tf_op jit(solution)/shard_map/ppermute | solution.py:41
  39.4 11.7 %collective-permute-start.10 = (bf16[256,1024]{1,0:T(8,128)(2,1)S(1)}, bf16[256,1024]{1,0:T(8,128)(2,1)S(1)}, u32[]{:S(2)}, u32[]{:S(2)}) collective-permute-start(bf16[256,1024]{1,0:T(8,128)(2,1)S(1)} %collective-permute-done.6), channel_id=1, source_target_pairs={{0,4},{4,8},{8,12},{12,14},{14,10},{10,6},{6,2},{2,0},{1,5},{5,9},... | collective-permute-start | bytes 1572872 | tf_op jit(solution)/shard_map/ppermute | solution.py:47
  40.0 10.2 %collective-permute-start.9 = (bf16[256,512]{1,0:T(8,128)(2,1)S(1)}, bf16[256,512]{1,0:T(8,128)(2,1)S(1)}, u32[]{:S(2)}, u32[]{:S(2)}) collective-permute-start(bf16[256,512]{1,0:T(8,128)(2,1)S(1)} %constant_dynamic-slice_fusion.3), channel_id=1, source_target_pairs={{0,16},{16,0},{1,17},{17,1},{2,18},{18,2},{3,19},{19,3},{4,20},{20... | collective-permute-start | bytes 786440 | tf_op jit(solution)/shard_map/ppermute | solution.py:41
  40.3 11.5 %collective-permute-start.12 = (bf16[256,1024]{1,0:T(8,128)(2,1)S(1)}, bf16[256,1024]{1,0:T(8,128)(2,1)S(1)}, u32[]{:S(2)}, u32[]{:S(2)}) collective-permute-start(bf16[256,1024]{1,0:T(8,128)(2,1)S(1)} %collective-permute-done.8), channel_id=1, source_target_pairs={{0,2},{4,0},{8,4},{12,8},{14,12},{10,14},{6,10},{2,6},{1,3},{5,1},... | collective-permute-start | bytes 1572872 | tf_op jit(solution)/shard_map/ppermute | solution.py:50
  44.6 37.6 %collective-permute-start.16 = (s32[2,2]{1,0:T(2,128)S(1)}, s32[2,2]{1,0:T(2,128)S(1)}, u32[]{:S(2)}, u32[]{:S(2)}) collective-permute-start(s32[2,2]{1,0:T(2,128)S(1)} %bitcast.121), channel_id=1, source_target_pairs={{0,1},{1,0},{2,3},{3,2},{4,5},{5,4},{6,7},{7,6},{8,9},{9,8},{10,11... | collective-permute-start | bytes 56 | tf_op jit(solution)/shard_map/ppermute | solution.py:17
  51.2 5.3 %collective-permute-start.11 = (bf16[256,512]{1,0:T(8,128)(2,1)S(1)}, bf16[256,512]{1,0:T(8,128)(2,1)S(1)}, u32[]{:S(2)}, u32[]{:S(2)}) collective-permute-start(bf16[256,512]{1,0:T(8,128)(2,1)S(1)} %constant_dynamic-slice_fusion.2), channel_id=1, source_target_pairs={{0,16},{16,0},{1,17},{17,1},{2,18},{18,2},{3,19},{19,3},{4,20},{20... | collective-permute-start | bytes 786440 | tf_op jit(solution)/shard_map/ppermute | solution.py:41
  51.6 11.3 %collective-permute-start.14 = (bf16[256,1024]{1,0:T(8,128)(2,1)S(1)}, bf16[256,1024]{1,0:T(8,128)(2,1)S(1)}, u32[]{:S(2)}, u32[]{:S(2)}) collective-permute-start(bf16[256,1024]{1,0:T(8,128)(2,1)S(1)} %collective-permute-done.10), channel_id=1, source_target_pairs={{0,4},{4,8},{8,12},{12,14},{14,10},{10,6},{6,2},{2,0},{1,5},{5,9},... | collective-permute-start | bytes 1572872 | tf_op jit(solution)/shard_map/ppermute | solution.py:47
  51.8 11.0 %collective-permute-start.13 = (bf16[256,512]{1,0:T(8,128)(2,1)S(1)}, bf16[256,512]{1,0:T(8,128)(2,1)S(1)}, u32[]{:S(2)}, u32[]{:S(2)}) collective-permute-start(bf16[256,512]{1,0:T(8,128)(2,1)S(1)} %constant_dynamic-slice_fusion.1), channel_id=1, source_target_pairs={{0,16},{16,0},{1,17},{17,1},{2,18},{18,2},{3,19},{19,3},{4,20},{20... | collective-permute-start | bytes 786440 | tf_op jit(solution)/shard_map/ppermute | solution.py:41
  56.5 54.3 %collective-permute-start.20 = (bf16[256,512]{0,1:T(8,128)(2,1)}, bf16[256,512]{0,1:T(8,128)(2,1)}, u32[]{:S(2)}, u32[]{:S(2)}) collective-permute-start(bf16[256,512]{0,1:T(8,128)(2,1)} %get-tuple-element.31), channel_id=1, source_target_pairs={{0,1},{1,0},{2,3},{3,2},{4,5},{5,4},{6,7},{7,6},{8,9},{9,8},{10,11... | collective-permute-start | bytes 786440 | tf_op jit(solution)/shard_map/ppermute | solution.py:17
  62.9 8.2 %collective-permute-start.15 = (bf16[256,512]{1,0:T(8,128)(2,1)S(1)}, bf16[256,512]{1,0:T(8,128)(2,1)S(1)}, u32[]{:S(2)}, u32[]{:S(2)}) collective-permute-start(bf16[256,512]{1,0:T(8,128)(2,1)S(1)} %constant_dynamic-slice_fusion), channel_id=1, source_target_pairs={{0,16},{16,0},{1,17},{17,1},{2,18},{18,2},{3,19},{19,3},{4,20},{20... | collective-permute-start | bytes 786440 | tf_op jit(solution)/shard_map/ppermute | solution.py:41
  75.9 9.6 %copy-start.4 = (bf16[2,256,4,128]{1,3,2,0:T(8,128)(2,1)}, bf16[2,256,4,128]{1,3,2,0:T(8,128)(2,1)S(1)}, u32[]{:S(2)}) copy-start(bf16[2,256,4,128]{1,3,2,0:T(8,128)(2,1)S(1)} %copy.14) | copy-start | bytes 1572868
  79.0 11.5 %collective-permute-start.17 = (f32[4,128,128]{2,1,0:T(8,128)}, f32[4,128,128]{2,1,0:T(8,128)}, u32[]{:S(2)}, u32[]{:S(2)}) collective-permute-start(f32[4,128,128]{2,1,0:T(8,128)} %fusion.40), channel_id=1, source_target_pairs={{0,2},{2,4},{4,6},{6,8},{8,10},{10,12},{12,14},{1,3},{3,5},{5,7},{... | collective-permute-start | bytes 786440 | tf_op jit(solution)/shard_map/ppermute | solution.py:64
  91.7 7.1 %collective-permute-start.18 = (f32[4,128,128]{2,1,0:T(8,128)S(1)}, f32[4,128,128]{2,1,0:T(8,128)S(1)}, u32[]{:S(2)}, u32[]{:S(2)}) collective-permute-start(f32[4,128,128]{2,1,0:T(8,128)S(1)} %fusion.86), channel_id=1, source_target_pairs={{0,4},{2,6},{4,8},{6,10},{8,12},{10,14},{1,5},{3,7},{5,9},{7,11},{... | collective-permute-start | bytes 786440 | tf_op jit(solution)/shard_map/ppermute | solution.py:64
  96.7 12.7 %copy-start.1 = (f32[2,4,128,128]{3,2,1,0:T(8,128)S(1)}, f32[2,4,128,128]{3,2,1,0:T(8,128)}, u32[]{:S(2)}) copy-start(f32[2,4,128,128]{3,2,1,0:T(8,128)} %copy-done) | copy-start | bytes 1572868
  98.9 10.4 %collective-permute-start.19 = (f32[4,128,128]{2,1,0:T(8,128)S(1)}, f32[4,128,128]{2,1,0:T(8,128)S(1)}, u32[]{:S(2)}, u32[]{:S(2)}) collective-permute-start(f32[4,128,128]{2,1,0:T(8,128)S(1)} %add.268), channel_id=1, source_target_pairs={{0,8},{2,10},{4,12},{6,14},{1,9},{3,11},{5,13},{7,15},{16,24},{18,... | collective-permute-start | bytes 786440 | tf_op jit(solution)/shard_map/ppermute | solution.py:64
  114.7 8.0 %collective-permute-start.21 = (f32[4,128,128]{2,1,0:T(8,128)S(1)}, f32[4,128,128]{2,1,0:T(8,128)S(1)}, u32[]{:S(2)}, u32[]{:S(2)}) collective-permute-start(f32[4,128,128]{2,1,0:T(8,128)S(1)} %fusion.41), channel_id=1, source_target_pairs={{2,0},{4,2},{6,4},{8,6},{10,8},{12,10},{14,12},{3,1},{5,3},{7,5},{... | collective-permute-start | bytes 786440 | tf_op jit(solution)/shard_map/ppermute | solution.py:64
  122.8 7.1 %collective-permute-start.22 = (f32[4,128,128]{2,1,0:T(8,128)S(1)}, f32[4,128,128]{2,1,0:T(8,128)S(1)}, u32[]{:S(2)}, u32[]{:S(2)}) collective-permute-start(f32[4,128,128]{2,1,0:T(8,128)S(1)} %fusion.85), channel_id=1, source_target_pairs={{4,0},{6,2},{8,4},{10,6},{12,8},{14,10},{5,1},{7,3},{9,5},{11,7},{... | collective-permute-start | bytes 786440 | tf_op jit(solution)/shard_map/ppermute | solution.py:64
  129.9 8.6 %copy-start.3 = (bf16[2,256,4,128]{3,2,1,0:T(4,128)(2,1)S(1)}, bf16[2,256,4,128]{3,2,1,0:T(4,128)(2,1)}, u32[]{:S(2)}) copy-start(bf16[2,256,4,128]{3,2,1,0:T(4,128)(2,1)} %copy-done.2) | copy-start | bytes 1572868
  130.0 8.5 %collective-permute-start.23 = (f32[4,128,128]{2,1,0:T(8,128)S(1)}, f32[4,128,128]{2,1,0:T(8,128)S(1)}, u32[]{:S(2)}, u32[]{:S(2)}) collective-permute-start(f32[4,128,128]{2,1,0:T(8,128)S(1)} %add.279), channel_id=1, source_target_pairs={{8,0},{10,2},{12,4},{14,6},{9,1},{11,3},{13,5},{15,7},{24,16},{26,... | collective-permute-start | bytes 786440 | tf_op jit(solution)/shard_map/ppermute | solution.py:64
  147.0 21.4 %collective-permute-start.25 = (f32[256,2048]{1,0:T(8,128)}, f32[256,2048]{1,0:T(8,128)}, u32[]{:S(2)}, u32[]{:S(2)}) collective-permute-start(f32[256,2048]{1,0:T(8,128)} %fusion), channel_id=1, source_target_pairs={{0,1},{1,0},{2,3},{3,2},{4,5},{5,4},{6,7},{7,6},{8,9},{9,8},{10,11... | collective-permute-start | bytes 6291464 | tf_op jit(solution)/shard_map/ppermute | solution.py:17
  161.7 5.7 %collective-permute-start.24 = (bf16[256,512]{1,0:T(8,128)(2,1)S(1)}, bf16[256,512]{1,0:T(8,128)(2,1)S(1)}, u32[]{:S(2)}, u32[]{:S(2)}) collective-permute-start(bf16[256,512]{1,0:T(8,128)(2,1)S(1)} %copy.22), channel_id=1, source_target_pairs={{0,1},{1,0},{2,3},{3,2},{4,5},{5,4},{6,7},{7,6},{8,9},{9,8},{10,11... | collective-permute-start | bytes 786440 | tf_op jit(solution)/shard_map/ppermute | solution.py:17
  (7 other events, 17.4 us)

commit v14 on v13

--- a/solution.py
+++ b/solution.py
@@ -70,12 +70,10 @@
 
 def dense_allow(block_masks, tokens):
     nb = tokens // BLK
-    gate = jnp.broadcast_to(
-        block_masks.astype(jnp.float32)[:, None, :, None], (nb, BLK, nb, BLK)
-    ).reshape(tokens, tokens)
+    gate = jnp.broadcast_to((block_masks != 0)[:, None, :, None], (nb, BLK, nb, BLK)).reshape(tokens, tokens)
     rows = lax.broadcasted_iota(jnp.int32, (tokens, tokens), 0)
     cols = lax.broadcasted_iota(jnp.int32, (tokens, tokens), 1)
-    return jnp.where(cols <= rows, gate, 0.0)
+    return gate & (cols <= rows)
 
 
 def on_device(clean, delta, cotangent, w_query, w_key, w_value, masks):
@@ -135,7 +133,7 @@
     allow = jax.vmap(dense_allow, in_axes=(0, None))(pair_masks, tok)
 
     scores = jnp.einsum("jthd,jshd->jhts", query, key, preferred_element_type=f32)
-    attn = (scores * allow[:, None]).astype(bf16)
+    attn = jnp.where(allow[:, None], scores, 0.0).astype(bf16)
     mixed = jnp.einsum("jhts,jshd->jthd", attn, value, preferred_element_type=f32)
     mixed = mixed + jnp.einsum("jthd,jhde->jthe", query, state_b, preferred_element_type=f32)
     root = jnp.sqrt(jnp.mean(mixed * mixed, axis=-1, keepdims=True) + EPSILON)
@@ -162,9 +160,8 @@
         jnp.concatenate([out_recv, out_b[0]], axis=1),
     )
 
-    d_attn = (
-        jnp.einsum("jthe,jshe->jhts", d_mixed_b, value, preferred_element_type=f32) * allow[:, None]
-    ).astype(bf16)
+    d_scores = jnp.einsum("jthe,jshe->jhts", d_mixed_b, value, preferred_element_type=f32)
+    d_attn = jnp.where(allow[:, None], d_scores, 0.0).astype(bf16)
     d_query = jnp.einsum("jhts,jshd->jthd", d_attn, key, preferred_element_type=f32)
     d_query = d_query + jnp.einsum("jthe,jhde->jthd", d_mixed_b, state_b, preferred_element_type=f32)
     d_key = jnp.einsum("jhts,jthd->jshd", d_attn, query, preferred_element_type=f32)

time: 172 us -> 171 us (level)
    select_n x1 -> x0, other arithmetic: 1.89 us -> none  [dense_allow(): return jnp.where(cols <= rows, gate, 0.0)]
where the time goes in v14:
time: 171 us; the launch traced here: 170 us
  starting transfers between devices  51.1 us (30%)
  waiting for transfers between devices  38.8 us (23%)
  matrix products  28.8 us (17%)
  local copies, waits for them, and re-layouts  26.7 us (16%)
  other arithmetic  14.6 us (9%)
  between operations  10.3 us (6%)
    ppermute x6, starting transfers between devices, swap(): return lax.ppermute(x, 'core', [(0, 1), (1, 0)])  26.5 us
    ppermute x6, waiting for transfers between devices, exclusive_scan(): got = lax.ppermute(incl, 'chip', perm)  26.3 us
    ppermute x6, starting transfers between devices, exclusive_scan(): got = lax.ppermute(incl, 'chip', perm)  14.8 us
    dot_general x3, matrix products, project(): jnp.dot(x_pair, w, preferred_element_type=f32).astype(bf16)  10.7 us
    ppermute x7, waiting for transfers between devices, land(): return (piece, lax.ppermute(sent, 'groups', partner))  9.94 us
    dynamic_update_slice x8, local copies, waits for them, and re-layouts, on_device(): w_ring = lax.dynamic_update_slice_in_dim(w_ring, ringed, src * span, axis=0)  9.03 us
    dot_general x2, matrix products, grad_rows(): lax.dot_general(d_lo, w_ring[:, :share], dims, preferred_element_type=f32)  6.24 us
    ppermute x7, starting transfers between devices, land(): return (piece, lax.ppermute(sent, 'groups', partner))  5.21 us
  transfers between devices with their start and end apart: 26, of which 13 were waited for; matrix products, arithmetic and copies ran while one was open for 28% of the time, Pallas kernels for 0%

profile of v14, /device:TPU:15, one launch (start us, length us, event | category | flops | bytes accessed | tf_op | source)
XLA Modules:
  0.0 170.4 jit_solution(8065741148187263907)
XLA Ops:
  5.0 2.5 %broadcast_in_dim.38 = bf16[2048,1024]{1,0:T(8,128)(2,1)} broadcast(bf16[]{:T(256)} %constant.97.clone.1), dimensions={} | broadcast | bytes 4194306 | tf_op jit(solution)/shard_map/broadcast_in_dim | solution.py:109
  29.3 1.9 %constant_dynamic-update-slice_fusion.6 = bf16[2048,1024]{1,0:T(8,128)(2,1)} fusion(bf16[2048,1024]{1,0:T(8,128)(2,1)} %get-tuple-element.10, bf16[256,1024]{1,0:T(8,128)(2,1)} %collective-permute-done.2, s32[]{:T(128)S(6)} %select_n.266), kind=kLoop, calls=%fused_computation.94 | loop fusion | bytes 1048580 | tf_op jit(solution)/shard_map/dynamic_update_slice | solution.py:112
  31.2 1.9 %constant_dynamic-update-slice_fusion.5 = bf16[2048,1024]{1,0:T(8,128)(2,1)} fusion(bf16[2048,1024]{1,0:T(8,128)(2,1)} %constant_dynamic-update-slice_fusion.6, bf16[256,1024]{1,0:T(8,128)(2,1)} %collective-permute-done.4, s32[]{:T(128)S(6)} %select_n.269), kind=kLoop, calls=%fused_computation.93 | loop fusion | bytes 1048580 | tf_op jit(solution)/shard_map/dynamic_update_slice | solution.py:112
  33.1 5.4 %collective-permute-done.5 = bf16[256,512]{1,0:T(8,128)(2,1)S(1)} collective-permute-done((bf16[256,512]{1,0:T(8,128)(2,1)S(1)}, bf16[256,512]{1,0:T(8,128)(2,1)S(1)}, u32[]{:S(2)}, u32[]{:S(2)}) %collective-permute-start.5) | collective-permute-done | bytes 262176 | tf_op jit(solution)/shard_map/ppermute | solution.py:41
  43.8 1.4 collective-permute-done.7
  45.2 4.3 %collective-permute-start.16 = (s32[2,2]{1,0:T(2,128)S(1)}, s32[2,2]{1,0:T(2,128)S(1)}, u32[]{:S(2)}, u32[]{:S(2)}) collective-permute-start(s32[2,2]{1,0:T(2,128)S(1)} %bitcast.121), channel_id=1, source_target_pairs={{0,1},{1,0},{2,3},{3,2},{4,5},{5,4},{6,7},{7,6},{8,9},{9,8},{10,11... | collective-permute-start | bytes 56 | tf_op jit(solution)/shard_map/ppermute | solution.py:17
  55.2 1.8 %collective-permute-done.11 = bf16[256,512]{1,0:T(8,128)(2,1)S(1)} collective-permute-done((bf16[256,512]{1,0:T(8,128)(2,1)S(1)}, bf16[256,512]{1,0:T(8,128)(2,1)S(1)}, u32[]{:S(2)}, u32[]{:S(2)}) %collective-permute-start.11) | collective-permute-done | bytes 262176 | tf_op jit(solution)/shard_map/ppermute | solution.py:41
  57.1 6.3 %collective-permute-start.20 = (bf16[256,512]{0,1:T(8,128)(2,1)}, bf16[256,512]{0,1:T(8,128)(2,1)}, u32[]{:S(2)}, u32[]{:S(2)}) collective-permute-start(bf16[256,512]{0,1:T(8,128)(2,1)} %get-tuple-element.31), channel_id=1, source_target_pairs={{0,1},{1,0},{2,3},{3,2},{4,5},{5,4},{6,7},{7,6},{8,9},{9,8},{10,11... | collective-permute-start | bytes 786440 | tf_op jit(solution)/shard_map/ppermute | solution.py:17
  64.7 3.5 %fusion.16 = bf16[512,512]{1,0:T(8,128)(2,1)S(1)} fusion(bf16[2048,1024]{1,0:T(8,128)(2,1)} %constant_dynamic-update-slice_fusion, bf16[256,2048]{1,0:T(8,128)(2,1)} %collective-permute-done, bf16[256,2048]{1,0:T(8,128)(2,1)} %add_convert_fusion.1), kind=kOutput, calls=%fused_computation.27 | convolution fusion | flops 1078198272 | bytes 4718592 | tf_op jit(solution)/shard_map/dot_general | solution.py:117
  68.2 3.5 %fusion.13 = bf16[512,512]{1,0:T(8,128)(2,1)S(1)} fusion(bf16[2048,1024]{1,0:T(8,128)(2,1)} %constant_dynamic-update-slice_fusion, bf16[256,2048]{1,0:T(8,128)(2,1)} %collective-permute-done, bf16[256,2048]{1,0:T(8,128)(2,1)} %add_convert_fusion.1), kind=kOutput, calls=%fused_computation.26 | convolution fusion | flops 1078198272 | bytes 4718592 | tf_op jit(solution)/shard_map/dot_general | solution.py:117
  71.8 3.8 %broadcast_select_fusion.2 = (bf16[512,512]{1,0:T(8,128)(2,1)}, bf16[512,512]{1,0:T(8,128)(2,1)S(1)}, bf16[512,512]{1,0:T(8,128)(2,1)}) fusion(bf16[512,512]{1,0:T(8,128)(2,1)S(1)} %fusion.13, pred[]{:T(512)S(6)} %eq.16, bf16[512,512]{1,0:T(8,128)(2,1)S(1)} %fusion.16, bf16[2048,512]{1,0:T(8,128)(2,1)S(1)} %constant_dynamic-update-slice_fusion.8, ...), kind=kOutput, calls=%fused_computation.44 | convolution fusion | flops 1078984704 | bytes 6815745 | tf_op jit(solution)/shard_map/dot_general | solution.py:117
  79.7 3.1 %collective-permute-start.17 = (f32[4,128,128]{2,1,0:T(8,128)}, f32[4,128,128]{2,1,0:T(8,128)}, u32[]{:S(2)}, u32[]{:S(2)}) collective-permute-start(f32[4,128,128]{2,1,0:T(8,128)} %fusion.40), channel_id=1, source_target_pairs={{0,2},{2,4},{4,6},{6,8},{8,10},{10,12},{12,14},{1,3},{3,5},{5,7},{... | collective-permute-start | bytes 786440 | tf_op jit(solution)/shard_map/ppermute | solution.py:64
  83.8 1.5 reshape.146
  85.2 1.6 broadcast_and_fusion
  86.8 2.0 %select_n.288 = bf16[2,256,4,128]{3,2,1,0:T(4,128)(2,1)} reshape(bf16[512,512]{1,0:T(8,128)(2,1)} %get-tuple-element.34) | data formatting | bytes 1048576 | tf_op jit(solution)/shard_map/jit(_where)/select_n | solution.py:122
  91.2 3.2 %collective-permute-start.18 = (f32[4,128,128]{2,1,0:T(8,128)S(1)}, f32[4,128,128]{2,1,0:T(8,128)S(1)}, u32[]{:S(2)}, u32[]{:S(2)}) collective-permute-start(f32[4,128,128]{2,1,0:T(8,128)S(1)} %fusion.86), channel_id=1, source_target_pairs={{0,4},{2,6},{4,8},{6,10},{8,12},{10,14},{1,5},{3,7},{5,9},{7,11},{... | collective-permute-start | bytes 786440 | tf_op jit(solution)/shard_map/ppermute | solution.py:64
  94.5 1.5 select_convert_fusion.1
  96.0 2.3 %collective-permute-done.18 = f32[4,128,128]{2,1,0:T(8,128)S(1)} collective-permute-done((f32[4,128,128]{2,1,0:T(8,128)S(1)}, f32[4,128,128]{2,1,0:T(8,128)S(1)}, u32[]{:S(2)}, u32[]{:S(2)}) %collective-permute-start.18) | collective-permute-done | bytes 262176 | tf_op jit(solution)/shard_map/ppermute | solution.py:64
  98.4 3.0 %collective-permute-start.19 = (f32[4,128,128]{2,1,0:T(8,128)S(1)}, f32[4,128,128]{2,1,0:T(8,128)S(1)}, u32[]{:S(2)}, u32[]{:S(2)}) collective-permute-start(f32[4,128,128]{2,1,0:T(8,128)S(1)} %add.268), channel_id=1, source_target_pairs={{0,8},{2,10},{4,12},{6,14},{1,9},{3,11},{5,13},{7,15},{16,24},{18,... | collective-permute-start | bytes 786440 | tf_op jit(solution)/shard_map/ppermute | solution.py:64
  101.8 7.0 %collective-permute-done.19 = f32[4,128,128]{2,1,0:T(8,128)S(1)} collective-permute-done((f32[4,128,128]{2,1,0:T(8,128)S(1)}, f32[4,128,128]{2,1,0:T(8,128)S(1)}, u32[]{:S(2)}, u32[]{:S(2)}) %collective-permute-start.19) | collective-permute-done | bytes 262176 | tf_op jit(solution)/shard_map/ppermute | solution.py:64
  113.8 1.9 %collective-permute-start.21 = (f32[4,128,128]{2,1,0:T(8,128)S(1)}, f32[4,128,128]{2,1,0:T(8,128)S(1)}, u32[]{:S(2)}, u32[]{:S(2)}) collective-permute-start(f32[4,128,128]{2,1,0:T(8,128)S(1)} %fusion.41), channel_id=1, source_target_pairs={{2,0},{4,2},{6,4},{8,6},{10,8},{12,10},{14,12},{3,1},{5,3},{7,5},{... | collective-permute-start | bytes 786440 | tf_op jit(solution)/shard_map/ppermute | solution.py:64
  116.3 5.6 %collective-permute-done.21 = f32[4,128,128]{2,1,0:T(8,128)S(1)} collective-permute-done((f32[4,128,128]{2,1,0:T(8,128)S(1)}, f32[4,128,128]{2,1,0:T(8,128)S(1)}, u32[]{:S(2)}, u32[]{:S(2)}) %collective-permute-start.21) | collective-permute-done | bytes 262176 | tf_op jit(solution)/shard_map/ppermute | solution.py:64
  121.9 2.1 %collective-permute-start.22 = (f32[4,128,128]{2,1,0:T(8,128)S(1)}, f32[4,128,128]{2,1,0:T(8,128)S(1)}, u32[]{:S(2)}, u32[]{:S(2)}) collective-permute-start(f32[4,128,128]{2,1,0:T(8,128)S(1)} %fusion.85), channel_id=1, source_target_pairs={{4,0},{6,2},{8,4},{10,6},{12,8},{14,10},{5,1},{7,3},{9,5},{11,7},{... | collective-permute-start | bytes 786440 | tf_op jit(solution)/shard_map/ppermute | solution.py:64
  124.4 4.6 %collective-permute-done.22 = f32[4,128,128]{2,1,0:T(8,128)S(1)} collective-permute-done((f32[4,128,128]{2,1,0:T(8,128)S(1)}, f32[4,128,128]{2,1,0:T(8,128)S(1)}, u32[]{:S(2)}, u32[]{:S(2)}) %collective-permute-start.22) | collective-permute-done | bytes 262176 | tf_op jit(solution)/shard_map/ppermute | solution.py:64
  129.1 1.4 collective-permute-start.23
  130.8 6.8 %collective-permute-done.23 = f32[4,128,128]{2,1,0:T(8,128)S(1)} collective-permute-done((f32[4,128,128]{2,1,0:T(8,128)S(1)}, f32[4,128,128]{2,1,0:T(8,128)S(1)}, u32[]{:S(2)}, u32[]{:S(2)}) %collective-permute-start.23) | collective-permute-done | bytes 262176 | tf_op jit(solution)/shard_map/ppermute | solution.py:64
  139.2 2.3 %fusion.6 = f32[256,2048]{1,0:T(8,128)S(1)} fusion(bf16[256,512]{0,1:T(8,128)(2,1)S(1)} %bitcast.120, bf16[2048,1024]{1,0:T(8,128)(2,1)} %constant_dynamic-update-slice_fusion), kind=kOutput, calls=%fused_computation.13 | convolution fusion | flops 536870912 | bytes 4456448 | tf_op jit(solution)/shard_map/dot_general | solution.py:181
  142.3 3.8 %fusion = f32[256,2048]{1,0:T(8,128)} fusion(f32[256,2048]{1,0:T(8,128)S(1)} %fusion.59, f32[256,2048]{1,0:T(8,128)S(1)} %fusion.6, bf16[256,512]{0,1:T(8,128)(2,1)S(1)} %bitcast.118, bf16[2048,1024]{1,0:T(8,128)(2,1)} %constant_dynamic-update-slice_fusion), kind=kOutput, calls=%fused_computation.1 | convolution fusion | flops 537919488 | bytes 8650752 | tf_op jit(solution)/shard_map/dot_general | solution.py:180
  146.1 14.4 %collective-permute-start.25 = (f32[256,2048]{1,0:T(8,128)}, f32[256,2048]{1,0:T(8,128)}, u32[]{:S(2)}, u32[]{:S(2)}) collective-permute-start(f32[256,2048]{1,0:T(8,128)} %fusion), channel_id=1, source_target_pairs={{0,1},{1,0},{2,3},{3,2},{4,5},{5,4},{6,7},{7,6},{8,9},{9,8},{10,11... | collective-permute-start | bytes 6291464 | tf_op jit(solution)/shard_map/ppermute | solution.py:17
  160.9 2.4 %fusion.8 = f32[256,2048]{1,0:T(8,128)S(1)} fusion(bf16[256,512]{0,1:T(8,128)(2,1)} %bitcast.117, bf16[2048,1024]{1,0:T(8,128)(2,1)} %constant_dynamic-update-slice_fusion), kind=kOutput, calls=%fused_computation.15 | convolution fusion | flops 536870912 | bytes 4456448 | tf_op jit(solution)/shard_map/dot_general | solution.py:181
  164.1 2.4 %fusion.1 = f32[256,2048]{1,0:T(8,128)S(1)} fusion(f32[256,2048]{1,0:T(8,128)S(1)} %fusion.58, f32[256,2048]{1,0:T(8,128)S(1)} %fusion.8, bf16[256,512]{0,1:T(8,128)(2,1)S(1)} %bitcast.115, bf16[2048,1024]{1,0:T(8,128)(2,1)} %constant_dynamic-update-slice_fusion), kind=kOutput, calls=%fused_computation.3 | convolution fusion | flops 537919488 | bytes 8650752 | tf_op jit(solution)/shard_map/dot_general | solution.py:180
  167.5 2.8 %add_convert_fusion = bf16[256,2048]{1,0:T(8,128)(2,1)} fusion(f32[256,2048]{1,0:T(8,128)S(1)} %fusion.1, f32[256,2048]{1,0:T(8,128)} %collective-permute-done.25), kind=kLoop, calls=%fused_computation.5 | loop fusion | flops 1048576 | bytes 5242880 | tf_op jit(solution)/shard_map/convert_element_type | solution.py:186
  (132 shorter events, 47.9 us)
Async XLA Ops:
  2.8 2.1 %collective-permute-start.1 = (bf16[128,1536]{1,0:T(8,128)(2,1)S(1)}, bf16[128,1536]{1,0:T(8,128)(2,1)S(1)}, u32[]{:S(2)}, u32[]{:S(2)}) collective-permute-start(bf16[128,1536]{1,0:T(8,128)(2,1)S(1)} %pad_maximum_fusion.5), channel_id=1, source_target_pairs={{0,1},{1,0},{2,3},{3,2},{4,5},{5,4},{6,7},{7,6},{8,9},{9,8},{10,11... | collective-permute-start | bytes 1179656 | tf_op jit(solution)/shard_map/ppermute | solution.py:17
  8.6 9.3 %copy-start.10 = (s32[8]{0:T(128)S(1)}, s32[8]{0:T(128)}, u32[]{:S(2)}) copy-start(s32[8]{0:T(128)} %constant.118.clone) | copy-start | bytes 100
  8.6 14.5 %copy-start.8 = (bf16[256,1024]{1,0:T(8,128)(2,1)S(1)}, bf16[256,1024]{1,0:T(8,128)(2,1)}, u32[]{:S(2)}) copy-start(bf16[256,1024]{1,0:T(8,128)(2,1)} %param.11) | copy-start | bytes 1572868
  8.6 15.7 %collective-permute-start.2 = (bf16[256,1024]{1,0:T(8,128)(2,1)}, bf16[256,1024]{1,0:T(8,128)(2,1)}, u32[]{:S(2)}, u32[]{:S(2)}) collective-permute-start(bf16[256,1024]{1,0:T(8,128)(2,1)} %get-tuple-element.11), channel_id=1, source_target_pairs={{0,4},{4,8},{8,12},{12,14},{14,10},{10,6},{6,2},{2,0},{1,5},{5,9},... | collective-permute-start | bytes 1572872 | tf_op jit(solution)/shard_map/ppermute | solution.py:47
  10.1 54.6 %collective-permute-start = (bf16[256,2048]{1,0:T(8,128)(2,1)}, bf16[256,2048]{1,0:T(8,128)(2,1)}, u32[]{:S(2)}, u32[]{:S(2)}) collective-permute-start(bf16[256,2048]{1,0:T(8,128)(2,1)} %add_convert_fusion.1), channel_id=1, source_target_pairs={{0,1},{1,0},{2,3},{3,2},{4,5},{5,4},{6,7},{7,6},{8,9},{9,8},{10,11... | collective-permute-start | bytes 3145736 | tf_op jit(solution)/shard_map/ppermute | solution.py:17
  10.8 15.0 %collective-permute-start.4 = (bf16[256,1024]{1,0:T(8,128)(2,1)}, bf16[256,1024]{1,0:T(8,128)(2,1)}, u32[]{:S(2)}, u32[]{:S(2)}) collective-permute-start(bf16[256,1024]{1,0:T(8,128)(2,1)} %get-tuple-element.11), channel_id=1, source_target_pairs={{0,2},{4,0},{8,4},{12,8},{14,12},{10,14},{6,10},{2,6},{1,3},{5,1},... | collective-permute-start | bytes 1572872 | tf_op jit(solution)/shard_map/ppermute | solution.py:50
  25.3 7.8 %collective-permute-start.3 = (bf16[256,512]{1,0:T(8,128)(2,1)S(1)}, bf16[256,512]{1,0:T(8,128)(2,1)S(1)}, u32[]{:S(2)}, u32[]{:S(2)}) collective-permute-start(bf16[256,512]{1,0:T(8,128)(2,1)S(1)} %constant_dynamic-slice_fusion.6), channel_id=1, source_target_pairs={{0,16},{16,0},{1,17},{17,1},{2,18},{18,2},{3,19},{19,3},{4,20},{20... | collective-permute-start | bytes 786440 | tf_op jit(solution)/shard_map/ppermute | solution.py:41
  25.6 13.1 %collective-permute-start.6 = (bf16[256,1024]{1,0:T(8,128)(2,1)}, bf16[256,1024]{1,0:T(8,128)(2,1)S(1)}, u32[]{:S(2)}, u32[]{:S(2)}) collective-permute-start(bf16[256,1024]{1,0:T(8,128)(2,1)} %collective-permute-done.2), channel_id=1, source_target_pairs={{0,4},{4,8},{8,12},{12,14},{14,10},{10,6},{6,2},{2,0},{1,5},{5,9},... | collective-permute-start | bytes 1572872 | tf_op jit(solution)/shard_map/ppermute | solution.py:47
  26.8 11.8 %collective-permute-start.5 = (bf16[256,512]{1,0:T(8,128)(2,1)S(1)}, bf16[256,512]{1,0:T(8,128)(2,1)S(1)}, u32[]{:S(2)}, u32[]{:S(2)}) collective-permute-start(bf16[256,512]{1,0:T(8,128)(2,1)S(1)} %constant_dynamic-slice_fusion.5), channel_id=1, source_target_pairs={{0,16},{16,0},{1,17},{17,1},{2,18},{18,2},{3,19},{19,3},{4,20},{20... | collective-permute-start | bytes 786440 | tf_op jit(solution)/shard_map/ppermute | solution.py:41
  28.1 12.5 %collective-permute-start.8 = (bf16[256,1024]{1,0:T(8,128)(2,1)}, bf16[256,1024]{1,0:T(8,128)(2,1)S(1)}, u32[]{:S(2)}, u32[]{:S(2)}) collective-permute-start(bf16[256,1024]{1,0:T(8,128)(2,1)} %collective-permute-done.4), channel_id=1, source_target_pairs={{0,2},{4,0},{8,4},{12,8},{14,12},{10,14},{6,10},{2,6},{1,3},{5,1},... | collective-permute-start | bytes 1572872 | tf_op jit(solution)/shard_map/ppermute | solution.py:50
  33.1 12.1 %copy-start.11 = (s32[1,2,2]{2,1,0:T(2,128)S(1)}, s32[1,2,2]{2,1,0:T(2,128)}, u32[]{:S(2)}) copy-start(s32[1,2,2]{2,1,0:T(2,128)} %param.15) | copy-start | bytes 52
  38.8 6.4 %collective-permute-start.7 = (bf16[256,512]{1,0:T(8,128)(2,1)S(1)}, bf16[256,512]{1,0:T(8,128)(2,1)S(1)}, u32[]{:S(2)}, u32[]{:S(2)}) collective-permute-start(bf16[256,512]{1,0:T(8,128)(2,1)S(1)} %constant_dynamic-slice_fusion.4), channel_id=1, source_target_pairs={{0,16},{16,0},{1,17},{17,1},{2,18},{18,2},{3,19},{19,3},{4,20},{20... | collective-permute-start | bytes 786440 | tf_op jit(solution)/shard_map/ppermute | solution.py:41
  40.0 11.7 %collective-permute-start.10 = (bf16[256,1024]{1,0:T(8,128)(2,1)S(1)}, bf16[256,1024]{1,0:T(8,128)(2,1)S(1)}, u32[]{:S(2)}, u32[]{:S(2)}) collective-permute-start(bf16[256,1024]{1,0:T(8,128)(2,1)S(1)} %collective-permute-done.6), channel_id=1, source_target_pairs={{0,4},{4,8},{8,12},{12,14},{14,10},{10,6},{6,2},{2,0},{1,5},{5,9},... | collective-permute-start | bytes 1572872 | tf_op jit(solution)/shard_map/ppermute | solution.py:47
  40.6 10.2 %collective-permute-start.9 = (bf16[256,512]{1,0:T(8,128)(2,1)S(1)}, bf16[256,512]{1,0:T(8,128)(2,1)S(1)}, u32[]{:S(2)}, u32[]{:S(2)}) collective-permute-start(bf16[256,512]{1,0:T(8,128)(2,1)S(1)} %constant_dynamic-slice_fusion.3), channel_id=1, source_target_pairs={{0,16},{16,0},{1,17},{17,1},{2,18},{18,2},{3,19},{19,3},{4,20},{20... | collective-permute-start | bytes 786440 | tf_op jit(solution)/shard_map/ppermute | solution.py:41
  40.9 11.5 %collective-permute-start.12 = (bf16[256,1024]{1,0:T(8,128)(2,1)S(1)}, bf16[256,1024]{1,0:T(8,128)(2,1)S(1)}, u32[]{:S(2)}, u32[]{:S(2)}) collective-permute-start(bf16[256,1024]{1,0:T(8,128)(2,1)S(1)} %collective-permute-done.8), channel_id=1, source_target_pairs={{0,2},{4,0},{8,4},{12,8},{14,12},{10,14},{6,10},{2,6},{1,3},{5,1},... | collective-permute-start | bytes 1572872 | tf_op jit(solution)/shard_map/ppermute | solution.py:50
  45.2 37.6 %collective-permute-start.16 = (s32[2,2]{1,0:T(2,128)S(1)}, s32[2,2]{1,0:T(2,128)S(1)}, u32[]{:S(2)}, u32[]{:S(2)}) collective-permute-start(s32[2,2]{1,0:T(2,128)S(1)} %bitcast.121), channel_id=1, source_target_pairs={{0,1},{1,0},{2,3},{3,2},{4,5},{5,4},{6,7},{7,6},{8,9},{9,8},{10,11... | collective-permute-start | bytes 56 | tf_op jit(solution)/shard_map/ppermute | solution.py:17
  51.8 5.3 %collective-permute-start.11 = (bf16[256,512]{1,0:T(8,128)(2,1)S(1)}, bf16[256,512]{1,0:T(8,128)(2,1)S(1)}, u32[]{:S(2)}, u32[]{:S(2)}) collective-permute-start(bf16[256,512]{1,0:T(8,128)(2,1)S(1)} %constant_dynamic-slice_fusion.2), channel_id=1, source_target_pairs={{0,16},{16,0},{1,17},{17,1},{2,18},{18,2},{3,19},{19,3},{4,20},{20... | collective-permute-start | bytes 786440 | tf_op jit(solution)/shard_map/ppermute | solution.py:41
  52.2 11.3 %collective-permute-start.14 = (bf16[256,1024]{1,0:T(8,128)(2,1)S(1)}, bf16[256,1024]{1,0:T(8,128)(2,1)S(1)}, u32[]{:S(2)}, u32[]{:S(2)}) collective-permute-start(bf16[256,1024]{1,0:T(8,128)(2,1)S(1)} %collective-permute-done.10), channel_id=1, source_target_pairs={{0,4},{4,8},{8,12},{12,14},{14,10},{10,6},{6,2},{2,0},{1,5},{5,9},... | collective-permute-start | bytes 1572872 | tf_op jit(solution)/shard_map/ppermute | solution.py:47
  52.4 11.0 %collective-permute-start.13 = (bf16[256,512]{1,0:T(8,128)(2,1)S(1)}, bf16[256,512]{1,0:T(8,128)(2,1)S(1)}, u32[]{:S(2)}, u32[]{:S(2)}) collective-permute-start(bf16[256,512]{1,0:T(8,128)(2,1)S(1)} %constant_dynamic-slice_fusion.1), channel_id=1, source_target_pairs={{0,16},{16,0},{1,17},{17,1},{2,18},{18,2},{3,19},{19,3},{4,20},{20... | collective-permute-start | bytes 786440 | tf_op jit(solution)/shard_map/ppermute | solution.py:41
  57.1 53.2 %collective-permute-start.20 = (bf16[256,512]{0,1:T(8,128)(2,1)}, bf16[256,512]{0,1:T(8,128)(2,1)}, u32[]{:S(2)}, u32[]{:S(2)}) collective-permute-start(bf16[256,512]{0,1:T(8,128)(2,1)} %get-tuple-element.31), channel_id=1, source_target_pairs={{0,1},{1,0},{2,3},{3,2},{4,5},{5,4},{6,7},{7,6},{8,9},{9,8},{10,11... | collective-permute-start | bytes 786440 | tf_op jit(solution)/shard_map/ppermute | solution.py:17
  63.5 8.2 %collective-permute-start.15 = (bf16[256,512]{1,0:T(8,128)(2,1)S(1)}, bf16[256,512]{1,0:T(8,128)(2,1)S(1)}, u32[]{:S(2)}, u32[]{:S(2)}) collective-permute-start(bf16[256,512]{1,0:T(8,128)(2,1)S(1)} %constant_dynamic-slice_fusion), channel_id=1, source_target_pairs={{0,16},{16,0},{1,17},{17,1},{2,18},{18,2},{3,19},{19,3},{4,20},{20... | collective-permute-start | bytes 786440 | tf_op jit(solution)/shard_map/ppermute | solution.py:41
  76.5 10.3 %copy-start.2 = (bf16[2,256,4,128]{1,3,2,0:T(8,128)(2,1)}, bf16[2,256,4,128]{1,3,2,0:T(8,128)(2,1)S(1)}, u32[]{:S(2)}) copy-start(bf16[2,256,4,128]{1,3,2,0:T(8,128)(2,1)S(1)} %copy.36) | copy-start | bytes 1572868
  79.7 10.4 %collective-permute-start.17 = (f32[4,128,128]{2,1,0:T(8,128)}, f32[4,128,128]{2,1,0:T(8,128)}, u32[]{:S(2)}, u32[]{:S(2)}) collective-permute-start(f32[4,128,128]{2,1,0:T(8,128)} %fusion.40), channel_id=1, source_target_pairs={{0,2},{2,4},{4,6},{6,8},{8,10},{10,12},{12,14},{1,3},{3,5},{5,7},{... | collective-permute-start | bytes 786440 | tf_op jit(solution)/shard_map/ppermute | solution.py:64
  91.2 7.1 %collective-permute-start.18 = (f32[4,128,128]{2,1,0:T(8,128)S(1)}, f32[4,128,128]{2,1,0:T(8,128)S(1)}, u32[]{:S(2)}, u32[]{:S(2)}) collective-permute-start(f32[4,128,128]{2,1,0:T(8,128)S(1)} %fusion.86), channel_id=1, source_target_pairs={{0,4},{2,6},{4,8},{6,10},{8,12},{10,14},{1,5},{3,7},{5,9},{7,11},{... | collective-permute-start | bytes 786440 | tf_op jit(solution)/shard_map/ppermute | solution.py:64
  96.0 12.8 %copy-start.1 = (f32[2,4,128,128]{3,2,1,0:T(8,128)S(1)}, f32[2,4,128,128]{3,2,1,0:T(8,128)}, u32[]{:S(2)}) copy-start(f32[2,4,128,128]{3,2,1,0:T(8,128)} %copy-done) | copy-start | bytes 1572868
  98.4 10.4 %collective-permute-start.19 = (f32[4,128,128]{2,1,0:T(8,128)S(1)}, f32[4,128,128]{2,1,0:T(8,128)S(1)}, u32[]{:S(2)}, u32[]{:S(2)}) collective-permute-start(f32[4,128,128]{2,1,0:T(8,128)S(1)} %add.268), channel_id=1, source_target_pairs={{0,8},{2,10},{4,12},{6,14},{1,9},{3,11},{5,13},{7,15},{16,24},{18,... | collective-permute-start | bytes 786440 | tf_op jit(solution)/shard_map/ppermute | solution.py:64
  113.8 8.0 %collective-permute-start.21 = (f32[4,128,128]{2,1,0:T(8,128)S(1)}, f32[4,128,128]{2,1,0:T(8,128)S(1)}, u32[]{:S(2)}, u32[]{:S(2)}) collective-permute-start(f32[4,128,128]{2,1,0:T(8,128)S(1)} %fusion.41), channel_id=1, source_target_pairs={{2,0},{4,2},{6,4},{8,6},{10,8},{12,10},{14,12},{3,1},{5,3},{7,5},{... | collective-permute-start | bytes 786440 | tf_op jit(solution)/shard_map/ppermute | solution.py:64
  121.9 7.1 %collective-permute-start.22 = (f32[4,128,128]{2,1,0:T(8,128)S(1)}, f32[4,128,128]{2,1,0:T(8,128)S(1)}, u32[]{:S(2)}, u32[]{:S(2)}) collective-permute-start(f32[4,128,128]{2,1,0:T(8,128)S(1)} %fusion.85), channel_id=1, source_target_pairs={{4,0},{6,2},{8,4},{10,6},{12,8},{14,10},{5,1},{7,3},{9,5},{11,7},{... | collective-permute-start | bytes 786440 | tf_op jit(solution)/shard_map/ppermute | solution.py:64
  129.0 8.6 %copy-start.5 = (bf16[2,256,4,128]{3,2,1,0:T(4,128)(2,1)S(1)}, bf16[2,256,4,128]{3,2,1,0:T(4,128)(2,1)}, u32[]{:S(2)}) copy-start(bf16[2,256,4,128]{3,2,1,0:T(4,128)(2,1)} %copy-done.4) | copy-start | bytes 1572868
  129.1 8.5 %collective-permute-start.23 = (f32[4,128,128]{2,1,0:T(8,128)S(1)}, f32[4,128,128]{2,1,0:T(8,128)S(1)}, u32[]{:S(2)}, u32[]{:S(2)}) collective-permute-start(f32[4,128,128]{2,1,0:T(8,128)S(1)} %add.279), channel_id=1, source_target_pairs={{8,0},{10,2},{12,4},{14,6},{9,1},{11,3},{13,5},{15,7},{24,16},{26,... | collective-permute-start | bytes 786440 | tf_op jit(solution)/shard_map/ppermute | solution.py:64
  146.1 21.4 %collective-permute-start.25 = (f32[256,2048]{1,0:T(8,128)}, f32[256,2048]{1,0:T(8,128)}, u32[]{:S(2)}, u32[]{:S(2)}) collective-permute-start(f32[256,2048]{1,0:T(8,128)} %fusion), channel_id=1, source_target_pairs={{0,1},{1,0},{2,3},{3,2},{4,5},{5,4},{6,7},{7,6},{8,9},{9,8},{10,11... | collective-permute-start | bytes 6291464 | tf_op jit(solution)/shard_map/ppermute | solution.py:17
  160.8 5.7 %collective-permute-start.24 = (bf16[256,512]{1,0:T(8,128)(2,1)S(1)}, bf16[256,512]{1,0:T(8,128)(2,1)S(1)}, u32[]{:S(2)}, u32[]{:S(2)}) collective-permute-start(bf16[256,512]{1,0:T(8,128)(2,1)S(1)} %copy.44), channel_id=1, source_target_pairs={{0,1},{1,0},{2,3},{3,2},{4,5},{5,4},{6,7},{7,6},{8,9},{9,8},{10,11... | collective-permute-start | bytes 786440 | tf_op jit(solution)/shard_map/ppermute | solution.py:17
  (7 other events, 25.0 us)

commit v15 on v14

--- a/solution.py
+++ b/solution.py
@@ -106,22 +106,21 @@
     parity = lax.axis_index("groups") % 2
     share = half
     width = 2 * half
-    w_ring = jnp.zeros((chips * span, width), bf16)
-    w_x = jnp.zeros((chips * span, share), bf16)
+    w_all = jnp.zeros((chips * span, width + share), bf16)
     for src, (ringed, swapped) in ring_gather(block, chips, c, parity):
-        w_ring = lax.dynamic_update_slice_in_dim(w_ring, ringed, src * span, axis=0)
-        w_x = lax.dynamic_update_slice_in_dim(w_x, swapped, src * span, axis=0)
-    even = parity == 0
-
-    def project(w):
-        return jnp.dot(x_pair, w, preferred_element_type=f32).astype(bf16).reshape(2, tok, heads, DH)
-
-    p_lo = project(w_ring[:, :share])
-    p_hi = project(w_ring[:, share:])
-    p_x = project(w_x)
-    query = jnp.where(even, p_lo, p_x)
-    key = jnp.where(even, p_hi, p_lo)
-    value = jnp.where(even, p_x, p_hi)
+        w_all = lax.dynamic_update_slice(w_all, ringed, (src * span, 0))
+        w_all = lax.dynamic_update_slice(w_all, swapped, (src * span, width))
+    at_q = parity * width
+    at_k = (1 - parity) * share
+    at_v = width - parity * share
+    p_all = jnp.dot(x_pair, w_all, preferred_element_type=f32).astype(bf16)
+
+    def pick(at):
+        return lax.dynamic_slice_in_dim(p_all, at, share, axis=1).reshape(2, tok, heads, DH)
+
+    query = pick(at_q)
+    key = pick(at_k)
+    value = pick(at_v)
 
     local = jnp.einsum("jthd,jthe->jhde", key, value, preferred_element_type=f32)
     state0 = exclusive_scan(local[0] + local[1], chips, False)
@@ -174,12 +173,12 @@
 
     def grad_rows(j):
         dims = (((1,), (1,)), ((), ()))
-        d_lo = jnp.where(even, dq_b[j], dk_b[j])
-        d_hi = jnp.where(even, dk_b[j], dv_b[j])
-        d_x = jnp.where(even, dv_b[j], dq_b[j])
-        g = lax.dot_general(d_lo, w_ring[:, :share], dims, preferred_element_type=f32)
-        g = g + lax.dot_general(d_hi, w_ring[:, share:], dims, preferred_element_type=f32)
-        return g + lax.dot_general(d_x, w_x, dims, preferred_element_type=f32)
+        g = None
+        for d, at in ((dq_b[j], at_q), (dk_b[j], at_k), (dv_b[j], at_v)):
+            w = lax.dynamic_slice_in_dim(w_all, at, share, axis=1)
+            t = lax.dot_general(d, w, dims, preferred_element_type=f32)
+            g = t if g is None else g + t
+        return g
 
     received = swap(grad_rows(1))
     own, received = lax.optimization_barrier((grad_rows(0), received))

time: 171 us -> 173 us (1.012); the launches traced: 170 us -> 170 us
  waiting for transfers between devices: 38.8 us -> 52.6 us
  starting transfers between devices: 51.1 us -> 44.4 us
  matrix products: 28.8 us -> 25.3 us
  other arithmetic: 14.6 us -> 12.7 us
  local copies, waits for them, and re-layouts: 26.7 us -> 24.8 us
    ppermute x4, waiting for transfers between devices: 1.03 us -> 10.8 us  [ring_gather(): fwd = lax.ppermute(fwd, 'chip', ahead)]
    ppermute x6, starting transfers between devices: 26.5 us -> 19.2 us  [swap(): return lax.ppermute(x, 'core', [(0, 1), (1, 0)])]
    select_n x5 -> x0, local copies, waits for them, and re-layouts: 5 us -> none  [the longest x2 3.26 us: on_device(): query = jnp.where(even, p_lo, p_x)]
    dynamic_update_slice x16, local copies, waits for them, and re-layouts: 9.22 us -> 13.1 us  [the longest x8 7.08 us: on_device(): w_all = lax.dynamic_update_slice(w_all, ringed, (src * span, 0))]
    ppermute x6, waiting for transfers between devices: 26.3 us -> 29.1 us  [exclusive_scan(): got = lax.ppermute(incl, 'chip', perm)]
    ppermute x7, waiting for transfers between devices: 9.94 us -> 12.7 us  [land(): return (piece, lax.ppermute(sent, 'groups', partner))]
    dot_general x9 -> x7, matrix products: 23.3 us -> 20.8 us  [the longest x6 14.3 us: grad_rows(): t = lax.dot_general(d, w, dims, preferred_element_type=f32)]
    dynamic_slice x7, local copies, waits for them, and re-layouts: 2.04 us -> 0.13 us  [land(): sent = lax.dynamic_slice_in_dim(piece, p * share, share, axis=1)]
  transfers between devices with their start and end apart: 26 -> 26, of which waited for: 13 -> 13; matrix products, arithmetic and copies ran while one was open for 28% -> 27% of each run, Pallas kernels for 0% -> 0%
where the time goes in v15:
time: 173 us; the launch traced here: 170 us
  waiting for transfers between devices  52.6 us (30%)
  starting transfers between devices  44.4 us (26%)
  matrix products  25.3 us (15%)
  local copies, waits for them, and re-layouts  24.8 us (14%)
  other arithmetic  12.7 us (7%)
  between operations  10.6 us (6%)
    ppermute x6, waiting for transfers between devices, exclusive_scan(): got = lax.ppermute(incl, 'chip', perm)  29.1 us
    ppermute x6, starting transfers between devices, swap(): return lax.ppermute(x, 'core', [(0, 1), (1, 0)])  19.2 us
    ppermute x6, starting transfers between devices, exclusive_scan(): got = lax.ppermute(incl, 'chip', perm)  15.8 us
    dot_general x6, matrix products, grad_rows(): t = lax.dot_general(d, w, dims, preferred_element_type=f32)  14.3 us
    ppermute x7, waiting for transfers between devices, land(): return (piece, lax.ppermute(sent, 'groups', partner))  12.7 us
    ppermute x4, waiting for transfers between devices, ring_gather(): fwd = lax.ppermute(fwd, 'chip', ahead)  10.8 us
    dynamic_update_slice x8, local copies, waits for them, and re-layouts, on_device(): w_all = lax.dynamic_update_slice(w_all, ringed, (src * span, 0))  7.08 us
    dot_general x1, matrix products, on_device(): p_all = jnp.dot(x_pair, w_all, preferred_element_type=f32).astype(bf16)  6.53 us
  transfers between devices with their start and end apart: 26, of which 13 were waited for; matrix products, arithmetic and copies ran while one was open for 27% of the time, Pallas kernels for 0%

profile of v15, /device:TPU:15, one launch (start us, length us, event | category | flops | bytes accessed | tf_op | source)
XLA Modules:
  0.0 170.5 jit_solution(376878254733304256)
XLA Ops:
  6.8 3.0 %broadcast_in_dim.33 = bf16[2048,1536]{1,0:T(8,128)(2,1)} broadcast(bf16[]{:T(256)} %constant.94.clone.1), dimensions={} | broadcast | bytes 6291458 | tf_op jit(solution)/shard_map/broadcast_in_dim | solution.py:109
  11.1 1.3 collective-permute-start.4
  12.4 2.6 %add_convert_fusion.1 = bf16[256,2048]{1,0:T(8,128)(2,1)} fusion(bf16[256,2048]{1,0:T(8,128)(2,1)S(1)} %copy-done, bf16[256,2048]{1,0:T(8,128)(2,1)} %param.9), kind=kLoop, calls=%fused_computation.11 | loop fusion | flops 2097152 | bytes 3145728 | tf_op jit(solution)/shard_map/convert_element_type | solution.py:91
  28.1 1.3 collective-permute-start.8
  30.2 4.6 %collective-permute-done.3 = bf16[256,512]{1,0:T(8,128)(2,1)S(1)} collective-permute-done((bf16[256,512]{1,0:T(8,128)(2,1)S(1)}, bf16[256,512]{1,0:T(8,128)(2,1)S(1)}, u32[]{:S(2)}, u32[]{:S(2)}) %collective-permute-start.3) | collective-permute-done | bytes 262176 | tf_op jit(solution)/shard_map/ppermute | solution.py:41
  36.7 3.7 %collective-permute-done.6 = bf16[256,1024]{1,0:T(8,128)(2,1)S(1)} collective-permute-done((bf16[256,1024]{1,0:T(8,128)(2,1)S(1)}, bf16[256,1024]{1,0:T(8,128)(2,1)S(1)}, u32[]{:S(2)}, u32[]{:S(2)}) %collective-permute-start.6) | collective-permute-done | bytes 524320 | tf_op jit(solution)/shard_map/ppermute | solution.py:47
  45.0 2.2 %collective-permute-done.7 = bf16[256,512]{1,0:T(8,128)(2,1)S(1)} collective-permute-done((bf16[256,512]{1,0:T(8,128)(2,1)S(1)}, bf16[256,512]{1,0:T(8,128)(2,1)S(1)}, u32[]{:S(2)}, u32[]{:S(2)}) %collective-permute-start.7) | collective-permute-done | bytes 262176 | tf_op jit(solution)/shard_map/ppermute | solution.py:41
  50.0 3.6 %collective-permute-done.10 = bf16[256,1024]{1,0:T(8,128)(2,1)S(1)} collective-permute-done((bf16[256,1024]{1,0:T(8,128)(2,1)S(1)}, bf16[256,1024]{1,0:T(8,128)(2,1)S(1)}, u32[]{:S(2)}, u32[]{:S(2)}) %collective-permute-start.10) | collective-permute-done | bytes 524320 | tf_op jit(solution)/shard_map/ppermute | solution.py:47
  55.0 3.2 %collective-permute-start.16 = (s32[2,2]{1,0:T(2,128)S(1)}, s32[2,2]{1,0:T(2,128)S(1)}, u32[]{:S(2)}, u32[]{:S(2)}) collective-permute-start(s32[2,2]{1,0:T(2,128)S(1)} %bitcast.119), channel_id=1, source_target_pairs={{0,1},{1,0},{2,3},{3,2},{4,5},{5,4},{6,7},{7,6},{8,9},{9,8},{10,11... | collective-permute-start | bytes 56 | tf_op jit(solution)/shard_map/ppermute | solution.py:17
  61.0 3.5 %collective-permute-done.14 = bf16[256,1024]{1,0:T(8,128)(2,1)S(1)} collective-permute-done((bf16[256,1024]{1,0:T(8,128)(2,1)S(1)}, bf16[256,1024]{1,0:T(8,128)(2,1)S(1)}, u32[]{:S(2)}, u32[]{:S(2)}) %collective-permute-start.14) | collective-permute-done | bytes 524320 | tf_op jit(solution)/shard_map/ppermute | solution.py:47
  67.2 5.7 %collective-permute-done.15 = bf16[256,512]{1,0:T(8,128)(2,1)S(1)} collective-permute-done((bf16[256,512]{1,0:T(8,128)(2,1)S(1)}, bf16[256,512]{1,0:T(8,128)(2,1)S(1)}, u32[]{:S(2)}, u32[]{:S(2)}) %collective-permute-start.15) | collective-permute-done | bytes 262176 | tf_op jit(solution)/shard_map/ppermute | solution.py:41
  73.6 6.5 %convolution_convert_fusion = bf16[512,1536]{1,0:T(8,128)(2,1)S(1)} fusion(bf16[2048,1536]{1,0:T(8,128)(2,1)} %constant_dynamic-update-slice_fusion.9, bf16[256,2048]{1,0:T(8,128)(2,1)S(1)} %collective-permute-done, bf16[256,2048]{1,0:T(8,128)(2,1)} %add_convert_fusion.1), kind=kOutput, calls=%fused_computation | convolution fusion | flops 3226206208 | bytes 9961472 | tf_op jit(solution)/shard_map/dot_general | solution.py:116
  81.9 2.4 %collective-permute-start.17 = (f32[4,128,128]{2,1,0:T(8,128)}, f32[4,128,128]{2,1,0:T(8,128)}, u32[]{:S(2)}, u32[]{:S(2)}) collective-permute-start(f32[4,128,128]{2,1,0:T(8,128)} %fusion.37), channel_id=1, source_target_pairs={{0,2},{2,4},{4,6},{6,8},{8,10},{10,12},{12,14},{1,3},{3,5},{5,7},{... | collective-permute-start | bytes 786440 | tf_op jit(solution)/shard_map/ppermute | solution.py:64
  85.3 4.0 %collective-permute-done.17 = f32[4,128,128]{2,1,0:T(8,128)} collective-permute-done((f32[4,128,128]{2,1,0:T(8,128)}, f32[4,128,128]{2,1,0:T(8,128)}, u32[]{:S(2)}, u32[]{:S(2)}) %collective-permute-start.17) | collective-permute-done | bytes 262176 | tf_op jit(solution)/shard_map/ppermute | solution.py:64
  90.3 3.2 %collective-permute-start.18 = (f32[4,128,128]{2,1,0:T(8,128)S(1)}, f32[4,128,128]{2,1,0:T(8,128)S(1)}, u32[]{:S(2)}, u32[]{:S(2)}) collective-permute-start(f32[4,128,128]{2,1,0:T(8,128)S(1)} %fusion.86), channel_id=1, source_target_pairs={{0,4},{2,6},{4,8},{6,10},{8,12},{10,14},{1,5},{3,7},{5,9},{7,11},{... | collective-permute-start | bytes 786440 | tf_op jit(solution)/shard_map/ppermute | solution.py:64
  94.0 3.4 %collective-permute-done.18 = f32[4,128,128]{2,1,0:T(8,128)S(1)} collective-permute-done((f32[4,128,128]{2,1,0:T(8,128)S(1)}, f32[4,128,128]{2,1,0:T(8,128)S(1)}, u32[]{:S(2)}, u32[]{:S(2)}) %collective-permute-start.18) | collective-permute-done | bytes 262176 | tf_op jit(solution)/shard_map/ppermute | solution.py:64
  97.4 4.3 %collective-permute-start.19 = (f32[4,128,128]{2,1,0:T(8,128)S(1)}, f32[4,128,128]{2,1,0:T(8,128)S(1)}, u32[]{:S(2)}, u32[]{:S(2)}) collective-permute-start(f32[4,128,128]{2,1,0:T(8,128)S(1)} %add.287), channel_id=1, source_target_pairs={{0,8},{2,10},{4,12},{6,14},{1,9},{3,11},{5,13},{7,15},{16,24},{18,... | collective-permute-start | bytes 786440 | tf_op jit(solution)/shard_map/ppermute | solution.py:64
  102.2 5.4 %collective-permute-done.19 = f32[4,128,128]{2,1,0:T(8,128)S(1)} collective-permute-done((f32[4,128,128]{2,1,0:T(8,128)S(1)}, f32[4,128,128]{2,1,0:T(8,128)S(1)}, u32[]{:S(2)}, u32[]{:S(2)}) %collective-permute-start.19) | collective-permute-done | bytes 262176 | tf_op jit(solution)/shard_map/ppermute | solution.py:64
  112.6 2.6 %collective-permute-start.21 = (f32[4,128,128]{2,1,0:T(8,128)S(1)}, f32[4,128,128]{2,1,0:T(8,128)S(1)}, u32[]{:S(2)}, u32[]{:S(2)}) collective-permute-start(f32[4,128,128]{2,1,0:T(8,128)S(1)} %fusion.38), channel_id=1, source_target_pairs={{2,0},{4,2},{6,4},{8,6},{10,8},{12,10},{14,12},{3,1},{5,3},{7,5},{... | collective-permute-start | bytes 786440 | tf_op jit(solution)/shard_map/ppermute | solution.py:64
  116.0 4.6 %collective-permute-done.21 = f32[4,128,128]{2,1,0:T(8,128)S(1)} collective-permute-done((f32[4,128,128]{2,1,0:T(8,128)S(1)}, f32[4,128,128]{2,1,0:T(8,128)S(1)}, u32[]{:S(2)}, u32[]{:S(2)}) %collective-permute-start.21) | collective-permute-done | bytes 262176 | tf_op jit(solution)/shard_map/ppermute | solution.py:64
  120.7 2.1 %collective-permute-start.22 = (f32[4,128,128]{2,1,0:T(8,128)S(1)}, f32[4,128,128]{2,1,0:T(8,128)S(1)}, u32[]{:S(2)}, u32[]{:S(2)}) collective-permute-start(f32[4,128,128]{2,1,0:T(8,128)S(1)} %fusion.85), channel_id=1, source_target_pairs={{4,0},{6,2},{8,4},{10,6},{12,8},{14,10},{5,1},{7,3},{9,5},{11,7},{... | collective-permute-start | bytes 786440 | tf_op jit(solution)/shard_map/ppermute | solution.py:64
  123.1 5.0 %collective-permute-done.22 = f32[4,128,128]{2,1,0:T(8,128)S(1)} collective-permute-done((f32[4,128,128]{2,1,0:T(8,128)S(1)}, f32[4,128,128]{2,1,0:T(8,128)S(1)}, u32[]{:S(2)}, u32[]{:S(2)}) %collective-permute-start.22) | collective-permute-done | bytes 262176 | tf_op jit(solution)/shard_map/ppermute | solution.py:64
  128.1 1.3 collective-permute-start.23
  129.5 6.7 %collective-permute-done.23 = f32[4,128,128]{2,1,0:T(8,128)S(1)} collective-permute-done((f32[4,128,128]{2,1,0:T(8,128)S(1)}, f32[4,128,128]{2,1,0:T(8,128)S(1)}, u32[]{:S(2)}, u32[]{:S(2)}) %collective-permute-start.23) | collective-permute-done | bytes 262176 | tf_op jit(solution)/shard_map/ppermute | solution.py:64
  137.1 2.4 %fusion.5 = f32[256,2048]{1,0:T(8,128)S(1)} fusion(bf16[256,512]{0,1:T(8,128)(2,1)S(1)} %bitcast.115, bf16[2048,1536]{1,0:T(8,128)(2,1)} %constant_dynamic-update-slice_fusion.9, s32[]{:T(128)S(6)} %select_n.230), kind=kOutput, calls=%fused_computation.12 | convolution fusion | flops 536870912 | bytes 4456452 | tf_op jit(solution)/shard_map/dot_general | solution.py:179
  139.5 2.4 %fusion.9 = f32[256,2048]{1,0:T(8,128)S(1)} fusion(bf16[256,512]{0,1:T(8,128)(2,1)S(1)} %bitcast.116, bf16[2048,1536]{1,0:T(8,128)(2,1)} %constant_dynamic-update-slice_fusion.9, s32[]{:T(128)S(6)} %select_n.232), kind=kOutput, calls=%fused_computation.16 | convolution fusion | flops 536870912 | bytes 4456452 | tf_op jit(solution)/shard_map/dot_general | solution.py:179
  141.8 2.4 %fusion = f32[256,2048]{1,0:T(8,128)S(1)} fusion(f32[256,2048]{1,0:T(8,128)S(1)} %fusion.5, f32[256,2048]{1,0:T(8,128)S(1)} %fusion.9, bf16[256,512]{0,1:T(8,128)(2,1)S(1)} %bitcast.112, bf16[2048,1536]{1,0:T(8,128)(2,1)} %constant_dynamic-update-slice_fusion.9, s32[]{:T(128)S(6)} %select_n.231), kind=kOutput, calls=%fused_computation.2 | convolution fusion | flops 537919488 | bytes 8650756 | tf_op jit(solution)/shard_map/dot_general | solution.py:179
  144.2 14.1 %collective-permute-start.25 = (f32[256,2048]{1,0:T(8,128)S(1)}, f32[256,2048]{1,0:T(8,128)}, u32[]{:S(2)}, u32[]{:S(2)}) collective-permute-start(f32[256,2048]{1,0:T(8,128)S(1)} %fusion), channel_id=1, source_target_pairs={{0,1},{1,0},{2,3},{3,2},{4,5},{5,4},{6,7},{7,6},{8,9},{9,8},{10,11... | collective-permute-start | bytes 6291464 | tf_op jit(solution)/shard_map/ppermute | solution.py:17
  159.4 2.4 %fusion.7 = f32[256,2048]{1,0:T(8,128)S(1)} fusion(bf16[256,512]{0,1:T(8,128)(2,1)S(1)} %bitcast.113, bf16[2048,1536]{1,0:T(8,128)(2,1)} %constant_dynamic-update-slice_fusion.9, s32[]{:T(128)S(6)} %select_n.230), kind=kOutput, calls=%fused_computation.14 | convolution fusion | flops 536870912 | bytes 4456452 | tf_op jit(solution)/shard_map/dot_general | solution.py:179
  161.8 2.4 %fusion.11 = f32[256,2048]{1,0:T(8,128)S(1)} fusion(bf16[256,512]{0,1:T(8,128)(2,1)S(1)} %bitcast.114, bf16[2048,1536]{1,0:T(8,128)(2,1)} %constant_dynamic-update-slice_fusion.9, s32[]{:T(128)S(6)} %select_n.232), kind=kOutput, calls=%fused_computation.18 | convolution fusion | flops 536870912 | bytes 4456452 | tf_op jit(solution)/shard_map/dot_general | solution.py:179
  164.2 2.4 %fusion.1 = f32[256,2048]{1,0:T(8,128)S(1)} fusion(f32[256,2048]{1,0:T(8,128)S(1)} %fusion.7, f32[256,2048]{1,0:T(8,128)S(1)} %fusion.11, bf16[256,512]{0,1:T(8,128)(2,1)S(1)} %bitcast.111, bf16[2048,1536]{1,0:T(8,128)(2,1)} %constant_dynamic-update-slice_fusion.9, s32[]{:T(128)S(6)} %select_n.231), kind=kOutput, calls=%fused_computation.4 | convolution fusion | flops 537919488 | bytes 8650756 | tf_op jit(solution)/shard_map/dot_general | solution.py:179
  167.6 2.8 %add_convert_fusion = bf16[256,2048]{1,0:T(8,128)(2,1)} fusion(f32[256,2048]{1,0:T(8,128)S(1)} %fusion.1, f32[256,2048]{1,0:T(8,128)} %collective-permute-done.25), kind=kLoop, calls=%fused_computation.8 | loop fusion | flops 1048576 | bytes 5242880 | tf_op jit(solution)/shard_map/convert_element_type | solution.py:185
  (116 shorter events, 42.5 us)
Async XLA Ops:
  2.8 9.6 %copy-start = (bf16[256,2048]{1,0:T(8,128)(2,1)S(1)}, bf16[256,2048]{1,0:T(8,128)(2,1)}, u32[]{:S(2)}) copy-start(bf16[256,2048]{1,0:T(8,128)(2,1)} %param.10) | copy-start | bytes 3145732
  2.8 3.0 %collective-permute-start.1 = (bf16[128,1536]{1,0:T(8,128)(2,1)S(1)}, bf16[128,1536]{1,0:T(8,128)(2,1)}, u32[]{:S(2)}, u32[]{:S(2)}) collective-permute-start(bf16[128,1536]{1,0:T(8,128)(2,1)S(1)} %pad_maximum_fusion.1), channel_id=1, source_target_pairs={{0,1},{1,0},{2,3},{3,2},{4,5},{5,4},{6,7},{7,6},{8,9},{9,8},{10,11... | collective-permute-start | bytes 1179656 | tf_op jit(solution)/shard_map/ppermute | solution.py:17
  5.6 103.5 %collective-permute-start.20 = (bf16[256,512]{0,1:T(8,128)(2,1)}, bf16[256,512]{0,1:T(8,128)(2,1)}, u32[]{:S(2)}, u32[]{:S(2)}) collective-permute-start(bf16[256,512]{0,1:T(8,128)(2,1)} %get-tuple-element.30), channel_id=1, source_target_pairs={{0,1},{1,0},{2,3},{3,2},{4,5},{5,4},{6,7},{7,6},{8,9},{9,8},{10,11... | collective-permute-start | bytes 786440 | tf_op jit(solution)/shard_map/ppermute | solution.py:17
  5.7 10.3 %copy-start.4 = (s32[8]{0:T(128)S(1)}, s32[8]{0:T(128)}, u32[]{:S(2)}) copy-start(s32[8]{0:T(128)} %constant.120.clone) | copy-start | bytes 100
  5.7 15.8 %copy-start.2 = (s32[8]{0:T(128)S(1)}, s32[8]{0:T(128)}, u32[]{:S(2)}) copy-start(s32[8]{0:T(128)} %constant.119.clone) | copy-start | bytes 100
  11.0 44.0 %copy-start.3 = (s32[1,2,2]{2,1,0:T(2,128)S(1)}, s32[1,2,2]{2,1,0:T(2,128)}, u32[]{:S(2)}) copy-start(s32[1,2,2]{2,1,0:T(2,128)} %param.15) | copy-start | bytes 52
  11.0 15.8 %collective-permute-start.2 = (bf16[256,1024]{1,0:T(8,128)(2,1)}, bf16[256,1024]{1,0:T(8,128)(2,1)S(1)}, u32[]{:S(2)}, u32[]{:S(2)}) collective-permute-start(bf16[256,1024]{1,0:T(8,128)(2,1)} %get-tuple-element.11), channel_id=1, source_target_pairs={{0,4},{4,8},{8,12},{12,14},{14,10},{10,6},{6,2},{2,0},{1,5},{5,9},... | collective-permute-start | bytes 1572872 | tf_op jit(solution)/shard_map/ppermute | solution.py:47
  11.1 16.9 %collective-permute-start.4 = (bf16[256,1024]{1,0:T(8,128)(2,1)}, bf16[256,1024]{1,0:T(8,128)(2,1)S(1)}, u32[]{:S(2)}, u32[]{:S(2)}) collective-permute-start(bf16[256,1024]{1,0:T(8,128)(2,1)} %get-tuple-element.11), channel_id=1, source_target_pairs={{0,2},{4,0},{8,4},{12,8},{14,12},{10,14},{6,10},{2,6},{1,3},{5,1},... | collective-permute-start | bytes 1572872 | tf_op jit(solution)/shard_map/ppermute | solution.py:50
  15.0 58.6 %collective-permute-start = (bf16[256,2048]{1,0:T(8,128)(2,1)}, bf16[256,2048]{1,0:T(8,128)(2,1)S(1)}, u32[]{:S(2)}, u32[]{:S(2)}) collective-permute-start(bf16[256,2048]{1,0:T(8,128)(2,1)} %add_convert_fusion.1), channel_id=1, source_target_pairs={{0,1},{1,0},{2,3},{3,2},{4,5},{5,4},{6,7},{7,6},{8,9},{9,8},{10,11... | collective-permute-start | bytes 3145736 | tf_op jit(solution)/shard_map/ppermute | solution.py:17
  26.8 8.0 %collective-permute-start.3 = (bf16[256,512]{1,0:T(8,128)(2,1)S(1)}, bf16[256,512]{1,0:T(8,128)(2,1)S(1)}, u32[]{:S(2)}, u32[]{:S(2)}) collective-permute-start(bf16[256,512]{1,0:T(8,128)(2,1)S(1)} %constant_dynamic-slice_fusion.9), channel_id=1, source_target_pairs={{0,16},{16,0},{1,17},{17,1},{2,18},{18,2},{3,19},{19,3},{4,20},{20... | collective-permute-start | bytes 786440 | tf_op jit(solution)/shard_map/ppermute | solution.py:41
  27.2 13.2 %collective-permute-start.6 = (bf16[256,1024]{1,0:T(8,128)(2,1)S(1)}, bf16[256,1024]{1,0:T(8,128)(2,1)S(1)}, u32[]{:S(2)}, u32[]{:S(2)}) collective-permute-start(bf16[256,1024]{1,0:T(8,128)(2,1)S(1)} %collective-permute-done.2), channel_id=1, source_target_pairs={{0,4},{4,8},{8,12},{12,14},{14,10},{10,6},{6,2},{2,0},{1,5},{5,9},... | collective-permute-start | bytes 1572872 | tf_op jit(solution)/shard_map/ppermute | solution.py:47
  28.1 14.7 %collective-permute-start.8 = (bf16[256,1024]{1,0:T(8,128)(2,1)S(1)}, bf16[256,1024]{1,0:T(8,128)(2,1)S(1)}, u32[]{:S(2)}, u32[]{:S(2)}) collective-permute-start(bf16[256,1024]{1,0:T(8,128)(2,1)S(1)} %collective-permute-done.4), channel_id=1, source_target_pairs={{0,2},{4,0},{8,4},{12,8},{14,12},{10,14},{6,10},{2,6},{1,3},{5,1},... | collective-permute-start | bytes 1572872 | tf_op jit(solution)/shard_map/ppermute | solution.py:50
  34.8 7.0 %collective-permute-start.5 = (bf16[256,512]{1,0:T(8,128)(2,1)S(1)}, bf16[256,512]{1,0:T(8,128)(2,1)S(1)}, u32[]{:S(2)}, u32[]{:S(2)}) collective-permute-start(bf16[256,512]{1,0:T(8,128)(2,1)S(1)} %constant_dynamic-slice_fusion.8), channel_id=1, source_target_pairs={{0,16},{16,0},{1,17},{17,1},{2,18},{18,2},{3,19},{19,3},{4,20},{20... | collective-permute-start | bytes 786440 | tf_op jit(solution)/shard_map/ppermute | solution.py:41
  40.4 6.8 %collective-permute-start.7 = (bf16[256,512]{1,0:T(8,128)(2,1)S(1)}, bf16[256,512]{1,0:T(8,128)(2,1)S(1)}, u32[]{:S(2)}, u32[]{:S(2)}) collective-permute-start(bf16[256,512]{1,0:T(8,128)(2,1)S(1)} %constant_dynamic-slice_fusion.7), channel_id=1, source_target_pairs={{0,16},{16,0},{1,17},{17,1},{2,18},{18,2},{3,19},{19,3},{4,20},{20... | collective-permute-start | bytes 786440 | tf_op jit(solution)/shard_map/ppermute | solution.py:41
  41.9 11.7 %collective-permute-start.10 = (bf16[256,1024]{1,0:T(8,128)(2,1)S(1)}, bf16[256,1024]{1,0:T(8,128)(2,1)S(1)}, u32[]{:S(2)}, u32[]{:S(2)}) collective-permute-start(bf16[256,1024]{1,0:T(8,128)(2,1)S(1)} %collective-permute-done.6), channel_id=1, source_target_pairs={{0,4},{4,8},{8,12},{12,14},{14,10},{10,6},{6,2},{2,0},{1,5},{5,9},... | collective-permute-start | bytes 1572872 | tf_op jit(solution)/shard_map/ppermute | solution.py:47
  42.8 12.2 %collective-permute-start.12 = (bf16[256,1024]{1,0:T(8,128)(2,1)S(1)}, bf16[256,1024]{1,0:T(8,128)(2,1)S(1)}, u32[]{:S(2)}, u32[]{:S(2)}) collective-permute-start(bf16[256,1024]{1,0:T(8,128)(2,1)S(1)} %collective-permute-done.8), channel_id=1, source_target_pairs={{0,2},{4,0},{8,4},{12,8},{14,12},{10,14},{6,10},{2,6},{1,3},{5,1},... | collective-permute-start | bytes 1572872 | tf_op jit(solution)/shard_map/ppermute | solution.py:50
  47.2 6.6 %collective-permute-start.9 = (bf16[256,512]{1,0:T(8,128)(2,1)S(1)}, bf16[256,512]{1,0:T(8,128)(2,1)S(1)}, u32[]{:S(2)}, u32[]{:S(2)}) collective-permute-start(bf16[256,512]{1,0:T(8,128)(2,1)S(1)} %constant_dynamic-slice_fusion.6), channel_id=1, source_target_pairs={{0,16},{16,0},{1,17},{17,1},{2,18},{18,2},{3,19},{19,3},{4,20},{20... | collective-permute-start | bytes 786440 | tf_op jit(solution)/shard_map/ppermute | solution.py:41
  53.6 10.8 %collective-permute-start.14 = (bf16[256,1024]{1,0:T(8,128)(2,1)S(1)}, bf16[256,1024]{1,0:T(8,128)(2,1)S(1)}, u32[]{:S(2)}, u32[]{:S(2)}) collective-permute-start(bf16[256,1024]{1,0:T(8,128)(2,1)S(1)} %collective-permute-done.10), channel_id=1, source_target_pairs={{0,4},{4,8},{8,12},{12,14},{14,10},{10,6},{6,2},{2,0},{1,5},{5,9},... | collective-permute-start | bytes 1572872 | tf_op jit(solution)/shard_map/ppermute | solution.py:47
  53.8 5.3 %collective-permute-start.11 = (bf16[256,512]{1,0:T(8,128)(2,1)S(1)}, bf16[256,512]{1,0:T(8,128)(2,1)S(1)}, u32[]{:S(2)}, u32[]{:S(2)}) collective-permute-start(bf16[256,512]{1,0:T(8,128)(2,1)S(1)} %constant_dynamic-slice_fusion.5), channel_id=1, source_target_pairs={{0,16},{16,0},{1,17},{17,1},{2,18},{18,2},{3,19},{19,3},{4,20},{20... | collective-permute-start | bytes 786440 | tf_op jit(solution)/shard_map/ppermute | solution.py:41
  55.0 29.3 %collective-permute-start.16 = (s32[2,2]{1,0:T(2,128)S(1)}, s32[2,2]{1,0:T(2,128)S(1)}, u32[]{:S(2)}, u32[]{:S(2)}) collective-permute-start(s32[2,2]{1,0:T(2,128)S(1)} %bitcast.119), channel_id=1, source_target_pairs={{0,1},{1,0},{2,3},{3,2},{4,5},{5,4},{6,7},{7,6},{8,9},{9,8},{10,11... | collective-permute-start | bytes 56 | tf_op jit(solution)/shard_map/ppermute | solution.py:17
  59.1 6.5 %collective-permute-start.13 = (bf16[256,512]{1,0:T(8,128)(2,1)S(1)}, bf16[256,512]{1,0:T(8,128)(2,1)S(1)}, u32[]{:S(2)}, u32[]{:S(2)}) collective-permute-start(bf16[256,512]{1,0:T(8,128)(2,1)S(1)} %constant_dynamic-slice_fusion.4), channel_id=1, source_target_pairs={{0,16},{16,0},{1,17},{17,1},{2,18},{18,2},{3,19},{19,3},{4,20},{20... | collective-permute-start | bytes 786440 | tf_op jit(solution)/shard_map/ppermute | solution.py:41
  64.5 8.4 %collective-permute-start.15 = (bf16[256,512]{1,0:T(8,128)(2,1)S(1)}, bf16[256,512]{1,0:T(8,128)(2,1)S(1)}, u32[]{:S(2)}, u32[]{:S(2)}) collective-permute-start(bf16[256,512]{1,0:T(8,128)(2,1)S(1)} %constant_dynamic-slice_fusion.3), channel_id=1, source_target_pairs={{0,16},{16,0},{1,17},{17,1},{2,18},{18,2},{3,19},{19,3},{4,20},{20... | collective-permute-start | bytes 786440 | tf_op jit(solution)/shard_map/ppermute | solution.py:41
  81.9 7.4 %collective-permute-start.17 = (f32[4,128,128]{2,1,0:T(8,128)}, f32[4,128,128]{2,1,0:T(8,128)}, u32[]{:S(2)}, u32[]{:S(2)}) collective-permute-start(f32[4,128,128]{2,1,0:T(8,128)} %fusion.37), channel_id=1, source_target_pairs={{0,2},{2,4},{4,6},{6,8},{8,10},{10,12},{12,14},{1,3},{3,5},{5,7},{... | collective-permute-start | bytes 786440 | tf_op jit(solution)/shard_map/ppermute | solution.py:64
  90.3 7.1 %collective-permute-start.18 = (f32[4,128,128]{2,1,0:T(8,128)S(1)}, f32[4,128,128]{2,1,0:T(8,128)S(1)}, u32[]{:S(2)}, u32[]{:S(2)}) collective-permute-start(f32[4,128,128]{2,1,0:T(8,128)S(1)} %fusion.86), channel_id=1, source_target_pairs={{0,4},{2,6},{4,8},{6,10},{8,12},{10,14},{1,5},{3,7},{5,9},{7,11},{... | collective-permute-start | bytes 786440 | tf_op jit(solution)/shard_map/ppermute | solution.py:64
  97.4 10.2 %collective-permute-start.19 = (f32[4,128,128]{2,1,0:T(8,128)S(1)}, f32[4,128,128]{2,1,0:T(8,128)S(1)}, u32[]{:S(2)}, u32[]{:S(2)}) collective-permute-start(f32[4,128,128]{2,1,0:T(8,128)S(1)} %add.287), channel_id=1, source_target_pairs={{0,8},{2,10},{4,12},{6,14},{1,9},{3,11},{5,13},{7,15},{16,24},{18,... | collective-permute-start | bytes 786440 | tf_op jit(solution)/shard_map/ppermute | solution.py:64
  112.6 8.0 %collective-permute-start.21 = (f32[4,128,128]{2,1,0:T(8,128)S(1)}, f32[4,128,128]{2,1,0:T(8,128)S(1)}, u32[]{:S(2)}, u32[]{:S(2)}) collective-permute-start(f32[4,128,128]{2,1,0:T(8,128)S(1)} %fusion.38), channel_id=1, source_target_pairs={{2,0},{4,2},{6,4},{8,6},{10,8},{12,10},{14,12},{3,1},{5,3},{7,5},{... | collective-permute-start | bytes 786440 | tf_op jit(solution)/shard_map/ppermute | solution.py:64
  120.7 7.4 %collective-permute-start.22 = (f32[4,128,128]{2,1,0:T(8,128)S(1)}, f32[4,128,128]{2,1,0:T(8,128)S(1)}, u32[]{:S(2)}, u32[]{:S(2)}) collective-permute-start(f32[4,128,128]{2,1,0:T(8,128)S(1)} %fusion.85), channel_id=1, source_target_pairs={{4,0},{6,2},{8,4},{10,6},{12,8},{14,10},{5,1},{7,3},{9,5},{11,7},{... | collective-permute-start | bytes 786440 | tf_op jit(solution)/shard_map/ppermute | solution.py:64
  128.1 8.1 %collective-permute-start.23 = (f32[4,128,128]{2,1,0:T(8,128)S(1)}, f32[4,128,128]{2,1,0:T(8,128)S(1)}, u32[]{:S(2)}, u32[]{:S(2)}) collective-permute-start(f32[4,128,128]{2,1,0:T(8,128)S(1)} %add.298), channel_id=1, source_target_pairs={{8,0},{10,2},{12,4},{14,6},{9,1},{11,3},{13,5},{15,7},{24,16},{26,... | collective-permute-start | bytes 786440 | tf_op jit(solution)/shard_map/ppermute | solution.py:64
  144.2 23.4 %collective-permute-start.25 = (f32[256,2048]{1,0:T(8,128)S(1)}, f32[256,2048]{1,0:T(8,128)}, u32[]{:S(2)}, u32[]{:S(2)}) collective-permute-start(f32[256,2048]{1,0:T(8,128)S(1)} %fusion), channel_id=1, source_target_pairs={{0,1},{1,0},{2,3},{3,2},{4,5},{5,4},{6,7},{7,6},{8,9},{9,8},{10,11... | collective-permute-start | bytes 6291464 | tf_op jit(solution)/shard_map/ppermute | solution.py:17
  159.3 7.3 %collective-permute-start.24 = (bf16[256,512]{1,0:T(8,128)(2,1)S(1)}, bf16[256,512]{1,0:T(8,128)(2,1)S(1)}, u32[]{:S(2)}, u32[]{:S(2)}) collective-permute-start(bf16[256,512]{1,0:T(8,128)(2,1)S(1)} %copy.39), channel_id=1, source_target_pairs={{0,1},{1,0},{2,3},{3,2},{4,5},{5,4},{6,7},{7,6},{8,9},{9,8},{10,11... | collective-permute-start | bytes 786440 | tf_op jit(solution)/shard_map/ppermute | solution.py:17
  161.8 4.9 %copy-start.1 = (bf16[256,512]{1,0:T(8,128)(2,1)S(1)}, bf16[256,512]{1,0:T(8,128)(2,1)}, u32[]{:S(2)}) copy-start(bf16[256,512]{1,0:T(8,128)(2,1)} %copy.40) | copy-start | bytes 786436

commit v16 on v15

--- a/solution.py
+++ b/solution.py
@@ -52,7 +52,7 @@
     return got
 
 
-def exclusive_scan(total, chips, reverse):
+def exclusive_scan(total, chips, reverse, side=()):
     incl = total
     excl = jnp.zeros_like(total)
     d = 1
@@ -62,10 +62,12 @@
         else:
             perm = [(i, i + d) for i in range(chips - d)]
         got = lax.ppermute(incl, "chip", perm)
+        if d == 1:
+            side, got = lax.optimization_barrier((side, got))
         incl = incl + got
         excl = excl + got
         d *= 2
-    return excl
+    return excl, side
 
 
 def dense_allow(block_masks, tokens):
@@ -123,7 +125,7 @@
     value = pick(at_v)
 
     local = jnp.einsum("jthd,jthe->jhde", key, value, preferred_element_type=f32)
-    state0 = exclusive_scan(local[0] + local[1], chips, False)
+    state0, _ = exclusive_scan(local[0] + local[1], chips, False)
     state_mine = jnp.where(first, state0, state0 + local[1])
     state_other = jnp.where(first, state0 + local[0], state0)
     state_b = jnp.stack([state_mine, state_other]).astype(bf16)
@@ -147,7 +149,15 @@
     d_mixed_b = d_mixed.astype(bf16)
     grad_local = jnp.einsum("jthd,jthe->jhde", query, d_mixed_b, preferred_element_type=f32)
 
-    later1 = exclusive_scan(grad_local[0] + grad_local[1], chips, True)
+    d_scores = jnp.einsum("jthe,jshe->jhts", d_mixed_b, value, preferred_element_type=f32)
+    d_attn = jnp.where(allow[:, None], d_scores, 0.0).astype(bf16)
+    d_query = jnp.einsum("jhts,jshd->jthd", d_attn, key, preferred_element_type=f32)
+    d_query = d_query + jnp.einsum("jthe,jhde->jthd", d_mixed_b, state_b, preferred_element_type=f32)
+    dq_b = d_query.astype(bf16).reshape(2, tok, half)
+    dims = (((1,), (1,)), ((), ()))
+    w_qcols = lax.dynamic_slice_in_dim(w_all, at_q, share, axis=1)
+    grad_q = [lax.dot_general(dq_b[j], w_qcols, dims, preferred_element_type=f32) for j in range(2)]
+    later1, grad_q = exclusive_scan(grad_local[0] + grad_local[1], chips, True, grad_q)
     later_mine = jnp.where(first, later1 + grad_local[1], later1)
     later_other = jnp.where(first, later1, later1 + grad_local[0])
     later_b = jnp.stack([later_mine, later_other]).astype(bf16)
@@ -159,25 +169,18 @@
         jnp.concatenate([out_recv, out_b[0]], axis=1),
     )
 
-    d_scores = jnp.einsum("jthe,jshe->jhts", d_mixed_b, value, preferred_element_type=f32)
-    d_attn = jnp.where(allow[:, None], d_scores, 0.0).astype(bf16)
-    d_query = jnp.einsum("jhts,jshd->jthd", d_attn, key, preferred_element_type=f32)
-    d_query = d_query + jnp.einsum("jthe,jhde->jthd", d_mixed_b, state_b, preferred_element_type=f32)
     d_key = jnp.einsum("jhts,jthd->jshd", d_attn, query, preferred_element_type=f32)
     d_key = d_key + jnp.einsum("jshe,jhde->jshd", value, later_b, preferred_element_type=f32)
     d_value = jnp.einsum("jhts,jthe->jshe", attn, d_mixed_b, preferred_element_type=f32)
     d_value = d_value + jnp.einsum("jshd,jhde->jshe", key, later_b, preferred_element_type=f32)
-    dq_b = d_query.astype(bf16).reshape(2, tok, half)
     dk_b = d_key.astype(bf16).reshape(2, tok, half)
     dv_b = d_value.astype(bf16).reshape(2, tok, half)
 
     def grad_rows(j):
-        dims = (((1,), (1,)), ((), ()))
-        g = None
-        for d, at in ((dq_b[j], at_q), (dk_b[j], at_k), (dv_b[j], at_v)):
+        g = grad_q[j]
+        for d, at in ((dk_b[j], at_k), (dv_b[j], at_v)):
             w = lax.dynamic_slice_in_dim(w_all, at, share, axis=1)
-            t = lax.dot_general(d, w, dims, preferred_element_type=f32)
-            g = t if g is None else g + t
+            g = g + lax.dot_general(d, w, dims, preferred_element_type=f32)
         return g
 
     received = swap(grad_rows(1))

time: 173 us -> 169 us (0.977)
  waiting for transfers between devices: 52.6 us -> 44.2 us
  matrix products: 25.3 us -> 27.9 us
  starting transfers between devices: 44.4 us -> 46.3 us
    ppermute x6, waiting for transfers between devices: 29.1 us -> 23 us  [exclusive_scan(): got = lax.ppermute(incl, 'chip', perm)]
    ppermute x7, waiting for transfers between devices: 12.7 us -> 10.1 us  [land(): return (piece, lax.ppermute(sent, 'groups', partner))]
    reshape x5, local copies, waits for them, and re-layouts: 0.91 us -> 2.7 us  [pick(): lax.dynamic_slice_in_dim(p_all, at, share, axis=1)]
  transfers between devices with their start and end apart: 26 -> 26, of which waited for: 13 -> 14; matrix products, arithmetic and copies ran while one was open for 27% -> 26% of each run, Pallas kernels for 0% -> 0%
where the time goes in v16:
time: 169 us; the launch traced here: 167 us
  starting transfers between devices  46.3 us (27%)
  waiting for transfers between devices  44.2 us (26%)
  matrix products  27.9 us (17%)
  local copies, waits for them, and re-layouts  25 us (15%)
  other arithmetic  12.9 us (8%)
  between operations  10.2 us (6%)
    ppermute x6, waiting for transfers between devices, exclusive_scan(): got = lax.ppermute(incl, 'chip', perm)  23 us
    ppermute x6, starting transfers between devices, swap(): return lax.ppermute(x, 'core', [(0, 1), (1, 0)])  19.8 us
    ppermute x6, starting transfers between devices, exclusive_scan(): got = lax.ppermute(incl, 'chip', perm)  17.3 us
    dot_general x4, matrix products, grad_rows(): g = g + lax.dot_general(d, w, dims, preferred_element_type=f32)  11 us
    ppermute x7, waiting for transfers between devices, land(): return (piece, lax.ppermute(sent, 'groups', partner))  10.1 us
    ppermute x4, waiting for transfers between devices, ring_gather(): fwd = lax.ppermute(fwd, 'chip', ahead)  9.85 us
    dynamic_update_slice x8, local copies, waits for them, and re-layouts, on_device(): w_all = lax.dynamic_update_slice(w_all, ringed, (src * span, 0))  7.1 us
    dot_general x1, matrix products, on_device(): p_all = jnp.dot(x_pair, w_all, preferred_element_type=f32).astype(bf16)  6.84 us
  transfers between devices with their start and end apart: 26, of which 14 were waited for; matrix products, arithmetic and copies ran while one was open for 26% of the time, Pallas kernels for 0%

profile of v16, /device:TPU:15, one launch (start us, length us, event | category | flops | bytes accessed | tf_op | source)
XLA Modules:
  0.0 166.6 jit_solution(8142007411912696339)
XLA Ops:
  3.8 1.3 collective-permute-done.1
  6.2 3.1 %broadcast_in_dim.33 = bf16[2048,1536]{1,0:T(8,128)(2,1)} broadcast(bf16[]{:T(256)} %constant.94.clone.1), dimensions={} | broadcast | bytes 6291458 | tf_op jit(solution)/shard_map/broadcast_in_dim | solution.py:111
  10.5 2.6 %add_convert_fusion.1 = bf16[256,2048]{1,0:T(8,128)(2,1)} fusion(bf16[256,2048]{1,0:T(8,128)(2,1)S(1)} %copy-done.2, bf16[256,2048]{1,0:T(8,128)(2,1)} %param.9), kind=kLoop, calls=%fused_computation.9 | loop fusion | flops 2097152 | bytes 3145728 | tf_op jit(solution)/shard_map/convert_element_type | solution.py:93
  30.5 3.7 %collective-permute-done.3 = bf16[256,512]{1,0:T(8,128)(2,1)S(1)} collective-permute-done((bf16[256,512]{1,0:T(8,128)(2,1)S(1)}, bf16[256,512]{1,0:T(8,128)(2,1)S(1)}, u32[]{:S(2)}, u32[]{:S(2)}) %collective-permute-start.3) | collective-permute-done | bytes 262176 | tf_op jit(solution)/shard_map/ppermute | solution.py:41
  36.0 3.7 %collective-permute-done.6 = bf16[256,1024]{1,0:T(8,128)(2,1)S(1)} collective-permute-done((bf16[256,1024]{1,0:T(8,128)(2,1)S(1)}, bf16[256,1024]{1,0:T(8,128)(2,1)S(1)}, u32[]{:S(2)}, u32[]{:S(2)}) %collective-permute-start.6) | collective-permute-done | bytes 524320 | tf_op jit(solution)/shard_map/ppermute | solution.py:47
  44.2 1.5 collective-permute-done.7
  48.5 3.7 %collective-permute-done.10 = bf16[256,1024]{1,0:T(8,128)(2,1)S(1)} collective-permute-done((bf16[256,1024]{1,0:T(8,128)(2,1)S(1)}, bf16[256,1024]{1,0:T(8,128)(2,1)S(1)}, u32[]{:S(2)}, u32[]{:S(2)}) %collective-permute-start.10) | collective-permute-done | bytes 524320 | tf_op jit(solution)/shard_map/ppermute | solution.py:47
  53.5 4.0 %collective-permute-start.20 = (bf16[256,512]{0,1:T(8,128)(2,1)}, bf16[256,512]{0,1:T(8,128)(2,1)S(1)}, u32[]{:S(2)}, u32[]{:S(2)}) collective-permute-start(bf16[256,512]{0,1:T(8,128)(2,1)} %get-tuple-element.36), channel_id=1, source_target_pairs={{0,1},{1,0},{2,3},{3,2},{4,5},{5,4},{6,7},{7,6},{8,9},{9,8},{10,11... | collective-permute-start | bytes 786440 | tf_op jit(solution)/shard_map/ppermute | solution.py:17
  60.2 2.4 %collective-permute-done.14 = bf16[256,1024]{1,0:T(8,128)(2,1)S(1)} collective-permute-done((bf16[256,1024]{1,0:T(8,128)(2,1)S(1)}, bf16[256,1024]{1,0:T(8,128)(2,1)S(1)}, u32[]{:S(2)}, u32[]{:S(2)}) %collective-permute-start.14) | collective-permute-done | bytes 524320 | tf_op jit(solution)/shard_map/ppermute | solution.py:47
  66.3 3.9 %collective-permute-done.15 = bf16[256,512]{1,0:T(8,128)(2,1)S(1)} collective-permute-done((bf16[256,512]{1,0:T(8,128)(2,1)S(1)}, bf16[256,512]{1,0:T(8,128)(2,1)S(1)}, u32[]{:S(2)}, u32[]{:S(2)}) %collective-permute-start.15) | collective-permute-done | bytes 262176 | tf_op jit(solution)/shard_map/ppermute | solution.py:41
  70.9 6.8 %convolution_convert_fusion = bf16[512,1536]{1,0:T(8,128)(2,1)S(1)} fusion(bf16[2048,1536]{1,0:T(8,128)(2,1)} %constant_dynamic-update-slice_fusion.9, bf16[256,2048]{1,0:T(8,128)(2,1)} %collective-permute-done, bf16[256,2048]{1,0:T(8,128)(2,1)} %add_convert_fusion.1), kind=kOutput, calls=%fused_computation | convolution fusion | flops 3226206208 | bytes 9961472 | tf_op jit(solution)/shard_map/dot_general | solution.py:118
  79.5 2.6 %collective-permute-start.17 = (f32[4,128,128]{2,1,0:T(8,128)}, f32[4,128,128]{2,1,0:T(8,128)}, u32[]{:S(2)}, u32[]{:S(2)}) collective-permute-start(f32[4,128,128]{2,1,0:T(8,128)} %fusion.41), channel_id=1, source_target_pairs={{0,2},{2,4},{4,6},{6,8},{8,10},{10,12},{12,14},{1,3},{3,5},{5,7},{... | collective-permute-start | bytes 786440 | tf_op jit(solution)/shard_map/ppermute | solution.py:64
  82.7 1.6 broadcast_and_fusion
  87.9 3.0 %collective-permute-start.18 = (f32[4,128,128]{2,1,0:T(8,128)S(1)}, f32[4,128,128]{2,1,0:T(8,128)S(1)}, u32[]{:S(2)}, u32[]{:S(2)}) collective-permute-start(f32[4,128,128]{2,1,0:T(8,128)S(1)} %fusion.90), channel_id=1, source_target_pairs={{0,4},{2,6},{4,8},{6,10},{8,12},{10,14},{1,5},{3,7},{5,9},{7,11},{... | collective-permute-start | bytes 786440 | tf_op jit(solution)/shard_map/ppermute | solution.py:64
  90.9 1.4 select_convert_fusion.1
  92.3 2.7 %collective-permute-done.18 = f32[4,128,128]{2,1,0:T(8,128)S(1)} collective-permute-done((f32[4,128,128]{2,1,0:T(8,128)S(1)}, f32[4,128,128]{2,1,0:T(8,128)S(1)}, u32[]{:S(2)}, u32[]{:S(2)}) %collective-permute-start.18) | collective-permute-done | bytes 262176 | tf_op jit(solution)/shard_map/ppermute | solution.py:64
  95.1 4.1 %collective-permute-start.19 = (f32[4,128,128]{2,1,0:T(8,128)S(1)}, f32[4,128,128]{2,1,0:T(8,128)S(1)}, u32[]{:S(2)}, u32[]{:S(2)}) collective-permute-start(f32[4,128,128]{2,1,0:T(8,128)S(1)} %add.286), channel_id=1, source_target_pairs={{0,8},{2,10},{4,12},{6,14},{1,9},{3,11},{5,13},{7,15},{16,24},{18,... | collective-permute-start | bytes 786440 | tf_op jit(solution)/shard_map/ppermute | solution.py:64
  99.7 6.0 %collective-permute-done.19 = f32[4,128,128]{2,1,0:T(8,128)S(1)} collective-permute-done((f32[4,128,128]{2,1,0:T(8,128)S(1)}, f32[4,128,128]{2,1,0:T(8,128)S(1)}, u32[]{:S(2)}, u32[]{:S(2)}) %collective-permute-start.19) | collective-permute-done | bytes 262176 | tf_op jit(solution)/shard_map/ppermute | solution.py:64
  109.2 2.4 %fusion.15 = f32[256,2048]{1,0:T(8,128)S(1)} fusion(bf16[256,512]{0,1:T(8,128)(2,1)S(1)} %bitcast.117, bf16[2048,1536]{1,0:T(8,128)(2,1)} %constant_dynamic-update-slice_fusion.9, s32[]{:T(128)S(6)} %select_n.230), kind=kOutput, calls=%fused_computation.18 | convolution fusion | flops 536870912 | bytes 4456452 | tf_op jit(solution)/shard_map/dot_general | solution.py:159
  111.6 3.7 %collective-permute-start.21 = (f32[4,128,128]{2,1,0:T(8,128)S(1)}, f32[4,128,128]{2,1,0:T(8,128)S(1)}, u32[]{:S(2)}, u32[]{:S(2)}) collective-permute-start(f32[4,128,128]{2,1,0:T(8,128)S(1)} %fusion.42), channel_id=1, source_target_pairs={{2,0},{4,2},{6,4},{8,6},{10,8},{12,10},{14,12},{3,1},{5,3},{7,5},{... | collective-permute-start | bytes 786440 | tf_op jit(solution)/shard_map/ppermute | solution.py:64
  115.4 2.4 %fusion.17 = f32[256,2048]{1,0:T(8,128)S(1)} fusion(bf16[256,512]{0,1:T(8,128)(2,1)S(1)} %bitcast.115, bf16[2048,1536]{1,0:T(8,128)(2,1)} %constant_dynamic-update-slice_fusion.9, s32[]{:T(128)S(6)} %select_n.230), kind=kOutput, calls=%fused_computation.20 | convolution fusion | flops 536870912 | bytes 4456452 | tf_op jit(solution)/shard_map/dot_general | solution.py:159
  117.7 2.1 %collective-permute-done.21 = f32[4,128,128]{2,1,0:T(8,128)S(1)} collective-permute-done((f32[4,128,128]{2,1,0:T(8,128)S(1)}, f32[4,128,128]{2,1,0:T(8,128)S(1)}, u32[]{:S(2)}, u32[]{:S(2)}) %collective-permute-start.21) | collective-permute-done | bytes 262176 | tf_op jit(solution)/shard_map/ppermute | solution.py:64
  119.9 2.4 %collective-permute-start.22 = (f32[4,128,128]{2,1,0:T(8,128)S(1)}, f32[4,128,128]{2,1,0:T(8,128)S(1)}, u32[]{:S(2)}, u32[]{:S(2)}) collective-permute-start(f32[4,128,128]{2,1,0:T(8,128)S(1)} %fusion.89), channel_id=1, source_target_pairs={{4,0},{6,2},{8,4},{10,6},{12,8},{14,10},{5,1},{7,3},{9,5},{11,7},{... | collective-permute-start | bytes 786440 | tf_op jit(solution)/shard_map/ppermute | solution.py:64
  122.6 5.3 %collective-permute-done.22 = f32[4,128,128]{2,1,0:T(8,128)S(1)} collective-permute-done((f32[4,128,128]{2,1,0:T(8,128)S(1)}, f32[4,128,128]{2,1,0:T(8,128)S(1)}, u32[]{:S(2)}, u32[]{:S(2)}) %collective-permute-start.22) | collective-permute-done | bytes 262176 | tf_op jit(solution)/shard_map/ppermute | solution.py:64
  128.0 1.4 collective-permute-start.23
  129.8 6.5 %collective-permute-done.23 = f32[4,128,128]{2,1,0:T(8,128)S(1)} collective-permute-done((f32[4,128,128]{2,1,0:T(8,128)S(1)}, f32[4,128,128]{2,1,0:T(8,128)S(1)}, u32[]{:S(2)}, u32[]{:S(2)}) %collective-permute-start.23) | collective-permute-done | bytes 262176 | tf_op jit(solution)/shard_map/ppermute | solution.py:64
  136.7 2.4 %fusion.11 = f32[256,2048]{1,0:T(8,128)S(1)} fusion(bf16[256,512]{0,1:T(8,128)(2,1)S(1)} %bitcast.118, bf16[2048,1536]{1,0:T(8,128)(2,1)} %constant_dynamic-update-slice_fusion.9, s32[]{:T(128)S(6)} %select_n.231), kind=kOutput, calls=%fused_computation.14 | convolution fusion | flops 536870912 | bytes 4456452 | tf_op jit(solution)/shard_map/dot_general | solution.py:183
  139.5 3.8 %add_add_fusion = f32[256,2048]{1,0:T(8,128)} fusion(f32[256,2048]{1,0:T(8,128)S(1)} %fusion.15, f32[256,2048]{1,0:T(8,128)S(1)} %fusion.11, bf16[256,512]{0,1:T(8,128)(2,1)S(1)} %bitcast.116, bf16[2048,1536]{1,0:T(8,128)(2,1)} %constant_dynamic-update-slice_fusion.9, s32[]{:T(128)S(6)} %select_n.229), kind=kOutput, calls=%fused_computation.5 | convolution fusion | flops 537919488 | bytes 8650756 | tf_op jit(solution)/shard_map/dot_general | solution.py:183
  143.3 14.3 %collective-permute-start.25 = (f32[256,2048]{1,0:T(8,128)}, f32[256,2048]{1,0:T(8,128)}, u32[]{:S(2)}, u32[]{:S(2)}) collective-permute-start(f32[256,2048]{1,0:T(8,128)} %add_add_fusion), channel_id=1, source_target_pairs={{0,1},{1,0},{2,3},{3,2},{4,5},{5,4},{6,7},{7,6},{8,9},{9,8},{10,11... | collective-permute-start | bytes 6291464 | tf_op jit(solution)/shard_map/ppermute | solution.py:17
  158.0 2.4 %fusion.13 = f32[256,2048]{1,0:T(8,128)S(1)} fusion(bf16[256,512]{0,1:T(8,128)(2,1)S(1)} %bitcast.113, bf16[2048,1536]{1,0:T(8,128)(2,1)} %constant_dynamic-update-slice_fusion.9, s32[]{:T(128)S(6)} %select_n.231), kind=kOutput, calls=%fused_computation.16 | convolution fusion | flops 536870912 | bytes 4456452 | tf_op jit(solution)/shard_map/dot_general | solution.py:183
  160.4 2.4 %add_add_fusion.1 = f32[256,2048]{1,0:T(8,128)S(1)} fusion(f32[256,2048]{1,0:T(8,128)S(1)} %fusion.17, f32[256,2048]{1,0:T(8,128)S(1)} %fusion.13, bf16[256,512]{0,1:T(8,128)(2,1)S(1)} %bitcast.114, bf16[2048,1536]{1,0:T(8,128)(2,1)} %constant_dynamic-update-slice_fusion.9, s32[]{:T(128)S(6)} %select_n.229), kind=kOutput, calls=%fused_computation.6 | convolution fusion | flops 537919488 | bytes 8650756 | tf_op jit(solution)/shard_map/dot_general | solution.py:183
  163.8 2.8 %add_convert_fusion = bf16[256,2048]{1,0:T(8,128)(2,1)} fusion(f32[256,2048]{1,0:T(8,128)S(1)} %add_add_fusion.1, f32[256,2048]{1,0:T(8,128)} %collective-permute-done.25), kind=kLoop, calls=%fused_computation.4 | loop fusion | flops 1048576 | bytes 5242880 | tf_op jit(solution)/shard_map/convert_element_type | solution.py:188
  (122 shorter events, 44.0 us)
Async XLA Ops:
  2.9 2.2 %collective-permute-start.1 = (bf16[128,1536]{1,0:T(8,128)(2,1)S(1)}, bf16[128,1536]{1,0:T(8,128)(2,1)}, u32[]{:S(2)}, u32[]{:S(2)}) collective-permute-start(bf16[128,1536]{1,0:T(8,128)(2,1)S(1)} %pad_maximum_fusion.1), channel_id=1, source_target_pairs={{0,1},{1,0},{2,3},{3,2},{4,5},{5,4},{6,7},{7,6},{8,9},{9,8},{10,11... | collective-permute-start | bytes 1179656 | tf_op jit(solution)/shard_map/ppermute | solution.py:17
  3.7 12.0 %copy-start.7 = (s32[8]{0:T(128)S(1)}, s32[8]{0:T(128)}, u32[]{:S(2)}) copy-start(s32[8]{0:T(128)} %constant.120.clone) | copy-start | bytes 100
  3.7 17.1 %copy-start.5 = (s32[8]{0:T(128)S(1)}, s32[8]{0:T(128)}, u32[]{:S(2)}) copy-start(s32[8]{0:T(128)} %constant.119.clone) | copy-start | bytes 100
  3.8 22.3 %copy-start.3 = (bf16[256,1024]{1,0:T(8,128)(2,1)S(1)}, bf16[256,1024]{1,0:T(8,128)(2,1)}, u32[]{:S(2)}) copy-start(bf16[256,1024]{1,0:T(8,128)(2,1)} %param.11) | copy-start | bytes 1572868
  10.3 16.7 %collective-permute-start.2 = (bf16[256,1024]{1,0:T(8,128)(2,1)}, bf16[256,1024]{1,0:T(8,128)(2,1)S(1)}, u32[]{:S(2)}, u32[]{:S(2)}) collective-permute-start(bf16[256,1024]{1,0:T(8,128)(2,1)} %get-tuple-element.17), channel_id=1, source_target_pairs={{0,4},{4,8},{8,12},{12,14},{14,10},{10,6},{6,2},{2,0},{1,5},{5,9},... | collective-permute-start | bytes 1572872 | tf_op jit(solution)/shard_map/ppermute | solution.py:47
  13.1 57.8 %collective-permute-start = (bf16[256,2048]{1,0:T(8,128)(2,1)}, bf16[256,2048]{1,0:T(8,128)(2,1)}, u32[]{:S(2)}, u32[]{:S(2)}) collective-permute-start(bf16[256,2048]{1,0:T(8,128)(2,1)} %add_convert_fusion.1), channel_id=1, source_target_pairs={{0,1},{1,0},{2,3},{3,2},{4,5},{5,4},{6,7},{7,6},{8,9},{9,8},{10,11... | collective-permute-start | bytes 3145736 | tf_op jit(solution)/shard_map/ppermute | solution.py:17
  13.7 68.4 %collective-permute-start.16 = (s32[2,2]{1,0:T(2,128)S(1)}, s32[2,2]{1,0:T(2,128)S(1)}, u32[]{:S(2)}, u32[]{:S(2)}) collective-permute-start(s32[2,2]{1,0:T(2,128)S(1)} %bitcast.121), channel_id=1, source_target_pairs={{0,1},{1,0},{2,3},{3,2},{4,5},{5,4},{6,7},{7,6},{8,9},{9,8},{10,11... | collective-permute-start | bytes 56 | tf_op jit(solution)/shard_map/ppermute | solution.py:17
  13.7 14.6 %collective-permute-start.4 = (bf16[256,1024]{1,0:T(8,128)(2,1)}, bf16[256,1024]{1,0:T(8,128)(2,1)S(1)}, u32[]{:S(2)}, u32[]{:S(2)}) collective-permute-start(bf16[256,1024]{1,0:T(8,128)(2,1)} %get-tuple-element.17), channel_id=1, source_target_pairs={{0,2},{4,0},{8,4},{12,8},{14,12},{10,14},{6,10},{2,6},{1,3},{5,1},... | collective-permute-start | bytes 1572872 | tf_op jit(solution)/shard_map/ppermute | solution.py:50
  27.1 7.1 %collective-permute-start.3 = (bf16[256,512]{1,0:T(8,128)(2,1)S(1)}, bf16[256,512]{1,0:T(8,128)(2,1)S(1)}, u32[]{:S(2)}, u32[]{:S(2)}) collective-permute-start(bf16[256,512]{1,0:T(8,128)(2,1)S(1)} %constant_dynamic-slice_fusion.9), channel_id=1, source_target_pairs={{0,16},{16,0},{1,17},{17,1},{2,18},{18,2},{3,19},{19,3},{4,20},{20... | collective-permute-start | bytes 786440 | tf_op jit(solution)/shard_map/ppermute | solution.py:41
  27.4 12.3 %collective-permute-start.6 = (bf16[256,1024]{1,0:T(8,128)(2,1)S(1)}, bf16[256,1024]{1,0:T(8,128)(2,1)S(1)}, u32[]{:S(2)}, u32[]{:S(2)}) collective-permute-start(bf16[256,1024]{1,0:T(8,128)(2,1)S(1)} %collective-permute-done.2), channel_id=1, source_target_pairs={{0,4},{4,8},{8,12},{12,14},{14,10},{10,6},{6,2},{2,0},{1,5},{5,9},... | collective-permute-start | bytes 1572872 | tf_op jit(solution)/shard_map/ppermute | solution.py:47
  28.3 13.7 %collective-permute-start.8 = (bf16[256,1024]{1,0:T(8,128)(2,1)S(1)}, bf16[256,1024]{1,0:T(8,128)(2,1)S(1)}, u32[]{:S(2)}, u32[]{:S(2)}) collective-permute-start(bf16[256,1024]{1,0:T(8,128)(2,1)S(1)} %collective-permute-done.4), channel_id=1, source_target_pairs={{0,2},{4,0},{8,4},{12,8},{14,12},{10,14},{6,10},{2,6},{1,3},{5,1},... | collective-permute-start | bytes 1572872 | tf_op jit(solution)/shard_map/ppermute | solution.py:50
  34.2 6.9 %collective-permute-start.5 = (bf16[256,512]{1,0:T(8,128)(2,1)S(1)}, bf16[256,512]{1,0:T(8,128)(2,1)S(1)}, u32[]{:S(2)}, u32[]{:S(2)}) collective-permute-start(bf16[256,512]{1,0:T(8,128)(2,1)S(1)} %constant_dynamic-slice_fusion.8), channel_id=1, source_target_pairs={{0,16},{16,0},{1,17},{17,1},{2,18},{18,2},{3,19},{19,3},{4,20},{20... | collective-permute-start | bytes 786440 | tf_op jit(solution)/shard_map/ppermute | solution.py:41
  39.8 5.9 %collective-permute-start.7 = (bf16[256,512]{1,0:T(8,128)(2,1)S(1)}, bf16[256,512]{1,0:T(8,128)(2,1)S(1)}, u32[]{:S(2)}, u32[]{:S(2)}) collective-permute-start(bf16[256,512]{1,0:T(8,128)(2,1)S(1)} %constant_dynamic-slice_fusion.7), channel_id=1, source_target_pairs={{0,16},{16,0},{1,17},{17,1},{2,18},{18,2},{3,19},{19,3},{4,20},{20... | collective-permute-start | bytes 786440 | tf_op jit(solution)/shard_map/ppermute | solution.py:41
  41.1 11.1 %collective-permute-start.10 = (bf16[256,1024]{1,0:T(8,128)(2,1)S(1)}, bf16[256,1024]{1,0:T(8,128)(2,1)S(1)}, u32[]{:S(2)}, u32[]{:S(2)}) collective-permute-start(bf16[256,1024]{1,0:T(8,128)(2,1)S(1)} %collective-permute-done.6), channel_id=1, source_target_pairs={{0,4},{4,8},{8,12},{12,14},{14,10},{10,6},{6,2},{2,0},{1,5},{5,9},... | collective-permute-start | bytes 1572872 | tf_op jit(solution)/shard_map/ppermute | solution.py:47
  42.0 11.5 %collective-permute-start.12 = (bf16[256,1024]{1,0:T(8,128)(2,1)S(1)}, bf16[256,1024]{1,0:T(8,128)(2,1)S(1)}, u32[]{:S(2)}, u32[]{:S(2)}) collective-permute-start(bf16[256,1024]{1,0:T(8,128)(2,1)S(1)} %collective-permute-done.8), channel_id=1, source_target_pairs={{0,2},{4,0},{8,4},{12,8},{14,12},{10,14},{6,10},{2,6},{1,3},{5,1},... | collective-permute-start | bytes 1572872 | tf_op jit(solution)/shard_map/ppermute | solution.py:50
  45.7 6.7 %collective-permute-start.9 = (bf16[256,512]{1,0:T(8,128)(2,1)S(1)}, bf16[256,512]{1,0:T(8,128)(2,1)S(1)}, u32[]{:S(2)}, u32[]{:S(2)}) collective-permute-start(bf16[256,512]{1,0:T(8,128)(2,1)S(1)} %constant_dynamic-slice_fusion.6), channel_id=1, source_target_pairs={{0,16},{16,0},{1,17},{17,1},{2,18},{18,2},{3,19},{19,3},{4,20},{20... | collective-permute-start | bytes 786440 | tf_op jit(solution)/shard_map/ppermute | solution.py:41
  52.2 10.4 %collective-permute-start.14 = (bf16[256,1024]{1,0:T(8,128)(2,1)S(1)}, bf16[256,1024]{1,0:T(8,128)(2,1)S(1)}, u32[]{:S(2)}, u32[]{:S(2)}) collective-permute-start(bf16[256,1024]{1,0:T(8,128)(2,1)S(1)} %collective-permute-done.10), channel_id=1, source_target_pairs={{0,4},{4,8},{8,12},{12,14},{14,10},{10,6},{6,2},{2,0},{1,5},{5,9},... | collective-permute-start | bytes 1572872 | tf_op jit(solution)/shard_map/ppermute | solution.py:47
  52.4 6.0 %collective-permute-start.11 = (bf16[256,512]{1,0:T(8,128)(2,1)S(1)}, bf16[256,512]{1,0:T(8,128)(2,1)S(1)}, u32[]{:S(2)}, u32[]{:S(2)}) collective-permute-start(bf16[256,512]{1,0:T(8,128)(2,1)S(1)} %constant_dynamic-slice_fusion.5), channel_id=1, source_target_pairs={{0,16},{16,0},{1,17},{17,1},{2,18},{18,2},{3,19},{19,3},{4,20},{20... | collective-permute-start | bytes 786440 | tf_op jit(solution)/shard_map/ppermute | solution.py:41
  53.5 53.6 %collective-permute-start.20 = (bf16[256,512]{0,1:T(8,128)(2,1)}, bf16[256,512]{0,1:T(8,128)(2,1)S(1)}, u32[]{:S(2)}, u32[]{:S(2)}) collective-permute-start(bf16[256,512]{0,1:T(8,128)(2,1)} %get-tuple-element.36), channel_id=1, source_target_pairs={{0,1},{1,0},{2,3},{3,2},{4,5},{5,4},{6,7},{7,6},{8,9},{9,8},{10,11... | collective-permute-start | bytes 786440 | tf_op jit(solution)/shard_map/ppermute | solution.py:17
  58.4 6.3 %collective-permute-start.13 = (bf16[256,512]{1,0:T(8,128)(2,1)S(1)}, bf16[256,512]{1,0:T(8,128)(2,1)S(1)}, u32[]{:S(2)}, u32[]{:S(2)}) collective-permute-start(bf16[256,512]{1,0:T(8,128)(2,1)S(1)} %constant_dynamic-slice_fusion.4), channel_id=1, source_target_pairs={{0,16},{16,0},{1,17},{17,1},{2,18},{18,2},{3,19},{19,3},{4,20},{20... | collective-permute-start | bytes 786440 | tf_op jit(solution)/shard_map/ppermute | solution.py:41
  62.6 7.6 %collective-permute-start.15 = (bf16[256,512]{1,0:T(8,128)(2,1)S(1)}, bf16[256,512]{1,0:T(8,128)(2,1)S(1)}, u32[]{:S(2)}, u32[]{:S(2)}) collective-permute-start(bf16[256,512]{1,0:T(8,128)(2,1)S(1)} %constant_dynamic-slice_fusion.3), channel_id=1, source_target_pairs={{0,16},{16,0},{1,17},{17,1},{2,18},{18,2},{3,19},{19,3},{4,20},{20... | collective-permute-start | bytes 786440 | tf_op jit(solution)/shard_map/ppermute | solution.py:41
  78.0 21.6 %copy-start = (bf16[2,256,4,128]{3,2,1,0:T(4,128)(2,1)}, bf16[2,256,4,128]{3,2,1,0:T(4,128)(2,1)S(1)}, u32[]{:S(2)}) copy-start(bf16[2,256,4,128]{3,2,1,0:T(4,128)(2,1)S(1)} %reshape.137) | copy-start | bytes 1572868
  79.5 7.4 %collective-permute-start.17 = (f32[4,128,128]{2,1,0:T(8,128)}, f32[4,128,128]{2,1,0:T(8,128)}, u32[]{:S(2)}, u32[]{:S(2)}) collective-permute-start(f32[4,128,128]{2,1,0:T(8,128)} %fusion.41), channel_id=1, source_target_pairs={{0,2},{2,4},{4,6},{6,8},{8,10},{10,12},{12,14},{1,3},{3,5},{5,7},{... | collective-permute-start | bytes 786440 | tf_op jit(solution)/shard_map/ppermute | solution.py:64
  87.9 7.1 %collective-permute-start.18 = (f32[4,128,128]{2,1,0:T(8,128)S(1)}, f32[4,128,128]{2,1,0:T(8,128)S(1)}, u32[]{:S(2)}, u32[]{:S(2)}) collective-permute-start(f32[4,128,128]{2,1,0:T(8,128)S(1)} %fusion.90), channel_id=1, source_target_pairs={{0,4},{2,6},{4,8},{6,10},{8,12},{10,14},{1,5},{3,7},{5,9},{7,11},{... | collective-permute-start | bytes 786440 | tf_op jit(solution)/shard_map/ppermute | solution.py:64
  92.3 15.3 %copy-start.4 = (pred[2,256,256]{2,1,0:T(8,128)(4,1)S(1)}, pred[2,256,256]{2,1,0:T(8,128)(4,1)}, u32[]{:S(2)}) copy-start(pred[2,256,256]{2,1,0:T(8,128)(4,1)} %broadcast_and_fusion) | copy-start | bytes 393220
  95.1 10.6 %collective-permute-start.19 = (f32[4,128,128]{2,1,0:T(8,128)S(1)}, f32[4,128,128]{2,1,0:T(8,128)S(1)}, u32[]{:S(2)}, u32[]{:S(2)}) collective-permute-start(f32[4,128,128]{2,1,0:T(8,128)S(1)} %add.286), channel_id=1, source_target_pairs={{0,8},{2,10},{4,12},{6,14},{1,9},{3,11},{5,13},{7,15},{16,24},{18,... | collective-permute-start | bytes 786440 | tf_op jit(solution)/shard_map/ppermute | solution.py:64
  111.6 8.2 %collective-permute-start.21 = (f32[4,128,128]{2,1,0:T(8,128)S(1)}, f32[4,128,128]{2,1,0:T(8,128)S(1)}, u32[]{:S(2)}, u32[]{:S(2)}) collective-permute-start(f32[4,128,128]{2,1,0:T(8,128)S(1)} %fusion.42), channel_id=1, source_target_pairs={{2,0},{4,2},{6,4},{8,6},{10,8},{12,10},{14,12},{3,1},{5,3},{7,5},{... | collective-permute-start | bytes 786440 | tf_op jit(solution)/shard_map/ppermute | solution.py:64
  119.9 8.1 %collective-permute-start.22 = (f32[4,128,128]{2,1,0:T(8,128)S(1)}, f32[4,128,128]{2,1,0:T(8,128)S(1)}, u32[]{:S(2)}, u32[]{:S(2)}) collective-permute-start(f32[4,128,128]{2,1,0:T(8,128)S(1)} %fusion.89), channel_id=1, source_target_pairs={{4,0},{6,2},{8,4},{10,6},{12,8},{14,10},{5,1},{7,3},{9,5},{11,7},{... | collective-permute-start | bytes 786440 | tf_op jit(solution)/shard_map/ppermute | solution.py:64
  128.0 11.1 %copy-start.1 = (bf16[2,256,4,128]{3,2,1,0:T(4,128)(2,1)S(1)}, bf16[2,256,4,128]{3,2,1,0:T(4,128)(2,1)}, u32[]{:S(2)}) copy-start(bf16[2,256,4,128]{3,2,1,0:T(4,128)(2,1)} %copy-done) | copy-start | bytes 1572868
  128.0 8.2 %collective-permute-start.23 = (f32[4,128,128]{2,1,0:T(8,128)S(1)}, f32[4,128,128]{2,1,0:T(8,128)S(1)}, u32[]{:S(2)}, u32[]{:S(2)}) collective-permute-start(f32[4,128,128]{2,1,0:T(8,128)S(1)} %add.298), channel_id=1, source_target_pairs={{8,0},{10,2},{12,4},{14,6},{9,1},{11,3},{13,5},{15,7},{24,16},{26,... | collective-permute-start | bytes 786440 | tf_op jit(solution)/shard_map/ppermute | solution.py:64
  143.3 20.4 %collective-permute-start.25 = (f32[256,2048]{1,0:T(8,128)}, f32[256,2048]{1,0:T(8,128)}, u32[]{:S(2)}, u32[]{:S(2)}) collective-permute-start(f32[256,2048]{1,0:T(8,128)} %add_add_fusion), channel_id=1, source_target_pairs={{0,1},{1,0},{2,3},{3,2},{4,5},{5,4},{6,7},{7,6},{8,9},{9,8},{10,11... | collective-permute-start | bytes 6291464 | tf_op jit(solution)/shard_map/ppermute | solution.py:17
  157.9 4.9 %collective-permute-start.24 = (bf16[256,512]{1,0:T(8,128)(2,1)S(1)}, bf16[256,512]{1,0:T(8,128)(2,1)S(1)}, u32[]{:S(2)}, u32[]{:S(2)}) collective-permute-start(bf16[256,512]{1,0:T(8,128)(2,1)S(1)} %copy.43), channel_id=1, source_target_pairs={{0,1},{1,0},{2,3},{3,2},{4,5},{5,4},{6,7},{7,6},{8,9},{9,8},{10,11... | collective-permute-start | bytes 786440 | tf_op jit(solution)/shard_map/ppermute | solution.py:17
  (2 other events, 19.9 us)

commit v17 on v16

--- a/solution.py
+++ b/solution.py
@@ -55,6 +55,8 @@
 def exclusive_scan(total, chips, reverse, side=()):
     incl = total
     excl = jnp.zeros_like(total)
+    side = tuple(side)
+    step = 0
     d = 1
     while d < chips:
         if reverse:
@@ -62,8 +64,10 @@
         else:
             perm = [(i, i + d) for i in range(chips - d)]
         got = lax.ppermute(incl, "chip", perm)
-        if d == 1:
-            side, got = lax.optimization_barrier((side, got))
+        if step < len(side):
+            item, got = lax.optimization_barrier((side[step], got))
+            side = side[:step] + (item,) + side[step + 1 :]
+        step += 1
         incl = incl + got
         excl = excl + got
         d *= 2
@@ -157,7 +161,12 @@
     dims = (((1,), (1,)), ((), ()))
     w_qcols = lax.dynamic_slice_in_dim(w_all, at_q, share, axis=1)
     grad_q = [lax.dot_general(dq_b[j], w_qcols, dims, preferred_element_type=f32) for j in range(2)]
-    later1, grad_q = exclusive_scan(grad_local[0] + grad_local[1], chips, True, grad_q)
+    dk_intra = jnp.einsum("jhts,jthd->jshd", d_attn, query, preferred_element_type=f32)
+    dv_intra = jnp.einsum("jhts,jthe->jshe", attn, d_mixed_b, preferred_element_type=f32)
+    later1, (gq0, gq1, (dk_intra, dv_intra)) = exclusive_scan(
+        grad_local[0] + grad_local[1], chips, True, (grad_q[0], grad_q[1], (dk_intra, dv_intra))
+    )
+    grad_q = [gq0, gq1]
     later_mine = jnp.where(first, later1 + grad_local[1], later1)
     later_other = jnp.where(first, later1, later1 + grad_local[0])
     later_b = jnp.stack([later_mine, later_other]).astype(bf16)
@@ -169,10 +178,8 @@
         jnp.concatenate([out_recv, out_b[0]], axis=1),
     )
 
-    d_key = jnp.einsum("jhts,jthd->jshd", d_attn, query, preferred_element_type=f32)
-    d_key = d_key + jnp.einsum("jshe,jhde->jshd", value, later_b, preferred_element_type=f32)
-    d_value = jnp.einsum("jhts,jthe->jshe", attn, d_mixed_b, preferred_element_type=f32)
-    d_value = d_value + jnp.einsum("jshd,jhde->jshe", key, later_b, preferred_element_type=f32)
+    d_key = dk_intra + jnp.einsum("jshe,jhde->jshd", value, later_b, preferred_element_type=f32)
+    d_value = dv_intra + jnp.einsum("jshd,jhde->jshe", key, later_b, preferred_element_type=f32)
     dk_b = d_key.astype(bf16).reshape(2, tok, half)
     dv_b = d_value.astype(bf16).reshape(2, tok, half)
 

time: 169 us -> 169 us (level)
  waiting for transfers between devices: 44.2 us -> 50.7 us
  starting transfers between devices: 46.3 us -> 41.6 us
    ppermute x6, waiting for transfers between devices: 23 us -> 27.2 us  [exclusive_scan(): got = lax.ppermute(incl, 'chip', perm)]
    ppermute x6, starting transfers between devices: 19.8 us -> 16.5 us  [swap(): return lax.ppermute(x, 'core', [(0, 1), (1, 0)])]
    ppermute x7, waiting for transfers between devices: 10.1 us -> 12.7 us  [land(): return (piece, lax.ppermute(sent, 'groups', partner))]
    reshape x5, local copies, waits for them, and re-layouts: 2.7 us -> 0.91 us  [pick(): lax.dynamic_slice_in_dim(p_all, at, share, axis=1)]
  transfers between devices with their start and end apart: 26 -> 26, of which waited for: 14 -> 14; matrix products, arithmetic and copies ran while one was open for 26% -> 29% of each run, Pallas kernels for 0% -> 0%
where the time goes in v17:
time: 169 us; the launch traced here: 167 us
  waiting for transfers between devices  50.7 us (30%)
  starting transfers between devices  41.6 us (25%)
  matrix products  26.8 us (16%)
  local copies, waits for them, and re-layouts  24.9 us (15%)
  other arithmetic  13.1 us (8%)
  between operations  9.59 us (6%)
    ppermute x6, waiting for transfers between devices, exclusive_scan(): got = lax.ppermute(incl, 'chip', perm)  27.2 us
    ppermute x6, starting transfers between devices, swap(): return lax.ppermute(x, 'core', [(0, 1), (1, 0)])  16.5 us
    ppermute x6, starting transfers between devices, exclusive_scan(): got = lax.ppermute(incl, 'chip', perm)  15.8 us
    ppermute x7, waiting for transfers between devices, land(): return (piece, lax.ppermute(sent, 'groups', partner))  12.7 us
    dot_general x4, matrix products, grad_rows(): g = g + lax.dot_general(d, w, dims, preferred_element_type=f32)  11.1 us
    ppermute x4, waiting for transfers between devices, ring_gather(): fwd = lax.ppermute(fwd, 'chip', ahead)  10.8 us
    dynamic_update_slice x8, local copies, waits for them, and re-layouts, on_device(): w_all = lax.dynamic_update_slice(w_all, ringed, (src * span, 0))  7.17 us
    dot_general x1, matrix products, on_device(): p_all = jnp.dot(x_pair, w_all, preferred_element_type=f32).astype(bf16)  6.53 us
  transfers between devices with their start and end apart: 26, of which 14 were waited for; matrix products, arithmetic and copies ran while one was open for 29% of the time, Pallas kernels for 0%

profile of v17, /device:TPU:15, one launch (start us, length us, event | category | flops | bytes accessed | tf_op | source)
XLA Modules:
  0.0 166.7 jit_solution(336346809446074920)
XLA Ops:
  6.8 3.0 %broadcast_in_dim.33 = bf16[2048,1536]{1,0:T(8,128)(2,1)} broadcast(bf16[]{:T(256)} %constant.94.clone.1), dimensions={} | broadcast | bytes 6291458 | tf_op jit(solution)/shard_map/broadcast_in_dim | solution.py:115
  11.2 1.3 collective-permute-start.4
  12.5 2.6 %add_convert_fusion.1 = bf16[256,2048]{1,0:T(8,128)(2,1)} fusion(bf16[256,2048]{1,0:T(8,128)(2,1)S(1)} %copy-done, bf16[256,2048]{1,0:T(8,128)(2,1)} %param.9), kind=kLoop, calls=%fused_computation.9 | loop fusion | flops 2097152 | bytes 3145728 | tf_op jit(solution)/shard_map/convert_element_type | solution.py:97
  29.2 4.6 %collective-permute-done.3 = bf16[256,512]{1,0:T(8,128)(2,1)S(1)} collective-permute-done((bf16[256,512]{1,0:T(8,128)(2,1)S(1)}, bf16[256,512]{1,0:T(8,128)(2,1)S(1)}, u32[]{:S(2)}, u32[]{:S(2)}) %collective-permute-start.3) | collective-permute-done | bytes 262176 | tf_op jit(solution)/shard_map/ppermute | solution.py:41
  35.7 3.7 %collective-permute-done.6 = bf16[256,1024]{1,0:T(8,128)(2,1)S(1)} collective-permute-done((bf16[256,1024]{1,0:T(8,128)(2,1)S(1)}, bf16[256,1024]{1,0:T(8,128)(2,1)S(1)}, u32[]{:S(2)}, u32[]{:S(2)}) %collective-permute-start.6) | collective-permute-done | bytes 524320 | tf_op jit(solution)/shard_map/ppermute | solution.py:47
  41.8 1.3 collective-permute-start.12
  44.0 2.2 %collective-permute-done.7 = bf16[256,512]{1,0:T(8,128)(2,1)S(1)} collective-permute-done((bf16[256,512]{1,0:T(8,128)(2,1)S(1)}, bf16[256,512]{1,0:T(8,128)(2,1)S(1)}, u32[]{:S(2)}, u32[]{:S(2)}) %collective-permute-start.7) | collective-permute-done | bytes 262176 | tf_op jit(solution)/shard_map/ppermute | solution.py:41
  49.0 3.6 %collective-permute-done.10 = bf16[256,1024]{1,0:T(8,128)(2,1)S(1)} collective-permute-done((bf16[256,1024]{1,0:T(8,128)(2,1)S(1)}, bf16[256,1024]{1,0:T(8,128)(2,1)S(1)}, u32[]{:S(2)}, u32[]{:S(2)}) %collective-permute-start.10) | collective-permute-done | bytes 524320 | tf_op jit(solution)/shard_map/ppermute | solution.py:47
  53.9 3.2 %collective-permute-start.16 = (s32[2,2]{1,0:T(2,128)S(1)}, s32[2,2]{1,0:T(2,128)S(1)}, u32[]{:S(2)}, u32[]{:S(2)}) collective-permute-start(s32[2,2]{1,0:T(2,128)S(1)} %bitcast.123), channel_id=1, source_target_pairs={{0,1},{1,0},{2,3},{3,2},{4,5},{5,4},{6,7},{7,6},{8,9},{9,8},{10,11... | collective-permute-start | bytes 56 | tf_op jit(solution)/shard_map/ppermute | solution.py:17
  59.9 3.5 %collective-permute-done.14 = bf16[256,1024]{1,0:T(8,128)(2,1)S(1)} collective-permute-done((bf16[256,1024]{1,0:T(8,128)(2,1)S(1)}, bf16[256,1024]{1,0:T(8,128)(2,1)S(1)}, u32[]{:S(2)}, u32[]{:S(2)}) %collective-permute-start.14) | collective-permute-done | bytes 524320 | tf_op jit(solution)/shard_map/ppermute | solution.py:47
  66.2 5.6 %collective-permute-done.15 = bf16[256,512]{1,0:T(8,128)(2,1)S(1)} collective-permute-done((bf16[256,512]{1,0:T(8,128)(2,1)S(1)}, bf16[256,512]{1,0:T(8,128)(2,1)S(1)}, u32[]{:S(2)}, u32[]{:S(2)}) %collective-permute-start.15) | collective-permute-done | bytes 262176 | tf_op jit(solution)/shard_map/ppermute | solution.py:41
  72.6 6.5 %convolution_convert_fusion = bf16[512,1536]{1,0:T(8,128)(2,1)S(1)} fusion(bf16[2048,1536]{1,0:T(8,128)(2,1)} %constant_dynamic-update-slice_fusion.9, bf16[256,2048]{1,0:T(8,128)(2,1)S(1)} %collective-permute-done, bf16[256,2048]{1,0:T(8,128)(2,1)} %add_convert_fusion.1), kind=kOutput, calls=%fused_computation | convolution fusion | flops 3226206208 | bytes 9961472 | tf_op jit(solution)/shard_map/dot_general | solution.py:122
  80.8 2.4 %collective-permute-start.17 = (f32[4,128,128]{2,1,0:T(8,128)}, f32[4,128,128]{2,1,0:T(8,128)}, u32[]{:S(2)}, u32[]{:S(2)}) collective-permute-start(f32[4,128,128]{2,1,0:T(8,128)} %fusion.37), channel_id=1, source_target_pairs={{0,2},{2,4},{4,6},{6,8},{8,10},{10,12},{12,14},{1,3},{3,5},{5,7},{... | collective-permute-start | bytes 786440 | tf_op jit(solution)/shard_map/ppermute | solution.py:66
  84.3 3.9 %collective-permute-done.17 = f32[4,128,128]{2,1,0:T(8,128)} collective-permute-done((f32[4,128,128]{2,1,0:T(8,128)}, f32[4,128,128]{2,1,0:T(8,128)}, u32[]{:S(2)}, u32[]{:S(2)}) %collective-permute-start.17) | collective-permute-done | bytes 262176 | tf_op jit(solution)/shard_map/ppermute | solution.py:66
  89.2 3.2 %collective-permute-start.18 = (f32[4,128,128]{2,1,0:T(8,128)S(1)}, f32[4,128,128]{2,1,0:T(8,128)S(1)}, u32[]{:S(2)}, u32[]{:S(2)}) collective-permute-start(f32[4,128,128]{2,1,0:T(8,128)S(1)} %fusion.84), channel_id=1, source_target_pairs={{0,4},{2,6},{4,8},{6,10},{8,12},{10,14},{1,5},{3,7},{5,9},{7,11},{... | collective-permute-start | bytes 786440 | tf_op jit(solution)/shard_map/ppermute | solution.py:66
  93.0 3.4 %collective-permute-done.18 = f32[4,128,128]{2,1,0:T(8,128)S(1)} collective-permute-done((f32[4,128,128]{2,1,0:T(8,128)S(1)}, f32[4,128,128]{2,1,0:T(8,128)S(1)}, u32[]{:S(2)}, u32[]{:S(2)}) %collective-permute-start.18) | collective-permute-done | bytes 262176 | tf_op jit(solution)/shard_map/ppermute | solution.py:66
  96.4 4.2 %collective-permute-start.19 = (f32[4,128,128]{2,1,0:T(8,128)S(1)}, f32[4,128,128]{2,1,0:T(8,128)S(1)}, u32[]{:S(2)}, u32[]{:S(2)}) collective-permute-start(f32[4,128,128]{2,1,0:T(8,128)S(1)} %add.284), channel_id=1, source_target_pairs={{0,8},{2,10},{4,12},{6,14},{1,9},{3,11},{5,13},{7,15},{16,24},{18,... | collective-permute-start | bytes 786440 | tf_op jit(solution)/shard_map/ppermute | solution.py:66
  101.1 5.5 %collective-permute-done.19 = f32[4,128,128]{2,1,0:T(8,128)S(1)} collective-permute-done((f32[4,128,128]{2,1,0:T(8,128)S(1)}, f32[4,128,128]{2,1,0:T(8,128)S(1)}, u32[]{:S(2)}, u32[]{:S(2)}) %collective-permute-start.19) | collective-permute-done | bytes 262176 | tf_op jit(solution)/shard_map/ppermute | solution.py:66
  112.4 2.8 %collective-permute-start.21 = (f32[4,128,128]{2,1,0:T(8,128)S(1)}, f32[4,128,128]{2,1,0:T(8,128)S(1)}, u32[]{:S(2)}, u32[]{:S(2)}) collective-permute-start(f32[4,128,128]{2,1,0:T(8,128)S(1)} %fusion.38), channel_id=1, source_target_pairs={{2,0},{4,2},{6,4},{8,6},{10,8},{12,10},{14,12},{3,1},{5,3},{7,5},{... | collective-permute-start | bytes 786440 | tf_op jit(solution)/shard_map/ppermute | solution.py:66
  115.2 2.4 %fusion.17 = f32[256,2048]{1,0:T(8,128)S(1)} fusion(bf16[256,512]{0,1:T(8,128)(2,1)S(1)} %bitcast.119, bf16[2048,1536]{1,0:T(8,128)(2,1)} %constant_dynamic-update-slice_fusion.9, s32[]{:T(128)S(6)} %select_n.230), kind=kOutput, calls=%fused_computation.20 | convolution fusion | flops 536870912 | bytes 4456452 | tf_op jit(solution)/shard_map/dot_general | solution.py:163
  117.6 2.9 %collective-permute-done.21 = f32[4,128,128]{2,1,0:T(8,128)S(1)} collective-permute-done((f32[4,128,128]{2,1,0:T(8,128)S(1)}, f32[4,128,128]{2,1,0:T(8,128)S(1)}, u32[]{:S(2)}, u32[]{:S(2)}) %collective-permute-start.21) | collective-permute-done | bytes 262176 | tf_op jit(solution)/shard_map/ppermute | solution.py:66
  120.5 1.9 %collective-permute-start.22 = (f32[4,128,128]{2,1,0:T(8,128)S(1)}, f32[4,128,128]{2,1,0:T(8,128)S(1)}, u32[]{:S(2)}, u32[]{:S(2)}) collective-permute-start(f32[4,128,128]{2,1,0:T(8,128)S(1)} %fusion.83), channel_id=1, source_target_pairs={{4,0},{6,2},{8,4},{10,6},{12,8},{14,10},{5,1},{7,3},{9,5},{11,7},{... | collective-permute-start | bytes 786440 | tf_op jit(solution)/shard_map/ppermute | solution.py:66
  122.4 2.4 %fusion.15 = f32[256,2048]{1,0:T(8,128)S(1)} fusion(bf16[256,512]{0,1:T(8,128)(2,1)S(1)} %bitcast.117, bf16[2048,1536]{1,0:T(8,128)(2,1)} %constant_dynamic-update-slice_fusion.9, s32[]{:T(128)S(6)} %select_n.230), kind=kOutput, calls=%fused_computation.18 | convolution fusion | flops 536870912 | bytes 4456452 | tf_op jit(solution)/shard_map/dot_general | solution.py:163
  124.8 3.1 %collective-permute-done.22 = f32[4,128,128]{2,1,0:T(8,128)S(1)} collective-permute-done((f32[4,128,128]{2,1,0:T(8,128)S(1)}, f32[4,128,128]{2,1,0:T(8,128)S(1)}, u32[]{:S(2)}, u32[]{:S(2)}) %collective-permute-start.22) | collective-permute-done | bytes 262176 | tf_op jit(solution)/shard_map/ppermute | solution.py:66
  128.0 1.3 collective-permute-start.23
  130.4 8.4 %collective-permute-done.23 = f32[4,128,128]{2,1,0:T(8,128)S(1)} collective-permute-done((f32[4,128,128]{2,1,0:T(8,128)S(1)}, f32[4,128,128]{2,1,0:T(8,128)S(1)}, u32[]{:S(2)}, u32[]{:S(2)}) %collective-permute-start.23) | collective-permute-done | bytes 262176 | tf_op jit(solution)/shard_map/ppermute | solution.py:66
  140.1 2.4 %fusion.11 = f32[256,2048]{1,0:T(8,128)S(1)} fusion(bf16[256,512]{0,1:T(8,128)(2,1)S(1)} %bitcast.118, bf16[2048,1536]{1,0:T(8,128)(2,1)} %constant_dynamic-update-slice_fusion.9, s32[]{:T(128)S(6)} %select_n.231), kind=kOutput, calls=%fused_computation.14 | convolution fusion | flops 536870912 | bytes 4456452 | tf_op jit(solution)/shard_map/dot_general | solution.py:190
  142.5 3.9 %add_add_fusion = f32[256,2048]{1,0:T(8,128)} fusion(f32[256,2048]{1,0:T(8,128)S(1)} %fusion.15, f32[256,2048]{1,0:T(8,128)S(1)} %fusion.11, bf16[256,512]{0,1:T(8,128)(2,1)S(1)} %bitcast.120, bf16[2048,1536]{1,0:T(8,128)(2,1)} %constant_dynamic-update-slice_fusion.9, s32[]{:T(128)S(6)} %select_n.229), kind=kOutput, calls=%fused_computation.5 | convolution fusion | flops 537919488 | bytes 8650756 | tf_op jit(solution)/shard_map/dot_general | solution.py:190
  146.4 11.4 %collective-permute-start.25 = (f32[256,2048]{1,0:T(8,128)}, f32[256,2048]{1,0:T(8,128)}, u32[]{:S(2)}, u32[]{:S(2)}) collective-permute-start(f32[256,2048]{1,0:T(8,128)} %add_add_fusion), channel_id=1, source_target_pairs={{0,1},{1,0},{2,3},{3,2},{4,5},{5,4},{6,7},{7,6},{8,9},{9,8},{10,11... | collective-permute-start | bytes 6291464 | tf_op jit(solution)/shard_map/ppermute | solution.py:17
  158.1 2.4 %fusion.13 = f32[256,2048]{1,0:T(8,128)S(1)} fusion(bf16[256,512]{0,1:T(8,128)(2,1)S(1)} %bitcast.115, bf16[2048,1536]{1,0:T(8,128)(2,1)} %constant_dynamic-update-slice_fusion.9, s32[]{:T(128)S(6)} %select_n.231), kind=kOutput, calls=%fused_computation.16 | convolution fusion | flops 536870912 | bytes 4456452 | tf_op jit(solution)/shard_map/dot_general | solution.py:190
  160.5 2.4 %add_add_fusion.1 = f32[256,2048]{1,0:T(8,128)S(1)} fusion(f32[256,2048]{1,0:T(8,128)S(1)} %fusion.17, f32[256,2048]{1,0:T(8,128)S(1)} %fusion.13, bf16[256,512]{0,1:T(8,128)(2,1)S(1)} %bitcast.116, bf16[2048,1536]{1,0:T(8,128)(2,1)} %constant_dynamic-update-slice_fusion.9, s32[]{:T(128)S(6)} %select_n.229), kind=kOutput, calls=%fused_computation.6 | convolution fusion | flops 537919488 | bytes 8650756 | tf_op jit(solution)/shard_map/dot_general | solution.py:190
  163.9 2.8 %add_convert_fusion = bf16[256,2048]{1,0:T(8,128)(2,1)} fusion(f32[256,2048]{1,0:T(8,128)S(1)} %add_add_fusion.1, f32[256,2048]{1,0:T(8,128)} %collective-permute-done.25), kind=kLoop, calls=%fused_computation.4 | loop fusion | flops 1048576 | bytes 5242880 | tf_op jit(solution)/shard_map/convert_element_type | solution.py:195
  (120 shorter events, 43.0 us)
Async XLA Ops:
  2.8 9.6 %copy-start = (bf16[256,2048]{1,0:T(8,128)(2,1)S(1)}, bf16[256,2048]{1,0:T(8,128)(2,1)}, u32[]{:S(2)}) copy-start(bf16[256,2048]{1,0:T(8,128)(2,1)} %param.10) | copy-start | bytes 3145732
  2.8 3.0 %collective-permute-start.1 = (bf16[128,1536]{1,0:T(8,128)(2,1)S(1)}, bf16[128,1536]{1,0:T(8,128)(2,1)}, u32[]{:S(2)}, u32[]{:S(2)}) collective-permute-start(bf16[128,1536]{1,0:T(8,128)(2,1)S(1)} %pad_maximum_fusion.1), channel_id=1, source_target_pairs={{0,1},{1,0},{2,3},{3,2},{4,5},{5,4},{6,7},{7,6},{8,9},{9,8},{10,11... | collective-permute-start | bytes 1179656 | tf_op jit(solution)/shard_map/ppermute | solution.py:17
  5.6 102.5 %collective-permute-start.20 = (bf16[256,512]{0,1:T(8,128)(2,1)}, bf16[256,512]{0,1:T(8,128)(2,1)}, u32[]{:S(2)}, u32[]{:S(2)}) collective-permute-start(bf16[256,512]{0,1:T(8,128)(2,1)} %get-tuple-element.44), channel_id=1, source_target_pairs={{0,1},{1,0},{2,3},{3,2},{4,5},{5,4},{6,7},{7,6},{8,9},{9,8},{10,11... | collective-permute-start | bytes 786440 | tf_op jit(solution)/shard_map/ppermute | solution.py:17
  5.7 10.3 %copy-start.5 = (s32[8]{0:T(128)S(1)}, s32[8]{0:T(128)}, u32[]{:S(2)}) copy-start(s32[8]{0:T(128)} %constant.120.clone) | copy-start | bytes 100
  5.7 14.9 %copy-start.3 = (s32[8]{0:T(128)S(1)}, s32[8]{0:T(128)}, u32[]{:S(2)}) copy-start(s32[8]{0:T(128)} %constant.119.clone) | copy-start | bytes 100
  11.0 42.9 %copy-start.4 = (s32[1,2,2]{2,1,0:T(2,128)S(1)}, s32[1,2,2]{2,1,0:T(2,128)}, u32[]{:S(2)}) copy-start(s32[1,2,2]{2,1,0:T(2,128)} %param.15) | copy-start | bytes 52
  11.0 14.8 %collective-permute-start.2 = (bf16[256,1024]{1,0:T(8,128)(2,1)}, bf16[256,1024]{1,0:T(8,128)(2,1)S(1)}, u32[]{:S(2)}, u32[]{:S(2)}) collective-permute-start(bf16[256,1024]{1,0:T(8,128)(2,1)} %get-tuple-element.25), channel_id=1, source_target_pairs={{0,4},{4,8},{8,12},{12,14},{14,10},{10,6},{6,2},{2,0},{1,5},{5,9},... | collective-permute-start | bytes 1572872 | tf_op jit(solution)/shard_map/ppermute | solution.py:47
  11.2 15.9 %collective-permute-start.4 = (bf16[256,1024]{1,0:T(8,128)(2,1)}, bf16[256,1024]{1,0:T(8,128)(2,1)S(1)}, u32[]{:S(2)}, u32[]{:S(2)}) collective-permute-start(bf16[256,1024]{1,0:T(8,128)(2,1)} %get-tuple-element.25), channel_id=1, source_target_pairs={{0,2},{4,0},{8,4},{12,8},{14,12},{10,14},{6,10},{2,6},{1,3},{5,1},... | collective-permute-start | bytes 1572872 | tf_op jit(solution)/shard_map/ppermute | solution.py:50
  15.1 57.5 %collective-permute-start = (bf16[256,2048]{1,0:T(8,128)(2,1)}, bf16[256,2048]{1,0:T(8,128)(2,1)S(1)}, u32[]{:S(2)}, u32[]{:S(2)}) collective-permute-start(bf16[256,2048]{1,0:T(8,128)(2,1)} %add_convert_fusion.1), channel_id=1, source_target_pairs={{0,1},{1,0},{2,3},{3,2},{4,5},{5,4},{6,7},{7,6},{8,9},{9,8},{10,11... | collective-permute-start | bytes 3145736 | tf_op jit(solution)/shard_map/ppermute | solution.py:17
  25.8 8.0 %collective-permute-start.3 = (bf16[256,512]{1,0:T(8,128)(2,1)S(1)}, bf16[256,512]{1,0:T(8,128)(2,1)S(1)}, u32[]{:S(2)}, u32[]{:S(2)}) collective-permute-start(bf16[256,512]{1,0:T(8,128)(2,1)S(1)} %constant_dynamic-slice_fusion.9), channel_id=1, source_target_pairs={{0,16},{16,0},{1,17},{17,1},{2,18},{18,2},{3,19},{19,3},{4,20},{20... | collective-permute-start | bytes 786440 | tf_op jit(solution)/shard_map/ppermute | solution.py:41
  26.1 13.2 %collective-permute-start.6 = (bf16[256,1024]{1,0:T(8,128)(2,1)S(1)}, bf16[256,1024]{1,0:T(8,128)(2,1)S(1)}, u32[]{:S(2)}, u32[]{:S(2)}) collective-permute-start(bf16[256,1024]{1,0:T(8,128)(2,1)S(1)} %collective-permute-done.2), channel_id=1, source_target_pairs={{0,4},{4,8},{8,12},{12,14},{14,10},{10,6},{6,2},{2,0},{1,5},{5,9},... | collective-permute-start | bytes 1572872 | tf_op jit(solution)/shard_map/ppermute | solution.py:47
  27.1 14.7 %collective-permute-start.8 = (bf16[256,1024]{1,0:T(8,128)(2,1)S(1)}, bf16[256,1024]{1,0:T(8,128)(2,1)S(1)}, u32[]{:S(2)}, u32[]{:S(2)}) collective-permute-start(bf16[256,1024]{1,0:T(8,128)(2,1)S(1)} %collective-permute-done.4), channel_id=1, source_target_pairs={{0,2},{4,0},{8,4},{12,8},{14,12},{10,14},{6,10},{2,6},{1,3},{5,1},... | collective-permute-start | bytes 1572872 | tf_op jit(solution)/shard_map/ppermute | solution.py:50
  33.8 7.0 %collective-permute-start.5 = (bf16[256,512]{1,0:T(8,128)(2,1)S(1)}, bf16[256,512]{1,0:T(8,128)(2,1)S(1)}, u32[]{:S(2)}, u32[]{:S(2)}) collective-permute-start(bf16[256,512]{1,0:T(8,128)(2,1)S(1)} %constant_dynamic-slice_fusion.8), channel_id=1, source_target_pairs={{0,16},{16,0},{1,17},{17,1},{2,18},{18,2},{3,19},{19,3},{4,20},{20... | collective-permute-start | bytes 786440 | tf_op jit(solution)/shard_map/ppermute | solution.py:41
  39.4 6.8 %collective-permute-start.7 = (bf16[256,512]{1,0:T(8,128)(2,1)S(1)}, bf16[256,512]{1,0:T(8,128)(2,1)S(1)}, u32[]{:S(2)}, u32[]{:S(2)}) collective-permute-start(bf16[256,512]{1,0:T(8,128)(2,1)S(1)} %constant_dynamic-slice_fusion.7), channel_id=1, source_target_pairs={{0,16},{16,0},{1,17},{17,1},{2,18},{18,2},{3,19},{19,3},{4,20},{20... | collective-permute-start | bytes 786440 | tf_op jit(solution)/shard_map/ppermute | solution.py:41
  40.9 11.7 %collective-permute-start.10 = (bf16[256,1024]{1,0:T(8,128)(2,1)S(1)}, bf16[256,1024]{1,0:T(8,128)(2,1)S(1)}, u32[]{:S(2)}, u32[]{:S(2)}) collective-permute-start(bf16[256,1024]{1,0:T(8,128)(2,1)S(1)} %collective-permute-done.6), channel_id=1, source_target_pairs={{0,4},{4,8},{8,12},{12,14},{14,10},{10,6},{6,2},{2,0},{1,5},{5,9},... | collective-permute-start | bytes 1572872 | tf_op jit(solution)/shard_map/ppermute | solution.py:47
  41.8 12.1 %collective-permute-start.12 = (bf16[256,1024]{1,0:T(8,128)(2,1)S(1)}, bf16[256,1024]{1,0:T(8,128)(2,1)S(1)}, u32[]{:S(2)}, u32[]{:S(2)}) collective-permute-start(bf16[256,1024]{1,0:T(8,128)(2,1)S(1)} %collective-permute-done.8), channel_id=1, source_target_pairs={{0,2},{4,0},{8,4},{12,8},{14,12},{10,14},{6,10},{2,6},{1,3},{5,1},... | collective-permute-start | bytes 1572872 | tf_op jit(solution)/shard_map/ppermute | solution.py:50
  46.2 6.7 %collective-permute-start.9 = (bf16[256,512]{1,0:T(8,128)(2,1)S(1)}, bf16[256,512]{1,0:T(8,128)(2,1)S(1)}, u32[]{:S(2)}, u32[]{:S(2)}) collective-permute-start(bf16[256,512]{1,0:T(8,128)(2,1)S(1)} %constant_dynamic-slice_fusion.6), channel_id=1, source_target_pairs={{0,16},{16,0},{1,17},{17,1},{2,18},{18,2},{3,19},{19,3},{4,20},{20... | collective-permute-start | bytes 786440 | tf_op jit(solution)/shard_map/ppermute | solution.py:41
  52.6 10.8 %collective-permute-start.14 = (bf16[256,1024]{1,0:T(8,128)(2,1)S(1)}, bf16[256,1024]{1,0:T(8,128)(2,1)S(1)}, u32[]{:S(2)}, u32[]{:S(2)}) collective-permute-start(bf16[256,1024]{1,0:T(8,128)(2,1)S(1)} %collective-permute-done.10), channel_id=1, source_target_pairs={{0,4},{4,8},{8,12},{12,14},{14,10},{10,6},{6,2},{2,0},{1,5},{5,9},... | collective-permute-start | bytes 1572872 | tf_op jit(solution)/shard_map/ppermute | solution.py:47
  52.8 5.3 %collective-permute-start.11 = (bf16[256,512]{1,0:T(8,128)(2,1)S(1)}, bf16[256,512]{1,0:T(8,128)(2,1)S(1)}, u32[]{:S(2)}, u32[]{:S(2)}) collective-permute-start(bf16[256,512]{1,0:T(8,128)(2,1)S(1)} %constant_dynamic-slice_fusion.5), channel_id=1, source_target_pairs={{0,16},{16,0},{1,17},{17,1},{2,18},{18,2},{3,19},{19,3},{4,20},{20... | collective-permute-start | bytes 786440 | tf_op jit(solution)/shard_map/ppermute | solution.py:41
  53.9 29.3 %collective-permute-start.16 = (s32[2,2]{1,0:T(2,128)S(1)}, s32[2,2]{1,0:T(2,128)S(1)}, u32[]{:S(2)}, u32[]{:S(2)}) collective-permute-start(s32[2,2]{1,0:T(2,128)S(1)} %bitcast.123), channel_id=1, source_target_pairs={{0,1},{1,0},{2,3},{3,2},{4,5},{5,4},{6,7},{7,6},{8,9},{9,8},{10,11... | collective-permute-start | bytes 56 | tf_op jit(solution)/shard_map/ppermute | solution.py:17
  58.1 6.5 %collective-permute-start.13 = (bf16[256,512]{1,0:T(8,128)(2,1)S(1)}, bf16[256,512]{1,0:T(8,128)(2,1)S(1)}, u32[]{:S(2)}, u32[]{:S(2)}) collective-permute-start(bf16[256,512]{1,0:T(8,128)(2,1)S(1)} %constant_dynamic-slice_fusion.4), channel_id=1, source_target_pairs={{0,16},{16,0},{1,17},{17,1},{2,18},{18,2},{3,19},{19,3},{4,20},{20... | collective-permute-start | bytes 786440 | tf_op jit(solution)/shard_map/ppermute | solution.py:41
  63.4 8.4 %collective-permute-start.15 = (bf16[256,512]{1,0:T(8,128)(2,1)S(1)}, bf16[256,512]{1,0:T(8,128)(2,1)S(1)}, u32[]{:S(2)}, u32[]{:S(2)}) collective-permute-start(bf16[256,512]{1,0:T(8,128)(2,1)S(1)} %constant_dynamic-slice_fusion.3), channel_id=1, source_target_pairs={{0,16},{16,0},{1,17},{17,1},{2,18},{18,2},{3,19},{19,3},{4,20},{20... | collective-permute-start | bytes 786440 | tf_op jit(solution)/shard_map/ppermute | solution.py:41
  80.8 7.4 %collective-permute-start.17 = (f32[4,128,128]{2,1,0:T(8,128)}, f32[4,128,128]{2,1,0:T(8,128)}, u32[]{:S(2)}, u32[]{:S(2)}) collective-permute-start(f32[4,128,128]{2,1,0:T(8,128)} %fusion.37), channel_id=1, source_target_pairs={{0,2},{2,4},{4,6},{6,8},{8,10},{10,12},{12,14},{1,3},{3,5},{5,7},{... | collective-permute-start | bytes 786440 | tf_op jit(solution)/shard_map/ppermute | solution.py:66
  89.2 7.1 %collective-permute-start.18 = (f32[4,128,128]{2,1,0:T(8,128)S(1)}, f32[4,128,128]{2,1,0:T(8,128)S(1)}, u32[]{:S(2)}, u32[]{:S(2)}) collective-permute-start(f32[4,128,128]{2,1,0:T(8,128)S(1)} %fusion.84), channel_id=1, source_target_pairs={{0,4},{2,6},{4,8},{6,10},{8,12},{10,14},{1,5},{3,7},{5,9},{7,11},{... | collective-permute-start | bytes 786440 | tf_op jit(solution)/shard_map/ppermute | solution.py:66
  96.4 10.2 %collective-permute-start.19 = (f32[4,128,128]{2,1,0:T(8,128)S(1)}, f32[4,128,128]{2,1,0:T(8,128)S(1)}, u32[]{:S(2)}, u32[]{:S(2)}) collective-permute-start(f32[4,128,128]{2,1,0:T(8,128)S(1)} %add.284), channel_id=1, source_target_pairs={{0,8},{2,10},{4,12},{6,14},{1,9},{3,11},{5,13},{7,15},{16,24},{18,... | collective-permute-start | bytes 786440 | tf_op jit(solution)/shard_map/ppermute | solution.py:66
  112.4 8.0 %collective-permute-start.21 = (f32[4,128,128]{2,1,0:T(8,128)S(1)}, f32[4,128,128]{2,1,0:T(8,128)S(1)}, u32[]{:S(2)}, u32[]{:S(2)}) collective-permute-start(f32[4,128,128]{2,1,0:T(8,128)S(1)} %fusion.38), channel_id=1, source_target_pairs={{2,0},{4,2},{6,4},{8,6},{10,8},{12,10},{14,12},{3,1},{5,3},{7,5},{... | collective-permute-start | bytes 786440 | tf_op jit(solution)/shard_map/ppermute | solution.py:66
  120.5 7.4 %collective-permute-start.22 = (f32[4,128,128]{2,1,0:T(8,128)S(1)}, f32[4,128,128]{2,1,0:T(8,128)S(1)}, u32[]{:S(2)}, u32[]{:S(2)}) collective-permute-start(f32[4,128,128]{2,1,0:T(8,128)S(1)} %fusion.83), channel_id=1, source_target_pairs={{4,0},{6,2},{8,4},{10,6},{12,8},{14,10},{5,1},{7,3},{9,5},{11,7},{... | collective-permute-start | bytes 786440 | tf_op jit(solution)/shard_map/ppermute | solution.py:66
  128.0 10.8 %collective-permute-start.23 = (f32[4,128,128]{2,1,0:T(8,128)S(1)}, f32[4,128,128]{2,1,0:T(8,128)S(1)}, u32[]{:S(2)}, u32[]{:S(2)}) collective-permute-start(f32[4,128,128]{2,1,0:T(8,128)S(1)} %add.296), channel_id=1, source_target_pairs={{8,0},{10,2},{12,4},{14,6},{9,1},{11,3},{13,5},{15,7},{24,16},{26,... | collective-permute-start | bytes 786440 | tf_op jit(solution)/shard_map/ppermute | solution.py:66
  140.1 17.8 %copy-start.1 = (bf16[1,256,4,128]{1,3,2,0:T(8,128)(2,1)S(1)}, bf16[1,256,4,128]{1,3,2,0:T(8,128)(2,1)}, u32[]{:S(2)}) copy-start(bf16[1,256,4,128]{1,3,2,0:T(8,128)(2,1)} %get-tuple-element.40) | copy-start | bytes 786436
  142.5 15.3 %copy-start.2 = (bf16[1,256,4,128]{1,3,2,0:T(8,128)(2,1)S(1)}, bf16[1,256,4,128]{1,3,2,0:T(8,128)(2,1)}, u32[]{:S(2)}) copy-start(bf16[1,256,4,128]{1,3,2,0:T(8,128)(2,1)} %get-tuple-element.39) | copy-start | bytes 786436
  146.4 17.5 %collective-permute-start.25 = (f32[256,2048]{1,0:T(8,128)}, f32[256,2048]{1,0:T(8,128)}, u32[]{:S(2)}, u32[]{:S(2)}) collective-permute-start(f32[256,2048]{1,0:T(8,128)} %add_add_fusion), channel_id=1, source_target_pairs={{0,1},{1,0},{2,3},{3,2},{4,5},{5,4},{6,7},{7,6},{8,9},{9,8},{10,11... | collective-permute-start | bytes 6291464 | tf_op jit(solution)/shard_map/ppermute | solution.py:17
  158.0 4.9 %collective-permute-start.24 = (bf16[256,512]{1,0:T(8,128)(2,1)S(1)}, bf16[256,512]{1,0:T(8,128)(2,1)S(1)}, u32[]{:S(2)}, u32[]{:S(2)}) collective-permute-start(bf16[256,512]{1,0:T(8,128)(2,1)S(1)} %copy.44), channel_id=1, source_target_pairs={{0,1},{1,0},{2,3},{3,2},{4,5},{5,4},{6,7},{7,6},{8,9},{9,8},{10,11... | collective-permute-start | bytes 786440 | tf_op jit(solution)/shard_map/ppermute | solution.py:17

commit v18 on v17

--- a/solution.py
+++ b/solution.py
@@ -119,14 +119,12 @@
     at_q = parity * width
     at_k = (1 - parity) * share
     at_v = width - parity * share
-    p_all = jnp.dot(x_pair, w_all, preferred_element_type=f32).astype(bf16)
-
-    def pick(at):
-        return lax.dynamic_slice_in_dim(p_all, at, share, axis=1).reshape(2, tok, heads, DH)
-
-    query = pick(at_q)
-    key = pick(at_k)
-    value = pick(at_v)
+    w_kv = lax.dynamic_slice_in_dim(w_all, at_k, width, axis=1)
+    p_kv = jnp.dot(x_pair, w_kv, preferred_element_type=f32).astype(bf16).reshape(2, tok, 2, heads, DH)
+    key = p_kv[:, :, 0]
+    value = p_kv[:, :, 1]
+    w_qcols = lax.dynamic_slice_in_dim(w_all, at_q, share, axis=1)
+    query = jnp.dot(x_pair, w_qcols, preferred_element_type=f32).astype(bf16).reshape(2, tok, heads, DH)
 
     local = jnp.einsum("jthd,jthe->jhde", key, value, preferred_element_type=f32)
     state0, _ = exclusive_scan(local[0] + local[1], chips, False)
@@ -159,7 +157,6 @@
     d_query = d_query + jnp.einsum("jthe,jhde->jthd", d_mixed_b, state_b, preferred_element_type=f32)
     dq_b = d_query.astype(bf16).reshape(2, tok, half)
     dims = (((1,), (1,)), ((), ()))
-    w_qcols = lax.dynamic_slice_in_dim(w_all, at_q, share, axis=1)
     grad_q = [lax.dot_general(dq_b[j], w_qcols, dims, preferred_element_type=f32) for j in range(2)]
     dk_intra = jnp.einsum("jhts,jthd->jshd", d_attn, query, preferred_element_type=f32)
     dv_intra = jnp.einsum("jhts,jthe->jshe", attn, d_mixed_b, preferred_element_type=f32)

time: 169 us -> 166 us (0.982); the launches traced: 167 us -> 166 us
  waiting for transfers between devices: 50.7 us -> 47.2 us
  matrix products: 26.8 us -> 28.9 us
    ppermute x6, waiting for transfers between devices: 27.2 us -> 24.2 us  [exclusive_scan(): got = lax.ppermute(incl, 'chip', perm)]
    dot_general x1 -> x2, matrix products: 6.53 us -> 8.67 us  [the longest x1 5.16 us: on_device(): jnp.dot(x_pair, w_kv, preferred_element_type=f32).astype(bf16)]
  transfers between devices with their start and end apart: 26 -> 26, of which waited for: 14 -> 12; matrix products, arithmetic and copies ran while one was open for 29% -> 31% of each run, Pallas kernels for 0% -> 0%
where the time goes in v18:
time: 166 us
  waiting for transfers between devices  47.2 us (28%)
  starting transfers between devices  41.7 us (25%)
  matrix products  28.9 us (17%)
  local copies, waits for them, and re-layouts  25.7 us (15%)
  other arithmetic  12.2 us (7%)
  between operations  10 us (6%)
    ppermute x6, waiting for transfers between devices, exclusive_scan(): got = lax.ppermute(incl, 'chip', perm)  24.2 us
    ppermute x6, starting transfers between devices, exclusive_scan(): got = lax.ppermute(incl, 'chip', perm)  16.9 us
    ppermute x6, starting transfers between devices, swap(): return lax.ppermute(x, 'core', [(0, 1), (1, 0)])  15.3 us
    ppermute x4, waiting for transfers between devices, ring_gather(): fwd = lax.ppermute(fwd, 'chip', ahead)  11.7 us
    ppermute x7, waiting for transfers between devices, land(): return (piece, lax.ppermute(sent, 'groups', partner))  11.3 us
    dot_general x4, matrix products, grad_rows(): g = g + lax.dot_general(d, w, dims, preferred_element_type=f32)  11.1 us
    dynamic_update_slice x8, local copies, waits for them, and re-layouts, on_device(): w_all = lax.dynamic_update_slice(w_all, ringed, (src * span, 0))  7.13 us
    dynamic_update_slice x8, local copies, waits for them, and re-layouts, on_device(): w_all = lax.dynamic_update_slice(w_all, swapped, (src * span, width))  5.98 us
  transfers between devices with their start and end apart: 26, of which 12 were waited for; matrix products, arithmetic and copies ran while one was open for 31% of the time, Pallas kernels for 0%

profile of v18, /device:TPU:15, one launch (start us, length us, event | category | flops | bytes accessed | tf_op | source)
XLA Modules:
  0.0 165.7 jit_solution(4612481044546902759)
XLA Ops:
  7.5 3.0 %broadcast_in_dim.33 = bf16[2048,1536]{1,0:T(8,128)(2,1)} broadcast(bf16[]{:T(256)} %constant.94.clone.1), dimensions={} | broadcast | bytes 6291458 | tf_op jit(solution)/shard_map/broadcast_in_dim | solution.py:115
  13.1 2.6 %add_convert_fusion.1 = bf16[256,2048]{1,0:T(8,128)(2,1)} fusion(bf16[256,2048]{1,0:T(8,128)(2,1)S(1)} %copy-done, bf16[256,2048]{1,0:T(8,128)(2,1)} %param.9), kind=kLoop, calls=%fused_computation.8 | loop fusion | flops 2097152 | bytes 3145728 | tf_op jit(solution)/shard_map/convert_element_type | solution.py:97
  31.6 4.0 %collective-permute-done.3 = bf16[256,512]{1,0:T(8,128)(2,1)S(1)} collective-permute-done((bf16[256,512]{1,0:T(8,128)(2,1)S(1)}, bf16[256,512]{1,0:T(8,128)(2,1)S(1)}, u32[]{:S(2)}, u32[]{:S(2)}) %collective-permute-start.3) | collective-permute-done | bytes 262176 | tf_op jit(solution)/shard_map/ppermute | solution.py:41
  37.5 3.7 %collective-permute-done.6 = bf16[256,1024]{1,0:T(8,128)(2,1)S(1)} collective-permute-done((bf16[256,1024]{1,0:T(8,128)(2,1)S(1)}, bf16[256,1024]{1,0:T(8,128)(2,1)S(1)}, u32[]{:S(2)}, u32[]{:S(2)}) %collective-permute-start.6) | collective-permute-done | bytes 524320 | tf_op jit(solution)/shard_map/ppermute | solution.py:47
  41.2 1.3 collective-permute-start.7
  45.5 1.8 %collective-permute-done.7 = bf16[256,512]{1,0:T(8,128)(2,1)S(1)} collective-permute-done((bf16[256,512]{1,0:T(8,128)(2,1)S(1)}, bf16[256,512]{1,0:T(8,128)(2,1)S(1)}, u32[]{:S(2)}, u32[]{:S(2)}) %collective-permute-start.7) | collective-permute-done | bytes 262176 | tf_op jit(solution)/shard_map/ppermute | solution.py:41
  50.2 3.7 %collective-permute-done.10 = bf16[256,1024]{1,0:T(8,128)(2,1)S(1)} collective-permute-done((bf16[256,1024]{1,0:T(8,128)(2,1)S(1)}, bf16[256,1024]{1,0:T(8,128)(2,1)S(1)}, u32[]{:S(2)}, u32[]{:S(2)}) %collective-permute-start.10) | collective-permute-done | bytes 524320 | tf_op jit(solution)/shard_map/ppermute | solution.py:47
  57.4 2.0 %collective-permute-done.11 = bf16[256,512]{1,0:T(8,128)(2,1)S(1)} collective-permute-done((bf16[256,512]{1,0:T(8,128)(2,1)S(1)}, bf16[256,512]{1,0:T(8,128)(2,1)S(1)}, u32[]{:S(2)}, u32[]{:S(2)}) %collective-permute-start.11) | collective-permute-done | bytes 262176 | tf_op jit(solution)/shard_map/ppermute | solution.py:41
  60.2 4.3 %collective-permute-done.14 = bf16[256,1024]{1,0:T(8,128)(2,1)S(1)} collective-permute-done((bf16[256,1024]{1,0:T(8,128)(2,1)S(1)}, bf16[256,1024]{1,0:T(8,128)(2,1)S(1)}, u32[]{:S(2)}, u32[]{:S(2)}) %collective-permute-start.14) | collective-permute-done | bytes 524320 | tf_op jit(solution)/shard_map/ppermute | solution.py:47
  67.3 3.4 %collective-permute-done.15 = bf16[256,512]{1,0:T(8,128)(2,1)S(1)} collective-permute-done((bf16[256,512]{1,0:T(8,128)(2,1)S(1)}, bf16[256,512]{1,0:T(8,128)(2,1)S(1)}, u32[]{:S(2)}, u32[]{:S(2)}) %collective-permute-start.15) | collective-permute-done | bytes 262176 | tf_op jit(solution)/shard_map/ppermute | solution.py:41
  71.4 5.2 %fusion.20 = bf16[512,1024]{1,0:T(8,128)(2,1)S(1)} fusion(bf16[2048,1536]{1,0:T(8,128)(2,1)} %constant_dynamic-update-slice_fusion.9, s32[]{:T(128)S(6)} %select_n.227, bf16[256,2048]{1,0:T(8,128)(2,1)} %collective-permute-done, bf16[256,2048]{1,0:T(8,128)(2,1)} %add_convert_fusion.1), kind=kOutput, calls=%fused_computation.23 | convolution fusion | flops 2152202240 | bytes 7340036 | tf_op jit(solution)/shard_map/dot_general | solution.py:123
  79.1 5.0 %collective-permute-start.17 = (f32[4,128,128]{2,1,0:T(8,128)}, f32[4,128,128]{2,1,0:T(8,128)S(1)}, u32[]{:S(2)}, u32[]{:S(2)}) collective-permute-start(f32[4,128,128]{2,1,0:T(8,128)} %fusion.43), channel_id=1, source_target_pairs={{0,2},{2,4},{4,6},{6,8},{8,10},{10,12},{12,14},{1,3},{3,5},{5,7},{... | collective-permute-start | bytes 786440 | tf_op jit(solution)/shard_map/ppermute | solution.py:66
  84.1 1.6 broadcast_and_fusion
  85.7 3.5 %fusion.24 = bf16[512,512]{1,0:T(8,128)(2,1)S(1)} fusion(bf16[2048,1536]{1,0:T(8,128)(2,1)} %constant_dynamic-update-slice_fusion.9, s32[]{:T(128)S(6)} %select_n.228, bf16[256,2048]{1,0:T(8,128)(2,1)} %collective-permute-done, bf16[256,2048]{1,0:T(8,128)(2,1)} %add_convert_fusion.1), kind=kOutput, calls=%fused_computation.33 | convolution fusion | flops 1078198272 | bytes 4718596 | tf_op jit(solution)/shard_map/dot_general | solution.py:127
  89.7 3.1 %collective-permute-start.18 = (f32[4,128,128]{2,1,0:T(8,128)S(1)}, f32[4,128,128]{2,1,0:T(8,128)S(1)}, u32[]{:S(2)}, u32[]{:S(2)}) collective-permute-start(f32[4,128,128]{2,1,0:T(8,128)S(1)} %fusion.90), channel_id=1, source_target_pairs={{0,4},{2,6},{4,8},{6,10},{8,12},{10,14},{1,5},{3,7},{5,9},{7,11},{... | collective-permute-start | bytes 786440 | tf_op jit(solution)/shard_map/ppermute | solution.py:66
  93.3 3.5 %collective-permute-done.18 = f32[4,128,128]{2,1,0:T(8,128)S(1)} collective-permute-done((f32[4,128,128]{2,1,0:T(8,128)S(1)}, f32[4,128,128]{2,1,0:T(8,128)S(1)}, u32[]{:S(2)}, u32[]{:S(2)}) %collective-permute-start.18) | collective-permute-done | bytes 262176 | tf_op jit(solution)/shard_map/ppermute | solution.py:66
  96.9 3.0 %collective-permute-start.19 = (f32[4,128,128]{2,1,0:T(8,128)S(1)}, f32[4,128,128]{2,1,0:T(8,128)S(1)}, u32[]{:S(2)}, u32[]{:S(2)}) collective-permute-start(f32[4,128,128]{2,1,0:T(8,128)S(1)} %add.281), channel_id=1, source_target_pairs={{0,8},{2,10},{4,12},{6,14},{1,9},{3,11},{5,13},{7,15},{16,24},{18,... | collective-permute-start | bytes 786440 | tf_op jit(solution)/shard_map/ppermute | solution.py:66
  100.4 5.9 %collective-permute-done.19 = f32[4,128,128]{2,1,0:T(8,128)S(1)} collective-permute-done((f32[4,128,128]{2,1,0:T(8,128)S(1)}, f32[4,128,128]{2,1,0:T(8,128)S(1)}, u32[]{:S(2)}, u32[]{:S(2)}) %collective-permute-start.19) | collective-permute-done | bytes 262176 | tf_op jit(solution)/shard_map/ppermute | solution.py:66
  109.2 2.5 %collective-permute-start.21 = (f32[4,128,128]{2,1,0:T(8,128)S(1)}, f32[4,128,128]{2,1,0:T(8,128)S(1)}, u32[]{:S(2)}, u32[]{:S(2)}) collective-permute-start(f32[4,128,128]{2,1,0:T(8,128)S(1)} %fusion.44), channel_id=1, source_target_pairs={{2,0},{4,2},{6,4},{8,6},{10,8},{12,10},{14,12},{3,1},{5,3},{7,5},{... | collective-permute-start | bytes 786440 | tf_op jit(solution)/shard_map/ppermute | solution.py:66
  111.7 2.4 %fusion.16 = f32[256,2048]{1,0:T(8,128)S(1)} fusion(bf16[256,512]{0,1:T(8,128)(2,1)S(1)} %bitcast.133, bf16[2048,1536]{1,0:T(8,128)(2,1)} %constant_dynamic-update-slice_fusion.9, s32[]{:T(128)S(6)} %select_n.228), kind=kOutput, calls=%fused_computation.19 | convolution fusion | flops 536870912 | bytes 4456452 | tf_op jit(solution)/shard_map/dot_general | solution.py:160
  114.1 3.1 %collective-permute-done.21 = f32[4,128,128]{2,1,0:T(8,128)S(1)} collective-permute-done((f32[4,128,128]{2,1,0:T(8,128)S(1)}, f32[4,128,128]{2,1,0:T(8,128)S(1)}, u32[]{:S(2)}, u32[]{:S(2)}) %collective-permute-start.21) | collective-permute-done | bytes 262176 | tf_op jit(solution)/shard_map/ppermute | solution.py:66
  117.2 1.9 %collective-permute-start.22 = (f32[4,128,128]{2,1,0:T(8,128)S(1)}, f32[4,128,128]{2,1,0:T(8,128)S(1)}, u32[]{:S(2)}, u32[]{:S(2)}) collective-permute-start(f32[4,128,128]{2,1,0:T(8,128)S(1)} %fusion.89), channel_id=1, source_target_pairs={{4,0},{6,2},{8,4},{10,6},{12,8},{14,10},{5,1},{7,3},{9,5},{11,7},{... | collective-permute-start | bytes 786440 | tf_op jit(solution)/shard_map/ppermute | solution.py:66
  119.2 2.4 %fusion.14 = f32[256,2048]{1,0:T(8,128)S(1)} fusion(bf16[256,512]{0,1:T(8,128)(2,1)S(1)} %bitcast.131, bf16[2048,1536]{1,0:T(8,128)(2,1)} %constant_dynamic-update-slice_fusion.9, s32[]{:T(128)S(6)} %select_n.228), kind=kOutput, calls=%fused_computation.17 | convolution fusion | flops 536870912 | bytes 4456452 | tf_op jit(solution)/shard_map/dot_general | solution.py:160
  121.5 5.6 %collective-permute-done.22 = f32[4,128,128]{2,1,0:T(8,128)S(1)} collective-permute-done((f32[4,128,128]{2,1,0:T(8,128)S(1)}, f32[4,128,128]{2,1,0:T(8,128)S(1)}, u32[]{:S(2)}, u32[]{:S(2)}) %collective-permute-start.22) | collective-permute-done | bytes 262176 | tf_op jit(solution)/shard_map/ppermute | solution.py:66
  127.1 1.3 collective-permute-start.23
  129.6 6.1 %collective-permute-done.23 = f32[4,128,128]{2,1,0:T(8,128)S(1)} collective-permute-done((f32[4,128,128]{2,1,0:T(8,128)S(1)}, f32[4,128,128]{2,1,0:T(8,128)S(1)}, u32[]{:S(2)}, u32[]{:S(2)}) %collective-permute-start.23) | collective-permute-done | bytes 262176 | tf_op jit(solution)/shard_map/ppermute | solution.py:66
  137.0 2.4 %fusion.10 = f32[256,2048]{1,0:T(8,128)S(1)} fusion(bf16[256,512]{0,1:T(8,128)(2,1)S(1)} %bitcast.132, bf16[2048,1536]{1,0:T(8,128)(2,1)} %constant_dynamic-update-slice_fusion.9, s32[]{:T(128)S(6)} %select_n.227), kind=kOutput, calls=%fused_computation.13 | convolution fusion | flops 536870912 | bytes 4456452 | tf_op jit(solution)/shard_map/dot_general | solution.py:187
  139.4 3.9 %add_add_fusion = f32[256,2048]{1,0:T(8,128)} fusion(f32[256,2048]{1,0:T(8,128)S(1)} %fusion.14, f32[256,2048]{1,0:T(8,128)S(1)} %fusion.10, bf16[256,512]{0,1:T(8,128)(2,1)S(1)} %bitcast.134, bf16[2048,1536]{1,0:T(8,128)(2,1)} %constant_dynamic-update-slice_fusion.9, s32[]{:T(128)S(6)} %select_n.242), kind=kOutput, calls=%fused_computation.4 | convolution fusion | flops 537919488 | bytes 8650756 | tf_op jit(solution)/shard_map/dot_general | solution.py:187
  143.3 13.4 %collective-permute-start.25 = (f32[256,2048]{1,0:T(8,128)}, f32[256,2048]{1,0:T(8,128)}, u32[]{:S(2)}, u32[]{:S(2)}) collective-permute-start(f32[256,2048]{1,0:T(8,128)} %add_add_fusion), channel_id=1, source_target_pairs={{0,1},{1,0},{2,3},{3,2},{4,5},{5,4},{6,7},{7,6},{8,9},{9,8},{10,11... | collective-permute-start | bytes 6291464 | tf_op jit(solution)/shard_map/ppermute | solution.py:17
  157.1 2.4 %fusion.12 = f32[256,2048]{1,0:T(8,128)S(1)} fusion(bf16[256,512]{0,1:T(8,128)(2,1)S(1)} %bitcast.129, bf16[2048,1536]{1,0:T(8,128)(2,1)} %constant_dynamic-update-slice_fusion.9, s32[]{:T(128)S(6)} %select_n.227), kind=kOutput, calls=%fused_computation.15 | convolution fusion | flops 536870912 | bytes 4456452 | tf_op jit(solution)/shard_map/dot_general | solution.py:187
  159.5 2.4 %add_add_fusion.1 = f32[256,2048]{1,0:T(8,128)S(1)} fusion(f32[256,2048]{1,0:T(8,128)S(1)} %fusion.16, f32[256,2048]{1,0:T(8,128)S(1)} %fusion.12, bf16[256,512]{0,1:T(8,128)(2,1)S(1)} %bitcast.130, bf16[2048,1536]{1,0:T(8,128)(2,1)} %constant_dynamic-update-slice_fusion.9, s32[]{:T(128)S(6)} %select_n.242), kind=kOutput, calls=%fused_computation.5 | convolution fusion | flops 537919488 | bytes 8650756 | tf_op jit(solution)/shard_map/dot_general | solution.py:187
  162.9 2.8 %add_convert_fusion = bf16[256,2048]{1,0:T(8,128)(2,1)} fusion(f32[256,2048]{1,0:T(8,128)S(1)} %add_add_fusion.1, f32[256,2048]{1,0:T(8,128)} %collective-permute-done.25), kind=kLoop, calls=%fused_computation.3 | loop fusion | flops 1048576 | bytes 5242880 | tf_op jit(solution)/shard_map/convert_element_type | solution.py:192
  (122 shorter events, 42.4 us)
Async XLA Ops:
  3.6 9.6 %copy-start = (bf16[256,2048]{1,0:T(8,128)(2,1)S(1)}, bf16[256,2048]{1,0:T(8,128)(2,1)}, u32[]{:S(2)}) copy-start(bf16[256,2048]{1,0:T(8,128)(2,1)} %param.10) | copy-start | bytes 3145732
  3.6 2.9 %collective-permute-start.1 = (bf16[128,1536]{1,0:T(8,128)(2,1)}, bf16[128,1536]{1,0:T(8,128)(2,1)}, u32[]{:S(2)}, u32[]{:S(2)}) collective-permute-start(bf16[128,1536]{1,0:T(8,128)(2,1)} %pad_maximum_fusion.6), channel_id=1, source_target_pairs={{0,1},{1,0},{2,3},{3,2},{4,5},{5,4},{6,7},{7,6},{8,9},{9,8},{10,11... | collective-permute-start | bytes 1179656 | tf_op jit(solution)/shard_map/ppermute | solution.py:17
  6.2 100.5 %collective-permute-start.20 = (bf16[256,512]{0,1:T(8,128)(2,1)}, bf16[256,512]{0,1:T(8,128)(2,1)S(1)}, u32[]{:S(2)}, u32[]{:S(2)}) collective-permute-start(bf16[256,512]{0,1:T(8,128)(2,1)} %get-tuple-element.43), channel_id=1, source_target_pairs={{0,1},{1,0},{2,3},{3,2},{4,5},{5,4},{6,7},{7,6},{8,9},{9,8},{10,11... | collective-permute-start | bytes 786440 | tf_op jit(solution)/shard_map/ppermute | solution.py:17
  6.4 10.3 %copy-start.5 = (s32[1,2,2]{2,1,0:T(2,128)S(1)}, s32[1,2,2]{2,1,0:T(2,128)}, u32[]{:S(2)}) copy-start(s32[1,2,2]{2,1,0:T(2,128)} %param.15) | copy-start | bytes 52
  6.4 10.3 %copy-start.6 = (s32[8]{0:T(128)S(1)}, s32[8]{0:T(128)}, u32[]{:S(2)}) copy-start(s32[8]{0:T(128)} %constant.120.clone) | copy-start | bytes 100
  6.4 15.4 %copy-start.4 = (s32[8]{0:T(128)S(1)}, s32[8]{0:T(128)}, u32[]{:S(2)}) copy-start(s32[8]{0:T(128)} %constant.119.clone) | copy-start | bytes 100
  11.6 16.5 %collective-permute-start.2 = (bf16[256,1024]{1,0:T(8,128)(2,1)}, bf16[256,1024]{1,0:T(8,128)(2,1)S(1)}, u32[]{:S(2)}, u32[]{:S(2)}) collective-permute-start(bf16[256,1024]{1,0:T(8,128)(2,1)} %get-tuple-element.25), channel_id=1, source_target_pairs={{0,4},{4,8},{8,12},{12,14},{14,10},{10,6},{6,2},{2,0},{1,5},{5,9},... | collective-permute-start | bytes 1572872 | tf_op jit(solution)/shard_map/ppermute | solution.py:47
  11.8 17.6 %collective-permute-start.4 = (bf16[256,1024]{1,0:T(8,128)(2,1)}, bf16[256,1024]{1,0:T(8,128)(2,1)S(1)}, u32[]{:S(2)}, u32[]{:S(2)}) collective-permute-start(bf16[256,1024]{1,0:T(8,128)(2,1)} %get-tuple-element.25), channel_id=1, source_target_pairs={{0,2},{4,0},{8,4},{12,8},{14,12},{10,14},{6,10},{2,6},{1,3},{5,1},... | collective-permute-start | bytes 1572872 | tf_op jit(solution)/shard_map/ppermute | solution.py:50
  15.7 55.7 %collective-permute-start = (bf16[256,2048]{1,0:T(8,128)(2,1)}, bf16[256,2048]{1,0:T(8,128)(2,1)}, u32[]{:S(2)}, u32[]{:S(2)}) collective-permute-start(bf16[256,2048]{1,0:T(8,128)(2,1)} %add_convert_fusion.1), channel_id=1, source_target_pairs={{0,1},{1,0},{2,3},{3,2},{4,5},{5,4},{6,7},{7,6},{8,9},{9,8},{10,11... | collective-permute-start | bytes 3145736 | tf_op jit(solution)/shard_map/ppermute | solution.py:17
  16.7 10.9 %collective-permute-start.16 = (s32[2,2]{1,0:T(2,128)S(1)}, s32[2,2]{1,0:T(2,128)S(1)}, u32[]{:S(2)}, u32[]{:S(2)}) collective-permute-start(s32[2,2]{1,0:T(2,128)S(1)} %bitcast.137), channel_id=1, source_target_pairs={{0,1},{1,0},{2,3},{3,2},{4,5},{5,4},{6,7},{7,6},{8,9},{9,8},{10,11... | collective-permute-start | bytes 56 | tf_op jit(solution)/shard_map/ppermute | solution.py:17
  28.2 7.4 %collective-permute-start.3 = (bf16[256,512]{1,0:T(8,128)(2,1)S(1)}, bf16[256,512]{1,0:T(8,128)(2,1)S(1)}, u32[]{:S(2)}, u32[]{:S(2)}) collective-permute-start(bf16[256,512]{1,0:T(8,128)(2,1)S(1)} %constant_dynamic-slice_fusion.6), channel_id=1, source_target_pairs={{0,16},{16,0},{1,17},{17,1},{2,18},{18,2},{3,19},{19,3},{4,20},{20... | collective-permute-start | bytes 786440 | tf_op jit(solution)/shard_map/ppermute | solution.py:41
  28.5 12.7 %collective-permute-start.6 = (bf16[256,1024]{1,0:T(8,128)(2,1)S(1)}, bf16[256,1024]{1,0:T(8,128)(2,1)S(1)}, u32[]{:S(2)}, u32[]{:S(2)}) collective-permute-start(bf16[256,1024]{1,0:T(8,128)(2,1)S(1)} %collective-permute-done.2), channel_id=1, source_target_pairs={{0,4},{4,8},{8,12},{12,14},{14,10},{10,6},{6,2},{2,0},{1,5},{5,9},... | collective-permute-start | bytes 1572872 | tf_op jit(solution)/shard_map/ppermute | solution.py:47
  29.4 14.0 %collective-permute-start.8 = (bf16[256,1024]{1,0:T(8,128)(2,1)S(1)}, bf16[256,1024]{1,0:T(8,128)(2,1)S(1)}, u32[]{:S(2)}, u32[]{:S(2)}) collective-permute-start(bf16[256,1024]{1,0:T(8,128)(2,1)S(1)} %collective-permute-done.4), channel_id=1, source_target_pairs={{0,2},{4,0},{8,4},{12,8},{14,12},{10,14},{6,10},{2,6},{1,3},{5,1},... | collective-permute-start | bytes 1572872 | tf_op jit(solution)/shard_map/ppermute | solution.py:50
  35.6 6.9 %collective-permute-start.5 = (bf16[256,512]{1,0:T(8,128)(2,1)S(1)}, bf16[256,512]{1,0:T(8,128)(2,1)S(1)}, u32[]{:S(2)}, u32[]{:S(2)}) collective-permute-start(bf16[256,512]{1,0:T(8,128)(2,1)S(1)} %constant_dynamic-slice_fusion.5), channel_id=1, source_target_pairs={{0,16},{16,0},{1,17},{17,1},{2,18},{18,2},{3,19},{19,3},{4,20},{20... | collective-permute-start | bytes 786440 | tf_op jit(solution)/shard_map/ppermute | solution.py:41
  41.2 6.2 %collective-permute-start.7 = (bf16[256,512]{1,0:T(8,128)(2,1)S(1)}, bf16[256,512]{1,0:T(8,128)(2,1)S(1)}, u32[]{:S(2)}, u32[]{:S(2)}) collective-permute-start(bf16[256,512]{1,0:T(8,128)(2,1)S(1)} %constant_dynamic-slice_fusion.4), channel_id=1, source_target_pairs={{0,16},{16,0},{1,17},{17,1},{2,18},{18,2},{3,19},{19,3},{4,20},{20... | collective-permute-start | bytes 786440 | tf_op jit(solution)/shard_map/ppermute | solution.py:41
  42.5 11.5 %collective-permute-start.10 = (bf16[256,1024]{1,0:T(8,128)(2,1)S(1)}, bf16[256,1024]{1,0:T(8,128)(2,1)S(1)}, u32[]{:S(2)}, u32[]{:S(2)}) collective-permute-start(bf16[256,1024]{1,0:T(8,128)(2,1)S(1)} %collective-permute-done.6), channel_id=1, source_target_pairs={{0,4},{4,8},{8,12},{12,14},{14,10},{10,6},{6,2},{2,0},{1,5},{5,9},... | collective-permute-start | bytes 1572872 | tf_op jit(solution)/shard_map/ppermute | solution.py:47
  43.4 11.8 %collective-permute-start.12 = (bf16[256,1024]{1,0:T(8,128)(2,1)S(1)}, bf16[256,1024]{1,0:T(8,128)(2,1)S(1)}, u32[]{:S(2)}, u32[]{:S(2)}) collective-permute-start(bf16[256,1024]{1,0:T(8,128)(2,1)S(1)} %collective-permute-done.8), channel_id=1, source_target_pairs={{0,2},{4,0},{8,4},{12,8},{14,12},{10,14},{6,10},{2,6},{1,3},{5,1},... | collective-permute-start | bytes 1572872 | tf_op jit(solution)/shard_map/ppermute | solution.py:50
  47.4 6.8 %collective-permute-start.9 = (bf16[256,512]{1,0:T(8,128)(2,1)S(1)}, bf16[256,512]{1,0:T(8,128)(2,1)S(1)}, u32[]{:S(2)}, u32[]{:S(2)}) collective-permute-start(bf16[256,512]{1,0:T(8,128)(2,1)S(1)} %constant_dynamic-slice_fusion.3), channel_id=1, source_target_pairs={{0,16},{16,0},{1,17},{17,1},{2,18},{18,2},{3,19},{19,3},{4,20},{20... | collective-permute-start | bytes 786440 | tf_op jit(solution)/shard_map/ppermute | solution.py:41
  53.9 10.5 %collective-permute-start.14 = (bf16[256,1024]{1,0:T(8,128)(2,1)S(1)}, bf16[256,1024]{1,0:T(8,128)(2,1)S(1)}, u32[]{:S(2)}, u32[]{:S(2)}) collective-permute-start(bf16[256,1024]{1,0:T(8,128)(2,1)S(1)} %collective-permute-done.10), channel_id=1, source_target_pairs={{0,4},{4,8},{8,12},{12,14},{14,10},{10,6},{6,2},{2,0},{1,5},{5,9},... | collective-permute-start | bytes 1572872 | tf_op jit(solution)/shard_map/ppermute | solution.py:47
  54.2 5.3 %collective-permute-start.11 = (bf16[256,512]{1,0:T(8,128)(2,1)S(1)}, bf16[256,512]{1,0:T(8,128)(2,1)S(1)}, u32[]{:S(2)}, u32[]{:S(2)}) collective-permute-start(bf16[256,512]{1,0:T(8,128)(2,1)S(1)} %constant_dynamic-slice_fusion.2), channel_id=1, source_target_pairs={{0,16},{16,0},{1,17},{17,1},{2,18},{18,2},{3,19},{19,3},{4,20},{20... | collective-permute-start | bytes 786440 | tf_op jit(solution)/shard_map/ppermute | solution.py:41
  55.3 10.4 %collective-permute-start.13 = (bf16[256,512]{1,0:T(8,128)(2,1)S(1)}, bf16[256,512]{1,0:T(8,128)(2,1)S(1)}, u32[]{:S(2)}, u32[]{:S(2)}) collective-permute-start(bf16[256,512]{1,0:T(8,128)(2,1)S(1)} %constant_dynamic-slice_fusion.1), channel_id=1, source_target_pairs={{0,16},{16,0},{1,17},{17,1},{2,18},{18,2},{3,19},{19,3},{4,20},{20... | collective-permute-start | bytes 786440 | tf_op jit(solution)/shard_map/ppermute | solution.py:41
  64.5 6.2 %collective-permute-start.15 = (bf16[256,512]{1,0:T(8,128)(2,1)S(1)}, bf16[256,512]{1,0:T(8,128)(2,1)S(1)}, u32[]{:S(2)}, u32[]{:S(2)}) collective-permute-start(bf16[256,512]{1,0:T(8,128)(2,1)S(1)} %constant_dynamic-slice_fusion), channel_id=1, source_target_pairs={{0,16},{16,0},{1,17},{17,1},{2,18},{18,2},{3,19},{19,3},{4,20},{20... | collective-permute-start | bytes 786440 | tf_op jit(solution)/shard_map/ppermute | solution.py:41
  79.1 10.5 %collective-permute-start.17 = (f32[4,128,128]{2,1,0:T(8,128)}, f32[4,128,128]{2,1,0:T(8,128)S(1)}, u32[]{:S(2)}, u32[]{:S(2)}) collective-permute-start(f32[4,128,128]{2,1,0:T(8,128)} %fusion.43), channel_id=1, source_target_pairs={{0,2},{2,4},{4,6},{6,8},{8,10},{10,12},{12,14},{1,3},{3,5},{5,7},{... | collective-permute-start | bytes 786440 | tf_op jit(solution)/shard_map/ppermute | solution.py:66
  89.7 7.1 %collective-permute-start.18 = (f32[4,128,128]{2,1,0:T(8,128)S(1)}, f32[4,128,128]{2,1,0:T(8,128)S(1)}, u32[]{:S(2)}, u32[]{:S(2)}) collective-permute-start(f32[4,128,128]{2,1,0:T(8,128)S(1)} %fusion.90), channel_id=1, source_target_pairs={{0,4},{2,6},{4,8},{6,10},{8,12},{10,14},{1,5},{3,7},{5,9},{7,11},{... | collective-permute-start | bytes 786440 | tf_op jit(solution)/shard_map/ppermute | solution.py:66
  96.9 9.4 %collective-permute-start.19 = (f32[4,128,128]{2,1,0:T(8,128)S(1)}, f32[4,128,128]{2,1,0:T(8,128)S(1)}, u32[]{:S(2)}, u32[]{:S(2)}) collective-permute-start(f32[4,128,128]{2,1,0:T(8,128)S(1)} %add.281), channel_id=1, source_target_pairs={{0,8},{2,10},{4,12},{6,14},{1,9},{3,11},{5,13},{7,15},{16,24},{18,... | collective-permute-start | bytes 786440 | tf_op jit(solution)/shard_map/ppermute | solution.py:66
  109.2 8.0 %collective-permute-start.21 = (f32[4,128,128]{2,1,0:T(8,128)S(1)}, f32[4,128,128]{2,1,0:T(8,128)S(1)}, u32[]{:S(2)}, u32[]{:S(2)}) collective-permute-start(f32[4,128,128]{2,1,0:T(8,128)S(1)} %fusion.44), channel_id=1, source_target_pairs={{2,0},{4,2},{6,4},{8,6},{10,8},{12,10},{14,12},{3,1},{5,3},{7,5},{... | collective-permute-start | bytes 786440 | tf_op jit(solution)/shard_map/ppermute | solution.py:66
  117.2 9.8 %collective-permute-start.22 = (f32[4,128,128]{2,1,0:T(8,128)S(1)}, f32[4,128,128]{2,1,0:T(8,128)S(1)}, u32[]{:S(2)}, u32[]{:S(2)}) collective-permute-start(f32[4,128,128]{2,1,0:T(8,128)S(1)} %fusion.89), channel_id=1, source_target_pairs={{4,0},{6,2},{8,4},{10,6},{12,8},{14,10},{5,1},{7,3},{9,5},{11,7},{... | collective-permute-start | bytes 786440 | tf_op jit(solution)/shard_map/ppermute | solution.py:66
  127.1 8.6 %collective-permute-start.23 = (f32[4,128,128]{2,1,0:T(8,128)S(1)}, f32[4,128,128]{2,1,0:T(8,128)S(1)}, u32[]{:S(2)}, u32[]{:S(2)}) collective-permute-start(f32[4,128,128]{2,1,0:T(8,128)S(1)} %add.293), channel_id=1, source_target_pairs={{8,0},{10,2},{12,4},{14,6},{9,1},{11,3},{13,5},{15,7},{24,16},{26,... | collective-permute-start | bytes 786440 | tf_op jit(solution)/shard_map/ppermute | solution.py:66
  137.0 19.9 %copy-start.1 = (bf16[1,256,4,128]{1,3,2,0:T(8,128)(2,1)S(1)}, bf16[1,256,4,128]{1,3,2,0:T(8,128)(2,1)}, u32[]{:S(2)}) copy-start(bf16[1,256,4,128]{1,3,2,0:T(8,128)(2,1)} %get-tuple-element.39) | copy-start | bytes 786436
  139.4 17.4 %copy-start.2 = (bf16[1,256,4,128]{1,3,2,0:T(8,128)(2,1)S(1)}, bf16[1,256,4,128]{1,3,2,0:T(8,128)(2,1)}, u32[]{:S(2)}) copy-start(bf16[1,256,4,128]{1,3,2,0:T(8,128)(2,1)} %get-tuple-element.38) | copy-start | bytes 786436
  143.3 19.6 %collective-permute-start.25 = (f32[256,2048]{1,0:T(8,128)}, f32[256,2048]{1,0:T(8,128)}, u32[]{:S(2)}, u32[]{:S(2)}) collective-permute-start(f32[256,2048]{1,0:T(8,128)} %add_add_fusion), channel_id=1, source_target_pairs={{0,1},{1,0},{2,3},{3,2},{4,5},{5,4},{6,7},{7,6},{8,9},{9,8},{10,11... | collective-permute-start | bytes 6291464 | tf_op jit(solution)/shard_map/ppermute | solution.py:17
  157.0 4.9 %collective-permute-start.24 = (bf16[256,512]{1,0:T(8,128)(2,1)S(1)}, bf16[256,512]{1,0:T(8,128)(2,1)S(1)}, u32[]{:S(2)}, u32[]{:S(2)}) collective-permute-start(bf16[256,512]{1,0:T(8,128)(2,1)S(1)} %copy.48), channel_id=1, source_target_pairs={{0,1},{1,0},{2,3},{3,2},{4,5},{5,4},{6,7},{7,6},{8,9},{9,8},{10,11... | collective-permute-start | bytes 786440 | tf_op jit(solution)/shard_map/ppermute | solution.py:17
  (1 other events, 7.1 us)

commit v19 on v18

--- a/solution.py
+++ b/solution.py
@@ -127,18 +127,18 @@
     query = jnp.dot(x_pair, w_qcols, preferred_element_type=f32).astype(bf16).reshape(2, tok, heads, DH)
 
     local = jnp.einsum("jthd,jthe->jhde", key, value, preferred_element_type=f32)
-    state0, _ = exclusive_scan(local[0] + local[1], chips, False)
+    pair_masks = jnp.stack([masks[0], swap(masks[0])])
+    allow = jax.vmap(dense_allow, in_axes=(0, None))(pair_masks, tok)
+    scores = jnp.einsum("jthd,jshd->jhts", query, key, preferred_element_type=f32)
+    attn = jnp.where(allow[:, None], scores, 0.0).astype(bf16)
+    intra = jnp.einsum("jhts,jshd->jthd", attn, value, preferred_element_type=f32)
+    state0, (_, intra) = exclusive_scan(local[0] + local[1], chips, False, ((), intra))
     state_mine = jnp.where(first, state0, state0 + local[1])
     state_other = jnp.where(first, state0 + local[0], state0)
     state_b = jnp.stack([state_mine, state_other]).astype(bf16)
 
-    pair_masks = jnp.stack([masks[0], swap(masks[0])])
-    allow = jax.vmap(dense_allow, in_axes=(0, None))(pair_masks, tok)
-
-    scores = jnp.einsum("jthd,jshd->jhts", query, key, preferred_element_type=f32)
-    attn = jnp.where(allow[:, None], scores, 0.0).astype(bf16)
-    mixed = jnp.einsum("jhts,jshd->jthd", attn, value, preferred_element_type=f32)
-    mixed = mixed + jnp.einsum("jthd,jhde->jthe", query, state_b, preferred_element_type=f32)
+
+    mixed = intra + jnp.einsum("jthd,jhde->jthe", query, state_b, preferred_element_type=f32)
     root = jnp.sqrt(jnp.mean(mixed * mixed, axis=-1, keepdims=True) + EPSILON)
     normed = mixed / root
 

time: 166 us -> 177 us (1.066)
  the two profiles are of different devices: /device:TPU:15 before, /device:TPU:0 now
where the time goes in v19:
time: 177 us; the launch traced here: 176 us
  waiting for transfers between devices  58.2 us (33%)
  starting transfers between devices  38.6 us (22%)
  matrix products  28.8 us (16%)
  local copies, waits for them, and re-layouts  26.7 us (15%)
  other arithmetic  13.1 us (7%)
  between operations  10.6 us (6%)
    ppermute x6, waiting for transfers between devices, exclusive_scan(): got = lax.ppermute(incl, 'chip', perm)  31.5 us
    ppermute x6, starting transfers between devices, exclusive_scan(): got = lax.ppermute(incl, 'chip', perm)  19.6 us
    ppermute x3, waiting for transfers between devices, ring_gather(): bwd = lax.ppermute(bwd, 'chip', behind)  17 us
    dot_general x4, matrix products, grad_rows(): g = g + lax.dot_general(d, w, dims, preferred_element_type=f32)  11 us
    ppermute x7, starting transfers between devices, land(): return (piece, lax.ppermute(sent, 'groups', partner))  8.66 us
    ppermute x7, waiting for transfers between devices, land(): return (piece, lax.ppermute(sent, 'groups', partner))  7.92 us
    ppermute x4, starting transfers between devices, ring_gather(): fwd = lax.ppermute(fwd, 'chip', ahead)  7.7 us
    dynamic_update_slice x8, local copies, waits for them, and re-layouts, on_device(): w_all = lax.dynamic_update_slice(w_all, ringed, (src * span, 0))  7.17 us
  transfers between devices with their start and end apart: 26, of which 14 were waited for; matrix products, arithmetic and copies ran while one was open for 19% of the time, Pallas kernels for 0%

profile of v19, /device:TPU:0, one launch (start us, length us, event | category | flops | bytes accessed | tf_op | source)
XLA Modules:
  0.0 176.1 jit_solution(14745873099557174641)
XLA Ops:
  4.3 1.6 collective-permute-done.1
  6.9 3.1 %broadcast_in_dim.33 = bf16[2048,1536]{1,0:T(8,128)(2,1)} broadcast(bf16[]{:T(256)} %constant.94.clone.1), dimensions={} | broadcast | bytes 6291458 | tf_op jit(solution)/shard_map/broadcast_in_dim | solution.py:115
  11.1 2.9 %collective-permute-start.2 = (bf16[256,1024]{1,0:T(8,128)(2,1)}, bf16[256,1024]{1,0:T(8,128)(2,1)S(1)}, u32[]{:S(2)}, u32[]{:S(2)}) collective-permute-start(bf16[256,1024]{1,0:T(8,128)(2,1)} %get-tuple-element.31), channel_id=1, source_target_pairs={{0,4},{4,8},{8,12},{12,14},{14,10},{10,6},{6,2},{2,0},{1,5},{5,9},... | collective-permute-start | bytes 1572872 | tf_op jit(solution)/shard_map/ppermute | solution.py:47
  27.6 2.0 %collective-permute-start.3 = (bf16[256,512]{1,0:T(8,128)(2,1)S(1)}, bf16[256,512]{1,0:T(8,128)(2,1)S(1)}, u32[]{:S(2)}, u32[]{:S(2)}) collective-permute-start(bf16[256,512]{1,0:T(8,128)(2,1)S(1)} %constant_dynamic-slice_fusion.6), channel_id=1, source_target_pairs={{0,16},{16,0},{1,17},{17,1},{2,18},{18,2},{3,19},{19,3},{4,20},{20... | collective-permute-start | bytes 786440 | tf_op jit(solution)/shard_map/ppermute | solution.py:41
  31.9 9.0 %collective-permute-done.4 = bf16[256,1024]{1,0:T(8,128)(2,1)S(1)} collective-permute-done((bf16[256,1024]{1,0:T(8,128)(2,1)}, bf16[256,1024]{1,0:T(8,128)(2,1)S(1)}, u32[]{:S(2)}, u32[]{:S(2)}) %collective-permute-start.4) | collective-permute-done | bytes 524320 | tf_op jit(solution)/shard_map/ppermute | solution.py:50
  40.9 1.6 collective-permute-start.5
  45.9 1.7 collective-permute-start.10
  47.6 2.3 %collective-permute-done.5 = bf16[256,512]{1,0:T(8,128)(2,1)S(1)} collective-permute-done((bf16[256,512]{1,0:T(8,128)(2,1)S(1)}, bf16[256,512]{1,0:T(8,128)(2,1)S(1)}, u32[]{:S(2)}, u32[]{:S(2)}) %collective-permute-start.5) | collective-permute-done | bytes 262176 | tf_op jit(solution)/shard_map/ppermute | solution.py:41
  50.6 4.6 %collective-permute-done.8 = bf16[256,1024]{1,0:T(8,128)(2,1)S(1)} collective-permute-done((bf16[256,1024]{1,0:T(8,128)(2,1)S(1)}, bf16[256,1024]{1,0:T(8,128)(2,1)S(1)}, u32[]{:S(2)}, u32[]{:S(2)}) %collective-permute-start.8) | collective-permute-done | bytes 524320 | tf_op jit(solution)/shard_map/ppermute | solution.py:50
  60.4 1.6 collective-permute-start.11
  63.8 3.5 %collective-permute-done.12 = bf16[256,1024]{1,0:T(8,128)(2,1)S(1)} collective-permute-done((bf16[256,1024]{1,0:T(8,128)(2,1)S(1)}, bf16[256,1024]{1,0:T(8,128)(2,1)S(1)}, u32[]{:S(2)}, u32[]{:S(2)}) %collective-permute-start.12) | collective-permute-done | bytes 524320 | tf_op jit(solution)/shard_map/ppermute | solution.py:50
  67.3 1.6 collective-permute-start.13
  72.4 3.3 %collective-permute-done.13 = bf16[256,512]{1,0:T(8,128)(2,1)S(1)} collective-permute-done((bf16[256,512]{1,0:T(8,128)(2,1)S(1)}, bf16[256,512]{1,0:T(8,128)(2,1)S(1)}, u32[]{:S(2)}, u32[]{:S(2)}) %collective-permute-start.13) | collective-permute-done | bytes 262176 | tf_op jit(solution)/shard_map/ppermute | solution.py:41
  79.2 3.5 %fusion.23 = bf16[512,512]{1,0:T(8,128)(2,1)S(1)} fusion(bf16[2048,1536]{1,0:T(8,128)(2,1)} %constant_dynamic-update-slice_fusion.9, s32[]{:T(128)S(6)} %select_n.228, bf16[256,2048]{1,0:T(8,128)(2,1)} %collective-permute-done, bf16[256,2048]{1,0:T(8,128)(2,1)} %add_convert_fusion.1), kind=kOutput, calls=%fused_computation.33 | convolution fusion | flops 1078198272 | bytes 4718596 | tf_op jit(solution)/shard_map/dot_general | solution.py:127
  83.1 5.2 %fusion.20 = bf16[512,1024]{1,0:T(8,128)(2,1)S(1)} fusion(bf16[2048,1536]{1,0:T(8,128)(2,1)} %constant_dynamic-update-slice_fusion.9, s32[]{:T(128)S(6)} %select_n.227, bf16[256,2048]{1,0:T(8,128)(2,1)} %collective-permute-done, bf16[256,2048]{1,0:T(8,128)(2,1)} %add_convert_fusion.1), kind=kOutput, calls=%fused_computation.23 | convolution fusion | flops 2152202240 | bytes 7340036 | tf_op jit(solution)/shard_map/dot_general | solution.py:123
  90.1 2.7 %collective-permute-start.17 = (f32[4,128,128]{2,1,0:T(8,128)S(1)}, f32[4,128,128]{2,1,0:T(8,128)S(1)}, u32[]{:S(2)}, u32[]{:S(2)}) collective-permute-start(f32[4,128,128]{2,1,0:T(8,128)S(1)} %fusion.41), channel_id=1, source_target_pairs={{0,2},{2,4},{4,6},{6,8},{8,10},{10,12},{12,14},{1,3},{3,5},{5,7},{... | collective-permute-start | bytes 786440 | tf_op jit(solution)/shard_map/ppermute | solution.py:66
  93.3 3.3 %collective-permute-done.17 = f32[4,128,128]{2,1,0:T(8,128)S(1)} collective-permute-done((f32[4,128,128]{2,1,0:T(8,128)S(1)}, f32[4,128,128]{2,1,0:T(8,128)S(1)}, u32[]{:S(2)}, u32[]{:S(2)}) %collective-permute-start.17) | collective-permute-done | bytes 262176 | tf_op jit(solution)/shard_map/ppermute | solution.py:66
  96.7 6.9 %collective-permute-start.18 = (f32[4,128,128]{2,1,0:T(8,128)S(1)}, f32[4,128,128]{2,1,0:T(8,128)S(1)}, u32[]{:S(2)}, u32[]{:S(2)}) collective-permute-start(f32[4,128,128]{2,1,0:T(8,128)S(1)} %fusion.88), channel_id=1, source_target_pairs={{0,4},{2,6},{4,8},{6,10},{8,12},{10,14},{1,5},{3,7},{5,9},{7,11},{... | collective-permute-start | bytes 786440 | tf_op jit(solution)/shard_map/ppermute | solution.py:66
  104.1 3.5 %collective-permute-done.18 = f32[4,128,128]{2,1,0:T(8,128)S(1)} collective-permute-done((f32[4,128,128]{2,1,0:T(8,128)S(1)}, f32[4,128,128]{2,1,0:T(8,128)S(1)}, u32[]{:S(2)}, u32[]{:S(2)}) %collective-permute-start.18) | collective-permute-done | bytes 262176 | tf_op jit(solution)/shard_map/ppermute | solution.py:66
  108.4 6.1 %collective-permute-start.19 = (f32[4,128,128]{2,1,0:T(8,128)}, f32[4,128,128]{2,1,0:T(8,128)}, u32[]{:S(2)}, u32[]{:S(2)}) collective-permute-start(f32[4,128,128]{2,1,0:T(8,128)} %add.278), channel_id=1, source_target_pairs={{0,8},{2,10},{4,12},{6,14},{1,9},{3,11},{5,13},{7,15},{16,24},{18,... | collective-permute-start | bytes 786440 | tf_op jit(solution)/shard_map/ppermute | solution.py:66
  114.4 2.0 %copy.63 = bf16[256,1024]{0,1:T(8,128)(2,1)} copy(bf16[256,1024]{1,0:T(8,128)(2,1)} %param.11) | data formatting | bytes 1048576 | tf_op jit(solution)/shard_map/reshape | solution.py:146
  116.5 1.8 broadcast_select_fusion
  125.9 2.4 %fusion.16 = f32[256,2048]{1,0:T(8,128)S(1)} fusion(bf16[256,512]{0,1:T(8,128)(2,1)S(1)} %bitcast.133, bf16[2048,1536]{1,0:T(8,128)(2,1)} %constant_dynamic-update-slice_fusion.9, s32[]{:T(128)S(6)} %select_n.228), kind=kOutput, calls=%fused_computation.19 | convolution fusion | flops 536870912 | bytes 4456452 | tf_op jit(solution)/shard_map/dot_general | solution.py:160
  128.3 6.8 %collective-permute-done.21 = f32[4,128,128]{2,1,0:T(8,128)S(1)} collective-permute-done((f32[4,128,128]{2,1,0:T(8,128)S(1)}, f32[4,128,128]{2,1,0:T(8,128)S(1)}, u32[]{:S(2)}, u32[]{:S(2)}) %collective-permute-start.21) | collective-permute-done | bytes 262176 | tf_op jit(solution)/shard_map/ppermute | solution.py:66
  136.4 2.4 %fusion.14 = f32[256,2048]{1,0:T(8,128)S(1)} fusion(bf16[256,512]{0,1:T(8,128)(2,1)S(1)} %bitcast.131, bf16[2048,1536]{1,0:T(8,128)(2,1)} %constant_dynamic-update-slice_fusion.9, s32[]{:T(128)S(6)} %select_n.228), kind=kOutput, calls=%fused_computation.17 | convolution fusion | flops 536870912 | bytes 4456452 | tf_op jit(solution)/shard_map/dot_general | solution.py:160
  138.8 6.0 %collective-permute-done.22 = f32[4,128,128]{2,1,0:T(8,128)S(1)} collective-permute-done((f32[4,128,128]{2,1,0:T(8,128)S(1)}, f32[4,128,128]{2,1,0:T(8,128)S(1)}, u32[]{:S(2)}, u32[]{:S(2)}) %collective-permute-start.22) | collective-permute-done | bytes 262176 | tf_op jit(solution)/shard_map/ppermute | solution.py:66
  147.2 11.9 %collective-permute-done.23 = f32[4,128,128]{2,1,0:T(8,128)S(1)} collective-permute-done((f32[4,128,128]{2,1,0:T(8,128)S(1)}, f32[4,128,128]{2,1,0:T(8,128)S(1)}, u32[]{:S(2)}, u32[]{:S(2)}) %collective-permute-start.23) | collective-permute-done | bytes 262176 | tf_op jit(solution)/shard_map/ppermute | solution.py:66
  160.4 2.4 %fusion.10 = f32[256,2048]{1,0:T(8,128)S(1)} fusion(bf16[256,512]{0,1:T(8,128)(2,1)S(1)} %bitcast.132, bf16[2048,1536]{1,0:T(8,128)(2,1)} %constant_dynamic-update-slice_fusion.9, s32[]{:T(128)S(6)} %select_n.227), kind=kOutput, calls=%fused_computation.13 | convolution fusion | flops 536870912 | bytes 4456452 | tf_op jit(solution)/shard_map/dot_general | solution.py:187
  162.8 3.9 %add_add_fusion = f32[256,2048]{1,0:T(8,128)} fusion(f32[256,2048]{1,0:T(8,128)S(1)} %fusion.14, f32[256,2048]{1,0:T(8,128)S(1)} %fusion.10, bf16[256,512]{0,1:T(8,128)(2,1)S(1)} %bitcast.134, bf16[2048,1536]{1,0:T(8,128)(2,1)} %constant_dynamic-update-slice_fusion.9, s32[]{:T(128)S(6)} %select_n.242), kind=kOutput, calls=%fused_computation.4 | convolution fusion | flops 537919488 | bytes 8650756 | tf_op jit(solution)/shard_map/dot_general | solution.py:187
  167.5 2.3 %fusion.12 = f32[256,2048]{1,0:T(8,128)S(1)} fusion(bf16[256,512]{0,1:T(8,128)(2,1)S(1)} %bitcast.129, bf16[2048,1536]{1,0:T(8,128)(2,1)} %constant_dynamic-update-slice_fusion.9, s32[]{:T(128)S(6)} %select_n.227), kind=kOutput, calls=%fused_computation.15 | convolution fusion | flops 536870912 | bytes 4456452 | tf_op jit(solution)/shard_map/dot_general | solution.py:187
  169.9 2.4 %add_add_fusion.1 = f32[256,2048]{1,0:T(8,128)S(1)} fusion(f32[256,2048]{1,0:T(8,128)S(1)} %fusion.16, f32[256,2048]{1,0:T(8,128)S(1)} %fusion.12, bf16[256,512]{0,1:T(8,128)(2,1)S(1)} %bitcast.130, bf16[2048,1536]{1,0:T(8,128)(2,1)} %constant_dynamic-update-slice_fusion.9, s32[]{:T(128)S(6)} %select_n.242), kind=kOutput, calls=%fused_computation.5 | convolution fusion | flops 537919488 | bytes 8650756 | tf_op jit(solution)/shard_map/dot_general | solution.py:187
  173.3 2.8 %add_convert_fusion = bf16[256,2048]{1,0:T(8,128)(2,1)} fusion(f32[256,2048]{1,0:T(8,128)S(1)} %add_add_fusion.1, f32[256,2048]{1,0:T(8,128)} %collective-permute-done.25), kind=kLoop, calls=%fused_computation.3 | loop fusion | flops 1048576 | bytes 5242880 | tf_op jit(solution)/shard_map/convert_element_type | solution.py:192
  (129 shorter events, 48.8 us)
Async XLA Ops:
  0.6 13.4 %copy-start.2 = (bf16[256,2048]{1,0:T(8,128)(2,1)S(1)}, bf16[256,2048]{1,0:T(8,128)(2,1)}, u32[]{:S(2)}) copy-start(bf16[256,2048]{1,0:T(8,128)(2,1)} %param.10) | copy-start | bytes 3145732
  0.6 13.4 %copy-start.3 = (bf16[256,2048]{1,0:T(8,128)(2,1)S(1)}, bf16[256,2048]{1,0:T(8,128)(2,1)}, u32[]{:S(2)}) copy-start(bf16[256,2048]{1,0:T(8,128)(2,1)} %param.9) | copy-start | bytes 3145732
  3.7 2.1 %collective-permute-start.1 = (bf16[128,1536]{1,0:T(8,128)(2,1)}, bf16[128,1536]{1,0:T(8,128)(2,1)}, u32[]{:S(2)}, u32[]{:S(2)}) collective-permute-start(bf16[128,1536]{1,0:T(8,128)(2,1)} %pad_maximum_fusion.6), channel_id=1, source_target_pairs={{0,1},{1,0},{2,3},{3,2},{4,5},{5,4},{6,7},{7,6},{8,9},{9,8},{10,11... | collective-permute-start | bytes 1179656 | tf_op jit(solution)/shard_map/ppermute | solution.py:17
  4.2 11.7 %copy-start.9 = (s32[8]{0:T(128)S(1)}, s32[8]{0:T(128)}, u32[]{:S(2)}) copy-start(s32[8]{0:T(128)} %constant.120.clone) | copy-start | bytes 100
  4.2 17.3 %copy-start.7 = (s32[8]{0:T(128)S(1)}, s32[8]{0:T(128)}, u32[]{:S(2)}) copy-start(s32[8]{0:T(128)} %constant.119.clone) | copy-start | bytes 100
  11.1 16.4 %collective-permute-start.2 = (bf16[256,1024]{1,0:T(8,128)(2,1)}, bf16[256,1024]{1,0:T(8,128)(2,1)S(1)}, u32[]{:S(2)}, u32[]{:S(2)}) collective-permute-start(bf16[256,1024]{1,0:T(8,128)(2,1)} %get-tuple-element.31), channel_id=1, source_target_pairs={{0,4},{4,8},{8,12},{12,14},{14,10},{10,6},{6,2},{2,0},{1,5},{5,9},... | collective-permute-start | bytes 1572872 | tf_op jit(solution)/shard_map/ppermute | solution.py:47
  15.4 63.8 %collective-permute-start = (bf16[256,2048]{1,0:T(8,128)(2,1)}, bf16[256,2048]{1,0:T(8,128)(2,1)}, u32[]{:S(2)}, u32[]{:S(2)}) collective-permute-start(bf16[256,2048]{1,0:T(8,128)(2,1)} %add_convert_fusion.1), channel_id=1, source_target_pairs={{0,1},{1,0},{2,3},{3,2},{4,5},{5,4},{6,7},{7,6},{8,9},{9,8},{10,11... | collective-permute-start | bytes 3145736 | tf_op jit(solution)/shard_map/ppermute | solution.py:17
  15.4 11.4 %collective-permute-start.16 = (s32[2,2]{1,0:T(2,128)S(1)}, s32[2,2]{1,0:T(2,128)S(1)}, u32[]{:S(2)}, u32[]{:S(2)}) collective-permute-start(s32[2,2]{1,0:T(2,128)S(1)} %bitcast.137), channel_id=1, source_target_pairs={{0,1},{1,0},{2,3},{3,2},{4,5},{5,4},{6,7},{7,6},{8,9},{9,8},{10,11... | collective-permute-start | bytes 56 | tf_op jit(solution)/shard_map/ppermute | solution.py:17
  26.8 14.1 %collective-permute-start.4 = (bf16[256,1024]{1,0:T(8,128)(2,1)}, bf16[256,1024]{1,0:T(8,128)(2,1)S(1)}, u32[]{:S(2)}, u32[]{:S(2)}) collective-permute-start(bf16[256,1024]{1,0:T(8,128)(2,1)} %get-tuple-element.31), channel_id=1, source_target_pairs={{0,2},{4,0},{8,4},{12,8},{14,12},{10,14},{6,10},{2,6},{1,3},{5,1},... | collective-permute-start | bytes 1572872 | tf_op jit(solution)/shard_map/ppermute | solution.py:50
  27.6 16.3 %collective-permute-start.3 = (bf16[256,512]{1,0:T(8,128)(2,1)S(1)}, bf16[256,512]{1,0:T(8,128)(2,1)S(1)}, u32[]{:S(2)}, u32[]{:S(2)}) collective-permute-start(bf16[256,512]{1,0:T(8,128)(2,1)S(1)} %constant_dynamic-slice_fusion.6), channel_id=1, source_target_pairs={{0,16},{16,0},{1,17},{17,1},{2,18},{18,2},{3,19},{19,3},{4,20},{20... | collective-permute-start | bytes 786440 | tf_op jit(solution)/shard_map/ppermute | solution.py:41
  29.6 15.9 %collective-permute-start.6 = (bf16[256,1024]{1,0:T(8,128)(2,1)S(1)}, bf16[256,1024]{1,0:T(8,128)(2,1)S(1)}, u32[]{:S(2)}, u32[]{:S(2)}) collective-permute-start(bf16[256,1024]{1,0:T(8,128)(2,1)S(1)} %collective-permute-done.2), channel_id=1, source_target_pairs={{0,4},{4,8},{8,12},{12,14},{14,10},{10,6},{6,2},{2,0},{1,5},{5,9},... | collective-permute-start | bytes 1572872 | tf_op jit(solution)/shard_map/ppermute | solution.py:47
  40.9 9.0 %collective-permute-start.5 = (bf16[256,512]{1,0:T(8,128)(2,1)S(1)}, bf16[256,512]{1,0:T(8,128)(2,1)S(1)}, u32[]{:S(2)}, u32[]{:S(2)}) collective-permute-start(bf16[256,512]{1,0:T(8,128)(2,1)S(1)} %constant_dynamic-slice_fusion.5), channel_id=1, source_target_pairs={{0,16},{16,0},{1,17},{17,1},{2,18},{18,2},{3,19},{19,3},{4,20},{20... | collective-permute-start | bytes 786440 | tf_op jit(solution)/shard_map/ppermute | solution.py:41
  42.5 12.7 %collective-permute-start.8 = (bf16[256,1024]{1,0:T(8,128)(2,1)S(1)}, bf16[256,1024]{1,0:T(8,128)(2,1)S(1)}, u32[]{:S(2)}, u32[]{:S(2)}) collective-permute-start(bf16[256,1024]{1,0:T(8,128)(2,1)S(1)} %collective-permute-done.4), channel_id=1, source_target_pairs={{0,2},{4,0},{8,4},{12,8},{14,12},{10,14},{6,10},{2,6},{1,3},{5,1},... | collective-permute-start | bytes 1572872 | tf_op jit(solution)/shard_map/ppermute | solution.py:50
  45.5 11.8 %collective-permute-start.7 = (bf16[256,512]{1,0:T(8,128)(2,1)S(1)}, bf16[256,512]{1,0:T(8,128)(2,1)S(1)}, u32[]{:S(2)}, u32[]{:S(2)}) collective-permute-start(bf16[256,512]{1,0:T(8,128)(2,1)S(1)} %constant_dynamic-slice_fusion.4), channel_id=1, source_target_pairs={{0,16},{16,0},{1,17},{17,1},{2,18},{18,2},{3,19},{19,3},{4,20},{20... | collective-permute-start | bytes 786440 | tf_op jit(solution)/shard_map/ppermute | solution.py:41
  45.9 12.9 %collective-permute-start.10 = (bf16[256,1024]{1,0:T(8,128)(2,1)S(1)}, bf16[256,1024]{1,0:T(8,128)(2,1)S(1)}, u32[]{:S(2)}, u32[]{:S(2)}) collective-permute-start(bf16[256,1024]{1,0:T(8,128)(2,1)S(1)} %collective-permute-done.6), channel_id=1, source_target_pairs={{0,4},{4,8},{8,12},{12,14},{14,10},{10,6},{6,2},{2,0},{1,5},{5,9},... | collective-permute-start | bytes 1572872 | tf_op jit(solution)/shard_map/ppermute | solution.py:47
  55.2 7.9 %collective-permute-start.9 = (bf16[256,512]{1,0:T(8,128)(2,1)S(1)}, bf16[256,512]{1,0:T(8,128)(2,1)S(1)}, u32[]{:S(2)}, u32[]{:S(2)}) collective-permute-start(bf16[256,512]{1,0:T(8,128)(2,1)S(1)} %constant_dynamic-slice_fusion.3), channel_id=1, source_target_pairs={{0,16},{16,0},{1,17},{17,1},{2,18},{18,2},{3,19},{19,3},{4,20},{20... | collective-permute-start | bytes 786440 | tf_op jit(solution)/shard_map/ppermute | solution.py:41
  55.8 11.5 %collective-permute-start.12 = (bf16[256,1024]{1,0:T(8,128)(2,1)S(1)}, bf16[256,1024]{1,0:T(8,128)(2,1)S(1)}, u32[]{:S(2)}, u32[]{:S(2)}) collective-permute-start(bf16[256,1024]{1,0:T(8,128)(2,1)S(1)} %collective-permute-done.8), channel_id=1, source_target_pairs={{0,2},{4,0},{8,4},{12,8},{14,12},{10,14},{6,10},{2,6},{1,3},{5,1},... | collective-permute-start | bytes 1572872 | tf_op jit(solution)/shard_map/ppermute | solution.py:50
  58.8 11.7 %collective-permute-start.14 = (bf16[256,1024]{1,0:T(8,128)(2,1)S(1)}, bf16[256,1024]{1,0:T(8,128)(2,1)S(1)}, u32[]{:S(2)}, u32[]{:S(2)}) collective-permute-start(bf16[256,1024]{1,0:T(8,128)(2,1)S(1)} %collective-permute-done.10), channel_id=1, source_target_pairs={{0,4},{4,8},{8,12},{12,14},{14,10},{10,6},{6,2},{2,0},{1,5},{5,9},... | collective-permute-start | bytes 1572872 | tf_op jit(solution)/shard_map/ppermute | solution.py:47
  60.4 9.4 %collective-permute-start.11 = (bf16[256,512]{1,0:T(8,128)(2,1)S(1)}, bf16[256,512]{1,0:T(8,128)(2,1)S(1)}, u32[]{:S(2)}, u32[]{:S(2)}) collective-permute-start(bf16[256,512]{1,0:T(8,128)(2,1)S(1)} %constant_dynamic-slice_fusion.2), channel_id=1, source_target_pairs={{0,16},{16,0},{1,17},{17,1},{2,18},{18,2},{3,19},{19,3},{4,20},{20... | collective-permute-start | bytes 786440 | tf_op jit(solution)/shard_map/ppermute | solution.py:41
  67.3 8.4 %collective-permute-start.13 = (bf16[256,512]{1,0:T(8,128)(2,1)S(1)}, bf16[256,512]{1,0:T(8,128)(2,1)S(1)}, u32[]{:S(2)}, u32[]{:S(2)}) collective-permute-start(bf16[256,512]{1,0:T(8,128)(2,1)S(1)} %constant_dynamic-slice_fusion.1), channel_id=1, source_target_pairs={{0,16},{16,0},{1,17},{17,1},{2,18},{18,2},{3,19},{19,3},{4,20},{20... | collective-permute-start | bytes 786440 | tf_op jit(solution)/shard_map/ppermute | solution.py:41
  70.5 8.0 %collective-permute-start.15 = (bf16[256,512]{1,0:T(8,128)(2,1)S(1)}, bf16[256,512]{1,0:T(8,128)(2,1)S(1)}, u32[]{:S(2)}, u32[]{:S(2)}) collective-permute-start(bf16[256,512]{1,0:T(8,128)(2,1)S(1)} %constant_dynamic-slice_fusion), channel_id=1, source_target_pairs={{0,16},{16,0},{1,17},{17,1},{2,18},{18,2},{3,19},{19,3},{4,20},{20... | collective-permute-start | bytes 786440 | tf_op jit(solution)/shard_map/ppermute | solution.py:41
  90.1 6.5 %collective-permute-start.17 = (f32[4,128,128]{2,1,0:T(8,128)S(1)}, f32[4,128,128]{2,1,0:T(8,128)S(1)}, u32[]{:S(2)}, u32[]{:S(2)}) collective-permute-start(f32[4,128,128]{2,1,0:T(8,128)S(1)} %fusion.41), channel_id=1, source_target_pairs={{0,2},{2,4},{4,6},{6,8},{8,10},{10,12},{12,14},{1,3},{3,5},{5,7},{... | collective-permute-start | bytes 786440 | tf_op jit(solution)/shard_map/ppermute | solution.py:66
  96.7 11.7 %copy-start.6 = (f32[4,128,128]{2,1,0:T(8,128)}, f32[4,128,128]{2,1,0:T(8,128)S(1)}, u32[]{:S(2)}) copy-start(f32[4,128,128]{2,1,0:T(8,128)S(1)} %collective-permute-done.17) | copy-start | bytes 786436
  96.7 10.8 %collective-permute-start.18 = (f32[4,128,128]{2,1,0:T(8,128)S(1)}, f32[4,128,128]{2,1,0:T(8,128)S(1)}, u32[]{:S(2)}, u32[]{:S(2)}) collective-permute-start(f32[4,128,128]{2,1,0:T(8,128)S(1)} %fusion.88), channel_id=1, source_target_pairs={{0,4},{2,6},{4,8},{6,10},{8,12},{10,14},{1,5},{3,7},{5,9},{7,11},{... | collective-permute-start | bytes 786440 | tf_op jit(solution)/shard_map/ppermute | solution.py:66
  108.4 9.9 %collective-permute-start.19 = (f32[4,128,128]{2,1,0:T(8,128)}, f32[4,128,128]{2,1,0:T(8,128)}, u32[]{:S(2)}, u32[]{:S(2)}) collective-permute-start(f32[4,128,128]{2,1,0:T(8,128)} %add.278), channel_id=1, source_target_pairs={{0,8},{2,10},{4,12},{6,14},{1,9},{3,11},{5,13},{7,15},{16,24},{18,... | collective-permute-start | bytes 786440 | tf_op jit(solution)/shard_map/ppermute | solution.py:66
  118.2 1.9 %collective-permute-start.20 = (bf16[256,512]{0,1:T(8,128)(2,1)}, bf16[256,512]{0,1:T(8,128)(2,1)}, u32[]{:S(2)}, u32[]{:S(2)}) collective-permute-start(bf16[256,512]{0,1:T(8,128)(2,1)} %get-tuple-element.49), channel_id=1, source_target_pairs={{0,1},{1,0},{2,3},{3,2},{4,5},{5,4},{6,7},{7,6},{8,9},{9,8},{10,11... | collective-permute-start | bytes 786440 | tf_op jit(solution)/shard_map/ppermute | solution.py:17
  124.4 21.8 %copy-start.1 = (bf16[2,4,256,256]{3,2,1,0:T(8,128)(2,1)S(1)}, bf16[2,4,256,256]{3,2,1,0:T(8,128)(2,1)}, u32[]{:S(2)}) copy-start(bf16[2,4,256,256]{3,2,1,0:T(8,128)(2,1)} %copy-done) | copy-start | bytes 3145732
  124.5 10.6 %collective-permute-start.21 = (f32[4,128,128]{2,1,0:T(8,128)S(1)}, f32[4,128,128]{2,1,0:T(8,128)S(1)}, u32[]{:S(2)}, u32[]{:S(2)}) collective-permute-start(f32[4,128,128]{2,1,0:T(8,128)S(1)} %fusion.42), channel_id=1, source_target_pairs={{2,0},{4,2},{6,4},{8,6},{10,8},{12,10},{14,12},{3,1},{5,3},{7,5},{... | collective-permute-start | bytes 786440 | tf_op jit(solution)/shard_map/ppermute | solution.py:66
  135.1 9.7 %collective-permute-start.22 = (f32[4,128,128]{2,1,0:T(8,128)S(1)}, f32[4,128,128]{2,1,0:T(8,128)S(1)}, u32[]{:S(2)}, u32[]{:S(2)}) collective-permute-start(f32[4,128,128]{2,1,0:T(8,128)S(1)} %fusion.87), channel_id=1, source_target_pairs={{4,0},{6,2},{8,4},{10,6},{12,8},{14,10},{5,1},{7,3},{9,5},{11,7},{... | collective-permute-start | bytes 786440 | tf_op jit(solution)/shard_map/ppermute | solution.py:66
  144.8 14.3 %collective-permute-start.23 = (f32[4,128,128]{2,1,0:T(8,128)S(1)}, f32[4,128,128]{2,1,0:T(8,128)S(1)}, u32[]{:S(2)}, u32[]{:S(2)}) collective-permute-start(f32[4,128,128]{2,1,0:T(8,128)S(1)} %add.289), channel_id=1, source_target_pairs={{8,0},{10,2},{12,4},{14,6},{9,1},{11,3},{13,5},{15,7},{24,16},{26,... | collective-permute-start | bytes 786440 | tf_op jit(solution)/shard_map/ppermute | solution.py:66
  166.6 6.6 %collective-permute-start.25 = (f32[256,2048]{1,0:T(8,128)}, f32[256,2048]{1,0:T(8,128)}, u32[]{:S(2)}, u32[]{:S(2)}) collective-permute-start(f32[256,2048]{1,0:T(8,128)} %add_add_fusion), channel_id=1, source_target_pairs={{0,1},{1,0},{2,3},{3,2},{4,5},{5,4},{6,7},{7,6},{8,9},{9,8},{10,11... | collective-permute-start | bytes 6291464 | tf_op jit(solution)/shard_map/ppermute | solution.py:17
  166.9 5.4 %collective-permute-start.24 = (bf16[256,512]{1,0:T(8,128)(2,1)S(1)}, bf16[256,512]{1,0:T(8,128)(2,1)S(1)}, u32[]{:S(2)}, u32[]{:S(2)}) collective-permute-start(bf16[256,512]{1,0:T(8,128)(2,1)S(1)} %copy.48), channel_id=1, source_target_pairs={{0,1},{1,0},{2,3},{3,2},{4,5},{5,4},{6,7},{7,6},{8,9},{9,8},{10,11... | collective-permute-start | bytes 786440 | tf_op jit(solution)/shard_map/ppermute | solution.py:17
  (4 other events, 34.3 us)

commit v20 on v18

--- a/solution.py
+++ b/solution.py
@@ -180,14 +180,16 @@
     dk_b = d_key.astype(bf16).reshape(2, tok, half)
     dv_b = d_value.astype(bf16).reshape(2, tok, half)
 
-    def grad_rows(j):
-        g = grad_q[j]
+    def grad_rows(j, lo=0, hi=tok):
+        g = grad_q[j][lo:hi]
         for d, at in ((dk_b[j], at_k), (dv_b[j], at_v)):
             w = lax.dynamic_slice_in_dim(w_all, at, share, axis=1)
-            g = g + lax.dot_general(d, w, dims, preferred_element_type=f32)
+            g = g + lax.dot_general(d[lo:hi], w, dims, preferred_element_type=f32)
         return g
 
-    received = swap(grad_rows(1))
+    first_part = swap(grad_rows(1, 0, tok // 2))
+    second_part = swap(grad_rows(1, tok // 2, tok))
+    received = jnp.concatenate([first_part, second_part], axis=0)
     own, received = lax.optimization_barrier((grad_rows(0), received))
     grad_input = (own + received).astype(bf16)
     return (output, grad_input)

time: 166 us -> 175 us (1.054)
  matrix products: 28.9 us -> 34.4 us
  local copies, waits for them, and re-layouts: 25.7 us -> 28.1 us
    dot_general x4 -> x6, matrix products: 11.1 us -> 16.6 us  [grad_rows(): g = g + lax.dot_general(d[lo:hi], w, dims, preferred_element_type=f32)]
    ppermute x6 -> x7, starting transfers between devices: 15.3 us -> 15.4 us  [swap(): return lax.ppermute(x, 'core', [(0, 1), (1, 0)])]
  transfers between devices with their start and end apart: 26 -> 27, of which waited for: 12 -> 12; matrix products, arithmetic and copies ran while one was open for 31% -> 34% of each run, Pallas kernels for 0% -> 0%
where the time goes in v20:
time: 175 us; the launch traced here: 174 us
  waiting for transfers between devices  47.3 us (27%)
  starting transfers between devices  41.8 us (24%)
  matrix products  34.4 us (20%)
  local copies, waits for them, and re-layouts  28.1 us (16%)
  other arithmetic  12.3 us (7%)
  between operations  10.2 us (6%)
    ppermute x6, waiting for transfers between devices, exclusive_scan(): got = lax.ppermute(incl, 'chip', perm)  24.3 us
    ppermute x6, starting transfers between devices, exclusive_scan(): got = lax.ppermute(incl, 'chip', perm)  16.8 us
    dot_general x6, matrix products, grad_rows(): g = g + lax.dot_general(d[lo:hi], w, dims, preferred_element_type=f32)  16.6 us
    ppermute x7, starting transfers between devices, swap(): return lax.ppermute(x, 'core', [(0, 1), (1, 0)])  15.4 us
    ppermute x4, waiting for transfers between devices, ring_gather(): fwd = lax.ppermute(fwd, 'chip', ahead)  11.7 us
    ppermute x7, waiting for transfers between devices, land(): return (piece, lax.ppermute(sent, 'groups', partner))  11.3 us
    dynamic_update_slice x8, local copies, waits for them, and re-layouts, on_device(): w_all = lax.dynamic_update_slice(w_all, ringed, (src * span, 0))  7.09 us
    dynamic_update_slice x8, local copies, waits for them, and re-layouts, on_device(): w_all = lax.dynamic_update_slice(w_all, swapped, (src * span, width))  6.03 us
  transfers between devices with their start and end apart: 27, of which 12 were waited for; matrix products, arithmetic and copies ran while one was open for 34% of the time, Pallas kernels for 0%

profile of v20, /device:TPU:15, one launch (start us, length us, event | category | flops | bytes accessed | tf_op | source)
XLA Modules:
  0.0 174.0 jit_solution(5344429158917148882)
XLA Ops:
  7.5 3.1 %broadcast_in_dim.33 = bf16[2048,1536]{1,0:T(8,128)(2,1)} broadcast(bf16[]{:T(256)} %constant.94.clone.1), dimensions={} | broadcast | bytes 6291458 | tf_op jit(solution)/shard_map/broadcast_in_dim | solution.py:115
  13.2 2.6 %add_convert_fusion.1 = bf16[256,2048]{1,0:T(8,128)(2,1)} fusion(bf16[256,2048]{1,0:T(8,128)(2,1)S(1)} %copy-done, bf16[256,2048]{1,0:T(8,128)(2,1)} %param.9), kind=kLoop, calls=%fused_computation.8 | loop fusion | flops 2097152 | bytes 3145728 | tf_op jit(solution)/shard_map/convert_element_type | solution.py:97
  31.7 4.1 %collective-permute-done.3 = bf16[256,512]{1,0:T(8,128)(2,1)S(1)} collective-permute-done((bf16[256,512]{1,0:T(8,128)(2,1)S(1)}, bf16[256,512]{1,0:T(8,128)(2,1)S(1)}, u32[]{:S(2)}, u32[]{:S(2)}) %collective-permute-start.3) | collective-permute-done | bytes 262176 | tf_op jit(solution)/shard_map/ppermute | solution.py:41
  37.5 3.7 %collective-permute-done.6 = bf16[256,1024]{1,0:T(8,128)(2,1)S(1)} collective-permute-done((bf16[256,1024]{1,0:T(8,128)(2,1)S(1)}, bf16[256,1024]{1,0:T(8,128)(2,1)S(1)}, u32[]{:S(2)}, u32[]{:S(2)}) %collective-permute-start.6) | collective-permute-done | bytes 524320 | tf_op jit(solution)/shard_map/ppermute | solution.py:47
  45.7 1.8 %collective-permute-done.7 = bf16[256,512]{1,0:T(8,128)(2,1)S(1)} collective-permute-done((bf16[256,512]{1,0:T(8,128)(2,1)S(1)}, bf16[256,512]{1,0:T(8,128)(2,1)S(1)}, u32[]{:S(2)}, u32[]{:S(2)}) %collective-permute-start.7) | collective-permute-done | bytes 262176 | tf_op jit(solution)/shard_map/ppermute | solution.py:41
  50.3 3.7 %collective-permute-done.10 = bf16[256,1024]{1,0:T(8,128)(2,1)S(1)} collective-permute-done((bf16[256,1024]{1,0:T(8,128)(2,1)S(1)}, bf16[256,1024]{1,0:T(8,128)(2,1)S(1)}, u32[]{:S(2)}, u32[]{:S(2)}) %collective-permute-start.10) | collective-permute-done | bytes 524320 | tf_op jit(solution)/shard_map/ppermute | solution.py:47
  57.5 2.0 %collective-permute-done.11 = bf16[256,512]{1,0:T(8,128)(2,1)S(1)} collective-permute-done((bf16[256,512]{1,0:T(8,128)(2,1)S(1)}, bf16[256,512]{1,0:T(8,128)(2,1)S(1)}, u32[]{:S(2)}, u32[]{:S(2)}) %collective-permute-start.11) | collective-permute-done | bytes 262176 | tf_op jit(solution)/shard_map/ppermute | solution.py:41
  60.3 4.3 %collective-permute-done.14 = bf16[256,1024]{1,0:T(8,128)(2,1)S(1)} collective-permute-done((bf16[256,1024]{1,0:T(8,128)(2,1)S(1)}, bf16[256,1024]{1,0:T(8,128)(2,1)S(1)}, u32[]{:S(2)}, u32[]{:S(2)}) %collective-permute-start.14) | collective-permute-done | bytes 524320 | tf_op jit(solution)/shard_map/ppermute | solution.py:47
  67.4 3.4 %collective-permute-done.15 = bf16[256,512]{1,0:T(8,128)(2,1)S(1)} collective-permute-done((bf16[256,512]{1,0:T(8,128)(2,1)S(1)}, bf16[256,512]{1,0:T(8,128)(2,1)S(1)}, u32[]{:S(2)}, u32[]{:S(2)}) %collective-permute-start.15) | collective-permute-done | bytes 262176 | tf_op jit(solution)/shard_map/ppermute | solution.py:41
  71.5 5.2 %fusion.22 = bf16[512,1024]{1,0:T(8,128)(2,1)S(1)} fusion(bf16[2048,1536]{1,0:T(8,128)(2,1)} %constant_dynamic-update-slice_fusion.9, s32[]{:T(128)S(6)} %select_n.229, bf16[256,2048]{1,0:T(8,128)(2,1)} %collective-permute-done, bf16[256,2048]{1,0:T(8,128)(2,1)} %add_convert_fusion.1), kind=kOutput, calls=%fused_computation.27 | convolution fusion | flops 2152202240 | bytes 7340036 | tf_op jit(solution)/shard_map/dot_general | solution.py:123
  79.2 5.1 %collective-permute-start.17 = (f32[4,128,128]{2,1,0:T(8,128)}, f32[4,128,128]{2,1,0:T(8,128)S(1)}, u32[]{:S(2)}, u32[]{:S(2)}) collective-permute-start(f32[4,128,128]{2,1,0:T(8,128)} %fusion.45), channel_id=1, source_target_pairs={{0,2},{2,4},{4,6},{6,8},{8,10},{10,12},{12,14},{1,3},{3,5},{5,7},{... | collective-permute-start | bytes 786440 | tf_op jit(solution)/shard_map/ppermute | solution.py:66
  84.3 1.6 broadcast_and_fusion
  85.9 3.5 %fusion.26 = bf16[512,512]{1,0:T(8,128)(2,1)S(1)} fusion(bf16[2048,1536]{1,0:T(8,128)(2,1)} %constant_dynamic-update-slice_fusion.9, s32[]{:T(128)S(6)} %select_n.230, bf16[256,2048]{1,0:T(8,128)(2,1)} %collective-permute-done, bf16[256,2048]{1,0:T(8,128)(2,1)} %add_convert_fusion.1), kind=kOutput, calls=%fused_computation.37 | convolution fusion | flops 1078198272 | bytes 4718596 | tf_op jit(solution)/shard_map/dot_general | solution.py:127
  89.9 3.0 %collective-permute-start.18 = (f32[4,128,128]{2,1,0:T(8,128)S(1)}, f32[4,128,128]{2,1,0:T(8,128)S(1)}, u32[]{:S(2)}, u32[]{:S(2)}) collective-permute-start(f32[4,128,128]{2,1,0:T(8,128)S(1)} %fusion.100), channel_id=1, source_target_pairs={{0,4},{2,6},{4,8},{6,10},{8,12},{10,14},{1,5},{3,7},{5,9},{7,11},{... | collective-permute-start | bytes 786440 | tf_op jit(solution)/shard_map/ppermute | solution.py:66
  93.4 3.6 %collective-permute-done.18 = f32[4,128,128]{2,1,0:T(8,128)S(1)} collective-permute-done((f32[4,128,128]{2,1,0:T(8,128)S(1)}, f32[4,128,128]{2,1,0:T(8,128)S(1)}, u32[]{:S(2)}, u32[]{:S(2)}) %collective-permute-start.18) | collective-permute-done | bytes 262176 | tf_op jit(solution)/shard_map/ppermute | solution.py:66
  97.0 2.9 %collective-permute-start.19 = (f32[4,128,128]{2,1,0:T(8,128)S(1)}, f32[4,128,128]{2,1,0:T(8,128)S(1)}, u32[]{:S(2)}, u32[]{:S(2)}) collective-permute-start(f32[4,128,128]{2,1,0:T(8,128)S(1)} %add.289), channel_id=1, source_target_pairs={{0,8},{2,10},{4,12},{6,14},{1,9},{3,11},{5,13},{7,15},{16,24},{18,... | collective-permute-start | bytes 786440 | tf_op jit(solution)/shard_map/ppermute | solution.py:66
  100.5 5.9 %collective-permute-done.19 = f32[4,128,128]{2,1,0:T(8,128)S(1)} collective-permute-done((f32[4,128,128]{2,1,0:T(8,128)S(1)}, f32[4,128,128]{2,1,0:T(8,128)S(1)}, u32[]{:S(2)}, u32[]{:S(2)}) %collective-permute-start.19) | collective-permute-done | bytes 262176 | tf_op jit(solution)/shard_map/ppermute | solution.py:66
  109.3 2.5 %collective-permute-start.21 = (f32[4,128,128]{2,1,0:T(8,128)S(1)}, f32[4,128,128]{2,1,0:T(8,128)S(1)}, u32[]{:S(2)}, u32[]{:S(2)}) collective-permute-start(f32[4,128,128]{2,1,0:T(8,128)S(1)} %fusion.46), channel_id=1, source_target_pairs={{2,0},{4,2},{6,4},{8,6},{10,8},{12,10},{14,12},{3,1},{5,3},{7,5},{... | collective-permute-start | bytes 786440 | tf_op jit(solution)/shard_map/ppermute | solution.py:66
  111.8 2.4 %fusion.18 = f32[256,2048]{1,0:T(8,128)S(1)} fusion(bf16[256,512]{0,1:T(8,128)(2,1)S(1)} %bitcast.136, bf16[2048,1536]{1,0:T(8,128)(2,1)} %constant_dynamic-update-slice_fusion.9, s32[]{:T(128)S(6)} %select_n.230), kind=kOutput, calls=%fused_computation.23 | convolution fusion | flops 536870912 | bytes 4456452 | tf_op jit(solution)/shard_map/dot_general | solution.py:160
  114.2 3.1 %collective-permute-done.21 = f32[4,128,128]{2,1,0:T(8,128)S(1)} collective-permute-done((f32[4,128,128]{2,1,0:T(8,128)S(1)}, f32[4,128,128]{2,1,0:T(8,128)S(1)}, u32[]{:S(2)}, u32[]{:S(2)}) %collective-permute-start.21) | collective-permute-done | bytes 262176 | tf_op jit(solution)/shard_map/ppermute | solution.py:66
  117.4 1.9 %collective-permute-start.22 = (f32[4,128,128]{2,1,0:T(8,128)S(1)}, f32[4,128,128]{2,1,0:T(8,128)S(1)}, u32[]{:S(2)}, u32[]{:S(2)}) collective-permute-start(f32[4,128,128]{2,1,0:T(8,128)S(1)} %fusion.99), channel_id=1, source_target_pairs={{4,0},{6,2},{8,4},{10,6},{12,8},{14,10},{5,1},{7,3},{9,5},{11,7},{... | collective-permute-start | bytes 786440 | tf_op jit(solution)/shard_map/ppermute | solution.py:66
  119.3 2.4 %fusion.16 = f32[256,2048]{1,0:T(8,128)S(1)} fusion(bf16[256,512]{0,1:T(8,128)(2,1)S(1)} %bitcast.135, bf16[2048,1536]{1,0:T(8,128)(2,1)} %constant_dynamic-update-slice_fusion.9, s32[]{:T(128)S(6)} %select_n.230), kind=kOutput, calls=%fused_computation.21 | convolution fusion | flops 536870912 | bytes 4456452 | tf_op jit(solution)/shard_map/dot_general | solution.py:160
  121.6 5.2 %collective-permute-done.22 = f32[4,128,128]{2,1,0:T(8,128)S(1)} collective-permute-done((f32[4,128,128]{2,1,0:T(8,128)S(1)}, f32[4,128,128]{2,1,0:T(8,128)S(1)}, u32[]{:S(2)}, u32[]{:S(2)}) %collective-permute-start.22) | collective-permute-done | bytes 262176 | tf_op jit(solution)/shard_map/ppermute | solution.py:66
  129.4 6.4 %collective-permute-done.23 = f32[4,128,128]{2,1,0:T(8,128)S(1)} collective-permute-done((f32[4,128,128]{2,1,0:T(8,128)S(1)}, f32[4,128,128]{2,1,0:T(8,128)S(1)}, u32[]{:S(2)}, u32[]{:S(2)}) %collective-permute-start.23) | collective-permute-done | bytes 262176 | tf_op jit(solution)/shard_map/ppermute | solution.py:66
  136.8 2.4 %fusion.10 = f32[128,2048]{1,0:T(8,128)S(1)} fusion(bf16[128,512]{0,1:T(8,128)(2,1)S(1)} %bitcast.142, bf16[2048,1536]{1,0:T(8,128)(2,1)} %constant_dynamic-update-slice_fusion.9, s32[]{:T(128)S(6)} %select_n.229), kind=kOutput, calls=%fused_computation.15 | convolution fusion | flops 268435456 | bytes 3276804 | tf_op jit(solution)/shard_map/dot_general | solution.py:187
  139.5 3.4 %add_add_fusion.1 = f32[128,2048]{1,0:T(8,128)} fusion(f32[128,2048]{1,0:T(8,128)S(1)} %fusion.10, f32[256,2048]{1,0:T(8,128)S(1)} %fusion.16, bf16[128,512]{0,1:T(8,128)(2,1)S(1)} %bitcast.141, bf16[2048,1536]{1,0:T(8,128)(2,1)} %constant_dynamic-update-slice_fusion.9, s32[]{:T(128)S(6)} %select_n.244), kind=kOutput, calls=%fused_computation.43 | convolution fusion | flops 268959744 | bytes 5373956 | tf_op jit(solution)/shard_map/dot_general | solution.py:187
  143.0 13.1 %collective-permute-start.26 = (f32[128,2048]{1,0:T(8,128)}, f32[128,2048]{1,0:T(8,128)}, u32[]{:S(2)}, u32[]{:S(2)}) collective-permute-start(f32[128,2048]{1,0:T(8,128)} %add_add_fusion.1), channel_id=1, source_target_pairs={{0,1},{1,0},{2,3},{3,2},{4,5},{5,4},{6,7},{7,6},{8,9},{9,8},{10,11... | collective-permute-start | bytes 3145736 | tf_op jit(solution)/shard_map/ppermute | solution.py:17
  156.1 2.4 %fusion.12 = f32[128,2048]{1,0:T(8,128)S(1)} fusion(bf16[128,512]{0,1:T(8,128)(2,1)S(1)} %bitcast.139, bf16[2048,1536]{1,0:T(8,128)(2,1)} %constant_dynamic-update-slice_fusion.9, s32[]{:T(128)S(6)} %select_n.229), kind=kOutput, calls=%fused_computation.17 | convolution fusion | flops 268435456 | bytes 3276804 | tf_op jit(solution)/shard_map/dot_general | solution.py:187
  158.5 3.4 %add_add_fusion.2 = f32[128,2048]{1,0:T(8,128)} fusion(f32[128,2048]{1,0:T(8,128)S(1)} %fusion.12, f32[256,2048]{1,0:T(8,128)S(1)} %fusion.16, bf16[128,512]{0,1:T(8,128)(2,1)S(1)} %bitcast.140, bf16[2048,1536]{1,0:T(8,128)(2,1)} %constant_dynamic-update-slice_fusion.9, s32[]{:T(128)S(6)} %select_n.244), kind=kOutput, calls=%fused_computation.44 | convolution fusion | flops 268959744 | bytes 5373956 | tf_op jit(solution)/shard_map/dot_general | solution.py:187
  165.2 2.5 %fusion.14 = f32[256,2048]{1,0:T(8,128)S(1)} fusion(bf16[256,512]{0,1:T(8,128)(2,1)} %bitcast.134, bf16[2048,1536]{1,0:T(8,128)(2,1)} %constant_dynamic-update-slice_fusion.9, s32[]{:T(128)S(6)} %select_n.229), kind=kOutput, calls=%fused_computation.19 | convolution fusion | flops 536870912 | bytes 4456452 | tf_op jit(solution)/shard_map/dot_general | solution.py:187
  167.7 2.4 %add_add_fusion = f32[256,2048]{1,0:T(8,128)S(1)} fusion(f32[256,2048]{1,0:T(8,128)S(1)} %fusion.18, f32[256,2048]{1,0:T(8,128)S(1)} %fusion.14, bf16[256,512]{0,1:T(8,128)(2,1)S(1)} %bitcast.133, bf16[2048,1536]{1,0:T(8,128)(2,1)} %constant_dynamic-update-slice_fusion.9, s32[]{:T(128)S(6)} %select_n.244), kind=kOutput, calls=%fused_computation.5 | convolution fusion | flops 537919488 | bytes 8650756 | tf_op jit(solution)/shard_map/dot_general | solution.py:187
  171.1 1.7 pad_maximum_fusion.1
  (129 shorter events, 49.1 us)
Async XLA Ops:
  3.6 9.6 %copy-start = (bf16[256,2048]{1,0:T(8,128)(2,1)S(1)}, bf16[256,2048]{1,0:T(8,128)(2,1)}, u32[]{:S(2)}) copy-start(bf16[256,2048]{1,0:T(8,128)(2,1)} %param.10) | copy-start | bytes 3145732
  3.6 2.9 %collective-permute-start.1 = (bf16[128,1536]{1,0:T(8,128)(2,1)}, bf16[128,1536]{1,0:T(8,128)(2,1)}, u32[]{:S(2)}, u32[]{:S(2)}) collective-permute-start(bf16[128,1536]{1,0:T(8,128)(2,1)} %pad_maximum_fusion.7), channel_id=1, source_target_pairs={{0,1},{1,0},{2,3},{3,2},{4,5},{5,4},{6,7},{7,6},{8,9},{9,8},{10,11... | collective-permute-start | bytes 1179656 | tf_op jit(solution)/shard_map/ppermute | solution.py:17
  6.2 100.6 %collective-permute-start.20 = (bf16[256,512]{0,1:T(8,128)(2,1)}, bf16[256,512]{0,1:T(8,128)(2,1)S(1)}, u32[]{:S(2)}, u32[]{:S(2)}) collective-permute-start(bf16[256,512]{0,1:T(8,128)(2,1)} %get-tuple-element.43), channel_id=1, source_target_pairs={{0,1},{1,0},{2,3},{3,2},{4,5},{5,4},{6,7},{7,6},{8,9},{9,8},{10,11... | collective-permute-start | bytes 786440 | tf_op jit(solution)/shard_map/ppermute | solution.py:17
  6.4 10.3 %copy-start.5 = (s32[1,2,2]{2,1,0:T(2,128)S(1)}, s32[1,2,2]{2,1,0:T(2,128)}, u32[]{:S(2)}) copy-start(s32[1,2,2]{2,1,0:T(2,128)} %param.15) | copy-start | bytes 52
  6.4 10.3 %copy-start.6 = (s32[8]{0:T(128)S(1)}, s32[8]{0:T(128)}, u32[]{:S(2)}) copy-start(s32[8]{0:T(128)} %constant.120.clone) | copy-start | bytes 100
  6.4 15.5 %copy-start.4 = (s32[8]{0:T(128)S(1)}, s32[8]{0:T(128)}, u32[]{:S(2)}) copy-start(s32[8]{0:T(128)} %constant.119.clone) | copy-start | bytes 100
  11.7 16.6 %collective-permute-start.2 = (bf16[256,1024]{1,0:T(8,128)(2,1)}, bf16[256,1024]{1,0:T(8,128)(2,1)S(1)}, u32[]{:S(2)}, u32[]{:S(2)}) collective-permute-start(bf16[256,1024]{1,0:T(8,128)(2,1)} %get-tuple-element.25), channel_id=1, source_target_pairs={{0,4},{4,8},{8,12},{12,14},{14,10},{10,6},{6,2},{2,0},{1,5},{5,9},... | collective-permute-start | bytes 1572872 | tf_op jit(solution)/shard_map/ppermute | solution.py:47
  11.8 17.7 %collective-permute-start.4 = (bf16[256,1024]{1,0:T(8,128)(2,1)}, bf16[256,1024]{1,0:T(8,128)(2,1)S(1)}, u32[]{:S(2)}, u32[]{:S(2)}) collective-permute-start(bf16[256,1024]{1,0:T(8,128)(2,1)} %get-tuple-element.25), channel_id=1, source_target_pairs={{0,2},{4,0},{8,4},{12,8},{14,12},{10,14},{6,10},{2,6},{1,3},{5,1},... | collective-permute-start | bytes 1572872 | tf_op jit(solution)/shard_map/ppermute | solution.py:50
  15.7 55.8 %collective-permute-start = (bf16[256,2048]{1,0:T(8,128)(2,1)}, bf16[256,2048]{1,0:T(8,128)(2,1)}, u32[]{:S(2)}, u32[]{:S(2)}) collective-permute-start(bf16[256,2048]{1,0:T(8,128)(2,1)} %add_convert_fusion.1), channel_id=1, source_target_pairs={{0,1},{1,0},{2,3},{3,2},{4,5},{5,4},{6,7},{7,6},{8,9},{9,8},{10,11... | collective-permute-start | bytes 3145736 | tf_op jit(solution)/shard_map/ppermute | solution.py:17
  16.7 10.9 %collective-permute-start.16 = (s32[2,2]{1,0:T(2,128)S(1)}, s32[2,2]{1,0:T(2,128)S(1)}, u32[]{:S(2)}, u32[]{:S(2)}) collective-permute-start(s32[2,2]{1,0:T(2,128)S(1)} %bitcast.143), channel_id=1, source_target_pairs={{0,1},{1,0},{2,3},{3,2},{4,5},{5,4},{6,7},{7,6},{8,9},{9,8},{10,11... | collective-permute-start | bytes 56 | tf_op jit(solution)/shard_map/ppermute | solution.py:17
  28.3 7.4 %collective-permute-start.3 = (bf16[256,512]{1,0:T(8,128)(2,1)S(1)}, bf16[256,512]{1,0:T(8,128)(2,1)S(1)}, u32[]{:S(2)}, u32[]{:S(2)}) collective-permute-start(bf16[256,512]{1,0:T(8,128)(2,1)S(1)} %constant_dynamic-slice_fusion.6), channel_id=1, source_target_pairs={{0,16},{16,0},{1,17},{17,1},{2,18},{18,2},{3,19},{19,3},{4,20},{20... | collective-permute-start | bytes 786440 | tf_op jit(solution)/shard_map/ppermute | solution.py:41
  28.6 12.7 %collective-permute-start.6 = (bf16[256,1024]{1,0:T(8,128)(2,1)S(1)}, bf16[256,1024]{1,0:T(8,128)(2,1)S(1)}, u32[]{:S(2)}, u32[]{:S(2)}) collective-permute-start(bf16[256,1024]{1,0:T(8,128)(2,1)S(1)} %collective-permute-done.2), channel_id=1, source_target_pairs={{0,4},{4,8},{8,12},{12,14},{14,10},{10,6},{6,2},{2,0},{1,5},{5,9},... | collective-permute-start | bytes 1572872 | tf_op jit(solution)/shard_map/ppermute | solution.py:47
  29.5 14.0 %collective-permute-start.8 = (bf16[256,1024]{1,0:T(8,128)(2,1)S(1)}, bf16[256,1024]{1,0:T(8,128)(2,1)S(1)}, u32[]{:S(2)}, u32[]{:S(2)}) collective-permute-start(bf16[256,1024]{1,0:T(8,128)(2,1)S(1)} %collective-permute-done.4), channel_id=1, source_target_pairs={{0,2},{4,0},{8,4},{12,8},{14,12},{10,14},{6,10},{2,6},{1,3},{5,1},... | collective-permute-start | bytes 1572872 | tf_op jit(solution)/shard_map/ppermute | solution.py:50
  35.7 6.9 %collective-permute-start.5 = (bf16[256,512]{1,0:T(8,128)(2,1)S(1)}, bf16[256,512]{1,0:T(8,128)(2,1)S(1)}, u32[]{:S(2)}, u32[]{:S(2)}) collective-permute-start(bf16[256,512]{1,0:T(8,128)(2,1)S(1)} %constant_dynamic-slice_fusion.5), channel_id=1, source_target_pairs={{0,16},{16,0},{1,17},{17,1},{2,18},{18,2},{3,19},{19,3},{4,20},{20... | collective-permute-start | bytes 786440 | tf_op jit(solution)/shard_map/ppermute | solution.py:41
  41.3 6.2 %collective-permute-start.7 = (bf16[256,512]{1,0:T(8,128)(2,1)S(1)}, bf16[256,512]{1,0:T(8,128)(2,1)S(1)}, u32[]{:S(2)}, u32[]{:S(2)}) collective-permute-start(bf16[256,512]{1,0:T(8,128)(2,1)S(1)} %constant_dynamic-slice_fusion.4), channel_id=1, source_target_pairs={{0,16},{16,0},{1,17},{17,1},{2,18},{18,2},{3,19},{19,3},{4,20},{20... | collective-permute-start | bytes 786440 | tf_op jit(solution)/shard_map/ppermute | solution.py:41
  42.6 11.5 %collective-permute-start.10 = (bf16[256,1024]{1,0:T(8,128)(2,1)S(1)}, bf16[256,1024]{1,0:T(8,128)(2,1)S(1)}, u32[]{:S(2)}, u32[]{:S(2)}) collective-permute-start(bf16[256,1024]{1,0:T(8,128)(2,1)S(1)} %collective-permute-done.6), channel_id=1, source_target_pairs={{0,4},{4,8},{8,12},{12,14},{14,10},{10,6},{6,2},{2,0},{1,5},{5,9},... | collective-permute-start | bytes 1572872 | tf_op jit(solution)/shard_map/ppermute | solution.py:47
  43.5 11.8 %collective-permute-start.12 = (bf16[256,1024]{1,0:T(8,128)(2,1)S(1)}, bf16[256,1024]{1,0:T(8,128)(2,1)S(1)}, u32[]{:S(2)}, u32[]{:S(2)}) collective-permute-start(bf16[256,1024]{1,0:T(8,128)(2,1)S(1)} %collective-permute-done.8), channel_id=1, source_target_pairs={{0,2},{4,0},{8,4},{12,8},{14,12},{10,14},{6,10},{2,6},{1,3},{5,1},... | collective-permute-start | bytes 1572872 | tf_op jit(solution)/shard_map/ppermute | solution.py:50
  47.5 6.7 %collective-permute-start.9 = (bf16[256,512]{1,0:T(8,128)(2,1)S(1)}, bf16[256,512]{1,0:T(8,128)(2,1)S(1)}, u32[]{:S(2)}, u32[]{:S(2)}) collective-permute-start(bf16[256,512]{1,0:T(8,128)(2,1)S(1)} %constant_dynamic-slice_fusion.3), channel_id=1, source_target_pairs={{0,16},{16,0},{1,17},{17,1},{2,18},{18,2},{3,19},{19,3},{4,20},{20... | collective-permute-start | bytes 786440 | tf_op jit(solution)/shard_map/ppermute | solution.py:41
  54.1 10.5 %collective-permute-start.14 = (bf16[256,1024]{1,0:T(8,128)(2,1)S(1)}, bf16[256,1024]{1,0:T(8,128)(2,1)S(1)}, u32[]{:S(2)}, u32[]{:S(2)}) collective-permute-start(bf16[256,1024]{1,0:T(8,128)(2,1)S(1)} %collective-permute-done.10), channel_id=1, source_target_pairs={{0,4},{4,8},{8,12},{12,14},{14,10},{10,6},{6,2},{2,0},{1,5},{5,9},... | collective-permute-start | bytes 1572872 | tf_op jit(solution)/shard_map/ppermute | solution.py:47
  54.2 5.3 %collective-permute-start.11 = (bf16[256,512]{1,0:T(8,128)(2,1)S(1)}, bf16[256,512]{1,0:T(8,128)(2,1)S(1)}, u32[]{:S(2)}, u32[]{:S(2)}) collective-permute-start(bf16[256,512]{1,0:T(8,128)(2,1)S(1)} %constant_dynamic-slice_fusion.2), channel_id=1, source_target_pairs={{0,16},{16,0},{1,17},{17,1},{2,18},{18,2},{3,19},{19,3},{4,20},{20... | collective-permute-start | bytes 786440 | tf_op jit(solution)/shard_map/ppermute | solution.py:41
  55.4 10.4 %collective-permute-start.13 = (bf16[256,512]{1,0:T(8,128)(2,1)S(1)}, bf16[256,512]{1,0:T(8,128)(2,1)S(1)}, u32[]{:S(2)}, u32[]{:S(2)}) collective-permute-start(bf16[256,512]{1,0:T(8,128)(2,1)S(1)} %constant_dynamic-slice_fusion.1), channel_id=1, source_target_pairs={{0,16},{16,0},{1,17},{17,1},{2,18},{18,2},{3,19},{19,3},{4,20},{20... | collective-permute-start | bytes 786440 | tf_op jit(solution)/shard_map/ppermute | solution.py:41
  64.6 6.1 %collective-permute-start.15 = (bf16[256,512]{1,0:T(8,128)(2,1)S(1)}, bf16[256,512]{1,0:T(8,128)(2,1)S(1)}, u32[]{:S(2)}, u32[]{:S(2)}) collective-permute-start(bf16[256,512]{1,0:T(8,128)(2,1)S(1)} %constant_dynamic-slice_fusion), channel_id=1, source_target_pairs={{0,16},{16,0},{1,17},{17,1},{2,18},{18,2},{3,19},{19,3},{4,20},{20... | collective-permute-start | bytes 786440 | tf_op jit(solution)/shard_map/ppermute | solution.py:41
  79.2 10.7 %collective-permute-start.17 = (f32[4,128,128]{2,1,0:T(8,128)}, f32[4,128,128]{2,1,0:T(8,128)S(1)}, u32[]{:S(2)}, u32[]{:S(2)}) collective-permute-start(f32[4,128,128]{2,1,0:T(8,128)} %fusion.45), channel_id=1, source_target_pairs={{0,2},{2,4},{4,6},{6,8},{8,10},{10,12},{12,14},{1,3},{3,5},{5,7},{... | collective-permute-start | bytes 786440 | tf_op jit(solution)/shard_map/ppermute | solution.py:66
  89.9 7.1 %collective-permute-start.18 = (f32[4,128,128]{2,1,0:T(8,128)S(1)}, f32[4,128,128]{2,1,0:T(8,128)S(1)}, u32[]{:S(2)}, u32[]{:S(2)}) collective-permute-start(f32[4,128,128]{2,1,0:T(8,128)S(1)} %fusion.100), channel_id=1, source_target_pairs={{0,4},{2,6},{4,8},{6,10},{8,12},{10,14},{1,5},{3,7},{5,9},{7,11},{... | collective-permute-start | bytes 786440 | tf_op jit(solution)/shard_map/ppermute | solution.py:66
  97.0 9.3 %collective-permute-start.19 = (f32[4,128,128]{2,1,0:T(8,128)S(1)}, f32[4,128,128]{2,1,0:T(8,128)S(1)}, u32[]{:S(2)}, u32[]{:S(2)}) collective-permute-start(f32[4,128,128]{2,1,0:T(8,128)S(1)} %add.289), channel_id=1, source_target_pairs={{0,8},{2,10},{4,12},{6,14},{1,9},{3,11},{5,13},{7,15},{16,24},{18,... | collective-permute-start | bytes 786440 | tf_op jit(solution)/shard_map/ppermute | solution.py:66
  109.3 8.0 %collective-permute-start.21 = (f32[4,128,128]{2,1,0:T(8,128)S(1)}, f32[4,128,128]{2,1,0:T(8,128)S(1)}, u32[]{:S(2)}, u32[]{:S(2)}) collective-permute-start(f32[4,128,128]{2,1,0:T(8,128)S(1)} %fusion.46), channel_id=1, source_target_pairs={{2,0},{4,2},{6,4},{8,6},{10,8},{12,10},{14,12},{3,1},{5,3},{7,5},{... | collective-permute-start | bytes 786440 | tf_op jit(solution)/shard_map/ppermute | solution.py:66
  117.4 9.5 %collective-permute-start.22 = (f32[4,128,128]{2,1,0:T(8,128)S(1)}, f32[4,128,128]{2,1,0:T(8,128)S(1)}, u32[]{:S(2)}, u32[]{:S(2)}) collective-permute-start(f32[4,128,128]{2,1,0:T(8,128)S(1)} %fusion.99), channel_id=1, source_target_pairs={{4,0},{6,2},{8,4},{10,6},{12,8},{14,10},{5,1},{7,3},{9,5},{11,7},{... | collective-permute-start | bytes 786440 | tf_op jit(solution)/shard_map/ppermute | solution.py:66
  126.9 8.9 %collective-permute-start.23 = (f32[4,128,128]{2,1,0:T(8,128)S(1)}, f32[4,128,128]{2,1,0:T(8,128)S(1)}, u32[]{:S(2)}, u32[]{:S(2)}) collective-permute-start(f32[4,128,128]{2,1,0:T(8,128)S(1)} %add.301), channel_id=1, source_target_pairs={{8,0},{10,2},{12,4},{14,6},{9,1},{11,3},{13,5},{15,7},{24,16},{26,... | collective-permute-start | bytes 786440 | tf_op jit(solution)/shard_map/ppermute | solution.py:66
  139.5 22.4 %copy-start.1 = (bf16[1,256,4,128]{1,3,2,0:T(8,128)(2,1)S(1)}, bf16[1,256,4,128]{1,3,2,0:T(8,128)(2,1)}, u32[]{:S(2)}) copy-start(bf16[1,256,4,128]{1,3,2,0:T(8,128)(2,1)} %get-tuple-element.38) | copy-start | bytes 786436
  143.0 28.1 %collective-permute-start.26 = (f32[128,2048]{1,0:T(8,128)}, f32[128,2048]{1,0:T(8,128)}, u32[]{:S(2)}, u32[]{:S(2)}) collective-permute-start(f32[128,2048]{1,0:T(8,128)} %add_add_fusion.1), channel_id=1, source_target_pairs={{0,1},{1,0},{2,3},{3,2},{4,5},{5,4},{6,7},{7,6},{8,9},{9,8},{10,11... | collective-permute-start | bytes 3145736 | tf_op jit(solution)/shard_map/ppermute | solution.py:17
  161.9 9.2 %collective-permute-start.25 = (f32[128,2048]{1,0:T(8,128)}, f32[128,2048]{1,0:T(8,128)}, u32[]{:S(2)}, u32[]{:S(2)}) collective-permute-start(f32[128,2048]{1,0:T(8,128)} %add_add_fusion.2), channel_id=1, source_target_pairs={{0,1},{1,0},{2,3},{3,2},{4,5},{5,4},{6,7},{7,6},{8,9},{9,8},{10,11... | collective-permute-start | bytes 3145736 | tf_op jit(solution)/shard_map/ppermute | solution.py:17
  164.6 5.5 %collective-permute-start.24 = (bf16[256,512]{1,0:T(8,128)(2,1)S(1)}, bf16[256,512]{1,0:T(8,128)(2,1)S(1)}, u32[]{:S(2)}, u32[]{:S(2)}) collective-permute-start(bf16[256,512]{1,0:T(8,128)(2,1)S(1)} %copy.48), channel_id=1, source_target_pairs={{0,1},{1,0},{2,3},{3,2},{4,5},{5,4},{6,7},{7,6},{8,9},{9,8},{10,11... | collective-permute-start | bytes 786440 | tf_op jit(solution)/shard_map/ppermute | solution.py:17
  (2 other events, 11.9 us)

commit v21 on v18

--- a/solution.py
+++ b/solution.py
@@ -169,11 +169,9 @@
     later_b = jnp.stack([later_mine, later_other]).astype(bf16)
     out_send, later_b = lax.optimization_barrier((out_b[1], later_b))
     out_recv = swap(out_send)
-    output = jnp.where(
-        first,
-        jnp.concatenate([out_b[0], out_recv], axis=1),
-        jnp.concatenate([out_recv, out_b[0]], axis=1),
-    )
+    output = jnp.zeros((tok, feat), bf16)
+    output = lax.dynamic_update_slice_in_dim(output, out_b[0], k * half, axis=1)
+    output = lax.dynamic_update_slice_in_dim(output, out_recv, (1 - k) * half, axis=1)
 
     d_key = dk_intra + jnp.einsum("jshe,jhde->jshd", value, later_b, preferred_element_type=f32)
     d_value = dv_intra + jnp.einsum("jshd,jhde->jshe", key, later_b, preferred_element_type=f32)

time: 166 us -> 169 us (1.018)
  local copies, waits for them, and re-layouts: 25.7 us -> 29 us
  transfers between devices with their start and end apart: 26 -> 26, of which waited for: 12 -> 12; matrix products, arithmetic and copies ran while one was open for 31% -> 32% of each run, Pallas kernels for 0% -> 0%
where the time goes in v21:
time: 169 us
  waiting for transfers between devices  47.2 us (28%)
  starting transfers between devices  41.6 us (25%)
  local copies, waits for them, and re-layouts  29 us (17%)
  matrix products  28.9 us (17%)
  other arithmetic  11.3 us (7%)
  between operations  10.6 us (6%)
    ppermute x6, waiting for transfers between devices, exclusive_scan(): got = lax.ppermute(incl, 'chip', perm)  24.3 us
    ppermute x6, starting transfers between devices, exclusive_scan(): got = lax.ppermute(incl, 'chip', perm)  16.7 us
    ppermute x6, starting transfers between devices, swap(): return lax.ppermute(x, 'core', [(0, 1), (1, 0)])  15.3 us
    ppermute x4, waiting for transfers between devices, ring_gather(): fwd = lax.ppermute(fwd, 'chip', ahead)  11.7 us
    ppermute x7, waiting for transfers between devices, land(): return (piece, lax.ppermute(sent, 'groups', partner))  11.3 us
    dot_general x4, matrix products, grad_rows(): g = g + lax.dot_general(d, w, dims, preferred_element_type=f32)  11 us
    dynamic_update_slice x8, local copies, waits for them, and re-layouts, on_device(): w_all = lax.dynamic_update_slice(w_all, ringed, (src * span, 0))  7.17 us
    dynamic_update_slice x8, local copies, waits for them, and re-layouts, on_device(): w_all = lax.dynamic_update_slice(w_all, swapped, (src * span, width))  5.97 us
  transfers between devices with their start and end apart: 26, of which 12 were waited for; matrix products, arithmetic and copies ran while one was open for 32% of the time, Pallas kernels for 0%

profile of v21, /device:TPU:15, one launch (start us, length us, event | category | flops | bytes accessed | tf_op | source)
XLA Modules:
  0.0 168.6 jit_solution(5740746289114110158)
XLA Ops:
  7.5 3.0 %broadcast_in_dim.37 = bf16[2048,1536]{1,0:T(8,128)(2,1)} broadcast(bf16[]{:T(256)} %constant.93.clone.1), dimensions={} | broadcast | bytes 6291458 | tf_op jit(solution)/shard_map/broadcast_in_dim | solution.py:115
  13.1 2.6 %add_convert_fusion.1 = bf16[256,2048]{1,0:T(8,128)(2,1)} fusion(bf16[256,2048]{1,0:T(8,128)(2,1)S(1)} %copy-done, bf16[256,2048]{1,0:T(8,128)(2,1)} %param.9), kind=kLoop, calls=%fused_computation.8 | loop fusion | flops 2097152 | bytes 3145728 | tf_op jit(solution)/shard_map/convert_element_type | solution.py:97
  32.2 4.0 %collective-permute-done.3 = bf16[256,512]{1,0:T(8,128)(2,1)S(1)} collective-permute-done((bf16[256,512]{1,0:T(8,128)(2,1)S(1)}, bf16[256,512]{1,0:T(8,128)(2,1)S(1)}, u32[]{:S(2)}, u32[]{:S(2)}) %collective-permute-start.3) | collective-permute-done | bytes 262176 | tf_op jit(solution)/shard_map/ppermute | solution.py:41
  38.1 3.7 %collective-permute-done.6 = bf16[256,1024]{1,0:T(8,128)(2,1)S(1)} collective-permute-done((bf16[256,1024]{1,0:T(8,128)(2,1)S(1)}, bf16[256,1024]{1,0:T(8,128)(2,1)S(1)}, u32[]{:S(2)}, u32[]{:S(2)}) %collective-permute-start.6) | collective-permute-done | bytes 524320 | tf_op jit(solution)/shard_map/ppermute | solution.py:47
  44.0 1.3 collective-permute-start.12
  46.2 1.8 %collective-permute-done.7 = bf16[256,512]{1,0:T(8,128)(2,1)S(1)} collective-permute-done((bf16[256,512]{1,0:T(8,128)(2,1)S(1)}, bf16[256,512]{1,0:T(8,128)(2,1)S(1)}, u32[]{:S(2)}, u32[]{:S(2)}) %collective-permute-start.7) | collective-permute-done | bytes 262176 | tf_op jit(solution)/shard_map/ppermute | solution.py:41
  50.8 3.7 %collective-permute-done.10 = bf16[256,1024]{1,0:T(8,128)(2,1)S(1)} collective-permute-done((bf16[256,1024]{1,0:T(8,128)(2,1)S(1)}, bf16[256,1024]{1,0:T(8,128)(2,1)S(1)}, u32[]{:S(2)}, u32[]{:S(2)}) %collective-permute-start.10) | collective-permute-done | bytes 524320 | tf_op jit(solution)/shard_map/ppermute | solution.py:47
  58.0 2.1 %collective-permute-done.11 = bf16[256,512]{1,0:T(8,128)(2,1)S(1)} collective-permute-done((bf16[256,512]{1,0:T(8,128)(2,1)S(1)}, bf16[256,512]{1,0:T(8,128)(2,1)S(1)}, u32[]{:S(2)}, u32[]{:S(2)}) %collective-permute-start.11) | collective-permute-done | bytes 262176 | tf_op jit(solution)/shard_map/ppermute | solution.py:41
  60.8 4.3 %collective-permute-done.14 = bf16[256,1024]{1,0:T(8,128)(2,1)S(1)} collective-permute-done((bf16[256,1024]{1,0:T(8,128)(2,1)S(1)}, bf16[256,1024]{1,0:T(8,128)(2,1)S(1)}, u32[]{:S(2)}, u32[]{:S(2)}) %collective-permute-start.14) | collective-permute-done | bytes 524320 | tf_op jit(solution)/shard_map/ppermute | solution.py:47
  67.9 3.4 %collective-permute-done.15 = bf16[256,512]{1,0:T(8,128)(2,1)S(1)} collective-permute-done((bf16[256,512]{1,0:T(8,128)(2,1)S(1)}, bf16[256,512]{1,0:T(8,128)(2,1)S(1)}, u32[]{:S(2)}, u32[]{:S(2)}) %collective-permute-start.15) | collective-permute-done | bytes 262176 | tf_op jit(solution)/shard_map/ppermute | solution.py:41
  72.0 5.2 %fusion.20 = bf16[512,1024]{1,0:T(8,128)(2,1)S(1)} fusion(bf16[2048,1536]{1,0:T(8,128)(2,1)} %constant_dynamic-update-slice_fusion.11, s32[]{:T(128)S(6)} %select_n.220, bf16[256,2048]{1,0:T(8,128)(2,1)} %collective-permute-done, bf16[256,2048]{1,0:T(8,128)(2,1)} %add_convert_fusion.1), kind=kOutput, calls=%fused_computation.23 | convolution fusion | flops 2152202240 | bytes 7340036 | tf_op jit(solution)/shard_map/dot_general | solution.py:123
  79.7 5.1 %collective-permute-start.17 = (f32[4,128,128]{2,1,0:T(8,128)}, f32[4,128,128]{2,1,0:T(8,128)S(1)}, u32[]{:S(2)}, u32[]{:S(2)}) collective-permute-start(f32[4,128,128]{2,1,0:T(8,128)} %fusion.43), channel_id=1, source_target_pairs={{0,2},{2,4},{4,6},{6,8},{8,10},{10,12},{12,14},{1,3},{3,5},{5,7},{... | collective-permute-start | bytes 786440 | tf_op jit(solution)/shard_map/ppermute | solution.py:66
  84.8 1.6 broadcast_and_fusion
  86.4 3.5 %fusion.24 = bf16[512,512]{1,0:T(8,128)(2,1)S(1)} fusion(bf16[2048,1536]{1,0:T(8,128)(2,1)} %constant_dynamic-update-slice_fusion.11, s32[]{:T(128)S(6)} %select_n.221, bf16[256,2048]{1,0:T(8,128)(2,1)} %collective-permute-done, bf16[256,2048]{1,0:T(8,128)(2,1)} %add_convert_fusion.1), kind=kOutput, calls=%fused_computation.33 | convolution fusion | flops 1078198272 | bytes 4718596 | tf_op jit(solution)/shard_map/dot_general | solution.py:127
  90.4 3.0 %collective-permute-start.18 = (f32[4,128,128]{2,1,0:T(8,128)S(1)}, f32[4,128,128]{2,1,0:T(8,128)S(1)}, u32[]{:S(2)}, u32[]{:S(2)}) collective-permute-start(f32[4,128,128]{2,1,0:T(8,128)S(1)} %fusion.90), channel_id=1, source_target_pairs={{0,4},{2,6},{4,8},{6,10},{8,12},{10,14},{1,5},{3,7},{5,9},{7,11},{... | collective-permute-start | bytes 786440 | tf_op jit(solution)/shard_map/ppermute | solution.py:66
  94.0 3.6 %collective-permute-done.18 = f32[4,128,128]{2,1,0:T(8,128)S(1)} collective-permute-done((f32[4,128,128]{2,1,0:T(8,128)S(1)}, f32[4,128,128]{2,1,0:T(8,128)S(1)}, u32[]{:S(2)}, u32[]{:S(2)}) %collective-permute-start.18) | collective-permute-done | bytes 262176 | tf_op jit(solution)/shard_map/ppermute | solution.py:66
  97.6 2.9 %collective-permute-start.19 = (f32[4,128,128]{2,1,0:T(8,128)S(1)}, f32[4,128,128]{2,1,0:T(8,128)S(1)}, u32[]{:S(2)}, u32[]{:S(2)}) collective-permute-start(f32[4,128,128]{2,1,0:T(8,128)S(1)} %add.283), channel_id=1, source_target_pairs={{0,8},{2,10},{4,12},{6,14},{1,9},{3,11},{5,13},{7,15},{16,24},{18,... | collective-permute-start | bytes 786440 | tf_op jit(solution)/shard_map/ppermute | solution.py:66
  101.0 5.9 %collective-permute-done.19 = f32[4,128,128]{2,1,0:T(8,128)S(1)} collective-permute-done((f32[4,128,128]{2,1,0:T(8,128)S(1)}, f32[4,128,128]{2,1,0:T(8,128)S(1)}, u32[]{:S(2)}, u32[]{:S(2)}) %collective-permute-start.19) | collective-permute-done | bytes 262176 | tf_op jit(solution)/shard_map/ppermute | solution.py:66
  109.8 2.5 %collective-permute-start.21 = (f32[4,128,128]{2,1,0:T(8,128)S(1)}, f32[4,128,128]{2,1,0:T(8,128)S(1)}, u32[]{:S(2)}, u32[]{:S(2)}) collective-permute-start(f32[4,128,128]{2,1,0:T(8,128)S(1)} %fusion.44), channel_id=1, source_target_pairs={{2,0},{4,2},{6,4},{8,6},{10,8},{12,10},{14,12},{3,1},{5,3},{7,5},{... | collective-permute-start | bytes 786440 | tf_op jit(solution)/shard_map/ppermute | solution.py:66
  112.3 2.4 %fusion.16 = f32[256,2048]{1,0:T(8,128)S(1)} fusion(bf16[256,512]{0,1:T(8,128)(2,1)S(1)} %bitcast.133, bf16[2048,1536]{1,0:T(8,128)(2,1)} %constant_dynamic-update-slice_fusion.11, s32[]{:T(128)S(6)} %select_n.221), kind=kOutput, calls=%fused_computation.19 | convolution fusion | flops 536870912 | bytes 4456452 | tf_op jit(solution)/shard_map/dot_general | solution.py:160
  114.7 3.1 %collective-permute-done.21 = f32[4,128,128]{2,1,0:T(8,128)S(1)} collective-permute-done((f32[4,128,128]{2,1,0:T(8,128)S(1)}, f32[4,128,128]{2,1,0:T(8,128)S(1)}, u32[]{:S(2)}, u32[]{:S(2)}) %collective-permute-start.21) | collective-permute-done | bytes 262176 | tf_op jit(solution)/shard_map/ppermute | solution.py:66
  117.9 1.9 %collective-permute-start.22 = (f32[4,128,128]{2,1,0:T(8,128)S(1)}, f32[4,128,128]{2,1,0:T(8,128)S(1)}, u32[]{:S(2)}, u32[]{:S(2)}) collective-permute-start(f32[4,128,128]{2,1,0:T(8,128)S(1)} %fusion.89), channel_id=1, source_target_pairs={{4,0},{6,2},{8,4},{10,6},{12,8},{14,10},{5,1},{7,3},{9,5},{11,7},{... | collective-permute-start | bytes 786440 | tf_op jit(solution)/shard_map/ppermute | solution.py:66
  119.8 2.4 %fusion.14 = f32[256,2048]{1,0:T(8,128)S(1)} fusion(bf16[256,512]{0,1:T(8,128)(2,1)S(1)} %bitcast.131, bf16[2048,1536]{1,0:T(8,128)(2,1)} %constant_dynamic-update-slice_fusion.11, s32[]{:T(128)S(6)} %select_n.221), kind=kOutput, calls=%fused_computation.17 | convolution fusion | flops 536870912 | bytes 4456452 | tf_op jit(solution)/shard_map/dot_general | solution.py:160
  122.1 5.5 %collective-permute-done.22 = f32[4,128,128]{2,1,0:T(8,128)S(1)} collective-permute-done((f32[4,128,128]{2,1,0:T(8,128)S(1)}, f32[4,128,128]{2,1,0:T(8,128)S(1)}, u32[]{:S(2)}, u32[]{:S(2)}) %collective-permute-start.22) | collective-permute-done | bytes 262176 | tf_op jit(solution)/shard_map/ppermute | solution.py:66
  127.7 1.3 collective-permute-start.23
  130.2 6.1 %collective-permute-done.23 = f32[4,128,128]{2,1,0:T(8,128)S(1)} collective-permute-done((f32[4,128,128]{2,1,0:T(8,128)S(1)}, f32[4,128,128]{2,1,0:T(8,128)S(1)}, u32[]{:S(2)}, u32[]{:S(2)}) %collective-permute-start.23) | collective-permute-done | bytes 262176 | tf_op jit(solution)/shard_map/ppermute | solution.py:66
  137.6 2.4 %fusion.10 = f32[256,2048]{1,0:T(8,128)S(1)} fusion(bf16[256,512]{0,1:T(8,128)(2,1)S(1)} %bitcast.132, bf16[2048,1536]{1,0:T(8,128)(2,1)} %constant_dynamic-update-slice_fusion.11, s32[]{:T(128)S(6)} %select_n.220), kind=kOutput, calls=%fused_computation.13 | convolution fusion | flops 536870912 | bytes 4456452 | tf_op jit(solution)/shard_map/dot_general | solution.py:185
  140.0 3.8 %add_add_fusion = f32[256,2048]{1,0:T(8,128)} fusion(f32[256,2048]{1,0:T(8,128)S(1)} %fusion.14, f32[256,2048]{1,0:T(8,128)S(1)} %fusion.10, bf16[256,512]{0,1:T(8,128)(2,1)S(1)} %bitcast.134, bf16[2048,1536]{1,0:T(8,128)(2,1)} %constant_dynamic-update-slice_fusion.11, s32[]{:T(128)S(6)} %select_n.234), kind=kOutput, calls=%fused_computation.4 | convolution fusion | flops 537919488 | bytes 8650756 | tf_op jit(solution)/shard_map/dot_general | solution.py:185
  143.8 13.4 %collective-permute-start.25 = (f32[256,2048]{1,0:T(8,128)}, f32[256,2048]{1,0:T(8,128)}, u32[]{:S(2)}, u32[]{:S(2)}) collective-permute-start(f32[256,2048]{1,0:T(8,128)} %add_add_fusion), channel_id=1, source_target_pairs={{0,1},{1,0},{2,3},{3,2},{4,5},{5,4},{6,7},{7,6},{8,9},{9,8},{10,11... | collective-permute-start | bytes 6291464 | tf_op jit(solution)/shard_map/ppermute | solution.py:17
  160.2 2.4 %fusion.12 = f32[256,2048]{1,0:T(8,128)S(1)} fusion(bf16[256,512]{0,1:T(8,128)(2,1)S(1)} %bitcast.129, bf16[2048,1536]{1,0:T(8,128)(2,1)} %constant_dynamic-update-slice_fusion.11, s32[]{:T(128)S(6)} %select_n.220), kind=kOutput, calls=%fused_computation.15 | convolution fusion | flops 536870912 | bytes 4456452 | tf_op jit(solution)/shard_map/dot_general | solution.py:185
  162.5 2.4 %add_add_fusion.1 = f32[256,2048]{1,0:T(8,128)S(1)} fusion(f32[256,2048]{1,0:T(8,128)S(1)} %fusion.16, f32[256,2048]{1,0:T(8,128)S(1)} %fusion.12, bf16[256,512]{0,1:T(8,128)(2,1)S(1)} %bitcast.130, bf16[2048,1536]{1,0:T(8,128)(2,1)} %constant_dynamic-update-slice_fusion.11, s32[]{:T(128)S(6)} %select_n.234), kind=kOutput, calls=%fused_computation.5 | convolution fusion | flops 537919488 | bytes 8650756 | tf_op jit(solution)/shard_map/dot_general | solution.py:185
  165.7 2.8 %add_convert_fusion = bf16[256,2048]{1,0:T(8,128)(2,1)} fusion(f32[256,2048]{1,0:T(8,128)S(1)} %add_add_fusion.1, f32[256,2048]{1,0:T(8,128)} %collective-permute-done.25), kind=kLoop, calls=%fused_computation.3 | loop fusion | flops 1048576 | bytes 5242880 | tf_op jit(solution)/shard_map/convert_element_type | solution.py:190
  (122 shorter events, 44.8 us)
Async XLA Ops:
  3.6 9.6 %copy-start = (bf16[256,2048]{1,0:T(8,128)(2,1)S(1)}, bf16[256,2048]{1,0:T(8,128)(2,1)}, u32[]{:S(2)}) copy-start(bf16[256,2048]{1,0:T(8,128)(2,1)} %param.10) | copy-start | bytes 3145732
  3.6 2.9 %collective-permute-start.1 = (bf16[128,1536]{1,0:T(8,128)(2,1)}, bf16[128,1536]{1,0:T(8,128)(2,1)}, u32[]{:S(2)}, u32[]{:S(2)}) collective-permute-start(bf16[128,1536]{1,0:T(8,128)(2,1)} %pad_maximum_fusion.6), channel_id=1, source_target_pairs={{0,1},{1,0},{2,3},{3,2},{4,5},{5,4},{6,7},{7,6},{8,9},{9,8},{10,11... | collective-permute-start | bytes 1179656 | tf_op jit(solution)/shard_map/ppermute | solution.py:17
  6.2 101.1 %collective-permute-start.20 = (bf16[256,512]{0,1:T(8,128)(2,1)}, bf16[256,512]{0,1:T(8,128)(2,1)S(1)}, u32[]{:S(2)}, u32[]{:S(2)}) collective-permute-start(bf16[256,512]{0,1:T(8,128)(2,1)} %get-tuple-element.41), channel_id=1, source_target_pairs={{0,1},{1,0},{2,3},{3,2},{4,5},{5,4},{6,7},{7,6},{8,9},{9,8},{10,11... | collective-permute-start | bytes 786440 | tf_op jit(solution)/shard_map/ppermute | solution.py:17
  6.4 10.3 %copy-start.4 = (s32[1,2,2]{2,1,0:T(2,128)S(1)}, s32[1,2,2]{2,1,0:T(2,128)}, u32[]{:S(2)}) copy-start(s32[1,2,2]{2,1,0:T(2,128)} %param.15) | copy-start | bytes 52
  6.4 10.3 %copy-start.5 = (s32[8]{0:T(128)S(1)}, s32[8]{0:T(128)}, u32[]{:S(2)}) copy-start(s32[8]{0:T(128)} %constant.121.clone) | copy-start | bytes 100
  6.4 16.0 %copy-start.3 = (s32[8]{0:T(128)S(1)}, s32[8]{0:T(128)}, u32[]{:S(2)}) copy-start(s32[8]{0:T(128)} %constant.120.clone) | copy-start | bytes 100
  11.7 17.1 %collective-permute-start.2 = (bf16[256,1024]{1,0:T(8,128)(2,1)}, bf16[256,1024]{1,0:T(8,128)(2,1)S(1)}, u32[]{:S(2)}, u32[]{:S(2)}) collective-permute-start(bf16[256,1024]{1,0:T(8,128)(2,1)} %get-tuple-element.25), channel_id=1, source_target_pairs={{0,4},{4,8},{8,12},{12,14},{14,10},{10,6},{6,2},{2,0},{1,5},{5,9},... | collective-permute-start | bytes 1572872 | tf_op jit(solution)/shard_map/ppermute | solution.py:47
  11.8 18.2 %collective-permute-start.4 = (bf16[256,1024]{1,0:T(8,128)(2,1)}, bf16[256,1024]{1,0:T(8,128)(2,1)S(1)}, u32[]{:S(2)}, u32[]{:S(2)}) collective-permute-start(bf16[256,1024]{1,0:T(8,128)(2,1)} %get-tuple-element.25), channel_id=1, source_target_pairs={{0,2},{4,0},{8,4},{12,8},{14,12},{10,14},{6,10},{2,6},{1,3},{5,1},... | collective-permute-start | bytes 1572872 | tf_op jit(solution)/shard_map/ppermute | solution.py:50
  15.7 56.3 %collective-permute-start = (bf16[256,2048]{1,0:T(8,128)(2,1)}, bf16[256,2048]{1,0:T(8,128)(2,1)}, u32[]{:S(2)}, u32[]{:S(2)}) collective-permute-start(bf16[256,2048]{1,0:T(8,128)(2,1)} %add_convert_fusion.1), channel_id=1, source_target_pairs={{0,1},{1,0},{2,3},{3,2},{4,5},{5,4},{6,7},{7,6},{8,9},{9,8},{10,11... | collective-permute-start | bytes 3145736 | tf_op jit(solution)/shard_map/ppermute | solution.py:17
  16.7 11.5 %collective-permute-start.16 = (s32[2,2]{1,0:T(2,128)S(1)}, s32[2,2]{1,0:T(2,128)S(1)}, u32[]{:S(2)}, u32[]{:S(2)}) collective-permute-start(s32[2,2]{1,0:T(2,128)S(1)} %bitcast.137), channel_id=1, source_target_pairs={{0,1},{1,0},{2,3},{3,2},{4,5},{5,4},{6,7},{7,6},{8,9},{9,8},{10,11... | collective-permute-start | bytes 56 | tf_op jit(solution)/shard_map/ppermute | solution.py:17
  28.8 7.4 %collective-permute-start.3 = (bf16[256,512]{1,0:T(8,128)(2,1)S(1)}, bf16[256,512]{1,0:T(8,128)(2,1)S(1)}, u32[]{:S(2)}, u32[]{:S(2)}) collective-permute-start(bf16[256,512]{1,0:T(8,128)(2,1)S(1)} %constant_dynamic-slice_fusion.6), channel_id=1, source_target_pairs={{0,16},{16,0},{1,17},{17,1},{2,18},{18,2},{3,19},{19,3},{4,20},{20... | collective-permute-start | bytes 786440 | tf_op jit(solution)/shard_map/ppermute | solution.py:41
  29.1 12.7 %collective-permute-start.6 = (bf16[256,1024]{1,0:T(8,128)(2,1)S(1)}, bf16[256,1024]{1,0:T(8,128)(2,1)S(1)}, u32[]{:S(2)}, u32[]{:S(2)}) collective-permute-start(bf16[256,1024]{1,0:T(8,128)(2,1)S(1)} %collective-permute-done.2), channel_id=1, source_target_pairs={{0,4},{4,8},{8,12},{12,14},{14,10},{10,6},{6,2},{2,0},{1,5},{5,9},... | collective-permute-start | bytes 1572872 | tf_op jit(solution)/shard_map/ppermute | solution.py:47
  30.1 14.0 %collective-permute-start.8 = (bf16[256,1024]{1,0:T(8,128)(2,1)S(1)}, bf16[256,1024]{1,0:T(8,128)(2,1)S(1)}, u32[]{:S(2)}, u32[]{:S(2)}) collective-permute-start(bf16[256,1024]{1,0:T(8,128)(2,1)S(1)} %collective-permute-done.4), channel_id=1, source_target_pairs={{0,2},{4,0},{8,4},{12,8},{14,12},{10,14},{6,10},{2,6},{1,3},{5,1},... | collective-permute-start | bytes 1572872 | tf_op jit(solution)/shard_map/ppermute | solution.py:50
  36.2 6.9 %collective-permute-start.5 = (bf16[256,512]{1,0:T(8,128)(2,1)S(1)}, bf16[256,512]{1,0:T(8,128)(2,1)S(1)}, u32[]{:S(2)}, u32[]{:S(2)}) collective-permute-start(bf16[256,512]{1,0:T(8,128)(2,1)S(1)} %constant_dynamic-slice_fusion.5), channel_id=1, source_target_pairs={{0,16},{16,0},{1,17},{17,1},{2,18},{18,2},{3,19},{19,3},{4,20},{20... | collective-permute-start | bytes 786440 | tf_op jit(solution)/shard_map/ppermute | solution.py:41
  41.8 6.2 %collective-permute-start.7 = (bf16[256,512]{1,0:T(8,128)(2,1)S(1)}, bf16[256,512]{1,0:T(8,128)(2,1)S(1)}, u32[]{:S(2)}, u32[]{:S(2)}) collective-permute-start(bf16[256,512]{1,0:T(8,128)(2,1)S(1)} %constant_dynamic-slice_fusion.4), channel_id=1, source_target_pairs={{0,16},{16,0},{1,17},{17,1},{2,18},{18,2},{3,19},{19,3},{4,20},{20... | collective-permute-start | bytes 786440 | tf_op jit(solution)/shard_map/ppermute | solution.py:41
  43.1 11.5 %collective-permute-start.10 = (bf16[256,1024]{1,0:T(8,128)(2,1)S(1)}, bf16[256,1024]{1,0:T(8,128)(2,1)S(1)}, u32[]{:S(2)}, u32[]{:S(2)}) collective-permute-start(bf16[256,1024]{1,0:T(8,128)(2,1)S(1)} %collective-permute-done.6), channel_id=1, source_target_pairs={{0,4},{4,8},{8,12},{12,14},{14,10},{10,6},{6,2},{2,0},{1,5},{5,9},... | collective-permute-start | bytes 1572872 | tf_op jit(solution)/shard_map/ppermute | solution.py:47
  44.0 11.8 %collective-permute-start.12 = (bf16[256,1024]{1,0:T(8,128)(2,1)S(1)}, bf16[256,1024]{1,0:T(8,128)(2,1)S(1)}, u32[]{:S(2)}, u32[]{:S(2)}) collective-permute-start(bf16[256,1024]{1,0:T(8,128)(2,1)S(1)} %collective-permute-done.8), channel_id=1, source_target_pairs={{0,2},{4,0},{8,4},{12,8},{14,12},{10,14},{6,10},{2,6},{1,3},{5,1},... | collective-permute-start | bytes 1572872 | tf_op jit(solution)/shard_map/ppermute | solution.py:50
  48.0 6.8 %collective-permute-start.9 = (bf16[256,512]{1,0:T(8,128)(2,1)S(1)}, bf16[256,512]{1,0:T(8,128)(2,1)S(1)}, u32[]{:S(2)}, u32[]{:S(2)}) collective-permute-start(bf16[256,512]{1,0:T(8,128)(2,1)S(1)} %constant_dynamic-slice_fusion.3), channel_id=1, source_target_pairs={{0,16},{16,0},{1,17},{17,1},{2,18},{18,2},{3,19},{19,3},{4,20},{20... | collective-permute-start | bytes 786440 | tf_op jit(solution)/shard_map/ppermute | solution.py:41
  54.6 10.5 %collective-permute-start.14 = (bf16[256,1024]{1,0:T(8,128)(2,1)S(1)}, bf16[256,1024]{1,0:T(8,128)(2,1)S(1)}, u32[]{:S(2)}, u32[]{:S(2)}) collective-permute-start(bf16[256,1024]{1,0:T(8,128)(2,1)S(1)} %collective-permute-done.10), channel_id=1, source_target_pairs={{0,4},{4,8},{8,12},{12,14},{14,10},{10,6},{6,2},{2,0},{1,5},{5,9},... | collective-permute-start | bytes 1572872 | tf_op jit(solution)/shard_map/ppermute | solution.py:47
  54.8 5.3 %collective-permute-start.11 = (bf16[256,512]{1,0:T(8,128)(2,1)S(1)}, bf16[256,512]{1,0:T(8,128)(2,1)S(1)}, u32[]{:S(2)}, u32[]{:S(2)}) collective-permute-start(bf16[256,512]{1,0:T(8,128)(2,1)S(1)} %constant_dynamic-slice_fusion.2), channel_id=1, source_target_pairs={{0,16},{16,0},{1,17},{17,1},{2,18},{18,2},{3,19},{19,3},{4,20},{20... | collective-permute-start | bytes 786440 | tf_op jit(solution)/shard_map/ppermute | solution.py:41
  55.9 10.5 %collective-permute-start.13 = (bf16[256,512]{1,0:T(8,128)(2,1)S(1)}, bf16[256,512]{1,0:T(8,128)(2,1)S(1)}, u32[]{:S(2)}, u32[]{:S(2)}) collective-permute-start(bf16[256,512]{1,0:T(8,128)(2,1)S(1)} %constant_dynamic-slice_fusion.1), channel_id=1, source_target_pairs={{0,16},{16,0},{1,17},{17,1},{2,18},{18,2},{3,19},{19,3},{4,20},{20... | collective-permute-start | bytes 786440 | tf_op jit(solution)/shard_map/ppermute | solution.py:41
  65.1 6.2 %collective-permute-start.15 = (bf16[256,512]{1,0:T(8,128)(2,1)S(1)}, bf16[256,512]{1,0:T(8,128)(2,1)S(1)}, u32[]{:S(2)}, u32[]{:S(2)}) collective-permute-start(bf16[256,512]{1,0:T(8,128)(2,1)S(1)} %constant_dynamic-slice_fusion), channel_id=1, source_target_pairs={{0,16},{16,0},{1,17},{17,1},{2,18},{18,2},{3,19},{19,3},{4,20},{20... | collective-permute-start | bytes 786440 | tf_op jit(solution)/shard_map/ppermute | solution.py:41
  79.7 10.6 %collective-permute-start.17 = (f32[4,128,128]{2,1,0:T(8,128)}, f32[4,128,128]{2,1,0:T(8,128)S(1)}, u32[]{:S(2)}, u32[]{:S(2)}) collective-permute-start(f32[4,128,128]{2,1,0:T(8,128)} %fusion.43), channel_id=1, source_target_pairs={{0,2},{2,4},{4,6},{6,8},{8,10},{10,12},{12,14},{1,3},{3,5},{5,7},{... | collective-permute-start | bytes 786440 | tf_op jit(solution)/shard_map/ppermute | solution.py:66
  86.4 7.0 %copy-start.2 = (pred[2,256,256]{2,1,0:T(8,128)(4,1)S(1)}, pred[2,256,256]{2,1,0:T(8,128)(4,1)}, u32[]{:S(2)}) copy-start(pred[2,256,256]{2,1,0:T(8,128)(4,1)} %broadcast_and_fusion) | copy-start | bytes 393220
  90.4 7.1 %collective-permute-start.18 = (f32[4,128,128]{2,1,0:T(8,128)S(1)}, f32[4,128,128]{2,1,0:T(8,128)S(1)}, u32[]{:S(2)}, u32[]{:S(2)}) collective-permute-start(f32[4,128,128]{2,1,0:T(8,128)S(1)} %fusion.90), channel_id=1, source_target_pairs={{0,4},{2,6},{4,8},{6,10},{8,12},{10,14},{1,5},{3,7},{5,9},{7,11},{... | collective-permute-start | bytes 786440 | tf_op jit(solution)/shard_map/ppermute | solution.py:66
  97.6 9.3 %collective-permute-start.19 = (f32[4,128,128]{2,1,0:T(8,128)S(1)}, f32[4,128,128]{2,1,0:T(8,128)S(1)}, u32[]{:S(2)}, u32[]{:S(2)}) collective-permute-start(f32[4,128,128]{2,1,0:T(8,128)S(1)} %add.283), channel_id=1, source_target_pairs={{0,8},{2,10},{4,12},{6,14},{1,9},{3,11},{5,13},{7,15},{16,24},{18,... | collective-permute-start | bytes 786440 | tf_op jit(solution)/shard_map/ppermute | solution.py:66
  109.8 8.0 %collective-permute-start.21 = (f32[4,128,128]{2,1,0:T(8,128)S(1)}, f32[4,128,128]{2,1,0:T(8,128)S(1)}, u32[]{:S(2)}, u32[]{:S(2)}) collective-permute-start(f32[4,128,128]{2,1,0:T(8,128)S(1)} %fusion.44), channel_id=1, source_target_pairs={{2,0},{4,2},{6,4},{8,6},{10,8},{12,10},{14,12},{3,1},{5,3},{7,5},{... | collective-permute-start | bytes 786440 | tf_op jit(solution)/shard_map/ppermute | solution.py:66
  117.9 9.8 %collective-permute-start.22 = (f32[4,128,128]{2,1,0:T(8,128)S(1)}, f32[4,128,128]{2,1,0:T(8,128)S(1)}, u32[]{:S(2)}, u32[]{:S(2)}) collective-permute-start(f32[4,128,128]{2,1,0:T(8,128)S(1)} %fusion.89), channel_id=1, source_target_pairs={{4,0},{6,2},{8,4},{10,6},{12,8},{14,10},{5,1},{7,3},{9,5},{11,7},{... | collective-permute-start | bytes 786440 | tf_op jit(solution)/shard_map/ppermute | solution.py:66
  127.7 8.6 %collective-permute-start.23 = (f32[4,128,128]{2,1,0:T(8,128)S(1)}, f32[4,128,128]{2,1,0:T(8,128)S(1)}, u32[]{:S(2)}, u32[]{:S(2)}) collective-permute-start(f32[4,128,128]{2,1,0:T(8,128)S(1)} %add.295), channel_id=1, source_target_pairs={{8,0},{10,2},{12,4},{14,6},{9,1},{11,3},{13,5},{15,7},{24,16},{26,... | collective-permute-start | bytes 786440 | tf_op jit(solution)/shard_map/ppermute | solution.py:66
  137.6 22.4 %copy-start.1 = (bf16[1,256,4,128]{1,3,2,0:T(8,128)(2,1)S(1)}, bf16[1,256,4,128]{1,3,2,0:T(8,128)(2,1)}, u32[]{:S(2)}) copy-start(bf16[1,256,4,128]{1,3,2,0:T(8,128)(2,1)} %get-tuple-element.42) | copy-start | bytes 786436
  143.8 21.9 %collective-permute-start.25 = (f32[256,2048]{1,0:T(8,128)}, f32[256,2048]{1,0:T(8,128)}, u32[]{:S(2)}, u32[]{:S(2)}) collective-permute-start(f32[256,2048]{1,0:T(8,128)} %add_add_fusion), channel_id=1, source_target_pairs={{0,1},{1,0},{2,3},{3,2},{4,5},{5,4},{6,7},{7,6},{8,9},{9,8},{10,11... | collective-permute-start | bytes 6291464 | tf_op jit(solution)/shard_map/ppermute | solution.py:17
  160.1 4.9 %collective-permute-start.24 = (bf16[256,512]{1,0:T(8,128)(2,1)S(1)}, bf16[256,512]{1,0:T(8,128)(2,1)S(1)}, u32[]{:S(2)}, u32[]{:S(2)}) collective-permute-start(bf16[256,512]{1,0:T(8,128)(2,1)S(1)} %copy.48), channel_id=1, source_target_pairs={{0,1},{1,0},{2,3},{3,2},{4,5},{5,4},{6,7},{7,6},{8,9},{9,8},{10,11... | collective-permute-start | bytes 786440 | tf_op jit(solution)/shard_map/ppermute | solution.py:17
